TPU v7x, 256 devices: a whole 4x4x8 slice. The times are simulated.
256 devices in a mesh: section: 8 (over x, core), dp: 32 (over y, z).
Axes of the slice: x: 4, y: 4, z: 8, core: 2. Of those that a mesh axis runs over, the one named last changes fastest.
Arguments:
- resid_in: bfloat16 [4, 1024, 2048], P(None, 'dp'), may hold values from -10 to 10
- dest_row: int32 [4, 1024], replicated, may hold values from 0 to 1023, as said below
- doc_ids: int32 [4, 1024], P(None, 'dp'), may hold values from 0 to 1023, as said below
- cotangent: bfloat16 [4, 1024, 2048], P(None, 'dp'), may hold values from -0.119628906 to 0.119628906
- gain: float32 [8, 2048], P('section'), may hold values from 0.5 to 1.5
- steer: float32 [8, 2048], P('section'), may hold values from -3 to 3
- w_query: bfloat16 [8, 2048, 1024], P('section', 'dp'), may hold values from -1 to 1
- w_keyval: bfloat16 [8, 2048, 512], P('section', 'dp'), may hold values from -1 to 1
- w_out: bfloat16 [8, 1024, 2048], P('section', None, 'dp'), may hold values from -0.1875 to 0.1875
Outputs:
- hidden_out: bfloat16 [8, 4, 1024, 2048], P('section', None, 'dp')
- grad_steer: float32 [8, 2048], P('section')
Inputs may be any that keep to these rules, and one draw needn't show every extreme that they name: Each row of dest_row is a permutation of 0 to 1023. Counting the tokens of one aligned block of 32 input tokens that go to one aligned block of 32 packed rows, no count exceeds 2, and some reach it in every micro-batch. doc_ids never falls along a row; every value is a row index r at which doc_ids equals r; each aligned block of 32 rows begins a document, so no document crosses such a block.
All inputs are finite; a program needn't handle non-finite values.
Results may differ from a plain program's by a relative error of at most 0.02.
Values may be sent and summed in bfloat16 or wider, within the bound.
No kernel may reach another device: no remote copies, remote signals or barrier semaphores. Data moves between devices by JAX's collectives and lax.ppermute only.
A program may use at most 64 MiB of HBM per device.

v0:
```python
import jax
import jax.numpy as jnp
from jax import lax
from jax.sharding import PartitionSpec as P

HD = 64


ROPE_BASE = 500000.0
EPSILON = 1e-05
MASKED = -1e30


def shifted(block, axis, distance):
    devices = range(lax.axis_size(axis))
    route = [(i - distance, i) for i in devices if i - distance in devices]
    return lax.ppermute(block, axis, route)


def rotate(values, positions):
    half_size = values.shape[-1] // 2
    freq_index = jnp.arange(half_size, dtype=jnp.float32)
    inverse = ROPE_BASE ** (-2.0 * freq_index / values.shape[-1])
    angles = positions.astype(jnp.float32)[:, None] * inverse[None, :]
    cosine = jnp.cos(angles)[:, None, :]
    sine_part = jnp.sin(angles)[:, None, :]
    first_half = values[..., :half_size]
    second = values[..., half_size:]
    return jnp.concatenate(
        [first_half * cosine - second * sine_part, second * cosine + first_half * sine_part],
        axis=-1,
    )


def layer(hidden_in, steering, gain_row, w_query, w_keyval, w_out, positions, documents):
    row_count = hidden_in.shape[0]
    head_size = HD
    kv_heads = w_keyval.shape[1] // (2 * head_size)
    query_heads = w_query.shape[1] // head_size
    group_size = query_heads // kv_heads
    residual = hidden_in.astype(jnp.float32) + steering
    normed = (
        residual
        * lax.rsqrt(jnp.mean(residual * residual, axis=-1, keepdims=True) + EPSILON)
        * gain_row
    ).astype(jnp.bfloat16)
    queries = jnp.dot(normed, w_query, preferred_element_type=jnp.float32).reshape(
        row_count, query_heads, head_size
    )
    keyval = jnp.dot(normed, w_keyval, preferred_element_type=jnp.float32)
    key_rows = rotate(
        keyval[:, : kv_heads * head_size].reshape(row_count, kv_heads, head_size), positions
    ).astype(jnp.bfloat16)
    values = (
        keyval[:, kv_heads * head_size :]
        .reshape(row_count, kv_heads, head_size)
        .astype(jnp.bfloat16)
    )
    queries = (
        rotate(queries, positions)
        .astype(jnp.bfloat16)
        .reshape(row_count, kv_heads, group_size, head_size)
    )
    scores = jnp.einsum(
        "rkgd,skd->kgrs", queries, key_rows, preferred_element_type=jnp.float32
    ) * head_size ** (-0.5)
    row_index = jnp.arange(row_count)
    allowed = (documents[:, None] == documents[None, :]) & (
        row_index[:, None] >= row_index[None, :]
    )
    scores = jnp.where(allowed[None, None], scores, MASKED)
    peak = jnp.max(scores, axis=-1, keepdims=True)
    weights = jnp.exp(scores - peak)
    weights = (weights / jnp.sum(weights, axis=-1, keepdims=True)).astype(jnp.bfloat16)
    mixed_heads = jnp.einsum(
        "kgrs,skd->rkgd", weights, values, preferred_element_type=jnp.float32
    ).astype(jnp.bfloat16)
    mixed_heads = mixed_heads.reshape(row_count, query_heads * head_size)
    return (residual + jnp.dot(mixed_heads, w_out, preferred_element_type=jnp.float32)).astype(
        jnp.bfloat16
    )


def plan_slots(target, device, row_count, capacity, dp_count):
    target_grid = target.reshape(dp_count, row_count)
    target_dev = target_grid // row_count
    target_off = target_grid % row_count
    row_order = jnp.arange(row_count, dtype=jnp.int32)
    matching = target_dev[:, :, None] == target_dev[:, None, :]
    earlier = row_order[None, :] < row_order[:, None]
    rank_ids = jnp.sum((matching & earlier[None]).astype(jnp.int32), axis=2)
    slot_ids = target_dev * capacity + rank_ids
    own_slot = lax.dynamic_index_in_dim(slot_ids, device, 0, keepdims=False)
    column_ids = jnp.arange(dp_count, dtype=jnp.int32)[:, None] * capacity + rank_ids
    landing = (target_dev == device)[None] & (target_off[None] == row_order[:, None, None])
    source_col = jnp.sum(jnp.where(landing, column_ids[None], 0), axis=(1, 2))
    return (own_slot, source_col)


def pack_rows(source_rows, own_slot, slot_count):
    selector = (jnp.arange(slot_count, dtype=jnp.int32)[:, None] == own_slot[None, :]).astype(
        jnp.bfloat16
    )
    return jnp.dot(selector, source_rows, preferred_element_type=jnp.float32).astype(jnp.bfloat16)


def unpack_rows(arrived, source_col):
    selector = (
        source_col[:, None] == jnp.arange(arrived.shape[0], dtype=jnp.int32)[None, :]
    ).astype(jnp.bfloat16)
    return jnp.dot(selector, arrived, preferred_element_type=jnp.float32).astype(jnp.bfloat16)


def body(resid_in, dest_row, doc_ids, cotangent, gain, steer, w_query, w_keyval, w_out):
    dp_count = lax.axis_size("dp")
    section_count = lax.axis_size("section")
    device = lax.axis_index("dp")
    section_idx = lax.axis_index("section")
    micro_count, row_count, width = resid_in.shape
    capacity = row_count // dp_count + 1
    slot_count = dp_count * capacity
    full_query, full_keyval, full_out = (
        lax.all_gather(w_query[0], "dp", axis=0, tiled=True),
        lax.all_gather(w_keyval[0], "dp", axis=0, tiled=True),
        lax.all_gather(w_out[0], "dp", axis=1, tiled=True),
    )
    gain_row = gain[0]
    steering = steer[0]
    plans = [
        plan_slots(dest_row[micro_idx], device, row_count, capacity, dp_count)
        for micro_idx in range(micro_count)
    ]
    pieces = []
    for micro_idx in range(micro_count):
        packed = pack_rows(resid_in[micro_idx], plans[micro_idx][0], slot_count).reshape(
            dp_count, capacity, width
        )
        arrived = lax.all_to_all(packed, "dp", split_axis=0, concat_axis=0, tiled=True)
        pieces.append(unpack_rows(arrived.reshape(slot_count, width), plans[micro_idx][1]))
    grouped = jnp.stack(pieces)
    global_rows = device * row_count + jnp.arange(row_count, dtype=jnp.int32)
    position_table = global_rows[None, :] - doc_ids

    def run_layer(hidden_in, steer_vec, positions, documents):
        return layer(
            hidden_in, steer_vec, gain_row, full_query, full_keyval, full_out, positions, documents
        )

    zero_block = jnp.zeros((row_count, width), jnp.bfloat16)
    step_count = micro_count + section_count - 1

    def forward_step(carry, step_idx):
        incoming, kept, produced = carry
        micro_idx = step_idx - section_idx
        active = (micro_idx >= 0) & (micro_idx < micro_count)
        chosen = jnp.clip(micro_idx, 0, micro_count - 1)
        first_in = lax.dynamic_index_in_dim(grouped, chosen, 0, keepdims=False)
        hidden_in = jnp.where(section_idx == 0, first_in, incoming)
        positions = lax.dynamic_index_in_dim(position_table, chosen, 0, keepdims=False)
        documents = lax.dynamic_index_in_dim(doc_ids, chosen, 0, keepdims=False)
        hidden_new = lax.cond(
            active, lambda: run_layer(hidden_in, steering, positions, documents), lambda: zero_block
        )
        old_kept = lax.dynamic_index_in_dim(kept, chosen, 0, keepdims=False)
        kept = lax.dynamic_update_index_in_dim(
            kept, jnp.where(active, hidden_in, old_kept), chosen, 0
        )
        old_out = lax.dynamic_index_in_dim(produced, chosen, 0, keepdims=False)
        produced = lax.dynamic_update_index_in_dim(
            produced, jnp.where(active, hidden_new, old_out), chosen, 0
        )
        sent = shifted(hidden_new, "section", 1)
        return ((sent, kept, produced), None)

    empty_stack = jnp.zeros((micro_count, row_count, width), jnp.bfloat16)
    (unused_in, kept, produced), unused_ys = lax.scan(
        forward_step,
        (zero_block, empty_stack, empty_stack),
        jnp.arange(step_count, dtype=jnp.int32),
    )

    def backward_step(carry, step_idx):
        incoming, grad_sum = carry
        micro_idx = step_idx - (section_count - 1 - section_idx)
        active = (micro_idx >= 0) & (micro_idx < micro_count)
        chosen = jnp.clip(micro_idx, 0, micro_count - 1)
        last_in = lax.dynamic_index_in_dim(cotangent, chosen, 0, keepdims=False)
        upstream = jnp.where(section_idx == section_count - 1, last_in, incoming)
        positions = lax.dynamic_index_in_dim(position_table, chosen, 0, keepdims=False)
        documents = lax.dynamic_index_in_dim(doc_ids, chosen, 0, keepdims=False)
        saved_in = lax.dynamic_index_in_dim(kept, chosen, 0, keepdims=False)

        def differentiate():

            def local(hidden_in, steer_vec):
                return run_layer(hidden_in, steer_vec, positions, documents)

            unused_out, pullback = jax.vjp(local, saved_in, steering)
            return pullback(upstream)

        grad_in, steer_part = lax.cond(
            active, differentiate, lambda: (zero_block, jnp.zeros_like(steering))
        )
        sent = shifted(grad_in, "section", -1)
        return ((sent, grad_sum + steer_part), None)

    (unused_grad, grad_sum), unused_zs = lax.scan(
        backward_step,
        (zero_block, jnp.zeros_like(steering)),
        jnp.arange(step_count, dtype=jnp.int32),
    )
    total = lax.psum(grad_sum, "dp")
    return (produced[None], total[None])


def solution(mesh):
    in_specs = (
        P(None, "dp", None),
        P(),
        P(None, "dp"),
        P(None, "dp", None),
        P("section", None),
        P("section", None),
        P("section", "dp", None),
        P("section", "dp", None),
        P("section", None, "dp"),
    )
    out_specs = (P("section", None, "dp", None), P("section", None))
    return jax.shard_map(body, mesh=mesh, in_specs=in_specs, out_specs=out_specs, check_vma=False)
```

profile of v0, /device:TPU:32, one launch (start us, length us, event | category | flops | bytes accessed | tf_op | source)
XLA Modules:
  0.0 934.6 jit_solution(14943596170563933842)
XLA Ops:
  15.6 11.4 %all-to-all-start = ((bf16[32,2,2048]{2,1,0:T(2,128)(2,1)}), bf16[32,2,2048]{2,1,0:T(2,128)(2,1)S(1)}, u32[]{:S(2)}, u32[]{:S(2)}) async-start(bf16[32,2,2048]{2,1,0:T(2,128)(2,1)} %reshape.889), calls=%async_computation | async-start | bytes 524288 | tf_op jit(solution)/shard_map/all_to_all | solution.py:138
  30.9 10.0 %all-to-all-done = bf16[32,2,2048]{2,1,0:T(2,128)(2,1)S(1)} async-done(((bf16[32,2,2048]{2,1,0:T(2,128)(2,1)}), bf16[32,2,2048]{2,1,0:T(2,128)(2,1)S(1)}, u32[]{:S(2)}, u32[]{:S(2)}) %all-to-all-start) | async-done | bytes 262176 | tf_op jit(solution)/shard_map/all_to_all | solution.py:138
  41.0 4.7 all-to-all-start.1
  47.7 10.3 %all-to-all-done.1 = bf16[32,2,2048]{2,1,0:T(2,128)(2,1)S(1)} async-done(((bf16[32,2,2048]{2,1,0:T(2,128)(2,1)}), bf16[32,2,2048]{2,1,0:T(2,128)(2,1)S(1)}, u32[]{:S(2)}, u32[]{:S(2)}) %all-to-all-start.1) | async-done | bytes 262176 | tf_op jit(solution)/shard_map/all_to_all | solution.py:138
  58.0 4.5 all-to-all-start.2
  64.0 11.6 %all-to-all-done.2 = bf16[32,2,2048]{2,1,0:T(2,128)(2,1)S(1)} async-done(((bf16[32,2,2048]{2,1,0:T(2,128)(2,1)}), bf16[32,2,2048]{2,1,0:T(2,128)(2,1)S(1)}, u32[]{:S(2)}, u32[]{:S(2)}) %all-to-all-start.2) | async-done | bytes 262176 | tf_op jit(solution)/shard_map/all_to_all | solution.py:138
  75.6 5.4 all-to-all-start.3
  84.0 10.1 %all-to-all-done.3 = bf16[32,2,2048]{2,1,0:T(2,128)(2,1)S(1)} async-done(((bf16[32,2,2048]{2,1,0:T(2,128)(2,1)}), bf16[32,2,2048]{2,1,0:T(2,128)(2,1)S(1)}, u32[]{:S(2)}, u32[]{:S(2)}) %all-to-all-start.3) | async-done | bytes 262176 | tf_op jit(solution)/shard_map/all_to_all | solution.py:138
  95.1 5.9 all-gather.11.cloned.1.call-done
  101.1 6.5 copy.80
  107.6 75.1 %all-gather.9.cloned.1.call-done = bf16[1,2048,1024]{2,1,0:T(8,128)(2,1)} async-done(((bf16[1,64,1024]{2,1,0:T(8,128)(2,1)}), bf16[1,2048,1024]{2,1,0:T(8,128)(2,1)}) %all-gather.9.cloned.1.call-update) | async-done | bytes 4194320 | tf_op jit(solution)/shard_map/all_gather | solution.py:123
  182.7 6.5 copy.82
  189.2 70.3 %all-gather.7.cloned.1.call-done = bf16[1,2048,512]{2,1,0:T(8,128)(2,1)} async-done(((bf16[1,64,512]{2,1,0:T(8,128)(2,1)}), bf16[1,2048,512]{2,1,0:T(8,128)(2,1)}) %all-gather.7.cloned.1.call-update) | async-done | bytes 2097168 | tf_op jit(solution)/shard_map/all_gather | solution.py:124
  259.6 156.2 %while.30 = (s32[]{:T(128)}, bf16[32,2048]{1,0:T(8,128)(2,1)S(1)}, bf16[4,32,2048]{2,1,0:T(8,128)(2,1)S(1)}, bf16[4,32,2048]{2,1,0:T(8,128)(2,1)S(1)}, s32[11]{0...) while((s32[]{:T(128)}, bf16[32,2048]{1,0:T(8,128)(2,1)S(1)}, ...), condition=%wide.region_14.15_spmd, body=%wide.region_8.14_spmd.sunk | while | flops 343888544 | bytes 14992390 | solution.py:176
  261.0 11.3 %conditional.5 = (bf16[32,2048]{1,0:T(8,128)(2,1)S(1)}) conditional(s32[]{:T(128)} %convert_element_type.419, () %tuple.130, (bf16[32,2048]{1,0:T(8,128)(2,1)S(1)}, f32[1,2048]{1,0:T(1,128)S(1)}, f32[1,2048]{1,0:T(1,128)S(1)}, bf16[2048,512]{1,0:T(8,128)(2,1)}, s32[4,32]{1,0:T(4,128)}, /*index=5*/s32[]{:T(128)}, s32[4,32]{1,0:T(4,128)}, ...), branch_computations={%region_9.9_spmd, %region_10.13_spmd} | conditional | flops 343691936 | bytes 12894860 | solution.py:161
  275.9 11.3 %conditional.5 = (bf16[32,2048]{1,0:T(8,128)(2,1)S(1)}) conditional(s32[]{:T(128)} %convert_element_type.419, () %tuple.130, (bf16[32,2048]{1,0:T(8,128)(2,1)S(1)}, f32[1,2048]{1,0:T(1,128)S(1)}, f32[1,2048]{1,0:T(1,128)S(1)}, bf16[2048,512]{1,0:T(8,128)(2,1)}, s32[4,32]{1,0:T(4,128)}, /*index=5*/s32[]{:T(128)}, s32[4,32]{1,0:T(4,128)}, ...), branch_computations={%region_9.9_spmd, %region_10.13_spmd} | conditional | flops 343691936 | bytes 12894860 | solution.py:161
  291.8 11.3 %conditional.5 = (bf16[32,2048]{1,0:T(8,128)(2,1)S(1)}) conditional(s32[]{:T(128)} %convert_element_type.419, () %tuple.130, (bf16[32,2048]{1,0:T(8,128)(2,1)S(1)}, f32[1,2048]{1,0:T(1,128)S(1)}, f32[1,2048]{1,0:T(1,128)S(1)}, bf16[2048,512]{1,0:T(8,128)(2,1)}, s32[4,32]{1,0:T(4,128)}, /*index=5*/s32[]{:T(128)}, s32[4,32]{1,0:T(4,128)}, ...), branch_computations={%region_9.9_spmd, %region_10.13_spmd} | conditional | flops 343691936 | bytes 12894860 | solution.py:161
  308.3 11.3 %conditional.5 = (bf16[32,2048]{1,0:T(8,128)(2,1)S(1)}) conditional(s32[]{:T(128)} %convert_element_type.419, () %tuple.130, (bf16[32,2048]{1,0:T(8,128)(2,1)S(1)}, f32[1,2048]{1,0:T(1,128)S(1)}, f32[1,2048]{1,0:T(1,128)S(1)}, bf16[2048,512]{1,0:T(8,128)(2,1)}, s32[4,32]{1,0:T(4,128)}, /*index=5*/s32[]{:T(128)}, s32[4,32]{1,0:T(4,128)}, ...), branch_computations={%region_9.9_spmd, %region_10.13_spmd} | conditional | flops 343691936 | bytes 12894860 | solution.py:161
  319.7 5.3 collective-permute-start
  327.3 16.6 %collective-permute-start = (bf16[32,2048]{1,0:T(8,128)(2,1)S(1)}, bf16[32,2048]{1,0:T(8,128)(2,1)S(1)}, u32[]{:S(2)}, u32[]{:S(2)}) collective-permute-start(bf16[32,2048]{1,0:T(8,128)(2,1)S(1)} %get-tuple-element.1094), channel_id=1, source_target_pairs={{0,32},{32,64},{64,96},{96,128},{128,160},{160,192},{192,224},{1,3... | collective-permute-start | bytes 393224 | tf_op jit(solution)/shard_map/while/body/eval_jaxpr/ppermute | solution.py:17
  346.3 5.3 collective-permute-start
  353.9 16.6 %collective-permute-start = (bf16[32,2048]{1,0:T(8,128)(2,1)S(1)}, bf16[32,2048]{1,0:T(8,128)(2,1)S(1)}, u32[]{:S(2)}, u32[]{:S(2)}) collective-permute-start(bf16[32,2048]{1,0:T(8,128)(2,1)S(1)} %get-tuple-element.1094), channel_id=1, source_target_pairs={{0,32},{32,64},{64,96},{96,128},{128,160},{160,192},{192,224},{1,3... | collective-permute-start | bytes 393224 | tf_op jit(solution)/shard_map/while/body/eval_jaxpr/ppermute | solution.py:17
  372.9 5.3 collective-permute-start
  380.5 10.2 %collective-permute-start = (bf16[32,2048]{1,0:T(8,128)(2,1)S(1)}, bf16[32,2048]{1,0:T(8,128)(2,1)S(1)}, u32[]{:S(2)}, u32[]{:S(2)}) collective-permute-start(bf16[32,2048]{1,0:T(8,128)(2,1)S(1)} %get-tuple-element.1094), channel_id=1, source_target_pairs={{0,32},{32,64},{64,96},{96,128},{128,160},{160,192},{192,224},{1,3... | collective-permute-start | bytes 393224 | tf_op jit(solution)/shard_map/while/body/eval_jaxpr/ppermute | solution.py:17
  393.1 5.3 collective-permute-start
  400.7 14.2 %collective-permute-start = (bf16[32,2048]{1,0:T(8,128)(2,1)S(1)}, bf16[32,2048]{1,0:T(8,128)(2,1)S(1)}, u32[]{:S(2)}, u32[]{:S(2)}) collective-permute-start(bf16[32,2048]{1,0:T(8,128)(2,1)S(1)} %get-tuple-element.1094), channel_id=1, source_target_pairs={{0,32},{32,64},{64,96},{96,128},{128,160},{160,192},{192,224},{1,3... | collective-permute-start | bytes 393224 | tf_op jit(solution)/shard_map/while/body/eval_jaxpr/ppermute | solution.py:17
  416.7 438.7 %while.31 = (s32[]{:T(128)}, bf16[32,2048]{1,0:T(8,128)(2,1)S(1)}, f32[2048]{0:T(1024)}, s32[11]{0:T(128)}, s32[]{:T(128)}, /*index=5*/pred[]{:T(512)}, bf16[4,3...) while((s32[]{:T(128)}, bf16[32,2048]{1,0:T(8,128)(2,1)S(1)}, ...), condition=%wide.region_26.27_spmd.clone, body=%wide.region_15.26_spmd.clone.sunk | while | flops 551212288 | bytes 31677904 | solution.py:207
  421.1 4.4 collective-permute-done.1
  430.6 9.4 %collective-permute-done.1 = bf16[32,2048]{1,0:T(8,128)(2,1)S(1)} collective-permute-done((bf16[32,2048]{1,0:T(8,128)(2,1)}, bf16[32,2048]{1,0:T(8,128)(2,1)S(1)}, u32[]{:S(2)}, u32[]{:S(2)}) %collective-permute-start.1) | collective-permute-done | bytes 131104 | tf_op jit(solution)/shard_map/while/body/eval_jaxpr/ppermute | solution.py:17
  445.2 3.9 collective-permute-done.1
  454.1 13.3 %collective-permute-done.1 = bf16[32,2048]{1,0:T(8,128)(2,1)S(1)} collective-permute-done((bf16[32,2048]{1,0:T(8,128)(2,1)}, bf16[32,2048]{1,0:T(8,128)(2,1)S(1)}, u32[]{:S(2)}, u32[]{:S(2)}) %collective-permute-start.1) | collective-permute-done | bytes 131104 | tf_op jit(solution)/shard_map/while/body/eval_jaxpr/ppermute | solution.py:17
  472.5 3.9 collective-permute-done.1
  481.5 9.3 collective-permute-done.1
  495.9 207.9 %collective-permute-done.1 = bf16[32,2048]{1,0:T(8,128)(2,1)S(1)} collective-permute-done((bf16[32,2048]{1,0:T(8,128)(2,1)}, bf16[32,2048]{1,0:T(8,128)(2,1)S(1)}, u32[]{:S(2)}, u32[]{:S(2)}) %collective-permute-start.1) | collective-permute-done | bytes 131104 | tf_op jit(solution)/shard_map/while/body/eval_jaxpr/ppermute | solution.py:17
  705.6 30.4 %conditional.6 = (bf16[32,2048]{1,0:T(8,128)(2,1)}, f32[2048]{0:T(1024)S(1)}) conditional(s32[]{:T(128)} %convert_element_type.420, () %tuple.133, (pred[]{:T(512)}, s32[]{:T(128)}, bf16[4,32,2048]{2,1,0:T(8,128)(2,1)}, bf16[32,2048]{1,0:T(8,128)(2,1)S(1)}, bf16[1024,2048]{1,0:T(8,128)(2,1)}, /*index=5*/s32[4,32]{1,0:T(4,128)}, ...), branch_computations={%region_16.16_spmd, %region_17.25_spmd} | conditional | flops 551208192 | bytes 31128680 | solution.py:201
  709.0 4.2 fusion.70
  714.9 3.6 convolution_convert_fusion.5
  738.5 3.9 collective-permute-done.1
  744.2 30.4 %conditional.6 = (bf16[32,2048]{1,0:T(8,128)(2,1)}, f32[2048]{0:T(1024)S(1)}) conditional(s32[]{:T(128)} %convert_element_type.420, () %tuple.133, (pred[]{:T(512)}, s32[]{:T(128)}, bf16[4,32,2048]{2,1,0:T(8,128)(2,1)}, bf16[32,2048]{1,0:T(8,128)(2,1)S(1)}, bf16[1024,2048]{1,0:T(8,128)(2,1)}, /*index=5*/s32[4,32]{1,0:T(4,128)}, ...), branch_computations={%region_16.16_spmd, %region_17.25_spmd} | conditional | flops 551208192 | bytes 31128680 | solution.py:201
  747.7 4.2 fusion.70
  753.5 3.6 convolution_convert_fusion.5
  777.2 3.9 collective-permute-done.1
  782.9 30.4 %conditional.6 = (bf16[32,2048]{1,0:T(8,128)(2,1)}, f32[2048]{0:T(1024)S(1)}) conditional(s32[]{:T(128)} %convert_element_type.420, () %tuple.133, (pred[]{:T(512)}, s32[]{:T(128)}, bf16[4,32,2048]{2,1,0:T(8,128)(2,1)}, bf16[32,2048]{1,0:T(8,128)(2,1)S(1)}, bf16[1024,2048]{1,0:T(8,128)(2,1)}, /*index=5*/s32[4,32]{1,0:T(4,128)}, ...), branch_computations={%region_16.16_spmd, %region_17.25_spmd} | conditional | flops 551208192 | bytes 31128680 | solution.py:201
  786.3 4.2 fusion.70
  815.8 3.9 collective-permute-done.1
  821.5 30.4 %conditional.6 = (bf16[32,2048]{1,0:T(8,128)(2,1)}, f32[2048]{0:T(1024)S(1)}) conditional(s32[]{:T(128)} %convert_element_type.420, () %tuple.133, (pred[]{:T(512)}, s32[]{:T(128)}, bf16[4,32,2048]{2,1,0:T(8,128)(2,1)}, bf16[32,2048]{1,0:T(8,128)(2,1)S(1)}, bf16[1024,2048]{1,0:T(8,128)(2,1)}, /*index=5*/s32[4,32]{1,0:T(4,128)}, ...), branch_computations={%region_16.16_spmd, %region_17.25_spmd} | conditional | flops 551208192 | bytes 31128680 | solution.py:201
  825.0 4.2 fusion.70
  855.3 72.8 %psum.7 = f32[1,2048]{1,0:T(1,128)} all-reduce(f32[1,2048]{1,0:T(1,128)} %bitcast.272), channel_id=1, replica_groups=mesh['section'=8,'dp'=32] {'dp'}, use_global_device_ids=true, to_apply=%region_27.28 | all-reduce | flops 2048 | bytes 16384 | tf_op jit(solution)/shard_map/psum | solution.py:212
  (573 shorter events, 237.3 us)
Async XLA Ops:
  7.2 93.9 %all-gather.11.cloned.1.call-start = ((), (), s32[]{:S(2)}) async-start(), calls=%async_computation.6 | async-start | bytes 4325376 | tf_op jit(solution)/shard_map/all_gather | solution.py:125
  7.9 174.8 %all-gather.9.cloned.1.call-start = ((), (), s32[]{:S(2)}) async-start(), calls=%async_computation.5 | async-start | bytes 4325376 | tf_op jit(solution)/shard_map/all_gather | solution.py:123
  8.6 250.8 %all-gather.7.cloned.1.call-start = ((), (), s32[]{:S(2)}) async-start(), calls=%async_computation.4 | async-start | bytes 2162688 | tf_op jit(solution)/shard_map/all_gather | solution.py:124
  15.6 25.3 %all-to-all-start = ((bf16[32,2,2048]{2,1,0:T(2,128)(2,1)}), bf16[32,2,2048]{2,1,0:T(2,128)(2,1)S(1)}, u32[]{:S(2)}, u32[]{:S(2)}) async-start(bf16[32,2,2048]{2,1,0:T(2,128)(2,1)} %reshape.889), calls=%async_computation | async-start | bytes 524288 | tf_op jit(solution)/shard_map/all_to_all | solution.py:138
  41.0 17.0 %all-to-all-start.1 = ((bf16[32,2,2048]{2,1,0:T(2,128)(2,1)}), bf16[32,2,2048]{2,1,0:T(2,128)(2,1)S(1)}, u32[]{:S(2)}, u32[]{:S(2)}) async-start(bf16[32,2,2048]{2,1,0:T(2,128)(2,1)} %reshape.891), calls=%async_computation.1 | async-start | bytes 524288 | tf_op jit(solution)/shard_map/all_to_all | solution.py:138
  58.0 17.6 %all-to-all-start.2 = ((bf16[32,2,2048]{2,1,0:T(2,128)(2,1)}), bf16[32,2,2048]{2,1,0:T(2,128)(2,1)S(1)}, u32[]{:S(2)}, u32[]{:S(2)}) async-start(bf16[32,2,2048]{2,1,0:T(2,128)(2,1)} %reshape.893), calls=%async_computation.2 | async-start | bytes 524288 | tf_op jit(solution)/shard_map/all_to_all | solution.py:138
  75.6 18.4 %all-to-all-start.3 = ((bf16[32,2,2048]{2,1,0:T(2,128)(2,1)}), bf16[32,2,2048]{2,1,0:T(2,128)(2,1)S(1)}, u32[]{:S(2)}, u32[]{:S(2)}) async-start(bf16[32,2,2048]{2,1,0:T(2,128)(2,1)} %reshape.895), calls=%async_computation.3 | async-start | bytes 524288 | tf_op jit(solution)/shard_map/all_to_all | solution.py:138
  182.7 76.9 %copy-start.1 = (f32[1,2048]{1,0:T(1,128)S(1)}, f32[1,2048]{1,0:T(1,128)}, u32[]{:S(2)}) copy-start(f32[1,2048]{1,0:T(1,128)} %param.22) | copy-start | bytes 24580
  182.7 77.0 %copy-start.5 = (f32[1,2048]{1,0:T(1,128)S(1)}, f32[1,2048]{1,0:T(1,128)}, u32[]{:S(2)}) copy-start(f32[1,2048]{1,0:T(1,128)} %param.21) | copy-start | bytes 24580
  272.3 2.3 collective-permute-start
  287.2 3.2 collective-permute-start
  303.1 3.9 collective-permute-start
  319.7 6.3 collective-permute-start
  327.3 17.6 %collective-permute-start = (bf16[32,2048]{1,0:T(8,128)(2,1)S(1)}, bf16[32,2048]{1,0:T(8,128)(2,1)S(1)}, u32[]{:S(2)}, u32[]{:S(2)}) collective-permute-start(bf16[32,2048]{1,0:T(8,128)(2,1)S(1)} %get-tuple-element.1094), channel_id=1, source_target_pairs={{0,32},{32,64},{64,96},{96,128},{128,160},{160,192},{192,224},{1,3... | collective-permute-start | bytes 393224 | tf_op jit(solution)/shard_map/while/body/eval_jaxpr/ppermute | solution.py:17
  346.3 6.3 collective-permute-start
  353.9 17.6 %collective-permute-start = (bf16[32,2048]{1,0:T(8,128)(2,1)S(1)}, bf16[32,2048]{1,0:T(8,128)(2,1)S(1)}, u32[]{:S(2)}, u32[]{:S(2)}) collective-permute-start(bf16[32,2048]{1,0:T(8,128)(2,1)S(1)} %get-tuple-element.1094), channel_id=1, source_target_pairs={{0,32},{32,64},{64,96},{96,128},{128,160},{160,192},{192,224},{1,3... | collective-permute-start | bytes 393224 | tf_op jit(solution)/shard_map/while/body/eval_jaxpr/ppermute | solution.py:17
  372.9 6.3 collective-permute-start
  380.5 11.1 %collective-permute-start = (bf16[32,2048]{1,0:T(8,128)(2,1)S(1)}, bf16[32,2048]{1,0:T(8,128)(2,1)S(1)}, u32[]{:S(2)}, u32[]{:S(2)}) collective-permute-start(bf16[32,2048]{1,0:T(8,128)(2,1)S(1)} %get-tuple-element.1094), channel_id=1, source_target_pairs={{0,32},{32,64},{64,96},{96,128},{128,160},{160,192},{192,224},{1,3... | collective-permute-start | bytes 393224 | tf_op jit(solution)/shard_map/while/body/eval_jaxpr/ppermute | solution.py:17
  393.1 6.3 collective-permute-start
  400.7 15.1 %collective-permute-start = (bf16[32,2048]{1,0:T(8,128)(2,1)S(1)}, bf16[32,2048]{1,0:T(8,128)(2,1)S(1)}, u32[]{:S(2)}, u32[]{:S(2)}) collective-permute-start(bf16[32,2048]{1,0:T(8,128)(2,1)S(1)} %get-tuple-element.1094), channel_id=1, source_target_pairs={{0,32},{32,64},{64,96},{96,128},{128,160},{160,192},{192,224},{1,3... | collective-permute-start | bytes 393224 | tf_op jit(solution)/shard_map/while/body/eval_jaxpr/ppermute | solution.py:17
  419.2 6.3 collective-permute-start.1
  428.0 12.0 %collective-permute-start.1 = (bf16[32,2048]{1,0:T(8,128)(2,1)}, bf16[32,2048]{1,0:T(8,128)(2,1)S(1)}, u32[]{:S(2)}, u32[]{:S(2)}) collective-permute-start(bf16[32,2048]{1,0:T(8,128)(2,1)} %get-tuple-element.977), channel_id=1, source_target_pairs={{32,0},{64,32},{96,64},{128,96},{160,128},{192,160},{224,192},{33,... | collective-permute-start | bytes 393224 | tf_op jit(solution)/shard_map/while/body/eval_jaxpr/ppermute | solution.py:17
  442.6 6.5 collective-permute-start.1
  451.5 15.9 %collective-permute-start.1 = (bf16[32,2048]{1,0:T(8,128)(2,1)}, bf16[32,2048]{1,0:T(8,128)(2,1)S(1)}, u32[]{:S(2)}, u32[]{:S(2)}) collective-permute-start(bf16[32,2048]{1,0:T(8,128)(2,1)} %get-tuple-element.977), channel_id=1, source_target_pairs={{32,0},{64,32},{96,64},{128,96},{160,128},{192,160},{224,192},{33,... | collective-permute-start | bytes 393224 | tf_op jit(solution)/shard_map/while/body/eval_jaxpr/ppermute | solution.py:17
  469.9 6.5 collective-permute-start.1
  478.9 11.9 %collective-permute-start.1 = (bf16[32,2048]{1,0:T(8,128)(2,1)}, bf16[32,2048]{1,0:T(8,128)(2,1)S(1)}, u32[]{:S(2)}, u32[]{:S(2)}) collective-permute-start(bf16[32,2048]{1,0:T(8,128)(2,1)} %get-tuple-element.977), channel_id=1, source_target_pairs={{32,0},{64,32},{96,64},{128,96},{160,128},{192,160},{224,192},{33,... | collective-permute-start | bytes 393224 | tf_op jit(solution)/shard_map/while/body/eval_jaxpr/ppermute | solution.py:17
  493.3 210.5 %collective-permute-start.1 = (bf16[32,2048]{1,0:T(8,128)(2,1)}, bf16[32,2048]{1,0:T(8,128)(2,1)S(1)}, u32[]{:S(2)}, u32[]{:S(2)}) collective-permute-start(bf16[32,2048]{1,0:T(8,128)(2,1)} %get-tuple-element.977), channel_id=1, source_target_pairs={{32,0},{64,32},{96,64},{128,96},{160,128},{192,160},{224,192},{33,... | collective-permute-start | bytes 393224 | tf_op jit(solution)/shard_map/while/body/eval_jaxpr/ppermute | solution.py:17
  709.0 5.8 copy-start.7
  709.0 5.8 copy-start.8
  719.5 10.1 %copy-start = (bf16[2048,512]{1,0:T(8,128)(2,1)S(1)}, bf16[2048,512]{1,0:T(8,128)(2,1)}, u32[]{:S(2)}) copy-start(bf16[2048,512]{1,0:T(8,128)(2,1)} %get-tuple-element.494) | copy-start | bytes 6291460 | tf_op jit(solution)/shard_map/while/body/eval_jaxpr/cond
  728.5 5.7 copy-start.17
  728.5 5.8 copy-start.15
  735.9 6.5 collective-permute-start.1
  747.6 5.8 copy-start.7
  747.7 5.8 copy-start.8
  758.1 10.1 %copy-start = (bf16[2048,512]{1,0:T(8,128)(2,1)S(1)}, bf16[2048,512]{1,0:T(8,128)(2,1)}, u32[]{:S(2)}) copy-start(bf16[2048,512]{1,0:T(8,128)(2,1)} %get-tuple-element.494) | copy-start | bytes 6291460 | tf_op jit(solution)/shard_map/while/body/eval_jaxpr/cond
  767.1 5.8 copy-start.15
  774.6 6.5 collective-permute-start.1
  786.3 5.8 copy-start.7
  786.3 5.8 copy-start.8
  796.8 10.1 %copy-start = (bf16[2048,512]{1,0:T(8,128)(2,1)S(1)}, bf16[2048,512]{1,0:T(8,128)(2,1)}, u32[]{:S(2)}) copy-start(bf16[2048,512]{1,0:T(8,128)(2,1)} %get-tuple-element.494) | copy-start | bytes 6291460 | tf_op jit(solution)/shard_map/while/body/eval_jaxpr/cond
  805.8 5.8 copy-start.15
  813.2 6.5 collective-permute-start.1
  824.9 5.8 copy-start.7
  825.0 5.8 copy-start.8
  835.4 10.1 %copy-start = (bf16[2048,512]{1,0:T(8,128)(2,1)S(1)}, bf16[2048,512]{1,0:T(8,128)(2,1)}, u32[]{:S(2)}) copy-start(bf16[2048,512]{1,0:T(8,128)(2,1)} %get-tuple-element.494) | copy-start | bytes 6291460 | tf_op jit(solution)/shard_map/while/body/eval_jaxpr/cond
  844.4 5.8 copy-start.15
  851.9 3.4 collective-permute-start.1
  (44 other events, 144.4 us)
Sparse Core Ops, SparseCore 0:
  10.6 90.4 all-gather.10
  103.7 78.9 all-gather.8
  185.3 74.1 all-gather.6
where the time goes:
time: 940 us; the launch traced here: 935 us
  waiting for transfers between devices  470 us (50%)
  starting transfers between devices  125 us (13%)
  matrix products  117 us (12%)
  blocking collectives  72.8 us (8%)
  local copies, waits for them, and re-layouts  68.4 us (7%)
  other arithmetic  50.3 us (5%)
  loops' own time  16.6 us (2%)
  between operations  14 us (1%)
    ppermute x22, waiting for transfers between devices, shifted(): return lax.ppermute(block, axis, route)  274 us
    ppermute x22, starting transfers between devices, shifted(): return lax.ppermute(block, axis, route)  99.3 us
    all_gather x1, waiting for transfers between devices, body(): lax.all_gather(w_query[0], 'dp', axis=0, tiled=True)  75.1 us
    psum x1, blocking collectives, body(): total = lax.psum(grad_sum, 'dp')  72.8 us
    all_gather x1, waiting for transfers between devices, body(): lax.all_gather(w_keyval[0], 'dp', axis=0, tiled=True)  70.3 us
    dot_general x12, matrix products, layer(): jnp.dot(normed, w_query, preferred_element_type=jnp.float32)  42 us
    all_to_all x4, waiting for transfers between devices, body(): lax.all_to_all(packed, 'dp', split_axis=0, concat_axis=0, tiled=True)  42 us
    dot_general x8, matrix products, layer(): jnp.dot(mixed_heads, w_out, preferred_element_type=jnp.float32)  26.5 us
  transfers between devices with their start and end apart: 29, of which 29 were waited for; matrix products, arithmetic and copies ran while one was open for 5% of the time, Pallas kernels for 0%

commit v1 on v0

v1 whole, which is shorter than its diff:
```python
import jax
import jax.numpy as jnp
from jax import lax
from jax.sharding import PartitionSpec as P

HD = 64


ROPE_BASE = 500000.0
EPSILON = 1e-05
MASKED = -1e30


def rotate(values, positions):
    half_size = values.shape[-1] // 2
    freq_index = jnp.arange(half_size, dtype=jnp.float32)
    inverse = ROPE_BASE ** (-2.0 * freq_index / values.shape[-1])
    angles = positions.astype(jnp.float32)[..., None] * inverse
    cosine = jnp.cos(angles)[..., None, :]
    sine_part = jnp.sin(angles)[..., None, :]
    first_half = values[..., :half_size]
    second = values[..., half_size:]
    return jnp.concatenate(
        [first_half * cosine - second * sine_part, second * cosine + first_half * sine_part],
        axis=-1,
    )


def layer(hidden_in, steering, gain_row, w_query, w_keyval, w_out, positions, documents):
    micro_count, row_count, width = hidden_in.shape
    head_size = HD
    kv_heads = w_keyval.shape[1] // (2 * head_size)
    query_heads = w_query.shape[1] // head_size
    group_size = query_heads // kv_heads
    residual = hidden_in.astype(jnp.float32) + steering
    normed = (
        residual
        * lax.rsqrt(jnp.mean(residual * residual, axis=-1, keepdims=True) + EPSILON)
        * gain_row
    ).astype(jnp.bfloat16)
    flat = normed.reshape(micro_count * row_count, width)
    queries = jnp.dot(flat, w_query, preferred_element_type=jnp.float32).reshape(
        micro_count, row_count, query_heads, head_size
    )
    keyval = jnp.dot(flat, w_keyval, preferred_element_type=jnp.float32).reshape(
        micro_count, row_count, 2 * kv_heads * head_size
    )
    key_rows = rotate(
        keyval[..., : kv_heads * head_size].reshape(micro_count, row_count, kv_heads, head_size),
        positions,
    ).astype(jnp.bfloat16)
    values = (
        keyval[..., kv_heads * head_size :]
        .reshape(micro_count, row_count, kv_heads, head_size)
        .astype(jnp.bfloat16)
    )
    queries = (
        rotate(queries, positions)
        .astype(jnp.bfloat16)
        .reshape(micro_count, row_count, kv_heads, group_size, head_size)
    )
    scores = jnp.einsum(
        "mrkgd,mskd->mkgrs", queries, key_rows, preferred_element_type=jnp.float32
    ) * head_size ** (-0.5)
    row_index = jnp.arange(row_count)
    allowed = (documents[:, :, None] == documents[:, None, :]) & (
        row_index[:, None] >= row_index[None, :]
    )
    scores = jnp.where(allowed[:, None, None], scores, MASKED)
    peak = jnp.max(scores, axis=-1, keepdims=True)
    weights = jnp.exp(scores - peak)
    weights = (weights / jnp.sum(weights, axis=-1, keepdims=True)).astype(jnp.bfloat16)
    mixed_heads = jnp.einsum(
        "mkgrs,mskd->mrkgd", weights, values, preferred_element_type=jnp.float32
    ).astype(jnp.bfloat16)
    mixed_heads = mixed_heads.reshape(micro_count * row_count, query_heads * head_size)
    projected = jnp.dot(mixed_heads, w_out, preferred_element_type=jnp.float32).reshape(
        micro_count, row_count, width
    )
    return (residual + projected).astype(jnp.bfloat16)


def plan_slots(target, device, row_count, capacity, dp_count):
    target_grid = target.reshape(dp_count, row_count)
    target_dev = target_grid // row_count
    target_off = target_grid % row_count
    row_order = jnp.arange(row_count, dtype=jnp.int32)
    matching = target_dev[:, :, None] == target_dev[:, None, :]
    earlier = row_order[None, :] < row_order[:, None]
    rank_ids = jnp.sum((matching & earlier[None]).astype(jnp.int32), axis=2)
    slot_ids = target_dev * capacity + rank_ids
    own_slot = lax.dynamic_index_in_dim(slot_ids, device, 0, keepdims=False)
    column_ids = jnp.arange(dp_count, dtype=jnp.int32)[:, None] * capacity + rank_ids
    landing = (target_dev == device)[None] & (target_off[None] == row_order[:, None, None])
    source_col = jnp.sum(jnp.where(landing, column_ids[None], 0), axis=(1, 2))
    return (own_slot, source_col)


def pack_rows(source_rows, own_slot, slot_count):
    selector = (jnp.arange(slot_count, dtype=jnp.int32)[:, None] == own_slot[None, :]).astype(
        jnp.bfloat16
    )
    return jnp.dot(selector, source_rows, preferred_element_type=jnp.float32).astype(jnp.bfloat16)


def unpack_rows(arrived, source_col):
    selector = (
        source_col[:, None] == jnp.arange(arrived.shape[0], dtype=jnp.int32)[None, :]
    ).astype(jnp.bfloat16)
    return jnp.dot(selector, arrived, preferred_element_type=jnp.float32).astype(jnp.bfloat16)


def body(resid_in, dest_row, doc_ids, cotangent, gain, steer, w_query, w_keyval, w_out):
    dp_count = lax.axis_size("dp")
    section_count = lax.axis_size("section")
    device = lax.axis_index("dp")
    section_idx = lax.axis_index("section")
    micro_count, row_count, width = resid_in.shape
    capacity = row_count // dp_count + 1
    slot_count = dp_count * capacity
    full_query, full_keyval, full_out = (
        lax.all_gather(w_query[0], "dp", axis=0, tiled=True),
        lax.all_gather(w_keyval[0], "dp", axis=0, tiled=True),
        lax.all_gather(w_out[0], "dp", axis=1, tiled=True),
    )
    gain_row = gain[0]
    steering = steer[0]
    plans = [
        plan_slots(dest_row[micro_idx], device, row_count, capacity, dp_count)
        for micro_idx in range(micro_count)
    ]
    packed = jnp.stack(
        [
            pack_rows(resid_in[micro_idx], plans[micro_idx][0], slot_count).reshape(
                dp_count, capacity, width
            )
            for micro_idx in range(micro_count)
        ],
        axis=1,
    )
    arrived = lax.all_to_all(packed, "dp", split_axis=0, concat_axis=0, tiled=True)
    grouped = jnp.stack(
        [
            unpack_rows(arrived[:, micro_idx].reshape(slot_count, width), plans[micro_idx][1])
            for micro_idx in range(micro_count)
        ]
    )
    global_rows = device * row_count + jnp.arange(row_count, dtype=jnp.int32)
    positions = global_rows[None, :] - doc_ids

    def run_layer(hidden_in, steer_vec):
        return layer(
            hidden_in, steer_vec, gain_row, full_query, full_keyval, full_out, positions, doc_ids
        )

    zero_block = jnp.zeros((micro_count, row_count, width), jnp.bfloat16)
    forward_route = [(i, i + 1) for i in range(section_count - 1)]
    backward_route = [(i + 1, i) for i in range(section_count - 1)]

    def forward_step(carry, step):
        incoming, kept, produced = carry
        active = section_idx == step
        hidden_in = jnp.where(step == 0, grouped, incoming)
        kept = jnp.where(active, hidden_in, kept)
        hidden_new = lax.cond(active, lambda: run_layer(hidden_in, steering), lambda: zero_block)
        produced = jnp.where(active, hidden_new, produced)
        sent = lax.ppermute(hidden_new, "section", forward_route)
        return ((sent, kept, produced), None)

    (unused_in, kept, produced), unused_ys = lax.scan(
        forward_step,
        (zero_block, zero_block, zero_block),
        jnp.arange(section_count, dtype=jnp.int32),
    )

    def backward_step(carry, step):
        incoming, grad_sum = carry
        active = section_idx == step
        upstream = jnp.where(step == section_count - 1, cotangent, incoming)

        def differentiate():
            unused_out, pullback = jax.vjp(run_layer, kept, steering)
            return pullback(upstream)

        grad_in, steer_part = lax.cond(
            active, differentiate, lambda: (zero_block, jnp.zeros_like(steering))
        )
        sent = lax.ppermute(grad_in, "section", backward_route)
        return ((sent, grad_sum + steer_part), None)

    (unused_grad, grad_sum), unused_zs = lax.scan(
        backward_step,
        (zero_block, jnp.zeros_like(steering)),
        jnp.arange(section_count - 1, -1, -1, dtype=jnp.int32),
    )
    total = lax.psum(grad_sum, "dp")
    return (produced[None], total[None])


def solution(mesh):
    in_specs = (
        P(None, "dp", None),
        P(),
        P(None, "dp"),
        P(None, "dp", None),
        P("section", None),
        P("section", None),
        P("section", "dp", None),
        P("section", "dp", None),
        P("section", None, "dp"),
    )
    out_specs = (P("section", None, "dp", None), P("section", None))
    return jax.shard_map(body, mesh=mesh, in_specs=in_specs, out_specs=out_specs, check_vma=False)
```

time: 940 us -> 967 us (1.029)
  waiting for transfers between devices: 470 us -> 578 us
  matrix products: 117 us -> 39.5 us
    ppermute x22 -> x16, waiting for transfers between devices: 274 us -> 372 us  [the longest x8 371 us: backward_step(): sent = lax.ppermute(grad_in, 'section', backward_route)]
    all_gather x1, waiting for transfers between devices: 5.94 us -> 74.7 us  [body(): lax.all_gather(w_out[0], 'dp', axis=1, tiled=True)]
    dot_general x48 -> x12, matrix products: 83.9 us -> 26.5 us  [the longest x3 12 us: layer(): jnp.dot(flat, w_query, preferred_element_type=jnp.float32)]
    all_gather x1, waiting for transfers between devices: 75.1 us -> 32.3 us  [body(): lax.all_gather(w_query[0], 'dp', axis=0, tiled=True)]
    dot_general x8 -> x2, matrix products: 26.5 us -> 6.62 us  [layer(): jnp.dot(mixed_heads, w_out, preferred_element_type=jnp.float32)]
    ppermute x22 -> x16, starting transfers between devices: 99.3 us -> 119 us  [the longest x8 108 us: forward_step(): sent = lax.ppermute(hidden_new, 'section', forward_route)]
    select_n x0 -> x17, other arithmetic: none -> 17.4 us  [the longest x8 14.2 us: forward_step(): produced = jnp.where(active, hidden_new, produced)]
    reshape x40 -> x6, local copies, waits for them, and re-layouts: 19.2 us -> 3.9 us  [the longest x1 1.44 us: layer(): jnp.dot(flat, w_query, preferred_element_type=jnp.float32)]
  transfers between devices with their start and end apart: 29 -> 20, of which waited for: 29 -> 13; matrix products, arithmetic and copies ran while one was open for 5% -> 6% of each run, Pallas kernels for 0% -> 0%
where the time goes in v1:
time: 967 us; the launch traced here: 964 us
  waiting for transfers between devices  578 us (60%)
  starting transfers between devices  130 us (13%)
  blocking collectives  72.8 us (8%)
  local copies, waits for them, and re-layouts  59.4 us (6%)
  other arithmetic  54 us (6%)
  matrix products  39.5 us (4%)
  loops' own time  16.4 us (2%)
  between operations  14 us (1%)
    ppermute x8, waiting for transfers between devices, backward_step(): sent = lax.ppermute(grad_in, 'section', backward_route)  371 us
    ppermute x8, starting transfers between devices, forward_step(): sent = lax.ppermute(hidden_new, 'section', forward_route)  108 us
    all_gather x1, waiting for transfers between devices, body(): lax.all_gather(w_out[0], 'dp', axis=1, tiled=True)  74.7 us
    psum x1, blocking collectives, body(): total = lax.psum(grad_sum, 'dp')  72.8 us
    all_gather x1, waiting for transfers between devices, body(): lax.all_gather(w_keyval[0], 'dp', axis=0, tiled=True)  70.3 us
    all_gather x1, waiting for transfers between devices, body(): lax.all_gather(w_query[0], 'dp', axis=0, tiled=True)  32.3 us
    all_to_all x1, waiting for transfers between devices, body(): lax.all_to_all(packed, 'dp', split_axis=0, concat_axis=0, tiled=True)  27 us
  transfers between devices with their start and end apart: 20, of which 13 were waited for; matrix products, arithmetic and copies ran while one was open for 6% of the time, Pallas kernels for 0%

profile of v1, /device:TPU:32, one launch (start us, length us, event | category | flops | bytes accessed | tf_op | source)
XLA Modules:
  0.0 964.0 jit_solution(17783899758612930752)
XLA Ops:
  10.7 2.9 convert_reduce_fusion.4
  18.9 2.4 pad_maximum_fusion.3
  21.3 11.4 %all-to-all-start = ((bf16[32,4,2,2048]{3,2,1,0:T(2,128)(2,1)}), bf16[32,4,2,2048]{3,2,1,0:T(2,128)(2,1)S(1)}, u32[]{:S(2)}, u32[]{:S(2)}) async-start(bf16[32,4,2,2048]{3,2,1,0:T(2,128)(2,1)} %pad_maximum_fusion.3), calls=%async_computation | async-start | bytes 2097152 | tf_op jit(solution)/shard_map/all_to_all | solution.py:141
  37.4 27.0 %all-to-all-done = bf16[32,4,2,2048]{3,2,1,0:T(2,128)(2,1)S(1)} async-done(((bf16[32,4,2,2048]{3,2,1,0:T(2,128)(2,1)}), bf16[32,4,2,2048]{3,2,1,0:T(2,128)(2,1)S(1)}, u32[]{:S(2)}, u32[]{:S(2)}) %all-to-all-start) | async-done | bytes 1048608 | tf_op jit(solution)/shard_map/all_to_all | solution.py:141
  66.6 32.3 %all-gather.9.cloned.1.call-done = bf16[1,2048,1024]{2,1,0:T(8,128)(2,1)} async-done(((bf16[1,64,1024]{2,1,0:T(8,128)(2,1)}), bf16[1,2048,1024]{2,1,0:T(8,128)(2,1)}) %all-gather.9.cloned.1.call-update) | async-done | bytes 4194320 | tf_op jit(solution)/shard_map/all_gather | solution.py:122
  99.0 6.5 copy.79
  105.5 74.7 %all-gather.11.cloned.1.call-done = bf16[1,1024,2048]{1,2,0:T(8,128)(2,1)} async-done(((bf16[1,1024,64]{1,2,0:T(8,128)(2,1)}), bf16[1,1024,2048]{1,2,0:T(8,128)(2,1)}) %all-gather.11.cloned.1.call-update) | async-done | bytes 4194320 | tf_op jit(solution)/shard_map/all_gather | solution.py:124
  180.2 6.5 copy.80
  186.7 70.3 %all-gather.7.cloned.1.call-done = bf16[1,2048,512]{2,1,0:T(8,128)(2,1)} async-done(((bf16[1,64,512]{2,1,0:T(8,128)(2,1)}), bf16[1,2048,512]{2,1,0:T(8,128)(2,1)}) %all-gather.7.cloned.1.call-update) | async-done | bytes 2097168 | tf_op jit(solution)/shard_map/all_gather | solution.py:123
  257.0 157.5 %while.28 = (s32[]{:T(128)}, bf16[4,32,2048]{2,1,0:T(8,128)(2,1)S(1)}, bf16[4,32,2048]{2,1,0:T(8,128)(2,1)S(1)}, bf16[4,32,2048]{2,1,0:T(8,128)(2,1)}, s32[8]{0:...) while((s32[]{:T(128)}, ...), condition=%wide.region_14.15_spmd.clone, body=%wide.region_8.14_spmd.clone.sunk | while | flops 1376075008 | bytes 24693816 | solution.py:170
  259.0 17.9 %conditional.6 = (bf16[4,32,2048]{2,1,0:T(8,128)(2,1)S(1)}) conditional(s32[]{:T(128)} %convert_element_type.335, () %tuple.113, (bf16[4,32,2048]{2,1,0:T(8,128)(2,1)S(1)}, f32[1,2048]{1,0:T(1,128)}, f32[1,2048]{1,0:T(1,128)}, bf16[2048,512]{1,0:T(8,128)(2,1)}, s32[4,32]{1,0:T(4,128)}, /*index=5*/s32[4,32]{1,0:T(4,128)}, ...), branch_computations={%region_9.9_spmd, %region_10.13_spmd} | conditional | flops 1374764288 | bytes 18402056 | solution.py:165
  260.0 2.1 fusion.9
  263.6 4.5 fusion.19
  271.3 2.2 fusion.15
  274.1 2.9 fusion.6
  281.9 20.2 %collective-permute-start = (bf16[4,32,2048]{2,1,0:T(8,128)(2,1)S(1)}, bf16[4,32,2048]{2,1,0:T(8,128)(2,1)S(1)}, u32[]{:S(2)}, u32[]{:S(2)}) collective-permute-start(bf16[4,32,2048]{2,1,0:T(8,128)(2,1)S(1)} %get-tuple-element.784), channel_id=1, source_target_pairs={{0,32},{32,64},{64,96},{96,128},{128,160},{160,192},{192,224},{1,3... | collective-permute-start | bytes 1572872 | tf_op jit(solution)/shard_map/while/body/eval_jaxpr/ppermute | solution.py:167
  302.0 1.9 select_select_fusion.5
  306.0 6.1 collective-permute-start
  312.1 1.9 select_select_fusion.5
  316.1 26.5 %collective-permute-start = (bf16[4,32,2048]{2,1,0:T(8,128)(2,1)S(1)}, bf16[4,32,2048]{2,1,0:T(8,128)(2,1)S(1)}, u32[]{:S(2)}, u32[]{:S(2)}) collective-permute-start(bf16[4,32,2048]{2,1,0:T(8,128)(2,1)S(1)} %get-tuple-element.784), channel_id=1, source_target_pairs={{0,32},{32,64},{64,96},{96,128},{128,160},{160,192},{192,224},{1,3... | collective-permute-start | bytes 1572872 | tf_op jit(solution)/shard_map/while/body/eval_jaxpr/ppermute | solution.py:167
  342.5 1.9 select_select_fusion.5
  346.5 8.6 collective-permute-start
  355.1 1.9 select_select_fusion.5
  359.1 13.1 %collective-permute-start = (bf16[4,32,2048]{2,1,0:T(8,128)(2,1)S(1)}, bf16[4,32,2048]{2,1,0:T(8,128)(2,1)S(1)}, u32[]{:S(2)}, u32[]{:S(2)}) collective-permute-start(bf16[4,32,2048]{2,1,0:T(8,128)(2,1)S(1)} %get-tuple-element.784), channel_id=1, source_target_pairs={{0,32},{32,64},{64,96},{96,128},{128,160},{160,192},{192,224},{1,3... | collective-permute-start | bytes 1572872 | tf_op jit(solution)/shard_map/while/body/eval_jaxpr/ppermute | solution.py:167
  372.2 1.9 select_select_fusion.5
  376.1 8.6 collective-permute-start
  384.7 1.9 select_select_fusion.5
  388.7 24.0 %collective-permute-start = (bf16[4,32,2048]{2,1,0:T(8,128)(2,1)S(1)}, bf16[4,32,2048]{2,1,0:T(8,128)(2,1)S(1)}, u32[]{:S(2)}, u32[]{:S(2)}) collective-permute-start(bf16[4,32,2048]{2,1,0:T(8,128)(2,1)S(1)} %get-tuple-element.784), channel_id=1, source_target_pairs={{0,32},{32,64},{64,96},{96,128},{128,160},{160,192},{192,224},{1,3... | collective-permute-start | bytes 1572872 | tf_op jit(solution)/shard_map/while/body/eval_jaxpr/ppermute | solution.py:167
  412.7 1.9 select_select_fusion.5
  415.5 469.1 %while.29 = (s32[]{:T(128)}, bf16[4,32,2048]{2,1,0:T(8,128)(2,1)}, f32[2048]{0:T(1024)}, s32[8]{0:T(128)}, s32[]{:T(128)}, /*index=5*/bf16[4,32,2048]{2,1,0:T(8,...) while((s32[]{:T(128)}, bf16[4,32,2048]{2,1,0:T(8,128)(2,1)}, ...), condition=%wide.region_26.27_spmd.clone, body=%wide.region_15.26_spmd.clone.sunk | while | flops 2205098752 | bytes 54051516 | solution.py:191
  417.5 1.5 conditional.7
  421.6 7.6 collective-permute-done.1
  436.2 13.3 %collective-permute-done.1 = bf16[4,32,2048]{2,1,0:T(8,128)(2,1)S(1)} collective-permute-done((bf16[4,32,2048]{2,1,0:T(8,128)(2,1)}, bf16[4,32,2048]{2,1,0:T(8,128)(2,1)S(1)}, u32[]{:S(2)}, u32[]{:S(2)}) %collective-permute-start.1) | collective-permute-done | bytes 524320 | tf_op jit(solution)/shard_map/while/body/eval_jaxpr/ppermute | solution.py:188
  456.5 8.1 collective-permute-done.1
  471.6 23.7 %collective-permute-done.1 = bf16[4,32,2048]{2,1,0:T(8,128)(2,1)S(1)} collective-permute-done((bf16[4,32,2048]{2,1,0:T(8,128)(2,1)}, bf16[4,32,2048]{2,1,0:T(8,128)(2,1)S(1)}, u32[]{:S(2)}, u32[]{:S(2)}) %collective-permute-start.1) | collective-permute-done | bytes 524320 | tf_op jit(solution)/shard_map/while/body/eval_jaxpr/ppermute | solution.py:188
  502.3 8.1 collective-permute-done.1
  517.4 12.8 %collective-permute-done.1 = bf16[4,32,2048]{2,1,0:T(8,128)(2,1)S(1)} collective-permute-done((bf16[4,32,2048]{2,1,0:T(8,128)(2,1)}, bf16[4,32,2048]{2,1,0:T(8,128)(2,1)S(1)}, u32[]{:S(2)}, u32[]{:S(2)}) %collective-permute-start.1) | collective-permute-done | bytes 524320 | tf_op jit(solution)/shard_map/while/body/eval_jaxpr/ppermute | solution.py:188
  537.2 295.9 %collective-permute-done.1 = bf16[4,32,2048]{2,1,0:T(8,128)(2,1)S(1)} collective-permute-done((bf16[4,32,2048]{2,1,0:T(8,128)(2,1)}, bf16[4,32,2048]{2,1,0:T(8,128)(2,1)S(1)}, u32[]{:S(2)}, u32[]{:S(2)}) %collective-permute-start.1) | collective-permute-done | bytes 524320 | tf_op jit(solution)/shard_map/while/body/eval_jaxpr/ppermute | solution.py:188
  836.0 43.7 %conditional.7 = (bf16[4,32,2048]{2,1,0:T(8,128)(2,1)}, f32[2048]{0:T(1024)}) conditional(s32[]{:T(128)} %convert_element_type.336, () %tuple.116, (s32[]{:T(128)}, bf16[4,32,2048]{2,1,0:T(8,128)(2,1)}, bf16[4,32,2048]{2,1,0:T(8,128)(2,1)}, bf16[1024,2048]{1,0:T(8,128)(2,1)}, s32[4,32]{1,0:T(4,128)}, ...), branch_computations={%region_16.16_spmd, %region_17.25_spmd} | conditional | flops 2205094656 | bytes 49832296 | solution.py:185
  837.5 2.1 fusion.47
  841.8 4.6 fusion.71
  852.2 3.7 convolution_convert_fusion.5
  857.1 1.5 fusion.54
  861.1 2.0 fusion.62
  867.2 1.8 fusion.49
  872.3 2.9 fusion.139
  877.1 2.6 fusion.78
  884.6 72.8 %psum.7 = f32[1,2048]{1,0:T(1,128)} all-reduce(f32[1,2048]{1,0:T(1,128)} %bitcast.243), channel_id=1, replica_groups=mesh['section'=8,'dp'=32] {'dp'}, use_global_device_ids=true, to_apply=%region_27.28 | all-reduce | flops 2048 | bytes 16384 | tf_op jit(solution)/shard_map/psum | solution.py:196
  (253 shorter events, 113.5 us)
Async XLA Ops:
  7.2 91.8 %all-gather.9.cloned.1.call-start = ((), (), s32[]{:S(2)}) async-start(), calls=%async_computation.2 | async-start | bytes 4325376 | tf_op jit(solution)/shard_map/all_gather | solution.py:122
  7.9 172.3 %all-gather.11.cloned.1.call-start = ((), (), s32[]{:S(2)}) async-start(), calls=%async_computation.3 | async-start | bytes 4325376 | tf_op jit(solution)/shard_map/all_gather | solution.py:124
  8.6 248.3 %all-gather.7.cloned.1.call-start = ((), (), s32[]{:S(2)}) async-start(), calls=%async_computation.1 | async-start | bytes 2162688 | tf_op jit(solution)/shard_map/all_gather | solution.py:123
  21.3 43.1 %all-to-all-start = ((bf16[32,4,2,2048]{3,2,1,0:T(2,128)(2,1)}), bf16[32,4,2,2048]{3,2,1,0:T(2,128)(2,1)S(1)}, u32[]{:S(2)}, u32[]{:S(2)}) async-start(bf16[32,4,2,2048]{3,2,1,0:T(2,128)(2,1)} %pad_maximum_fusion.3), calls=%async_computation | async-start | bytes 2097152 | tf_op jit(solution)/shard_map/all_to_all | solution.py:141
  277.0 2.8 collective-permute-start
  281.9 22.1 %collective-permute-start = (bf16[4,32,2048]{2,1,0:T(8,128)(2,1)S(1)}, bf16[4,32,2048]{2,1,0:T(8,128)(2,1)S(1)}, u32[]{:S(2)}, u32[]{:S(2)}) collective-permute-start(bf16[4,32,2048]{2,1,0:T(8,128)(2,1)S(1)} %get-tuple-element.784), channel_id=1, source_target_pairs={{0,32},{32,64},{64,96},{96,128},{128,160},{160,192},{192,224},{1,3... | collective-permute-start | bytes 1572872 | tf_op jit(solution)/shard_map/while/body/eval_jaxpr/ppermute | solution.py:167
  306.0 8.0 collective-permute-start
  316.1 28.4 %collective-permute-start = (bf16[4,32,2048]{2,1,0:T(8,128)(2,1)S(1)}, bf16[4,32,2048]{2,1,0:T(8,128)(2,1)S(1)}, u32[]{:S(2)}, u32[]{:S(2)}) collective-permute-start(bf16[4,32,2048]{2,1,0:T(8,128)(2,1)S(1)} %get-tuple-element.784), channel_id=1, source_target_pairs={{0,32},{32,64},{64,96},{96,128},{128,160},{160,192},{192,224},{1,3... | collective-permute-start | bytes 1572872 | tf_op jit(solution)/shard_map/while/body/eval_jaxpr/ppermute | solution.py:167
  346.5 10.5 %collective-permute-start = (bf16[4,32,2048]{2,1,0:T(8,128)(2,1)S(1)}, bf16[4,32,2048]{2,1,0:T(8,128)(2,1)S(1)}, u32[]{:S(2)}, u32[]{:S(2)}) collective-permute-start(bf16[4,32,2048]{2,1,0:T(8,128)(2,1)S(1)} %get-tuple-element.784), channel_id=1, source_target_pairs={{0,32},{32,64},{64,96},{96,128},{128,160},{160,192},{192,224},{1,3... | collective-permute-start | bytes 1572872 | tf_op jit(solution)/shard_map/while/body/eval_jaxpr/ppermute | solution.py:167
  359.1 15.0 %collective-permute-start = (bf16[4,32,2048]{2,1,0:T(8,128)(2,1)S(1)}, bf16[4,32,2048]{2,1,0:T(8,128)(2,1)S(1)}, u32[]{:S(2)}, u32[]{:S(2)}) collective-permute-start(bf16[4,32,2048]{2,1,0:T(8,128)(2,1)S(1)} %get-tuple-element.784), channel_id=1, source_target_pairs={{0,32},{32,64},{64,96},{96,128},{128,160},{160,192},{192,224},{1,3... | collective-permute-start | bytes 1572872 | tf_op jit(solution)/shard_map/while/body/eval_jaxpr/ppermute | solution.py:167
  376.1 10.5 %collective-permute-start = (bf16[4,32,2048]{2,1,0:T(8,128)(2,1)S(1)}, bf16[4,32,2048]{2,1,0:T(8,128)(2,1)S(1)}, u32[]{:S(2)}, u32[]{:S(2)}) collective-permute-start(bf16[4,32,2048]{2,1,0:T(8,128)(2,1)S(1)} %get-tuple-element.784), channel_id=1, source_target_pairs={{0,32},{32,64},{64,96},{96,128},{128,160},{160,192},{192,224},{1,3... | collective-permute-start | bytes 1572872 | tf_op jit(solution)/shard_map/while/body/eval_jaxpr/ppermute | solution.py:167
  388.7 25.9 %collective-permute-start = (bf16[4,32,2048]{2,1,0:T(8,128)(2,1)S(1)}, bf16[4,32,2048]{2,1,0:T(8,128)(2,1)S(1)}, u32[]{:S(2)}, u32[]{:S(2)}) collective-permute-start(bf16[4,32,2048]{2,1,0:T(8,128)(2,1)S(1)} %get-tuple-element.784), channel_id=1, source_target_pairs={{0,32},{32,64},{64,96},{96,128},{128,160},{160,192},{192,224},{1,3... | collective-permute-start | bytes 1572872 | tf_op jit(solution)/shard_map/while/body/eval_jaxpr/ppermute | solution.py:167
  419.0 10.2 %collective-permute-start.1 = (bf16[4,32,2048]{2,1,0:T(8,128)(2,1)}, bf16[4,32,2048]{2,1,0:T(8,128)(2,1)S(1)}, u32[]{:S(2)}, u32[]{:S(2)}) collective-permute-start(bf16[4,32,2048]{2,1,0:T(8,128)(2,1)} %get-tuple-element.682), channel_id=1, source_target_pairs={{32,0},{64,32},{96,64},{128,96},{160,128},{192,160},{224,192},{33,... | collective-permute-start | bytes 1572872 | tf_op jit(solution)/shard_map/while/body/eval_jaxpr/ppermute | solution.py:188
  429.2 0.9 copy-start.1
  433.6 15.9 %collective-permute-start.1 = (bf16[4,32,2048]{2,1,0:T(8,128)(2,1)}, bf16[4,32,2048]{2,1,0:T(8,128)(2,1)S(1)}, u32[]{:S(2)}, u32[]{:S(2)}) collective-permute-start(bf16[4,32,2048]{2,1,0:T(8,128)(2,1)} %get-tuple-element.682), channel_id=1, source_target_pairs={{32,0},{64,32},{96,64},{128,96},{160,128},{192,160},{224,192},{33,... | collective-permute-start | bytes 1572872 | tf_op jit(solution)/shard_map/while/body/eval_jaxpr/ppermute | solution.py:188
  449.5 0.9 copy-start.1
  453.9 10.7 %collective-permute-start.1 = (bf16[4,32,2048]{2,1,0:T(8,128)(2,1)}, bf16[4,32,2048]{2,1,0:T(8,128)(2,1)S(1)}, u32[]{:S(2)}, u32[]{:S(2)}) collective-permute-start(bf16[4,32,2048]{2,1,0:T(8,128)(2,1)} %get-tuple-element.682), channel_id=1, source_target_pairs={{32,0},{64,32},{96,64},{128,96},{160,128},{192,160},{224,192},{33,... | collective-permute-start | bytes 1572872 | tf_op jit(solution)/shard_map/while/body/eval_jaxpr/ppermute | solution.py:188
  464.6 0.9 copy-start.1
  469.0 26.3 %collective-permute-start.1 = (bf16[4,32,2048]{2,1,0:T(8,128)(2,1)}, bf16[4,32,2048]{2,1,0:T(8,128)(2,1)S(1)}, u32[]{:S(2)}, u32[]{:S(2)}) collective-permute-start(bf16[4,32,2048]{2,1,0:T(8,128)(2,1)} %get-tuple-element.682), channel_id=1, source_target_pairs={{32,0},{64,32},{96,64},{128,96},{160,128},{192,160},{224,192},{33,... | collective-permute-start | bytes 1572872 | tf_op jit(solution)/shard_map/while/body/eval_jaxpr/ppermute | solution.py:188
  495.3 0.9 copy-start.1
  499.7 10.7 %collective-permute-start.1 = (bf16[4,32,2048]{2,1,0:T(8,128)(2,1)}, bf16[4,32,2048]{2,1,0:T(8,128)(2,1)S(1)}, u32[]{:S(2)}, u32[]{:S(2)}) collective-permute-start(bf16[4,32,2048]{2,1,0:T(8,128)(2,1)} %get-tuple-element.682), channel_id=1, source_target_pairs={{32,0},{64,32},{96,64},{128,96},{160,128},{192,160},{224,192},{33,... | collective-permute-start | bytes 1572872 | tf_op jit(solution)/shard_map/while/body/eval_jaxpr/ppermute | solution.py:188
  510.4 0.9 copy-start.1
  514.8 15.4 %collective-permute-start.1 = (bf16[4,32,2048]{2,1,0:T(8,128)(2,1)}, bf16[4,32,2048]{2,1,0:T(8,128)(2,1)S(1)}, u32[]{:S(2)}, u32[]{:S(2)}) collective-permute-start(bf16[4,32,2048]{2,1,0:T(8,128)(2,1)} %get-tuple-element.682), channel_id=1, source_target_pairs={{32,0},{64,32},{96,64},{128,96},{160,128},{192,160},{224,192},{33,... | collective-permute-start | bytes 1572872 | tf_op jit(solution)/shard_map/while/body/eval_jaxpr/ppermute | solution.py:188
  530.2 0.9 copy-start.1
  534.6 298.5 %collective-permute-start.1 = (bf16[4,32,2048]{2,1,0:T(8,128)(2,1)}, bf16[4,32,2048]{2,1,0:T(8,128)(2,1)S(1)}, u32[]{:S(2)}, u32[]{:S(2)}) collective-permute-start(bf16[4,32,2048]{2,1,0:T(8,128)(2,1)} %get-tuple-element.682), channel_id=1, source_target_pairs={{32,0},{64,32},{96,64},{128,96},{160,128},{192,160},{224,192},{33,... | collective-permute-start | bytes 1572872 | tf_op jit(solution)/shard_map/while/body/eval_jaxpr/ppermute | solution.py:188
  833.1 0.9 copy-start.1
  836.9 4.8 copy-start.20
  839.6 0.7 copy-start.13
  841.8 6.6 copy-start.2
  841.8 6.6 copy-start.4
  849.4 1.6 copy-start.8
  857.1 2.4 copy-start.11
  857.1 4.0 copy-start.9
  861.1 3.0 copy-start.10
  861.1 3.0 copy-start.12
  861.1 3.0 copy-start.18
  863.1 1.9 copy-start.7
  863.2 1.8 copy-start.14
  864.0 1.2 copy-start.15
  864.1 3.2 copy-start.3
  864.1 3.1 copy-start.5
  864.1 3.1 copy-start.19
  869.5 5.8 copy-start
  869.5 5.8 copy-start.6
  872.3 4.8 copy-start.17
  872.3 4.8 copy-start.21
  879.7 4.0 collective-permute-start.1
  883.7 0.9 copy-start.1
  (1 other events, 0.5 us)
Sparse Core Ops, SparseCore 0:
  10.6 88.3 all-gather.8
  101.6 78.5 all-gather.10
  182.8 74.1 all-gather.6

commit v2 on v1

--- a/solution.py
+++ b/solution.py
@@ -11,13 +11,17 @@
 MASKED = -1e30
 
 
-def rotate(values, positions):
+def rope_tables(positions):
+    half_size = HD // 2
+    freq_index = jnp.arange(half_size, dtype=jnp.float32)
+    inverse = ROPE_BASE ** (-2.0 * freq_index / HD)
+    angles = positions.astype(jnp.float32)[..., None] * inverse
+    return (jnp.cos(angles)[..., None, :], jnp.sin(angles)[..., None, :])
+
+
+def rotate(values, tables):
     half_size = values.shape[-1] // 2
-    freq_index = jnp.arange(half_size, dtype=jnp.float32)
-    inverse = ROPE_BASE ** (-2.0 * freq_index / values.shape[-1])
-    angles = positions.astype(jnp.float32)[..., None] * inverse
-    cosine = jnp.cos(angles)[..., None, :]
-    sine_part = jnp.sin(angles)[..., None, :]
+    cosine, sine_part = tables
     first_half = values[..., :half_size]
     second = values[..., half_size:]
     return jnp.concatenate(
@@ -26,11 +30,11 @@
     )
 
 
-def layer(hidden_in, steering, gain_row, w_query, w_keyval, w_out, positions, documents):
-    micro_count, row_count, width = hidden_in.shape
+def layer(hidden_in, steering, gain_row, w_qkv, w_out, tables, allowed):
+    row_count, width = hidden_in.shape
     head_size = HD
-    kv_heads = w_keyval.shape[1] // (2 * head_size)
-    query_heads = w_query.shape[1] // head_size
+    query_heads = w_out.shape[0] // head_size
+    kv_heads = (w_qkv.shape[1] - query_heads * head_size) // (2 * head_size)
     group_size = query_heads // kv_heads
     residual = hidden_in.astype(jnp.float32) + steering
     normed = (
@@ -38,46 +42,47 @@
         * lax.rsqrt(jnp.mean(residual * residual, axis=-1, keepdims=True) + EPSILON)
         * gain_row
     ).astype(jnp.bfloat16)
-    flat = normed.reshape(micro_count * row_count, width)
-    queries = jnp.dot(flat, w_query, preferred_element_type=jnp.float32).reshape(
-        micro_count, row_count, query_heads, head_size
-    )
-    keyval = jnp.dot(flat, w_keyval, preferred_element_type=jnp.float32).reshape(
-        micro_count, row_count, 2 * kv_heads * head_size
-    )
+    projected_in = jnp.dot(normed, w_qkv, preferred_element_type=jnp.float32)
+    query_cols = query_heads * head_size
+    queries = projected_in[:, :query_cols].reshape(row_count, query_heads, head_size)
+    keyval = projected_in[:, query_cols:]
     key_rows = rotate(
-        keyval[..., : kv_heads * head_size].reshape(micro_count, row_count, kv_heads, head_size),
-        positions,
+        keyval[:, : kv_heads * head_size].reshape(row_count, kv_heads, head_size), tables
     ).astype(jnp.bfloat16)
     values = (
-        keyval[..., kv_heads * head_size :]
-        .reshape(micro_count, row_count, kv_heads, head_size)
+        keyval[:, kv_heads * head_size :]
+        .reshape(row_count, kv_heads, head_size)
         .astype(jnp.bfloat16)
     )
     queries = (
-        rotate(queries, positions)
+        rotate(queries, tables)
         .astype(jnp.bfloat16)
-        .reshape(micro_count, row_count, kv_heads, group_size, head_size)
+        .reshape(row_count, kv_heads, group_size, head_size)
     )
     scores = jnp.einsum(
-        "mrkgd,mskd->mkgrs", queries, key_rows, preferred_element_type=jnp.float32
+        "rkgd,skd->kgrs", queries, key_rows, preferred_element_type=jnp.float32
     ) * head_size ** (-0.5)
-    row_index = jnp.arange(row_count)
-    allowed = (documents[:, :, None] == documents[:, None, :]) & (
-        row_index[:, None] >= row_index[None, :]
-    )
-    scores = jnp.where(allowed[:, None, None], scores, MASKED)
+    scores = jnp.where(allowed[None, None], scores, MASKED)
     peak = jnp.max(scores, axis=-1, keepdims=True)
     weights = jnp.exp(scores - peak)
     weights = (weights / jnp.sum(weights, axis=-1, keepdims=True)).astype(jnp.bfloat16)
     mixed_heads = jnp.einsum(
-        "mkgrs,mskd->mrkgd", weights, values, preferred_element_type=jnp.float32
-    ).astype(jnp.bfloat16)
-    mixed_heads = mixed_heads.reshape(micro_count * row_count, query_heads * head_size)
-    projected = jnp.dot(mixed_heads, w_out, preferred_element_type=jnp.float32).reshape(
-        micro_count, row_count, width
-    )
-    return (residual + projected).astype(jnp.bfloat16)
+        "kgrs,skd->rkgd", weights, values, preferred_element_type=jnp.float32
+    ).astype(jnp.bfloat16)
+    mixed_heads = mixed_heads.reshape(row_count, query_heads * head_size)
+    return (residual + jnp.dot(mixed_heads, w_out, preferred_element_type=jnp.float32)).astype(
+        jnp.bfloat16
+    )
+
+
+def butterfly_sum(values, axis):
+    count = lax.axis_size(axis)
+    distance = 1
+    while distance < count:
+        route = [(i, i ^ distance) for i in range(count)]
+        values = values + lax.ppermute(values, axis, route)
+        distance *= 2
+    return values
 
 
 def plan_slots(target, device, row_count, capacity, dp_count):
@@ -118,11 +123,10 @@
     micro_count, row_count, width = resid_in.shape
     capacity = row_count // dp_count + 1
     slot_count = dp_count * capacity
-    full_query, full_keyval, full_out = (
-        lax.all_gather(w_query[0], "dp", axis=0, tiled=True),
-        lax.all_gather(w_keyval[0], "dp", axis=0, tiled=True),
-        lax.all_gather(w_out[0], "dp", axis=1, tiled=True),
-    )
+    full_qkv = lax.all_gather(
+        jnp.concatenate([w_query[0], w_keyval[0]], axis=1), "dp", axis=0, tiled=True
+    )
+    full_out = lax.all_gather(w_out[0], "dp", axis=1, tiled=True)
     gain_row = gain[0]
     steering = steer[0]
     plans = [
@@ -146,14 +150,21 @@
         ]
     )
     global_rows = device * row_count + jnp.arange(row_count, dtype=jnp.int32)
-    positions = global_rows[None, :] - doc_ids
+    flat_count = micro_count * row_count
+    tables = rope_tables((global_rows[None, :] - doc_ids).reshape(flat_count))
+    micro_of = jnp.arange(flat_count, dtype=jnp.int32) // row_count
+    doc_keys = doc_ids.reshape(flat_count) + micro_of * (dp_count * row_count)
+    flat_index = jnp.arange(flat_count, dtype=jnp.int32)
+    allowed = (doc_keys[:, None] == doc_keys[None, :]) & (
+        flat_index[:, None] >= flat_index[None, :]
+    )
+    grouped = grouped.reshape(flat_count, width)
+    cotangent = cotangent.reshape(flat_count, width)
 
     def run_layer(hidden_in, steer_vec):
-        return layer(
-            hidden_in, steer_vec, gain_row, full_query, full_keyval, full_out, positions, doc_ids
-        )
-
-    zero_block = jnp.zeros((micro_count, row_count, width), jnp.bfloat16)
+        return layer(hidden_in, steer_vec, gain_row, full_qkv, full_out, tables, allowed)
+
+    zero_block = jnp.zeros((flat_count, width), jnp.bfloat16)
     forward_route = [(i, i + 1) for i in range(section_count - 1)]
     backward_route = [(i + 1, i) for i in range(section_count - 1)]
 
@@ -193,8 +204,8 @@
         (zero_block, jnp.zeros_like(steering)),
         jnp.arange(section_count - 1, -1, -1, dtype=jnp.int32),
     )
-    total = lax.psum(grad_sum, "dp")
-    return (produced[None], total[None])
+    total = butterfly_sum(grad_sum, "dp")
+    return (produced.reshape(1, micro_count, row_count, width), total[None])
 
 
 def solution(mesh):

time: 967 us -> 578 us (0.60)
  waiting for transfers between devices: 578 us -> 333 us
  blocking collectives: 72.8 us -> 0 us
  starting transfers between devices: 130 us -> 104 us
  local copies, waits for them, and re-layouts: 59.4 us -> 34.4 us
  matrix products: 39.5 us -> 24.9 us
    ppermute x8, waiting for transfers between devices: 371 us -> 175 us  [backward_step(): sent = lax.ppermute(grad_in, 'section', backward_route)]
    psum x1 -> x0, blocking collectives: 72.8 us -> none  [body(): total = lax.psum(grad_sum, 'dp')]
    all_gather x3 -> x2, waiting for transfers between devices: 177 us -> 112 us  [the longest x1 81.3 us: body(): lax.all_gather(jnp.concatenate([w_query[0], w_keyval[0]], axis=1), 'dp',...]
    ppermute x8, starting transfers between devices: 108 us -> 75.7 us  [forward_step(): sent = lax.ppermute(hidden_new, 'section', forward_route)]
    ppermute x0 -> x5, waiting for transfers between devices: none -> 18.1 us  [butterfly_sum(): values = values + lax.ppermute(values, axis, route)]
    dot_general x12 -> x10, matrix products: 26.5 us -> 12.4 us  [the longest x3 9.89 us: layer(): projected_in = jnp.dot(normed, w_qkv, preferred_element_type=jnp.float32)]
    mul x0 -> x17, other arithmetic: none -> 11.9 us  [the longest x16 11.4 us: rope_tables(): angles = positions.astype(jnp.float32)[..., None] * inverse]
    add x8, other arithmetic: 10.5 us -> 0.05 us  [backward_step(): return ((sent, grad_sum + steer_part), None)]
  transfers between devices with their start and end apart: 20 -> 24, of which waited for: 13 -> 17; matrix products, arithmetic and copies ran while one was open for 6% -> 7% of each run, Pallas kernels for 0% -> 0%
where the time goes in v2:
time: 578 us; the launch traced here: 576 us
  waiting for transfers between devices  333 us (58%)
  starting transfers between devices  104 us (18%)
  other arithmetic  46.8 us (8%)
  local copies, waits for them, and re-layouts  34.4 us (6%)
  matrix products  24.9 us (4%)
  loops' own time  18.7 us (3%)
  between operations  14.4 us (2%)
    ppermute x8, waiting for transfers between devices, backward_step(): sent = lax.ppermute(grad_in, 'section', backward_route)  175 us
    all_gather x1, waiting for transfers between devices, body(): lax.all_gather(jnp.concatenate([w_query[0], w_keyval[0]], axis=1), 'dp',...  81.3 us
    ppermute x8, starting transfers between devices, forward_step(): sent = lax.ppermute(hidden_new, 'section', forward_route)  75.7 us
    all_gather x1, waiting for transfers between devices, body(): full_out = lax.all_gather(w_out[0], 'dp', axis=1, tiled=True)  30.8 us
    all_to_all x1, waiting for transfers between devices, body(): lax.all_to_all(packed, 'dp', split_axis=0, concat_axis=0, tiled=True)  26.5 us
    dynamic_slice x16, local copies, waits for them, and re-layouts, body(): lax.scan(forward_step, (zero_block, zero_block, zero_block), jnp.arange(s...  20.6 us
    ppermute x5, waiting for transfers between devices, butterfly_sum(): values = values + lax.ppermute(values, axis, route)  18.1 us
    select_n x8, other arithmetic, forward_step(): produced = jnp.where(active, hidden_new, produced)  14.3 us
  transfers between devices with their start and end apart: 24, of which 17 were waited for; matrix products, arithmetic and copies ran while one was open for 7% of the time, Pallas kernels for 0%

profile of v2, /device:TPU:32, one launch (start us, length us, event | category | flops | bytes accessed | tf_op | source)
XLA Modules:
  0.0 576.0 jit_solution(5351562655568085448)
XLA Ops:
  8.0 1.6 pad_maximum_fusion.5
  10.9 2.9 convert_reduce_fusion.4
  19.2 2.4 pad_maximum_fusion.3
  21.6 11.4 %all-to-all-start = ((bf16[32,4,2,2048]{3,2,1,0:T(2,128)(2,1)}), bf16[32,4,2,2048]{3,2,1,0:T(2,128)(2,1)S(1)}, u32[]{:S(2)}, u32[]{:S(2)}) async-start(bf16[32,4,2,2048]{3,2,1,0:T(2,128)(2,1)} %pad_maximum_fusion.3), calls=%async_computation | async-start | bytes 2097152 | tf_op jit(solution)/shard_map/all_to_all | solution.py:145
  38.1 26.5 %all-to-all-done = bf16[32,4,2,2048]{3,2,1,0:T(2,128)(2,1)S(1)} async-done(((bf16[32,4,2,2048]{3,2,1,0:T(2,128)(2,1)}), bf16[32,4,2,2048]{3,2,1,0:T(2,128)(2,1)S(1)}, u32[]{:S(2)}, u32[]{:S(2)}) %all-to-all-start) | async-done | bytes 1048608 | tf_op jit(solution)/shard_map/all_to_all | solution.py:145
  67.7 30.8 %all-gather.6.cloned.1.call-done = bf16[1,1024,2048]{1,2,0:T(8,128)(2,1)} async-done(((bf16[1,1024,64]{1,2,0:T(8,128)(2,1)}), bf16[1,1024,2048]{1,2,0:T(8,128)(2,1)}) %all-gather.6.cloned.1.call-update) | async-done | bytes 4194320 | tf_op jit(solution)/shard_map/all_gather | solution.py:129
  98.5 6.5 %copy.70 = bf16[1024,2048]{1,0:T(8,128)(2,1)} copy(bf16[1024,2048]{0,1:T(8,128)(2,1)} %bitcast.211) | data formatting | bytes 8388608
  105.0 81.3 %all-gather.4.cloned.1.call-done = bf16[2048,1536]{1,0:T(8,128)(2,1)} async-done(((bf16[64,1536]{1,0:T(8,128)(2,1)}), bf16[2048,1536]{1,0:T(8,128)(2,1)}) %all-gather.4.cloned.1.call-update) | async-done | bytes 6291472 | tf_op jit(solution)/shard_map/all_gather | solution.py:126
  187.0 131.7 %while.32 = (s32[]{:T(128)}, bf16[128,2048]{1,0:T(8,128)(2,1)S(1)}, bf16[128,2048]{1,0:T(8,128)(2,1)S(1)}, bf16[128,2048]{1,0:T(8,128)(2,1)}, s32[8]{0:T(128)}, ...) while((s32[]{:T(128)}, bf16[128,2048]{1,0:T(8,128)(2,1)S(1)}, ...), condition=%wide.region_14.15_spmd.clone.clone.clone, body=%wide.region_8.14_spmd.clone.clone.clone.sunk | while | flops 1452071296 | bytes 27381712 | solution.py:181
  187.0 1.4 dynamic_slice.80
  191.8 9.8 %conditional.10 = (bf16[128,2048]{1,0:T(8,128)(2,1)S(1)}) conditional(s32[]{:T(128)} %convert_element_type.314, () %tuple.131, (bf16[128,2048]{1,0:T(8,128)(2,1)S(1)}, f32[1,2048]{1,0:T(1,128)S(1)}, f32[1,2048]{1,0:T(1,128)S(1)}, bf16[2048,1536]{1,0:T(8,128)(2,1)}, s32[128]{0:T(128)}, /*index=5*/f32[128,1,32]{0,2,1:T(8,128)S(1)}, ...), branch_computations={%region_9.9_spmd, %region_10.13_spmd} | conditional | flops 1450756480 | bytes 20941832 | solution.py:176
  192.1 3.8 fusion.18
  198.7 2.9 fusion.13
  208.2 12.0 %collective-permute-start = (bf16[128,2048]{1,0:T(8,128)(2,1)S(1)}, bf16[128,2048]{1,0:T(8,128)(2,1)S(1)}, u32[]{:S(2)}, u32[]{:S(2)}) collective-permute-start(bf16[128,2048]{1,0:T(8,128)(2,1)S(1)} %get-tuple-element.980), channel_id=1, source_target_pairs={{0,32},{32,64},{64,96},{96,128},{128,160},{160,192},{192,224},{1,3... | collective-permute-start | bytes 1572872 | tf_op jit(solution)/shard_map/while/body/eval_jaxpr/ppermute | solution.py:178
  220.2 1.9 select_select_fusion.5
  225.9 6.1 %collective-permute-start = (bf16[128,2048]{1,0:T(8,128)(2,1)S(1)}, bf16[128,2048]{1,0:T(8,128)(2,1)S(1)}, u32[]{:S(2)}, u32[]{:S(2)}) collective-permute-start(bf16[128,2048]{1,0:T(8,128)(2,1)S(1)} %get-tuple-element.980), channel_id=1, source_target_pairs={{0,32},{32,64},{64,96},{96,128},{128,160},{160,192},{192,224},{1,3... | collective-permute-start | bytes 1572872 | tf_op jit(solution)/shard_map/while/body/eval_jaxpr/ppermute | solution.py:178
  232.0 1.9 select_select_fusion.5
  237.7 18.3 %collective-permute-start = (bf16[128,2048]{1,0:T(8,128)(2,1)S(1)}, bf16[128,2048]{1,0:T(8,128)(2,1)S(1)}, u32[]{:S(2)}, u32[]{:S(2)}) collective-permute-start(bf16[128,2048]{1,0:T(8,128)(2,1)S(1)} %get-tuple-element.980), channel_id=1, source_target_pairs={{0,32},{32,64},{64,96},{96,128},{128,160},{160,192},{192,224},{1,3... | collective-permute-start | bytes 1572872 | tf_op jit(solution)/shard_map/while/body/eval_jaxpr/ppermute | solution.py:178
  256.0 1.9 select_select_fusion.5
  261.7 8.6 %collective-permute-start = (bf16[128,2048]{1,0:T(8,128)(2,1)S(1)}, bf16[128,2048]{1,0:T(8,128)(2,1)S(1)}, u32[]{:S(2)}, u32[]{:S(2)}) collective-permute-start(bf16[128,2048]{1,0:T(8,128)(2,1)S(1)} %get-tuple-element.980), channel_id=1, source_target_pairs={{0,32},{32,64},{64,96},{96,128},{128,160},{160,192},{192,224},{1,3... | collective-permute-start | bytes 1572872 | tf_op jit(solution)/shard_map/while/body/eval_jaxpr/ppermute | solution.py:178
  270.3 1.9 select_select_fusion.5
  276.0 8.6 %collective-permute-start = (bf16[128,2048]{1,0:T(8,128)(2,1)S(1)}, bf16[128,2048]{1,0:T(8,128)(2,1)S(1)}, u32[]{:S(2)}, u32[]{:S(2)}) collective-permute-start(bf16[128,2048]{1,0:T(8,128)(2,1)S(1)} %get-tuple-element.980), channel_id=1, source_target_pairs={{0,32},{32,64},{64,96},{96,128},{128,160},{160,192},{192,224},{1,3... | collective-permute-start | bytes 1572872 | tf_op jit(solution)/shard_map/while/body/eval_jaxpr/ppermute | solution.py:178
  284.6 1.9 select_select_fusion.5
  290.3 8.6 %collective-permute-start = (bf16[128,2048]{1,0:T(8,128)(2,1)S(1)}, bf16[128,2048]{1,0:T(8,128)(2,1)S(1)}, u32[]{:S(2)}, u32[]{:S(2)}) collective-permute-start(bf16[128,2048]{1,0:T(8,128)(2,1)S(1)} %get-tuple-element.980), channel_id=1, source_target_pairs={{0,32},{32,64},{64,96},{96,128},{128,160},{160,192},{192,224},{1,3... | collective-permute-start | bytes 1572872 | tf_op jit(solution)/shard_map/while/body/eval_jaxpr/ppermute | solution.py:178
  298.9 1.9 select_select_fusion.5
  304.6 12.2 %collective-permute-start = (bf16[128,2048]{1,0:T(8,128)(2,1)S(1)}, bf16[128,2048]{1,0:T(8,128)(2,1)S(1)}, u32[]{:S(2)}, u32[]{:S(2)}) collective-permute-start(bf16[128,2048]{1,0:T(8,128)(2,1)S(1)} %get-tuple-element.980), channel_id=1, source_target_pairs={{0,32},{32,64},{64,96},{96,128},{128,160},{160,192},{192,224},{1,3... | collective-permute-start | bytes 1572872 | tf_op jit(solution)/shard_map/while/body/eval_jaxpr/ppermute | solution.py:178
  316.8 1.9 select_select_fusion.5
  318.7 224.3 %while.33 = (s32[]{:T(128)}, bf16[128,2048]{1,0:T(8,128)(2,1)S(1)}, f32[2048]{0:T(1024)}, s32[8]{0:T(128)}, s32[]{:T(128)}, /*index=5*/bf16[128,2048]{1,0:T(8,12...) while((s32[]{:T(128)}, bf16[128,2048]{1,0:T(8,128)(2,1)S(1)}, ...), condition=%wide.region_26.27_spmd.clone.clone.clone, body=%wide.region_15.26_spmd.clone.clone.clone.sunk | while | flops 2336234240 | bytes 66223192 | solution.py:202
  323.1 8.6 %collective-permute-done.1 = bf16[128,2048]{1,0:T(8,128)(2,1)S(1)} collective-permute-done((bf16[128,2048]{1,0:T(8,128)(2,1)S(1)}, bf16[128,2048]{1,0:T(8,128)(2,1)S(1)}, u32[]{:S(2)}, u32[]{:S(2)}) %collective-permute-start.1) | collective-permute-done | bytes 524320 | tf_op jit(solution)/shard_map/while/body/eval_jaxpr/ppermute | solution.py:199
  335.8 9.9 %collective-permute-done.1 = bf16[128,2048]{1,0:T(8,128)(2,1)S(1)} collective-permute-done((bf16[128,2048]{1,0:T(8,128)(2,1)S(1)}, bf16[128,2048]{1,0:T(8,128)(2,1)S(1)}, u32[]{:S(2)}, u32[]{:S(2)}) %collective-permute-start.1) | collective-permute-done | bytes 524320 | tf_op jit(solution)/shard_map/while/body/eval_jaxpr/ppermute | solution.py:199
  349.8 9.2 %collective-permute-done.1 = bf16[128,2048]{1,0:T(8,128)(2,1)S(1)} collective-permute-done((bf16[128,2048]{1,0:T(8,128)(2,1)S(1)}, bf16[128,2048]{1,0:T(8,128)(2,1)S(1)}, u32[]{:S(2)}, u32[]{:S(2)}) %collective-permute-start.1) | collective-permute-done | bytes 524320 | tf_op jit(solution)/shard_map/while/body/eval_jaxpr/ppermute | solution.py:199
  363.1 13.0 %collective-permute-done.1 = bf16[128,2048]{1,0:T(8,128)(2,1)S(1)} collective-permute-done((bf16[128,2048]{1,0:T(8,128)(2,1)S(1)}, bf16[128,2048]{1,0:T(8,128)(2,1)S(1)}, u32[]{:S(2)}, u32[]{:S(2)}) %collective-permute-start.1) | collective-permute-done | bytes 524320 | tf_op jit(solution)/shard_map/while/body/eval_jaxpr/ppermute | solution.py:199
  380.2 9.2 %collective-permute-done.1 = bf16[128,2048]{1,0:T(8,128)(2,1)S(1)} collective-permute-done((bf16[128,2048]{1,0:T(8,128)(2,1)S(1)}, bf16[128,2048]{1,0:T(8,128)(2,1)S(1)}, u32[]{:S(2)}, u32[]{:S(2)}) %collective-permute-start.1) | collective-permute-done | bytes 524320 | tf_op jit(solution)/shard_map/while/body/eval_jaxpr/ppermute | solution.py:199
  393.4 9.4 %collective-permute-done.1 = bf16[128,2048]{1,0:T(8,128)(2,1)S(1)} collective-permute-done((bf16[128,2048]{1,0:T(8,128)(2,1)S(1)}, bf16[128,2048]{1,0:T(8,128)(2,1)S(1)}, u32[]{:S(2)}, u32[]{:S(2)}) %collective-permute-start.1) | collective-permute-done | bytes 524320 | tf_op jit(solution)/shard_map/while/body/eval_jaxpr/ppermute | solution.py:199
  406.9 113.1 %collective-permute-done.1 = bf16[128,2048]{1,0:T(8,128)(2,1)S(1)} collective-permute-done((bf16[128,2048]{1,0:T(8,128)(2,1)S(1)}, bf16[128,2048]{1,0:T(8,128)(2,1)S(1)}, u32[]{:S(2)}, u32[]{:S(2)}) %collective-permute-start.1) | collective-permute-done | bytes 524320 | tf_op jit(solution)/shard_map/while/body/eval_jaxpr/ppermute | solution.py:199
  522.7 16.6 %conditional.11 = (bf16[128,2048]{1,0:T(8,128)(2,1)S(1)}, f32[2048]{0:T(1024)S(1)}) conditional(s32[]{:T(128)} %convert_element_type.315, () %tuple.134, (s32[]{:T(128)}, bf16[128,2048]{1,0:T(8,128)(2,1)S(1)}, bf16[128,2048]{1,0:T(8,128)(2,1)S(1)}, bf16[1024,2048]{1,0:T(8,128)(2,1)}, s32[128]{0:T(128)}, ...), branch_computations={%region_16.16_spmd, %region_17.25_spmd} | conditional | flops 2336226048 | bytes 63887432 | solution.py:196
  523.4 3.7 convolution_convert_fusion.4
  528.4 3.8 fusion.55
  536.5 2.3 multiply_reduce_fusion.1
  540.6 2.5 collective-permute-done.1
  543.6 3.3 collective-permute-done.2
  547.7 1.8 collective-permute-start.3
  549.4 2.8 collective-permute-done.3
  552.2 2.7 collective-permute-start.4
  554.9 4.9 collective-permute-done.4
  560.0 3.4 collective-permute-done.5
  563.4 1.4 collective-permute-start.6
  564.9 3.7 collective-permute-done.6
  (287 shorter events, 76.1 us)
Async XLA Ops:
  7.2 26.3 %copy-start.5 = (s32[4,32]{1,0:T(4,128)S(1)}, s32[4,32]{1,0:T(4,128)}, u32[]{:S(2)}) copy-start(s32[4,32]{1,0:T(4,128)} %param.19) | copy-start | bytes 1540
  7.2 91.3 %all-gather.6.cloned.1.call-start = ((), (), s32[]{:S(2)}) async-start(), calls=%async_computation.2 | async-start | bytes 4325376 | tf_op jit(solution)/shard_map/all_gather | solution.py:129
  7.9 178.4 %all-gather.4.cloned.1.call-start = ((), (), s32[]{:S(2)}) async-start(), calls=%async_computation.1 | async-start | bytes 6488064 | tf_op jit(solution)/shard_map/all_gather | solution.py:126
  21.6 43.0 %all-to-all-start = ((bf16[32,4,2,2048]{3,2,1,0:T(2,128)(2,1)}), bf16[32,4,2,2048]{3,2,1,0:T(2,128)(2,1)S(1)}, u32[]{:S(2)}, u32[]{:S(2)}) async-start(bf16[32,4,2,2048]{3,2,1,0:T(2,128)(2,1)} %pad_maximum_fusion.3), calls=%async_computation | async-start | bytes 2097152 | tf_op jit(solution)/shard_map/all_to_all | solution.py:145
  65.6 121.3 %copy-start.1 = (f32[1,2048]{1,0:T(1,128)S(1)}, f32[1,2048]{1,0:T(1,128)}, u32[]{:S(2)}) copy-start(f32[1,2048]{1,0:T(1,128)} %param.22) | copy-start | bytes 24580
  65.6 121.3 %copy-start.2 = (f32[1,2048]{1,0:T(1,128)S(1)}, f32[1,2048]{1,0:T(1,128)}, u32[]{:S(2)}) copy-start(f32[1,2048]{1,0:T(1,128)} %param.21) | copy-start | bytes 24580
  187.0 131.8 %copy-start = (bf16[4,32,2048]{2,1,0:T(8,128)(2,1)S(1)}, bf16[4,32,2048]{2,1,0:T(8,128)(2,1)}, u32[]{:S(2)}) copy-start(bf16[4,32,2048]{2,1,0:T(8,128)(2,1)} %param.20) | copy-start | bytes 1572868
  201.6 2.8 collective-permute-start
  208.2 14.0 %collective-permute-start = (bf16[128,2048]{1,0:T(8,128)(2,1)S(1)}, bf16[128,2048]{1,0:T(8,128)(2,1)S(1)}, u32[]{:S(2)}, u32[]{:S(2)}) collective-permute-start(bf16[128,2048]{1,0:T(8,128)(2,1)S(1)} %get-tuple-element.980), channel_id=1, source_target_pairs={{0,32},{32,64},{64,96},{96,128},{128,160},{160,192},{192,224},{1,3... | collective-permute-start | bytes 1572872 | tf_op jit(solution)/shard_map/while/body/eval_jaxpr/ppermute | solution.py:178
  225.9 8.0 %collective-permute-start = (bf16[128,2048]{1,0:T(8,128)(2,1)S(1)}, bf16[128,2048]{1,0:T(8,128)(2,1)S(1)}, u32[]{:S(2)}, u32[]{:S(2)}) collective-permute-start(bf16[128,2048]{1,0:T(8,128)(2,1)S(1)} %get-tuple-element.980), channel_id=1, source_target_pairs={{0,32},{32,64},{64,96},{96,128},{128,160},{160,192},{192,224},{1,3... | collective-permute-start | bytes 1572872 | tf_op jit(solution)/shard_map/while/body/eval_jaxpr/ppermute | solution.py:178
  237.7 20.2 %collective-permute-start = (bf16[128,2048]{1,0:T(8,128)(2,1)S(1)}, bf16[128,2048]{1,0:T(8,128)(2,1)S(1)}, u32[]{:S(2)}, u32[]{:S(2)}) collective-permute-start(bf16[128,2048]{1,0:T(8,128)(2,1)S(1)} %get-tuple-element.980), channel_id=1, source_target_pairs={{0,32},{32,64},{64,96},{96,128},{128,160},{160,192},{192,224},{1,3... | collective-permute-start | bytes 1572872 | tf_op jit(solution)/shard_map/while/body/eval_jaxpr/ppermute | solution.py:178
  261.7 10.5 %collective-permute-start = (bf16[128,2048]{1,0:T(8,128)(2,1)S(1)}, bf16[128,2048]{1,0:T(8,128)(2,1)S(1)}, u32[]{:S(2)}, u32[]{:S(2)}) collective-permute-start(bf16[128,2048]{1,0:T(8,128)(2,1)S(1)} %get-tuple-element.980), channel_id=1, source_target_pairs={{0,32},{32,64},{64,96},{96,128},{128,160},{160,192},{192,224},{1,3... | collective-permute-start | bytes 1572872 | tf_op jit(solution)/shard_map/while/body/eval_jaxpr/ppermute | solution.py:178
  276.0 10.5 %collective-permute-start = (bf16[128,2048]{1,0:T(8,128)(2,1)S(1)}, bf16[128,2048]{1,0:T(8,128)(2,1)S(1)}, u32[]{:S(2)}, u32[]{:S(2)}) collective-permute-start(bf16[128,2048]{1,0:T(8,128)(2,1)S(1)} %get-tuple-element.980), channel_id=1, source_target_pairs={{0,32},{32,64},{64,96},{96,128},{128,160},{160,192},{192,224},{1,3... | collective-permute-start | bytes 1572872 | tf_op jit(solution)/shard_map/while/body/eval_jaxpr/ppermute | solution.py:178
  290.3 10.5 %collective-permute-start = (bf16[128,2048]{1,0:T(8,128)(2,1)S(1)}, bf16[128,2048]{1,0:T(8,128)(2,1)S(1)}, u32[]{:S(2)}, u32[]{:S(2)}) collective-permute-start(bf16[128,2048]{1,0:T(8,128)(2,1)S(1)} %get-tuple-element.980), channel_id=1, source_target_pairs={{0,32},{32,64},{64,96},{96,128},{128,160},{160,192},{192,224},{1,3... | collective-permute-start | bytes 1572872 | tf_op jit(solution)/shard_map/while/body/eval_jaxpr/ppermute | solution.py:178
  304.6 14.1 %collective-permute-start = (bf16[128,2048]{1,0:T(8,128)(2,1)S(1)}, bf16[128,2048]{1,0:T(8,128)(2,1)S(1)}, u32[]{:S(2)}, u32[]{:S(2)}) collective-permute-start(bf16[128,2048]{1,0:T(8,128)(2,1)S(1)} %get-tuple-element.980), channel_id=1, source_target_pairs={{0,32},{32,64},{64,96},{96,128},{128,160},{160,192},{192,224},{1,3... | collective-permute-start | bytes 1572872 | tf_op jit(solution)/shard_map/while/body/eval_jaxpr/ppermute | solution.py:178
  321.6 1.4 copy-start.3
  321.7 9.9 %collective-permute-start.1 = (bf16[128,2048]{1,0:T(8,128)(2,1)S(1)}, bf16[128,2048]{1,0:T(8,128)(2,1)S(1)}, u32[]{:S(2)}, u32[]{:S(2)}) collective-permute-start(bf16[128,2048]{1,0:T(8,128)(2,1)S(1)} %get-tuple-element.878), channel_id=1, source_target_pairs={{32,0},{64,32},{96,64},{128,96},{160,128},{192,160},{224,192},{33,... | collective-permute-start | bytes 1572872 | tf_op jit(solution)/shard_map/while/body/eval_jaxpr/ppermute | solution.py:199
  323.1 8.6 %copy-start.4 = (f32[2048]{0:T(1024)}, f32[2048]{0:T(1024)S(1)}, u32[]{:S(2)}) copy-start(f32[2048]{0:T(1024)S(1)} %select_add_fusion.2) | copy-start | bytes 24580 | tf_op jit(solution)/shard_map/while
  334.4 1.4 copy-start.3
  334.5 11.2 %collective-permute-start.1 = (bf16[128,2048]{1,0:T(8,128)(2,1)S(1)}, bf16[128,2048]{1,0:T(8,128)(2,1)S(1)}, u32[]{:S(2)}, u32[]{:S(2)}) collective-permute-start(bf16[128,2048]{1,0:T(8,128)(2,1)S(1)} %get-tuple-element.878), channel_id=1, source_target_pairs={{32,0},{64,32},{96,64},{128,96},{160,128},{192,160},{224,192},{33,... | collective-permute-start | bytes 1572872 | tf_op jit(solution)/shard_map/while/body/eval_jaxpr/ppermute | solution.py:199
  335.8 9.9 %copy-start.4 = (f32[2048]{0:T(1024)}, f32[2048]{0:T(1024)S(1)}, u32[]{:S(2)}) copy-start(f32[2048]{0:T(1024)S(1)} %select_add_fusion.2) | copy-start | bytes 24580 | tf_op jit(solution)/shard_map/while
  348.4 1.4 copy-start.3
  348.5 10.5 %collective-permute-start.1 = (bf16[128,2048]{1,0:T(8,128)(2,1)S(1)}, bf16[128,2048]{1,0:T(8,128)(2,1)S(1)}, u32[]{:S(2)}, u32[]{:S(2)}) collective-permute-start(bf16[128,2048]{1,0:T(8,128)(2,1)S(1)} %get-tuple-element.878), channel_id=1, source_target_pairs={{32,0},{64,32},{96,64},{128,96},{160,128},{192,160},{224,192},{33,... | collective-permute-start | bytes 1572872 | tf_op jit(solution)/shard_map/while/body/eval_jaxpr/ppermute | solution.py:199
  349.8 9.2 %copy-start.4 = (f32[2048]{0:T(1024)}, f32[2048]{0:T(1024)S(1)}, u32[]{:S(2)}) copy-start(f32[2048]{0:T(1024)S(1)} %select_add_fusion.2) | copy-start | bytes 24580 | tf_op jit(solution)/shard_map/while
  361.6 1.4 copy-start.3
  361.7 14.3 %collective-permute-start.1 = (bf16[128,2048]{1,0:T(8,128)(2,1)S(1)}, bf16[128,2048]{1,0:T(8,128)(2,1)S(1)}, u32[]{:S(2)}, u32[]{:S(2)}) collective-permute-start(bf16[128,2048]{1,0:T(8,128)(2,1)S(1)} %get-tuple-element.878), channel_id=1, source_target_pairs={{32,0},{64,32},{96,64},{128,96},{160,128},{192,160},{224,192},{33,... | collective-permute-start | bytes 1572872 | tf_op jit(solution)/shard_map/while/body/eval_jaxpr/ppermute | solution.py:199
  363.1 13.0 %copy-start.4 = (f32[2048]{0:T(1024)}, f32[2048]{0:T(1024)S(1)}, u32[]{:S(2)}) copy-start(f32[2048]{0:T(1024)S(1)} %select_add_fusion.2) | copy-start | bytes 24580 | tf_op jit(solution)/shard_map/while
  378.7 1.4 copy-start.3
  378.8 10.5 %collective-permute-start.1 = (bf16[128,2048]{1,0:T(8,128)(2,1)S(1)}, bf16[128,2048]{1,0:T(8,128)(2,1)S(1)}, u32[]{:S(2)}, u32[]{:S(2)}) collective-permute-start(bf16[128,2048]{1,0:T(8,128)(2,1)S(1)} %get-tuple-element.878), channel_id=1, source_target_pairs={{32,0},{64,32},{96,64},{128,96},{160,128},{192,160},{224,192},{33,... | collective-permute-start | bytes 1572872 | tf_op jit(solution)/shard_map/while/body/eval_jaxpr/ppermute | solution.py:199
  380.2 9.2 %copy-start.4 = (f32[2048]{0:T(1024)}, f32[2048]{0:T(1024)S(1)}, u32[]{:S(2)}) copy-start(f32[2048]{0:T(1024)S(1)} %select_add_fusion.2) | copy-start | bytes 24580 | tf_op jit(solution)/shard_map/while
  392.0 1.4 copy-start.3
  392.1 10.7 %collective-permute-start.1 = (bf16[128,2048]{1,0:T(8,128)(2,1)S(1)}, bf16[128,2048]{1,0:T(8,128)(2,1)S(1)}, u32[]{:S(2)}, u32[]{:S(2)}) collective-permute-start(bf16[128,2048]{1,0:T(8,128)(2,1)S(1)} %get-tuple-element.878), channel_id=1, source_target_pairs={{32,0},{64,32},{96,64},{128,96},{160,128},{192,160},{224,192},{33,... | collective-permute-start | bytes 1572872 | tf_op jit(solution)/shard_map/while/body/eval_jaxpr/ppermute | solution.py:199
  393.4 9.4 %copy-start.4 = (f32[2048]{0:T(1024)}, f32[2048]{0:T(1024)S(1)}, u32[]{:S(2)}) copy-start(f32[2048]{0:T(1024)S(1)} %select_add_fusion.2) | copy-start | bytes 24580 | tf_op jit(solution)/shard_map/while
  405.5 1.4 copy-start.3
  405.6 114.4 %collective-permute-start.1 = (bf16[128,2048]{1,0:T(8,128)(2,1)S(1)}, bf16[128,2048]{1,0:T(8,128)(2,1)S(1)}, u32[]{:S(2)}, u32[]{:S(2)}) collective-permute-start(bf16[128,2048]{1,0:T(8,128)(2,1)S(1)} %get-tuple-element.878), channel_id=1, source_target_pairs={{32,0},{64,32},{96,64},{128,96},{160,128},{192,160},{224,192},{33,... | collective-permute-start | bytes 1572872 | tf_op jit(solution)/shard_map/while/body/eval_jaxpr/ppermute | solution.py:199
  406.9 113.1 %copy-start.4 = (f32[2048]{0:T(1024)}, f32[2048]{0:T(1024)S(1)}, u32[]{:S(2)}) copy-start(f32[2048]{0:T(1024)S(1)} %select_add_fusion.2) | copy-start | bytes 24580 | tf_op jit(solution)/shard_map/while
  522.7 17.9 %copy-start.3 = (f32[2048]{0:T(1024)S(1)}, f32[2048]{0:T(1024)}, u32[]{:S(2)}) copy-start(f32[2048]{0:T(1024)} %get-tuple-element.950) | copy-start | bytes 24580 | tf_op jit(solution)/shard_map/while
  533.4 2.7 slice-start
  534.3 2.2 slice-start.1
  539.3 3.8 collective-permute-start.1
  540.6 2.5 copy-start.4
  543.1 3.9 collective-permute-start.2
  547.7 4.5 collective-permute-start.3
  552.2 7.6 %collective-permute-start.4 = (f32[2048]{0:T(1024)S(1)}, f32[2048]{0:T(1024)S(1)}, u32[]{:S(2)}, u32[]{:S(2)}) collective-permute-start(f32[2048]{0:T(1024)S(1)} %add.305), channel_id=1, source_target_pairs={{0,4},{1,5},{2,6},{3,7},{4,0},{5,1},{6,2},{7,3},{8,12},{9,13},{10,... | collective-permute-start | bytes 24584 | tf_op jit(solution)/shard_map/ppermute | solution.py:83
  559.8 3.7 collective-permute-start.5
  563.4 5.2 collective-permute-start.6
Sparse Core Ops, SparseCore 0:
  10.6 87.8 all-gather.5
  101.0 85.2 all-gather.3

commit v3 on v2

--- a/solution.py
+++ b/solution.py
@@ -30,10 +30,10 @@
     )
 
 
-def layer(hidden_in, steering, gain_row, w_qkv, w_out, tables, allowed):
+def layer(hidden_in, steering, gain_row, w_qkv, w_out_t, tables, allowed):
     row_count, width = hidden_in.shape
     head_size = HD
-    query_heads = w_out.shape[0] // head_size
+    query_heads = w_out_t.shape[1] // head_size
     kv_heads = (w_qkv.shape[1] - query_heads * head_size) // (2 * head_size)
     group_size = query_heads // kv_heads
     residual = hidden_in.astype(jnp.float32) + steering
@@ -70,9 +70,10 @@
         "kgrs,skd->rkgd", weights, values, preferred_element_type=jnp.float32
     ).astype(jnp.bfloat16)
     mixed_heads = mixed_heads.reshape(row_count, query_heads * head_size)
-    return (residual + jnp.dot(mixed_heads, w_out, preferred_element_type=jnp.float32)).astype(
-        jnp.bfloat16
-    )
+    projected = lax.dot_general(
+        mixed_heads, w_out_t, (((1,), (1,)), ((), ())), preferred_element_type=jnp.float32
+    )
+    return (residual + projected).astype(jnp.bfloat16)
 
 
 def butterfly_sum(values, axis):
@@ -123,10 +124,12 @@
     micro_count, row_count, width = resid_in.shape
     capacity = row_count // dp_count + 1
     slot_count = dp_count * capacity
-    full_qkv = lax.all_gather(
-        jnp.concatenate([w_query[0], w_keyval[0]], axis=1), "dp", axis=0, tiled=True
-    )
-    full_out = lax.all_gather(w_out[0], "dp", axis=1, tiled=True)
+    qkv_cols = w_query.shape[2] + w_keyval.shape[2]
+    full_slab = lax.all_gather(
+        jnp.concatenate([w_query[0], w_keyval[0], w_out[0].T], axis=1), "dp", axis=0, tiled=True
+    )
+    full_qkv = full_slab[:, :qkv_cols]
+    full_out_t = full_slab[:, qkv_cols:]
     gain_row = gain[0]
     steering = steer[0]
     plans = [
@@ -162,7 +165,7 @@
     cotangent = cotangent.reshape(flat_count, width)
 
     def run_layer(hidden_in, steer_vec):
-        return layer(hidden_in, steer_vec, gain_row, full_qkv, full_out, tables, allowed)
+        return layer(hidden_in, steer_vec, gain_row, full_qkv, full_out_t, tables, allowed)
 
     zero_block = jnp.zeros((flat_count, width), jnp.bfloat16)
     forward_route = [(i, i + 1) for i in range(section_count - 1)]

time: 578 us -> 622 us (1.076)
  local copies, waits for them, and re-layouts: 34.4 us -> 48.8 us
  other arithmetic: 46.8 us -> 61.1 us
  starting transfers between devices: 104 us -> 112 us
    ppermute x8, waiting for transfers between devices: 175 us -> 228 us  [backward_step(): sent = lax.ppermute(grad_in, 'section', backward_route)]
    all_gather x2 -> x1, waiting for transfers between devices: 112 us -> 61.9 us  [body(): lax.all_gather(jnp.concatenate([w_query[0], w_keyval[0], w_out[0].T], axi...]
    slice x0 -> x2, local copies, waits for them, and re-layouts: none -> 10.3 us  [the longest x1 5.77 us: body(): full_qkv = full_slab[:, :qkv_cols]]
    ge x32, local copies, waits for them, and re-layouts: 0.25 us -> 10.1 us  [body(): flat_index[:, None] >= flat_index[None, :]]
    add x8, other arithmetic: 0.05 us -> 9.76 us  [backward_step(): return ((sent, grad_sum + steer_part), None)]
    unnamed x9 -> x6, local copies, waits for them, and re-layouts: 6.57 us -> 0.01 us
  transfers between devices with their start and end apart: 24 -> 23, of which waited for: 17 -> 16; matrix products, arithmetic and copies ran while one was open for 7% -> 7% of each run, Pallas kernels for 0% -> 0%
where the time goes in v3:
time: 622 us; the launch traced here: 620 us
  waiting for transfers between devices  337 us (54%)
  starting transfers between devices  112 us (18%)
  other arithmetic  61.1 us (10%)
  local copies, waits for them, and re-layouts  48.8 us (8%)
  matrix products  29.2 us (5%)
  loops' own time  17.9 us (3%)
  between operations  14.3 us (2%)
    ppermute x8, waiting for transfers between devices, backward_step(): sent = lax.ppermute(grad_in, 'section', backward_route)  228 us
    ppermute x8, starting transfers between devices, forward_step(): sent = lax.ppermute(hidden_new, 'section', forward_route)  78.9 us
    all_gather x1, waiting for transfers between devices, body(): lax.all_gather(jnp.concatenate([w_query[0], w_keyval[0], w_out[0].T], axi...  61.9 us
    all_to_all x1, waiting for transfers between devices, body(): lax.all_to_all(packed, 'dp', split_axis=0, concat_axis=0, tiled=True)  31.5 us
    dynamic_slice x16, local copies, waits for them, and re-layouts, body(): lax.scan(forward_step, (zero_block, zero_block, zero_block), jnp.arange(s...  15.1 us
    ppermute x5, waiting for transfers between devices, butterfly_sum(): values = values + lax.ppermute(values, axis, route)  14.4 us
    select_n x8, other arithmetic, forward_step(): produced = jnp.where(active, hidden_new, produced)  14.2 us
  transfers between devices with their start and end apart: 23, of which 16 were waited for; matrix products, arithmetic and copies ran while one was open for 7% of the time, Pallas kernels for 0%

profile of v3, /device:TPU:32, one launch (start us, length us, event | category | flops | bytes accessed | tf_op | source)
XLA Modules:
  0.0 619.9 jit_solution(16629257227800717719)
XLA Ops:
  7.2 1.7 pad_maximum_fusion.5
  10.3 2.9 convert_reduce_fusion.4
  18.5 2.4 pad_maximum_fusion.3
  20.9 11.4 %all-to-all-start = ((bf16[32,4,2,2048]{3,2,1,0:T(2,128)(2,1)}), bf16[32,4,2,2048]{3,2,1,0:T(2,128)(2,1)S(1)}, u32[]{:S(2)}, u32[]{:S(2)}) async-start(bf16[32,4,2,2048]{3,2,1,0:T(2,128)(2,1)} %pad_maximum_fusion.3), calls=%async_computation | async-start | bytes 2097152 | tf_op jit(solution)/shard_map/all_to_all | solution.py:148
  37.6 31.5 %all-to-all-done = bf16[32,4,2,2048]{3,2,1,0:T(2,128)(2,1)S(1)} async-done(((bf16[32,4,2,2048]{3,2,1,0:T(2,128)(2,1)}), bf16[32,4,2,2048]{3,2,1,0:T(2,128)(2,1)S(1)}, u32[]{:S(2)}, u32[]{:S(2)}) %all-to-all-start) | async-done | bytes 1048608 | tf_op jit(solution)/shard_map/all_to_all | solution.py:148
  72.2 61.9 %all-gather.2.cloned.1.call-done = bf16[2048,2560]{1,0:T(8,128)(2,1)} async-done(((bf16[64,2560]{1,0:T(8,128)(2,1)}), bf16[2048,2560]{1,0:T(8,128)(2,1)}) %all-gather.2.cloned.1.call-update) | async-done | bytes 10485776 | tf_op jit(solution)/shard_map/all_gather | solution.py:128
  134.1 5.8 slice.131
  139.8 4.6 slice.132
  144.5 135.5 %while.32 = (s32[]{:T(128)}, bf16[128,2048]{1,0:T(8,128)(2,1)S(1)}, bf16[128,2048]{1,0:T(8,128)(2,1)S(1)}, bf16[128,2048]{1,0:T(8,128)(2,1)}, s32[8]{0:T(128)S(1...) while((s32[]{:T(128)}, bf16[128,2048]{1,0:T(8,128)(2,1)S(1)}, ...), condition=%wide.region_14.15_spmd.clone.clone.clone, body=%wide.region_8.14_spmd.clone.clone.clone.sunk | while | flops 1452071296 | bytes 27643884 | solution.py:184
  149.2 10.5 %conditional.10 = (bf16[128,2048]{1,0:T(8,128)(2,1)S(1)}) conditional(s32[]{:T(128)} %convert_element_type.314, () %tuple.127, (bf16[128,2048]{1,0:T(8,128)(2,1)S(1)}, f32[1,2048]{1,0:T(1,128)S(1)}, f32[1,2048]{1,0:T(1,128)S(1)}, bf16[2048,1536]{1,0:T(8,128)(2,1)}, s32[128]{0:T(128)}, /*index=5*/f32[128,1,32]{0,2,1:T(8,128)S(1)}, ...), branch_computations={%region_9.9_spmd, %region_10.13_spmd} | conditional | flops 1450756480 | bytes 21204004 | solution.py:179
  149.5 3.8 fusion.18
  156.1 3.7 fusion.13
  166.4 12.8 %collective-permute-start = (bf16[128,2048]{1,0:T(8,128)(2,1)S(1)}, bf16[128,2048]{1,0:T(8,128)(2,1)S(1)}, u32[]{:S(2)}, u32[]{:S(2)}) collective-permute-start(bf16[128,2048]{1,0:T(8,128)(2,1)S(1)} %get-tuple-element.924), channel_id=1, source_target_pairs={{0,32},{32,64},{64,96},{96,128},{128,160},{160,192},{192,224},{1,3... | collective-permute-start | bytes 1572872 | tf_op jit(solution)/shard_map/while/body/eval_jaxpr/ppermute | solution.py:181
  179.2 1.9 select_select_fusion.5
  184.9 6.1 collective-permute-start
  191.0 1.9 select_select_fusion.5
  196.7 19.1 %collective-permute-start = (bf16[128,2048]{1,0:T(8,128)(2,1)S(1)}, bf16[128,2048]{1,0:T(8,128)(2,1)S(1)}, u32[]{:S(2)}, u32[]{:S(2)}) collective-permute-start(bf16[128,2048]{1,0:T(8,128)(2,1)S(1)} %get-tuple-element.924), channel_id=1, source_target_pairs={{0,32},{32,64},{64,96},{96,128},{128,160},{160,192},{192,224},{1,3... | collective-permute-start | bytes 1572872 | tf_op jit(solution)/shard_map/while/body/eval_jaxpr/ppermute | solution.py:181
  215.8 1.9 select_select_fusion.5
  221.5 8.6 %collective-permute-start = (bf16[128,2048]{1,0:T(8,128)(2,1)S(1)}, bf16[128,2048]{1,0:T(8,128)(2,1)S(1)}, u32[]{:S(2)}, u32[]{:S(2)}) collective-permute-start(bf16[128,2048]{1,0:T(8,128)(2,1)S(1)} %get-tuple-element.924), channel_id=1, source_target_pairs={{0,32},{32,64},{64,96},{96,128},{128,160},{160,192},{192,224},{1,3... | collective-permute-start | bytes 1572872 | tf_op jit(solution)/shard_map/while/body/eval_jaxpr/ppermute | solution.py:181
  230.1 1.9 select_select_fusion.5
  235.7 8.6 %collective-permute-start = (bf16[128,2048]{1,0:T(8,128)(2,1)S(1)}, bf16[128,2048]{1,0:T(8,128)(2,1)S(1)}, u32[]{:S(2)}, u32[]{:S(2)}) collective-permute-start(bf16[128,2048]{1,0:T(8,128)(2,1)S(1)} %get-tuple-element.924), channel_id=1, source_target_pairs={{0,32},{32,64},{64,96},{96,128},{128,160},{160,192},{192,224},{1,3... | collective-permute-start | bytes 1572872 | tf_op jit(solution)/shard_map/while/body/eval_jaxpr/ppermute | solution.py:181
  244.3 1.9 select_select_fusion.5
  250.0 8.6 %collective-permute-start = (bf16[128,2048]{1,0:T(8,128)(2,1)S(1)}, bf16[128,2048]{1,0:T(8,128)(2,1)S(1)}, u32[]{:S(2)}, u32[]{:S(2)}) collective-permute-start(bf16[128,2048]{1,0:T(8,128)(2,1)S(1)} %get-tuple-element.924), channel_id=1, source_target_pairs={{0,32},{32,64},{64,96},{96,128},{128,160},{160,192},{192,224},{1,3... | collective-permute-start | bytes 1572872 | tf_op jit(solution)/shard_map/while/body/eval_jaxpr/ppermute | solution.py:181
  258.6 1.9 select_select_fusion.5
  264.3 13.8 %collective-permute-start = (bf16[128,2048]{1,0:T(8,128)(2,1)S(1)}, bf16[128,2048]{1,0:T(8,128)(2,1)S(1)}, u32[]{:S(2)}, u32[]{:S(2)}) collective-permute-start(bf16[128,2048]{1,0:T(8,128)(2,1)S(1)} %get-tuple-element.924), channel_id=1, source_target_pairs={{0,32},{32,64},{64,96},{96,128},{128,160},{160,192},{192,224},{1,3... | collective-permute-start | bytes 1572872 | tf_op jit(solution)/shard_map/while/body/eval_jaxpr/ppermute | solution.py:181
  278.0 1.9 select_select_fusion.5
  280.0 306.1 %while.33 = (s32[]{:T(128)}, bf16[128,2048]{1,0:T(8,128)(2,1)S(1)}, f32[2048]{0:T(1024)}, s32[8]{0:T(128)}, s32[]{:T(128)}, /*index=5*/bf16[128,2048]{1,0:T(8,12...) while((s32[]{:T(128)}, bf16[128,2048]{1,0:T(8,128)(2,1)S(1)}, ...), condition=%wide.region_26.27_spmd.clone.clone.clone, body=%wide.region_15.26_spmd.clone.clone.clone.sunk | while | flops 2336234240 | bytes 80584168 | solution.py:205
  286.2 8.2 %collective-permute-done.1 = bf16[128,2048]{1,0:T(8,128)(2,1)S(1)} collective-permute-done((bf16[128,2048]{1,0:T(8,128)(2,1)}, bf16[128,2048]{1,0:T(8,128)(2,1)S(1)}, u32[]{:S(2)}, u32[]{:S(2)}) %collective-permute-start.1) | collective-permute-done | bytes 524320 | tf_op jit(solution)/shard_map/while/body/eval_jaxpr/ppermute | solution.py:202
  301.1 8.8 %collective-permute-done.1 = bf16[128,2048]{1,0:T(8,128)(2,1)S(1)} collective-permute-done((bf16[128,2048]{1,0:T(8,128)(2,1)}, bf16[128,2048]{1,0:T(8,128)(2,1)S(1)}, u32[]{:S(2)}, u32[]{:S(2)}) %collective-permute-start.1) | collective-permute-done | bytes 524320 | tf_op jit(solution)/shard_map/while/body/eval_jaxpr/ppermute | solution.py:202
  316.6 8.1 %collective-permute-done.1 = bf16[128,2048]{1,0:T(8,128)(2,1)S(1)} collective-permute-done((bf16[128,2048]{1,0:T(8,128)(2,1)}, bf16[128,2048]{1,0:T(8,128)(2,1)S(1)}, u32[]{:S(2)}, u32[]{:S(2)}) %collective-permute-start.1) | collective-permute-done | bytes 524320 | tf_op jit(solution)/shard_map/while/body/eval_jaxpr/ppermute | solution.py:202
  331.4 13.5 %collective-permute-done.1 = bf16[128,2048]{1,0:T(8,128)(2,1)S(1)} collective-permute-done((bf16[128,2048]{1,0:T(8,128)(2,1)}, bf16[128,2048]{1,0:T(8,128)(2,1)S(1)}, u32[]{:S(2)}, u32[]{:S(2)}) %collective-permute-start.1) | collective-permute-done | bytes 524320 | tf_op jit(solution)/shard_map/while/body/eval_jaxpr/ppermute | solution.py:202
  351.6 8.1 %collective-permute-done.1 = bf16[128,2048]{1,0:T(8,128)(2,1)S(1)} collective-permute-done((bf16[128,2048]{1,0:T(8,128)(2,1)}, bf16[128,2048]{1,0:T(8,128)(2,1)S(1)}, u32[]{:S(2)}, u32[]{:S(2)}) %collective-permute-start.1) | collective-permute-done | bytes 524320 | tf_op jit(solution)/shard_map/while/body/eval_jaxpr/ppermute | solution.py:202
  366.3 8.3 %collective-permute-done.1 = bf16[128,2048]{1,0:T(8,128)(2,1)S(1)} collective-permute-done((bf16[128,2048]{1,0:T(8,128)(2,1)}, bf16[128,2048]{1,0:T(8,128)(2,1)S(1)}, u32[]{:S(2)}, u32[]{:S(2)}) %collective-permute-start.1) | collective-permute-done | bytes 524320 | tf_op jit(solution)/shard_map/while/body/eval_jaxpr/ppermute | solution.py:202
  381.3 171.8 %collective-permute-done.1 = bf16[128,2048]{1,0:T(8,128)(2,1)S(1)} collective-permute-done((bf16[128,2048]{1,0:T(8,128)(2,1)}, bf16[128,2048]{1,0:T(8,128)(2,1)S(1)}, u32[]{:S(2)}, u32[]{:S(2)}) %collective-permute-start.1) | collective-permute-done | bytes 524320 | tf_op jit(solution)/shard_map/while/body/eval_jaxpr/ppermute | solution.py:202
  556.3 25.8 %conditional.11 = (bf16[128,2048]{1,0:T(8,128)(2,1)}, f32[2048]{0:T(1024)S(1)}) conditional(s32[]{:T(128)} %convert_element_type.315, () %tuple.130, (s32[]{:T(128)}, bf16[128,2048]{1,0:T(8,128)(2,1)}, bf16[128,2048]{1,0:T(8,128)(2,1)S(1)}, bf16[2048,1024]{1,0:T(8,128)(2,1)}, s32[128]{0:T(128)}, /*index=5*/bf16[128,2048]{1,0:T(8,128)(2,1)S(1)}, ...), branch_computations={%region_16.16_spmd, %region_17.25_spmd} | conditional | flops 2336226048 | bytes 78314008 | solution.py:199
  556.6 3.9 fusion.55
  564.3 2.9 convolution_convert_fusion.4
  568.0 2.4 fusion.39
  571.2 1.8 fusion.47
  573.0 1.9 fusion.50
  578.5 2.3 multiply_reduce_fusion.1
  586.1 2.2 collective-permute-start.2
  588.3 1.8 collective-permute-done.2
  590.8 3.6 collective-permute-start.3
  596.0 3.8 collective-permute-start.4
  599.9 3.7 collective-permute-done.4
  603.8 3.4 collective-permute-done.5
  608.7 3.7 collective-permute-done.6
  (285 shorter events, 109.0 us)
Async XLA Ops:
  7.2 25.2 %copy-start.19 = (s32[4,32]{1,0:T(4,128)S(1)}, s32[4,32]{1,0:T(4,128)}, u32[]{:S(2)}) copy-start(s32[4,32]{1,0:T(4,128)} %param.19) | copy-start | bytes 1540
  7.2 126.9 %all-gather.2.cloned.1.call-start = ((), (), s32[]{:S(2)}) async-start(), calls=%async_computation.1 | async-start | bytes 10813440 | tf_op jit(solution)/shard_map/all_gather | solution.py:128
  20.9 48.2 %all-to-all-start = ((bf16[32,4,2,2048]{3,2,1,0:T(2,128)(2,1)}), bf16[32,4,2,2048]{3,2,1,0:T(2,128)(2,1)S(1)}, u32[]{:S(2)}, u32[]{:S(2)}) async-start(bf16[32,4,2,2048]{3,2,1,0:T(2,128)(2,1)} %pad_maximum_fusion.3), calls=%async_computation | async-start | bytes 2097152 | tf_op jit(solution)/shard_map/all_to_all | solution.py:148
  139.8 4.6 copy-start.5
  139.8 4.6 copy-start.13
  149.2 4.7 copy-start.6
  159.8 2.8 collective-permute-start
  166.4 14.7 %collective-permute-start = (bf16[128,2048]{1,0:T(8,128)(2,1)S(1)}, bf16[128,2048]{1,0:T(8,128)(2,1)S(1)}, u32[]{:S(2)}, u32[]{:S(2)}) collective-permute-start(bf16[128,2048]{1,0:T(8,128)(2,1)S(1)} %get-tuple-element.924), channel_id=1, source_target_pairs={{0,32},{32,64},{64,96},{96,128},{128,160},{160,192},{192,224},{1,3... | collective-permute-start | bytes 1572872 | tf_op jit(solution)/shard_map/while/body/eval_jaxpr/ppermute | solution.py:181
  184.9 8.0 %collective-permute-start = (bf16[128,2048]{1,0:T(8,128)(2,1)S(1)}, bf16[128,2048]{1,0:T(8,128)(2,1)S(1)}, u32[]{:S(2)}, u32[]{:S(2)}) collective-permute-start(bf16[128,2048]{1,0:T(8,128)(2,1)S(1)} %get-tuple-element.924), channel_id=1, source_target_pairs={{0,32},{32,64},{64,96},{96,128},{128,160},{160,192},{192,224},{1,3... | collective-permute-start | bytes 1572872 | tf_op jit(solution)/shard_map/while/body/eval_jaxpr/ppermute | solution.py:181
  196.7 21.0 %collective-permute-start = (bf16[128,2048]{1,0:T(8,128)(2,1)S(1)}, bf16[128,2048]{1,0:T(8,128)(2,1)S(1)}, u32[]{:S(2)}, u32[]{:S(2)}) collective-permute-start(bf16[128,2048]{1,0:T(8,128)(2,1)S(1)} %get-tuple-element.924), channel_id=1, source_target_pairs={{0,32},{32,64},{64,96},{96,128},{128,160},{160,192},{192,224},{1,3... | collective-permute-start | bytes 1572872 | tf_op jit(solution)/shard_map/while/body/eval_jaxpr/ppermute | solution.py:181
  221.5 10.5 %collective-permute-start = (bf16[128,2048]{1,0:T(8,128)(2,1)S(1)}, bf16[128,2048]{1,0:T(8,128)(2,1)S(1)}, u32[]{:S(2)}, u32[]{:S(2)}) collective-permute-start(bf16[128,2048]{1,0:T(8,128)(2,1)S(1)} %get-tuple-element.924), channel_id=1, source_target_pairs={{0,32},{32,64},{64,96},{96,128},{128,160},{160,192},{192,224},{1,3... | collective-permute-start | bytes 1572872 | tf_op jit(solution)/shard_map/while/body/eval_jaxpr/ppermute | solution.py:181
  235.7 10.5 %collective-permute-start = (bf16[128,2048]{1,0:T(8,128)(2,1)S(1)}, bf16[128,2048]{1,0:T(8,128)(2,1)S(1)}, u32[]{:S(2)}, u32[]{:S(2)}) collective-permute-start(bf16[128,2048]{1,0:T(8,128)(2,1)S(1)} %get-tuple-element.924), channel_id=1, source_target_pairs={{0,32},{32,64},{64,96},{96,128},{128,160},{160,192},{192,224},{1,3... | collective-permute-start | bytes 1572872 | tf_op jit(solution)/shard_map/while/body/eval_jaxpr/ppermute | solution.py:181
  250.0 10.5 %collective-permute-start = (bf16[128,2048]{1,0:T(8,128)(2,1)S(1)}, bf16[128,2048]{1,0:T(8,128)(2,1)S(1)}, u32[]{:S(2)}, u32[]{:S(2)}) collective-permute-start(bf16[128,2048]{1,0:T(8,128)(2,1)S(1)} %get-tuple-element.924), channel_id=1, source_target_pairs={{0,32},{32,64},{64,96},{96,128},{128,160},{160,192},{192,224},{1,3... | collective-permute-start | bytes 1572872 | tf_op jit(solution)/shard_map/while/body/eval_jaxpr/ppermute | solution.py:181
  264.3 15.7 %collective-permute-start = (bf16[128,2048]{1,0:T(8,128)(2,1)S(1)}, bf16[128,2048]{1,0:T(8,128)(2,1)S(1)}, u32[]{:S(2)}, u32[]{:S(2)}) collective-permute-start(bf16[128,2048]{1,0:T(8,128)(2,1)S(1)} %get-tuple-element.924), channel_id=1, source_target_pairs={{0,32},{32,64},{64,96},{96,128},{128,160},{160,192},{192,224},{1,3... | collective-permute-start | bytes 1572872 | tf_op jit(solution)/shard_map/while/body/eval_jaxpr/ppermute | solution.py:181
  284.3 10.2 %collective-permute-start.1 = (bf16[128,2048]{1,0:T(8,128)(2,1)}, bf16[128,2048]{1,0:T(8,128)(2,1)S(1)}, u32[]{:S(2)}, u32[]{:S(2)}) collective-permute-start(bf16[128,2048]{1,0:T(8,128)(2,1)} %get-tuple-element.822), channel_id=1, source_target_pairs={{32,0},{64,32},{96,64},{128,96},{160,128},{192,160},{224,192},{33,... | collective-permute-start | bytes 1572872 | tf_op jit(solution)/shard_map/while/body/eval_jaxpr/ppermute | solution.py:202
  298.5 11.4 %collective-permute-start.1 = (bf16[128,2048]{1,0:T(8,128)(2,1)}, bf16[128,2048]{1,0:T(8,128)(2,1)S(1)}, u32[]{:S(2)}, u32[]{:S(2)}) collective-permute-start(bf16[128,2048]{1,0:T(8,128)(2,1)} %get-tuple-element.822), channel_id=1, source_target_pairs={{32,0},{64,32},{96,64},{128,96},{160,128},{192,160},{224,192},{33,... | collective-permute-start | bytes 1572872 | tf_op jit(solution)/shard_map/while/body/eval_jaxpr/ppermute | solution.py:202
  314.0 10.7 %collective-permute-start.1 = (bf16[128,2048]{1,0:T(8,128)(2,1)}, bf16[128,2048]{1,0:T(8,128)(2,1)S(1)}, u32[]{:S(2)}, u32[]{:S(2)}) collective-permute-start(bf16[128,2048]{1,0:T(8,128)(2,1)} %get-tuple-element.822), channel_id=1, source_target_pairs={{32,0},{64,32},{96,64},{128,96},{160,128},{192,160},{224,192},{33,... | collective-permute-start | bytes 1572872 | tf_op jit(solution)/shard_map/while/body/eval_jaxpr/ppermute | solution.py:202
  328.8 16.1 %collective-permute-start.1 = (bf16[128,2048]{1,0:T(8,128)(2,1)}, bf16[128,2048]{1,0:T(8,128)(2,1)S(1)}, u32[]{:S(2)}, u32[]{:S(2)}) collective-permute-start(bf16[128,2048]{1,0:T(8,128)(2,1)} %get-tuple-element.822), channel_id=1, source_target_pairs={{32,0},{64,32},{96,64},{128,96},{160,128},{192,160},{224,192},{33,... | collective-permute-start | bytes 1572872 | tf_op jit(solution)/shard_map/while/body/eval_jaxpr/ppermute | solution.py:202
  349.0 10.7 %collective-permute-start.1 = (bf16[128,2048]{1,0:T(8,128)(2,1)}, bf16[128,2048]{1,0:T(8,128)(2,1)S(1)}, u32[]{:S(2)}, u32[]{:S(2)}) collective-permute-start(bf16[128,2048]{1,0:T(8,128)(2,1)} %get-tuple-element.822), channel_id=1, source_target_pairs={{32,0},{64,32},{96,64},{128,96},{160,128},{192,160},{224,192},{33,... | collective-permute-start | bytes 1572872 | tf_op jit(solution)/shard_map/while/body/eval_jaxpr/ppermute | solution.py:202
  363.7 10.9 %collective-permute-start.1 = (bf16[128,2048]{1,0:T(8,128)(2,1)}, bf16[128,2048]{1,0:T(8,128)(2,1)S(1)}, u32[]{:S(2)}, u32[]{:S(2)}) collective-permute-start(bf16[128,2048]{1,0:T(8,128)(2,1)} %get-tuple-element.822), channel_id=1, source_target_pairs={{32,0},{64,32},{96,64},{128,96},{160,128},{192,160},{224,192},{33,... | collective-permute-start | bytes 1572872 | tf_op jit(solution)/shard_map/while/body/eval_jaxpr/ppermute | solution.py:202
  378.7 174.4 %collective-permute-start.1 = (bf16[128,2048]{1,0:T(8,128)(2,1)}, bf16[128,2048]{1,0:T(8,128)(2,1)S(1)}, u32[]{:S(2)}, u32[]{:S(2)}) collective-permute-start(bf16[128,2048]{1,0:T(8,128)(2,1)} %get-tuple-element.822), channel_id=1, source_target_pairs={{32,0},{64,32},{96,64},{128,96},{160,128},{192,160},{224,192},{33,... | collective-permute-start | bytes 1572872 | tf_op jit(solution)/shard_map/while/body/eval_jaxpr/ppermute | solution.py:202
  556.3 7.9 %copy-start.1 = (bf16[128,2048]{1,0:T(8,128)(2,1)}, bf16[128,2048]{1,0:T(8,128)(2,1)S(1)}, u32[]{:S(2)}) copy-start(bf16[128,2048]{1,0:T(8,128)(2,1)S(1)} %get-tuple-element.204) | copy-start | bytes 1572868 | tf_op jit(solution)/shard_map/while/body/eval_jaxpr/cond
  556.5 4.6 copy-start.17
  556.6 4.5 copy-start.15
  556.6 7.7 %copy-start.3 = (bf16[128,2048]{1,0:T(8,128)(2,1)S(1)}, bf16[128,2048]{1,0:T(8,128)(2,1)}, u32[]{:S(2)}) copy-start(bf16[128,2048]{1,0:T(8,128)(2,1)} %get-tuple-element.203) | copy-start | bytes 1572868 | tf_op jit(solution)/shard_map/while/body/eval_jaxpr/cond
  560.9 7.1 %copy-start.7 = (bf16[128,16,32]{0,2,1:T(8,128)(2,1)}, bf16[128,16,32]{0,2,1:T(8,128)(2,1)S(1)}, u32[]{:S(2)}) copy-start(bf16[128,16,32]{0,2,1:T(8,128)(2,1)S(1)} %get-tuple-element.616) | copy-start | bytes 393220 | tf_op jit(solution)/shard_map/while/body/eval_jaxpr/cond
  560.9 7.1 %copy-start.8 = (bf16[128,16,32]{0,2,1:T(8,128)(2,1)}, bf16[128,16,32]{0,2,1:T(8,128)(2,1)S(1)}, u32[]{:S(2)}) copy-start(bf16[128,16,32]{0,2,1:T(8,128)(2,1)S(1)} %get-tuple-element.617) | copy-start | bytes 393220 | tf_op jit(solution)/shard_map/while/body/eval_jaxpr/cond
  561.1 6.9 %copy-start.9 = (bf16[128,4,32]{0,2,1:T(8,128)(2,1)}, bf16[128,4,32]{0,2,1:T(8,128)(2,1)S(1)}, u32[]{:S(2)}) copy-start(bf16[128,4,32]{0,2,1:T(8,128)(2,1)S(1)} %get-tuple-element.620) | copy-start | bytes 98308 | tf_op jit(solution)/shard_map/while/body/eval_jaxpr/cond
  561.1 6.9 %copy-start.11 = (bf16[128,4,32]{0,2,1:T(8,128)(2,1)}, bf16[128,4,32]{0,2,1:T(8,128)(2,1)S(1)}, u32[]{:S(2)}) copy-start(bf16[128,4,32]{0,2,1:T(8,128)(2,1)S(1)} %get-tuple-element.621) | copy-start | bytes 98308 | tf_op jit(solution)/shard_map/while/body/eval_jaxpr/cond
  562.4 1.0 copy-start
  568.0 10.5 %slice-start = ((s8[6291456]{0:T(1024)(128)(4,1)}), s8[2097152]{0:T(1024)(128)(4,1)S(1)}, s32[]{:S(2)}) async-start(s8[6291456]{0:T(1024)(128)(4,1)} %bitcast.187), calls=%async_computation.2 | async-start | bytes 4194304 | tf_op jit(solution)/shard_map/while/body/eval_jaxpr/cond
  571.1 7.0 %copy-start.14 = (bf16[4,64,128]{2,1,0:T(8,128)(2,1)S(1)}, bf16[4,64,128]{2,1,0:T(8,128)(2,1)}, u32[]{:S(2)}) copy-start(bf16[4,64,128]{2,1,0:T(8,128)(2,1)} %fusion.39) | copy-start | bytes 196612 | tf_op jit(solution)/shard_map/while/body/eval_jaxpr/cond
  571.1 7.0 %copy-start.10 = (bf16[128,4,32]{0,2,1:T(8,128)(2,1)S(1)}, bf16[128,4,32]{0,2,1:T(8,128)(2,1)}, u32[]{:S(2)}) copy-start(bf16[128,4,32]{0,2,1:T(8,128)(2,1)} %copy-done.9) | copy-start | bytes 98308 | tf_op jit(solution)/shard_map/while/body/eval_jaxpr/cond
  571.1 7.0 %copy-start.12 = (bf16[128,4,32]{0,2,1:T(8,128)(2,1)S(1)}, bf16[128,4,32]{0,2,1:T(8,128)(2,1)}, u32[]{:S(2)}) copy-start(bf16[128,4,32]{0,2,1:T(8,128)(2,1)} %copy-done.11) | copy-start | bytes 98308 | tf_op jit(solution)/shard_map/while/body/eval_jaxpr/cond
  573.0 5.4 slice-start.1
  578.0 2.8 copy-start.18
  578.0 2.8 copy-start.2
  578.0 2.8 copy-start.4
  578.0 2.8 copy-start.16
  582.1 4.0 collective-permute-start.1
  586.1 4.1 collective-permute-start.2
  590.8 5.2 collective-permute-start.3
  596.0 7.6 %collective-permute-start.4 = (f32[2048]{0:T(1024)S(1)}, f32[2048]{0:T(1024)S(1)}, u32[]{:S(2)}, u32[]{:S(2)}) collective-permute-start(f32[2048]{0:T(1024)S(1)} %add.305), channel_id=1, source_target_pairs={{0,4},{1,5},{2,6},{3,7},{4,0},{5,1},{6,2},{7,3},{8,12},{9,13},{10,... | collective-permute-start | bytes 24584 | tf_op jit(solution)/shard_map/ppermute | solution.py:84
  603.6 3.7 collective-permute-start.5
  607.3 5.2 collective-permute-start.6
Sparse Core Ops, SparseCore 0:
  10.6 123.4 all-gather.1

commit v4 on v2

--- a/solution.py
+++ b/solution.py
@@ -123,10 +123,13 @@
     micro_count, row_count, width = resid_in.shape
     capacity = row_count // dp_count + 1
     slot_count = dp_count * capacity
-    full_qkv = lax.all_gather(
-        jnp.concatenate([w_query[0], w_keyval[0]], axis=1), "dp", axis=0, tiled=True
-    )
-    full_out = lax.all_gather(w_out[0], "dp", axis=1, tiled=True)
+    qkv_cols = w_query.shape[2] + w_keyval.shape[2]
+    full_slab = lax.all_gather(
+        jnp.concatenate([w_query[0], w_keyval[0], w_out[0].T], axis=1), "dp", axis=0, tiled=True
+    )
+    full_qkv, full_out = lax.optimization_barrier(
+        (full_slab[:, :qkv_cols], full_slab[:, qkv_cols:].T)
+    )
     gain_row = gain[0]
     steering = steer[0]
     plans = [

time: 578 us -> 627 us (1.085)
  local copies, waits for them, and re-layouts: 34.4 us -> 54.9 us
  other arithmetic: 46.8 us -> 61.1 us
  waiting for transfers between devices: 333 us -> 340 us
    ppermute x8, waiting for transfers between devices: 175 us -> 232 us  [backward_step(): sent = lax.ppermute(grad_in, 'section', backward_route)]
    all_gather x2 -> x1, waiting for transfers between devices: 112 us -> 61.9 us  [body(): lax.all_gather(jnp.concatenate([w_query[0], w_keyval[0], w_out[0].T], axi...]
    ge x32, local copies, waits for them, and re-layouts: 0.25 us -> 10.1 us  [body(): flat_index[:, None] >= flat_index[None, :]]
    add x8, other arithmetic: 0.05 us -> 9.76 us  [backward_step(): return ((sent, grad_sum + steer_part), None)]
  transfers between devices with their start and end apart: 24 -> 23, of which waited for: 17 -> 16; matrix products, arithmetic and copies ran while one was open for 7% -> 7% of each run, Pallas kernels for 0% -> 0%
where the time goes in v4:
time: 627 us; the launch traced here: 624 us
  waiting for transfers between devices  340 us (54%)
  starting transfers between devices  109 us (17%)
  other arithmetic  61.1 us (10%)
  local copies, waits for them, and re-layouts  54.9 us (9%)
  matrix products  29.2 us (5%)
  loops' own time  16 us (3%)
  between operations  14.3 us (2%)
    ppermute x8, waiting for transfers between devices, backward_step(): sent = lax.ppermute(grad_in, 'section', backward_route)  232 us
    ppermute x8, starting transfers between devices, forward_step(): sent = lax.ppermute(hidden_new, 'section', forward_route)  75.7 us
    all_gather x1, waiting for transfers between devices, body(): lax.all_gather(jnp.concatenate([w_query[0], w_keyval[0], w_out[0].T], axi...  61.9 us
    all_to_all x1, waiting for transfers between devices, body(): lax.all_to_all(packed, 'dp', split_axis=0, concat_axis=0, tiled=True)  31.5 us
    dynamic_slice x16, local copies, waits for them, and re-layouts, body(): lax.scan(forward_step, (zero_block, zero_block, zero_block), jnp.arange(s...  14.7 us
    ppermute x5, waiting for transfers between devices, butterfly_sum(): values = values + lax.ppermute(values, axis, route)  14.3 us
    select_n x8, other arithmetic, forward_step(): produced = jnp.where(active, hidden_new, produced)  14.2 us
  transfers between devices with their start and end apart: 23, of which 16 were waited for; matrix products, arithmetic and copies ran while one was open for 7% of the time, Pallas kernels for 0%

profile of v4, /device:TPU:32, one launch (start us, length us, event | category | flops | bytes accessed | tf_op | source)
XLA Modules:
  0.0 624.4 jit_solution(16720171767642633761)
XLA Ops:
  10.3 2.9 convert_reduce_fusion.4
  18.5 2.4 pad_maximum_fusion.3
  20.9 11.4 %all-to-all-start = ((bf16[32,4,2,2048]{3,2,1,0:T(2,128)(2,1)}), bf16[32,4,2,2048]{3,2,1,0:T(2,128)(2,1)S(1)}, u32[]{:S(2)}, u32[]{:S(2)}) async-start(bf16[32,4,2,2048]{3,2,1,0:T(2,128)(2,1)} %pad_maximum_fusion.3), calls=%async_computation | async-start | bytes 2097152 | tf_op jit(solution)/shard_map/all_to_all | solution.py:148
  37.6 31.5 %all-to-all-done = bf16[32,4,2,2048]{3,2,1,0:T(2,128)(2,1)S(1)} async-done(((bf16[32,4,2,2048]{3,2,1,0:T(2,128)(2,1)}), bf16[32,4,2,2048]{3,2,1,0:T(2,128)(2,1)S(1)}, u32[]{:S(2)}, u32[]{:S(2)}) %all-to-all-start) | async-done | bytes 1048608 | tf_op jit(solution)/shard_map/all_to_all | solution.py:148
  72.2 61.9 %all-gather.2.cloned.1.call-done = bf16[2048,2560]{1,0:T(8,128)(2,1)} async-done(((bf16[64,2560]{1,0:T(8,128)(2,1)}), bf16[2048,2560]{1,0:T(8,128)(2,1)}) %all-gather.2.cloned.1.call-update) | async-done | bytes 10485776 | tf_op jit(solution)/shard_map/all_gather | solution.py:127
  134.1 5.8 slice.131
  139.8 4.5 slice_bitcast_fusion
  144.4 6.5 %copy.72 = bf16[1024,2048]{1,0:T(8,128)(2,1)} copy(bf16[1024,2048]{0,1:T(8,128)(2,1)} %slice_bitcast_fusion) | data formatting | bytes 8388608
  151.0 128.8 %while.32 = (s32[]{:T(128)}, bf16[128,2048]{1,0:T(8,128)(2,1)S(1)}, bf16[128,2048]{1,0:T(8,128)(2,1)S(1)}, bf16[128,2048]{1,0:T(8,128)(2,1)}, s32[8]{0:T(128)S(1...) while((s32[]{:T(128)}, bf16[128,2048]{1,0:T(8,128)(2,1)S(1)}, ...), condition=%wide.region_14.15_spmd.clone.clone.clone, body=%wide.region_8.14_spmd.clone.clone.clone.sunk | while | flops 1452071296 | bytes 27643884 | solution.py:184
  155.4 9.8 %conditional.10 = (bf16[128,2048]{1,0:T(8,128)(2,1)S(1)}) conditional(s32[]{:T(128)} %convert_element_type.314, () %tuple.137, (bf16[128,2048]{1,0:T(8,128)(2,1)S(1)}, f32[1,2048]{1,0:T(1,128)S(1)}, f32[1,2048]{1,0:T(1,128)S(1)}, bf16[2048,1536]{1,0:T(8,128)(2,1)}, s32[128]{0:T(128)}, /*index=5*/f32[128,1,32]{0,2,1:T(8,128)S(1)}, ...), branch_computations={%region_9.9_spmd, %region_10.13_spmd} | conditional | flops 1450756480 | bytes 21204004 | solution.py:179
  155.6 3.8 fusion.18
  162.2 2.9 fusion.13
  171.4 12.0 %collective-permute-start = (bf16[128,2048]{1,0:T(8,128)(2,1)S(1)}, bf16[128,2048]{1,0:T(8,128)(2,1)S(1)}, u32[]{:S(2)}, u32[]{:S(2)}) collective-permute-start(bf16[128,2048]{1,0:T(8,128)(2,1)S(1)} %get-tuple-element.1040), channel_id=1, source_target_pairs={{0,32},{32,64},{64,96},{96,128},{128,160},{160,192},{192,224},{1,3... | collective-permute-start | bytes 1572872 | tf_op jit(solution)/shard_map/while/body/eval_jaxpr/ppermute | solution.py:181
  183.5 1.9 select_select_fusion.5
  188.8 6.1 collective-permute-start
  194.9 1.9 select_select_fusion.5
  200.2 18.3 %collective-permute-start = (bf16[128,2048]{1,0:T(8,128)(2,1)S(1)}, bf16[128,2048]{1,0:T(8,128)(2,1)S(1)}, u32[]{:S(2)}, u32[]{:S(2)}) collective-permute-start(bf16[128,2048]{1,0:T(8,128)(2,1)S(1)} %get-tuple-element.1040), channel_id=1, source_target_pairs={{0,32},{32,64},{64,96},{96,128},{128,160},{160,192},{192,224},{1,3... | collective-permute-start | bytes 1572872 | tf_op jit(solution)/shard_map/while/body/eval_jaxpr/ppermute | solution.py:181
  218.6 1.9 select_select_fusion.5
  223.9 8.6 %collective-permute-start = (bf16[128,2048]{1,0:T(8,128)(2,1)S(1)}, bf16[128,2048]{1,0:T(8,128)(2,1)S(1)}, u32[]{:S(2)}, u32[]{:S(2)}) collective-permute-start(bf16[128,2048]{1,0:T(8,128)(2,1)S(1)} %get-tuple-element.1040), channel_id=1, source_target_pairs={{0,32},{32,64},{64,96},{96,128},{128,160},{160,192},{192,224},{1,3... | collective-permute-start | bytes 1572872 | tf_op jit(solution)/shard_map/while/body/eval_jaxpr/ppermute | solution.py:181
  232.5 1.9 select_select_fusion.5
  237.8 8.6 %collective-permute-start = (bf16[128,2048]{1,0:T(8,128)(2,1)S(1)}, bf16[128,2048]{1,0:T(8,128)(2,1)S(1)}, u32[]{:S(2)}, u32[]{:S(2)}) collective-permute-start(bf16[128,2048]{1,0:T(8,128)(2,1)S(1)} %get-tuple-element.1040), channel_id=1, source_target_pairs={{0,32},{32,64},{64,96},{96,128},{128,160},{160,192},{192,224},{1,3... | collective-permute-start | bytes 1572872 | tf_op jit(solution)/shard_map/while/body/eval_jaxpr/ppermute | solution.py:181
  246.4 1.9 select_select_fusion.5
  251.7 8.6 %collective-permute-start = (bf16[128,2048]{1,0:T(8,128)(2,1)S(1)}, bf16[128,2048]{1,0:T(8,128)(2,1)S(1)}, u32[]{:S(2)}, u32[]{:S(2)}) collective-permute-start(bf16[128,2048]{1,0:T(8,128)(2,1)S(1)} %get-tuple-element.1040), channel_id=1, source_target_pairs={{0,32},{32,64},{64,96},{96,128},{128,160},{160,192},{192,224},{1,3... | collective-permute-start | bytes 1572872 | tf_op jit(solution)/shard_map/while/body/eval_jaxpr/ppermute | solution.py:181
  260.3 1.9 select_select_fusion.5
  265.7 12.2 %collective-permute-start = (bf16[128,2048]{1,0:T(8,128)(2,1)S(1)}, bf16[128,2048]{1,0:T(8,128)(2,1)S(1)}, u32[]{:S(2)}, u32[]{:S(2)}) collective-permute-start(bf16[128,2048]{1,0:T(8,128)(2,1)S(1)} %get-tuple-element.1040), channel_id=1, source_target_pairs={{0,32},{32,64},{64,96},{96,128},{128,160},{160,192},{192,224},{1,3... | collective-permute-start | bytes 1572872 | tf_op jit(solution)/shard_map/while/body/eval_jaxpr/ppermute | solution.py:181
  277.9 1.9 select_select_fusion.5
  279.8 310.8 %while.33 = (s32[]{:T(128)}, bf16[128,2048]{1,0:T(8,128)(2,1)S(1)}, f32[2048]{0:T(1024)}, s32[8]{0:T(128)}, s32[]{:T(128)}, /*index=5*/bf16[128,2048]{1,0:T(8,12...) while((s32[]{:T(128)}, bf16[128,2048]{1,0:T(8,128)(2,1)S(1)}, ...), condition=%wide.region_26.27_spmd.clone.clone.clone, body=%wide.region_15.26_spmd.clone.clone.clone.sunk | while | flops 2336234240 | bytes 80584168 | solution.py:205
  286.1 8.2 %collective-permute-done.1 = bf16[128,2048]{1,0:T(8,128)(2,1)S(1)} collective-permute-done((bf16[128,2048]{1,0:T(8,128)(2,1)}, bf16[128,2048]{1,0:T(8,128)(2,1)S(1)}, u32[]{:S(2)}, u32[]{:S(2)}) %collective-permute-start.1) | collective-permute-done | bytes 524320 | tf_op jit(solution)/shard_map/while/body/eval_jaxpr/ppermute | solution.py:202
  301.1 8.8 %collective-permute-done.1 = bf16[128,2048]{1,0:T(8,128)(2,1)S(1)} collective-permute-done((bf16[128,2048]{1,0:T(8,128)(2,1)}, bf16[128,2048]{1,0:T(8,128)(2,1)S(1)}, u32[]{:S(2)}, u32[]{:S(2)}) %collective-permute-start.1) | collective-permute-done | bytes 524320 | tf_op jit(solution)/shard_map/while/body/eval_jaxpr/ppermute | solution.py:202
  316.7 8.1 %collective-permute-done.1 = bf16[128,2048]{1,0:T(8,128)(2,1)S(1)} collective-permute-done((bf16[128,2048]{1,0:T(8,128)(2,1)}, bf16[128,2048]{1,0:T(8,128)(2,1)S(1)}, u32[]{:S(2)}, u32[]{:S(2)}) %collective-permute-start.1) | collective-permute-done | bytes 524320 | tf_op jit(solution)/shard_map/while/body/eval_jaxpr/ppermute | solution.py:202
  331.5 11.9 %collective-permute-done.1 = bf16[128,2048]{1,0:T(8,128)(2,1)S(1)} collective-permute-done((bf16[128,2048]{1,0:T(8,128)(2,1)}, bf16[128,2048]{1,0:T(8,128)(2,1)S(1)}, u32[]{:S(2)}, u32[]{:S(2)}) %collective-permute-start.1) | collective-permute-done | bytes 524320 | tf_op jit(solution)/shard_map/while/body/eval_jaxpr/ppermute | solution.py:202
  350.1 8.1 %collective-permute-done.1 = bf16[128,2048]{1,0:T(8,128)(2,1)S(1)} collective-permute-done((bf16[128,2048]{1,0:T(8,128)(2,1)}, bf16[128,2048]{1,0:T(8,128)(2,1)S(1)}, u32[]{:S(2)}, u32[]{:S(2)}) %collective-permute-start.1) | collective-permute-done | bytes 524320 | tf_op jit(solution)/shard_map/while/body/eval_jaxpr/ppermute | solution.py:202
  365.0 8.3 %collective-permute-done.1 = bf16[128,2048]{1,0:T(8,128)(2,1)S(1)} collective-permute-done((bf16[128,2048]{1,0:T(8,128)(2,1)}, bf16[128,2048]{1,0:T(8,128)(2,1)S(1)}, u32[]{:S(2)}, u32[]{:S(2)}) %collective-permute-start.1) | collective-permute-done | bytes 524320 | tf_op jit(solution)/shard_map/while/body/eval_jaxpr/ppermute | solution.py:202
  380.0 176.7 %collective-permute-done.1 = bf16[128,2048]{1,0:T(8,128)(2,1)S(1)} collective-permute-done((bf16[128,2048]{1,0:T(8,128)(2,1)}, bf16[128,2048]{1,0:T(8,128)(2,1)S(1)}, u32[]{:S(2)}, u32[]{:S(2)}) %collective-permute-start.1) | collective-permute-done | bytes 524320 | tf_op jit(solution)/shard_map/while/body/eval_jaxpr/ppermute | solution.py:202
  560.0 26.6 %conditional.11 = (bf16[128,2048]{1,0:T(8,128)(2,1)}, f32[2048]{0:T(1024)S(1)}) conditional(s32[]{:T(128)} %convert_element_type.315, () %tuple.140, (s32[]{:T(128)}, bf16[128,2048]{1,0:T(8,128)(2,1)}, bf16[128,2048]{1,0:T(8,128)(2,1)S(1)}, bf16[1024,2048]{1,0:T(8,128)(2,1)}, s32[128]{0:T(128)}, /*index=5*/bf16[128,2048]{1,0:T(8,128)(2,1)S(1)}, ...), branch_computations={%region_16.16_spmd, %region_17.25_spmd} | conditional | flops 2336226048 | bytes 78314008 | solution.py:199
  560.3 3.9 fusion.55
  568.0 3.7 convolution_convert_fusion.4
  572.6 2.5 fusion.39
  575.8 1.8 fusion.47
  577.6 1.9 fusion.50
  583.1 2.3 multiply_reduce_fusion.1
  590.6 2.2 collective-permute-start.2
  592.9 1.8 collective-permute-done.2
  595.4 3.6 collective-permute-start.3
  600.6 3.8 collective-permute-start.4
  604.4 3.7 collective-permute-done.4
  608.4 3.4 collective-permute-done.5
  613.3 3.7 collective-permute-done.6
  (286 shorter events, 110.3 us)
Async XLA Ops:
  7.2 25.2 %copy-start.19 = (s32[4,32]{1,0:T(4,128)S(1)}, s32[4,32]{1,0:T(4,128)}, u32[]{:S(2)}) copy-start(s32[4,32]{1,0:T(4,128)} %param.19) | copy-start | bytes 1540
  7.2 126.9 %all-gather.2.cloned.1.call-start = ((), (), s32[]{:S(2)}) async-start(), calls=%async_computation.1 | async-start | bytes 10813440 | tf_op jit(solution)/shard_map/all_gather | solution.py:127
  20.9 48.2 %all-to-all-start = ((bf16[32,4,2,2048]{3,2,1,0:T(2,128)(2,1)}), bf16[32,4,2,2048]{3,2,1,0:T(2,128)(2,1)S(1)}, u32[]{:S(2)}, u32[]{:S(2)}) async-start(bf16[32,4,2,2048]{3,2,1,0:T(2,128)(2,1)} %pad_maximum_fusion.3), calls=%async_computation | async-start | bytes 2097152 | tf_op jit(solution)/shard_map/all_to_all | solution.py:148
  144.4 6.6 %copy-start.5 = (f32[1,2048]{1,0:T(1,128)S(1)}, f32[1,2048]{1,0:T(1,128)}, u32[]{:S(2)}) copy-start(f32[1,2048]{1,0:T(1,128)} %param.22) | copy-start | bytes 24580
  144.4 6.6 %copy-start.13 = (f32[1,2048]{1,0:T(1,128)S(1)}, f32[1,2048]{1,0:T(1,128)}, u32[]{:S(2)}) copy-start(f32[1,2048]{1,0:T(1,128)} %param.21) | copy-start | bytes 24580
  155.4 4.7 copy-start.6
  165.2 2.8 collective-permute-start
  171.4 13.9 %collective-permute-start = (bf16[128,2048]{1,0:T(8,128)(2,1)S(1)}, bf16[128,2048]{1,0:T(8,128)(2,1)S(1)}, u32[]{:S(2)}, u32[]{:S(2)}) collective-permute-start(bf16[128,2048]{1,0:T(8,128)(2,1)S(1)} %get-tuple-element.1040), channel_id=1, source_target_pairs={{0,32},{32,64},{64,96},{96,128},{128,160},{160,192},{192,224},{1,3... | collective-permute-start | bytes 1572872 | tf_op jit(solution)/shard_map/while/body/eval_jaxpr/ppermute | solution.py:181
  188.8 8.0 %collective-permute-start = (bf16[128,2048]{1,0:T(8,128)(2,1)S(1)}, bf16[128,2048]{1,0:T(8,128)(2,1)S(1)}, u32[]{:S(2)}, u32[]{:S(2)}) collective-permute-start(bf16[128,2048]{1,0:T(8,128)(2,1)S(1)} %get-tuple-element.1040), channel_id=1, source_target_pairs={{0,32},{32,64},{64,96},{96,128},{128,160},{160,192},{192,224},{1,3... | collective-permute-start | bytes 1572872 | tf_op jit(solution)/shard_map/while/body/eval_jaxpr/ppermute | solution.py:181
  200.2 20.2 %collective-permute-start = (bf16[128,2048]{1,0:T(8,128)(2,1)S(1)}, bf16[128,2048]{1,0:T(8,128)(2,1)S(1)}, u32[]{:S(2)}, u32[]{:S(2)}) collective-permute-start(bf16[128,2048]{1,0:T(8,128)(2,1)S(1)} %get-tuple-element.1040), channel_id=1, source_target_pairs={{0,32},{32,64},{64,96},{96,128},{128,160},{160,192},{192,224},{1,3... | collective-permute-start | bytes 1572872 | tf_op jit(solution)/shard_map/while/body/eval_jaxpr/ppermute | solution.py:181
  223.9 10.5 %collective-permute-start = (bf16[128,2048]{1,0:T(8,128)(2,1)S(1)}, bf16[128,2048]{1,0:T(8,128)(2,1)S(1)}, u32[]{:S(2)}, u32[]{:S(2)}) collective-permute-start(bf16[128,2048]{1,0:T(8,128)(2,1)S(1)} %get-tuple-element.1040), channel_id=1, source_target_pairs={{0,32},{32,64},{64,96},{96,128},{128,160},{160,192},{192,224},{1,3... | collective-permute-start | bytes 1572872 | tf_op jit(solution)/shard_map/while/body/eval_jaxpr/ppermute | solution.py:181
  237.8 10.5 %collective-permute-start = (bf16[128,2048]{1,0:T(8,128)(2,1)S(1)}, bf16[128,2048]{1,0:T(8,128)(2,1)S(1)}, u32[]{:S(2)}, u32[]{:S(2)}) collective-permute-start(bf16[128,2048]{1,0:T(8,128)(2,1)S(1)} %get-tuple-element.1040), channel_id=1, source_target_pairs={{0,32},{32,64},{64,96},{96,128},{128,160},{160,192},{192,224},{1,3... | collective-permute-start | bytes 1572872 | tf_op jit(solution)/shard_map/while/body/eval_jaxpr/ppermute | solution.py:181
  251.7 10.5 %collective-permute-start = (bf16[128,2048]{1,0:T(8,128)(2,1)S(1)}, bf16[128,2048]{1,0:T(8,128)(2,1)S(1)}, u32[]{:S(2)}, u32[]{:S(2)}) collective-permute-start(bf16[128,2048]{1,0:T(8,128)(2,1)S(1)} %get-tuple-element.1040), channel_id=1, source_target_pairs={{0,32},{32,64},{64,96},{96,128},{128,160},{160,192},{192,224},{1,3... | collective-permute-start | bytes 1572872 | tf_op jit(solution)/shard_map/while/body/eval_jaxpr/ppermute | solution.py:181
  265.7 14.1 %collective-permute-start = (bf16[128,2048]{1,0:T(8,128)(2,1)S(1)}, bf16[128,2048]{1,0:T(8,128)(2,1)S(1)}, u32[]{:S(2)}, u32[]{:S(2)}) collective-permute-start(bf16[128,2048]{1,0:T(8,128)(2,1)S(1)} %get-tuple-element.1040), channel_id=1, source_target_pairs={{0,32},{32,64},{64,96},{96,128},{128,160},{160,192},{192,224},{1,3... | collective-permute-start | bytes 1572872 | tf_op jit(solution)/shard_map/while/body/eval_jaxpr/ppermute | solution.py:181
  284.2 10.2 %collective-permute-start.1 = (bf16[128,2048]{1,0:T(8,128)(2,1)}, bf16[128,2048]{1,0:T(8,128)(2,1)S(1)}, u32[]{:S(2)}, u32[]{:S(2)}) collective-permute-start(bf16[128,2048]{1,0:T(8,128)(2,1)} %get-tuple-element.938), channel_id=1, source_target_pairs={{32,0},{64,32},{96,64},{128,96},{160,128},{192,160},{224,192},{33,... | collective-permute-start | bytes 1572872 | tf_op jit(solution)/shard_map/while/body/eval_jaxpr/ppermute | solution.py:202
  298.5 11.4 %collective-permute-start.1 = (bf16[128,2048]{1,0:T(8,128)(2,1)}, bf16[128,2048]{1,0:T(8,128)(2,1)S(1)}, u32[]{:S(2)}, u32[]{:S(2)}) collective-permute-start(bf16[128,2048]{1,0:T(8,128)(2,1)} %get-tuple-element.938), channel_id=1, source_target_pairs={{32,0},{64,32},{96,64},{128,96},{160,128},{192,160},{224,192},{33,... | collective-permute-start | bytes 1572872 | tf_op jit(solution)/shard_map/while/body/eval_jaxpr/ppermute | solution.py:202
  314.1 10.7 %collective-permute-start.1 = (bf16[128,2048]{1,0:T(8,128)(2,1)}, bf16[128,2048]{1,0:T(8,128)(2,1)S(1)}, u32[]{:S(2)}, u32[]{:S(2)}) collective-permute-start(bf16[128,2048]{1,0:T(8,128)(2,1)} %get-tuple-element.938), channel_id=1, source_target_pairs={{32,0},{64,32},{96,64},{128,96},{160,128},{192,160},{224,192},{33,... | collective-permute-start | bytes 1572872 | tf_op jit(solution)/shard_map/while/body/eval_jaxpr/ppermute | solution.py:202
  328.9 14.5 %collective-permute-start.1 = (bf16[128,2048]{1,0:T(8,128)(2,1)}, bf16[128,2048]{1,0:T(8,128)(2,1)S(1)}, u32[]{:S(2)}, u32[]{:S(2)}) collective-permute-start(bf16[128,2048]{1,0:T(8,128)(2,1)} %get-tuple-element.938), channel_id=1, source_target_pairs={{32,0},{64,32},{96,64},{128,96},{160,128},{192,160},{224,192},{33,... | collective-permute-start | bytes 1572872 | tf_op jit(solution)/shard_map/while/body/eval_jaxpr/ppermute | solution.py:202
  347.5 10.7 %collective-permute-start.1 = (bf16[128,2048]{1,0:T(8,128)(2,1)}, bf16[128,2048]{1,0:T(8,128)(2,1)S(1)}, u32[]{:S(2)}, u32[]{:S(2)}) collective-permute-start(bf16[128,2048]{1,0:T(8,128)(2,1)} %get-tuple-element.938), channel_id=1, source_target_pairs={{32,0},{64,32},{96,64},{128,96},{160,128},{192,160},{224,192},{33,... | collective-permute-start | bytes 1572872 | tf_op jit(solution)/shard_map/while/body/eval_jaxpr/ppermute | solution.py:202
  362.4 10.9 %collective-permute-start.1 = (bf16[128,2048]{1,0:T(8,128)(2,1)}, bf16[128,2048]{1,0:T(8,128)(2,1)S(1)}, u32[]{:S(2)}, u32[]{:S(2)}) collective-permute-start(bf16[128,2048]{1,0:T(8,128)(2,1)} %get-tuple-element.938), channel_id=1, source_target_pairs={{32,0},{64,32},{96,64},{128,96},{160,128},{192,160},{224,192},{33,... | collective-permute-start | bytes 1572872 | tf_op jit(solution)/shard_map/while/body/eval_jaxpr/ppermute | solution.py:202
  377.4 179.3 %collective-permute-start.1 = (bf16[128,2048]{1,0:T(8,128)(2,1)}, bf16[128,2048]{1,0:T(8,128)(2,1)S(1)}, u32[]{:S(2)}, u32[]{:S(2)}) collective-permute-start(bf16[128,2048]{1,0:T(8,128)(2,1)} %get-tuple-element.938), channel_id=1, source_target_pairs={{32,0},{64,32},{96,64},{128,96},{160,128},{192,160},{224,192},{33,... | collective-permute-start | bytes 1572872 | tf_op jit(solution)/shard_map/while/body/eval_jaxpr/ppermute | solution.py:202
  560.0 7.9 %copy-start.1 = (bf16[128,2048]{1,0:T(8,128)(2,1)}, bf16[128,2048]{1,0:T(8,128)(2,1)S(1)}, u32[]{:S(2)}) copy-start(bf16[128,2048]{1,0:T(8,128)(2,1)S(1)} %get-tuple-element.204) | copy-start | bytes 1572868 | tf_op jit(solution)/shard_map/while/body/eval_jaxpr/cond
  560.3 4.6 copy-start.17
  560.3 4.6 copy-start.15
  560.3 7.7 %copy-start.3 = (bf16[128,2048]{1,0:T(8,128)(2,1)S(1)}, bf16[128,2048]{1,0:T(8,128)(2,1)}, u32[]{:S(2)}) copy-start(bf16[128,2048]{1,0:T(8,128)(2,1)} %get-tuple-element.203) | copy-start | bytes 1572868 | tf_op jit(solution)/shard_map/while/body/eval_jaxpr/cond
  564.6 7.9 %copy-start.7 = (bf16[128,16,32]{0,2,1:T(8,128)(2,1)}, bf16[128,16,32]{0,2,1:T(8,128)(2,1)S(1)}, u32[]{:S(2)}) copy-start(bf16[128,16,32]{0,2,1:T(8,128)(2,1)S(1)} %get-tuple-element.732) | copy-start | bytes 393220 | tf_op jit(solution)/shard_map/while/body/eval_jaxpr/cond
  564.6 7.9 %copy-start.8 = (bf16[128,16,32]{0,2,1:T(8,128)(2,1)}, bf16[128,16,32]{0,2,1:T(8,128)(2,1)S(1)}, u32[]{:S(2)}) copy-start(bf16[128,16,32]{0,2,1:T(8,128)(2,1)S(1)} %get-tuple-element.733) | copy-start | bytes 393220 | tf_op jit(solution)/shard_map/while/body/eval_jaxpr/cond
  564.8 7.8 %copy-start.9 = (bf16[128,4,32]{0,2,1:T(8,128)(2,1)}, bf16[128,4,32]{0,2,1:T(8,128)(2,1)S(1)}, u32[]{:S(2)}) copy-start(bf16[128,4,32]{0,2,1:T(8,128)(2,1)S(1)} %get-tuple-element.736) | copy-start | bytes 98308 | tf_op jit(solution)/shard_map/while/body/eval_jaxpr/cond
  564.8 7.7 %copy-start.11 = (bf16[128,4,32]{0,2,1:T(8,128)(2,1)}, bf16[128,4,32]{0,2,1:T(8,128)(2,1)S(1)}, u32[]{:S(2)}) copy-start(bf16[128,4,32]{0,2,1:T(8,128)(2,1)S(1)} %get-tuple-element.737) | copy-start | bytes 98308 | tf_op jit(solution)/shard_map/while/body/eval_jaxpr/cond
  566.2 1.0 copy-start
  572.6 10.5 %slice-start = ((s8[6291456]{0:T(1024)(128)(4,1)}), s8[2097152]{0:T(1024)(128)(4,1)S(1)}, s32[]{:S(2)}) async-start(s8[6291456]{0:T(1024)(128)(4,1)} %bitcast.189), calls=%async_computation.2 | async-start | bytes 4194304 | tf_op jit(solution)/shard_map/while/body/eval_jaxpr/cond
  575.6 7.0 %copy-start.14 = (bf16[4,64,128]{2,1,0:T(8,128)(2,1)S(1)}, bf16[4,64,128]{2,1,0:T(8,128)(2,1)}, u32[]{:S(2)}) copy-start(bf16[4,64,128]{2,1,0:T(8,128)(2,1)} %fusion.39) | copy-start | bytes 196612 | tf_op jit(solution)/shard_map/while/body/eval_jaxpr/cond
  575.7 7.0 %copy-start.10 = (bf16[128,4,32]{0,2,1:T(8,128)(2,1)S(1)}, bf16[128,4,32]{0,2,1:T(8,128)(2,1)}, u32[]{:S(2)}) copy-start(bf16[128,4,32]{0,2,1:T(8,128)(2,1)} %copy-done.9) | copy-start | bytes 98308 | tf_op jit(solution)/shard_map/while/body/eval_jaxpr/cond
  575.7 7.0 %copy-start.12 = (bf16[128,4,32]{0,2,1:T(8,128)(2,1)S(1)}, bf16[128,4,32]{0,2,1:T(8,128)(2,1)}, u32[]{:S(2)}) copy-start(bf16[128,4,32]{0,2,1:T(8,128)(2,1)} %copy-done.11) | copy-start | bytes 98308 | tf_op jit(solution)/shard_map/while/body/eval_jaxpr/cond
  577.6 5.4 slice-start.1
  582.6 2.8 copy-start.18
  582.6 2.8 copy-start.2
  582.6 2.8 copy-start.4
  582.6 2.8 copy-start.16
  586.6 4.0 collective-permute-start.1
  590.6 4.1 collective-permute-start.2
  595.4 5.2 collective-permute-start.3
  600.6 7.6 %collective-permute-start.4 = (f32[2048]{0:T(1024)S(1)}, f32[2048]{0:T(1024)S(1)}, u32[]{:S(2)}, u32[]{:S(2)}) collective-permute-start(f32[2048]{0:T(1024)S(1)} %add.305), channel_id=1, source_target_pairs={{0,4},{1,5},{2,6},{3,7},{4,0},{5,1},{6,2},{7,3},{8,12},{9,13},{10,... | collective-permute-start | bytes 24584 | tf_op jit(solution)/shard_map/ppermute | solution.py:83
  608.2 3.7 collective-permute-start.5
  611.8 5.2 collective-permute-start.6
Sparse Core Ops, SparseCore 0:
  10.6 123.4 all-gather.1

commit v5 on v2

--- a/solution.py
+++ b/solution.py
@@ -168,26 +168,22 @@
     forward_route = [(i, i + 1) for i in range(section_count - 1)]
     backward_route = [(i + 1, i) for i in range(section_count - 1)]
 
-    def forward_step(carry, step):
-        incoming, kept, produced = carry
+    def forward_step(carry, unused):
+        hidden_in, kept, produced, step = carry
         active = section_idx == step
-        hidden_in = jnp.where(step == 0, grouped, incoming)
         kept = jnp.where(active, hidden_in, kept)
         hidden_new = lax.cond(active, lambda: run_layer(hidden_in, steering), lambda: zero_block)
         produced = jnp.where(active, hidden_new, produced)
         sent = lax.ppermute(hidden_new, "section", forward_route)
-        return ((sent, kept, produced), None)
-
-    (unused_in, kept, produced), unused_ys = lax.scan(
-        forward_step,
-        (zero_block, zero_block, zero_block),
-        jnp.arange(section_count, dtype=jnp.int32),
-    )
-
-    def backward_step(carry, step):
-        incoming, grad_sum = carry
+        return ((sent, kept, produced, step + 1), None)
+
+    (unused_in, kept, produced, unused_step), unused_ys = lax.scan(
+        forward_step, (grouped, zero_block, zero_block, jnp.int32(0)), None, length=section_count
+    )
+
+    def backward_step(carry, unused):
+        upstream, grad_sum, step = carry
         active = section_idx == step
-        upstream = jnp.where(step == section_count - 1, cotangent, incoming)
 
         def differentiate():
             unused_out, pullback = jax.vjp(run_layer, kept, steering)
@@ -197,13 +193,15 @@
             active, differentiate, lambda: (zero_block, jnp.zeros_like(steering))
         )
         sent = lax.ppermute(grad_in, "section", backward_route)
-        return ((sent, grad_sum + steer_part), None)
-
-    (unused_grad, grad_sum), unused_zs = lax.scan(
+        return ((sent, grad_sum + steer_part, step - 1), None)
+
+    (unused_grad, grad_sum, unused_step), unused_zs = lax.scan(
         backward_step,
-        (zero_block, jnp.zeros_like(steering)),
-        jnp.arange(section_count - 1, -1, -1, dtype=jnp.int32),
-    )
+        (cotangent, jnp.zeros_like(steering), jnp.int32(section_count - 1)),
+        None,
+        length=section_count,
+    )
+
     total = butterfly_sum(grad_sum, "dp")
     return (produced.reshape(1, micro_count, row_count, width), total[None])
 

time: 578 us -> 539 us (0.933)
  local copies, waits for them, and re-layouts: 34.4 us -> 13.5 us
  loops' own time: 18.7 us -> 1.93 us
    dynamic_slice x16 -> x0, local copies, waits for them, and re-layouts: 20.6 us -> none  [body(): lax.scan(forward_step, (zero_block, zero_block, zero_block), jnp.arange(s...]
    another operation x2, loops' own time: 17.3 us -> 1.2 us  [the longest x1 0.74 us: body(): lax.scan(backward_step, (cotangent, jnp.zeros_like(steering), jnp.int32(s...]
  transfers between devices with their start and end apart: 24 -> 24, of which waited for: 17 -> 17; matrix products, arithmetic and copies ran while one was open for 7% -> 8% of each run, Pallas kernels for 0% -> 0%
where the time goes in v5:
time: 539 us; the launch traced here: 537 us
  waiting for transfers between devices  331 us (61%)
  starting transfers between devices  106 us (20%)
  other arithmetic  45.2 us (8%)
  matrix products  25.5 us (5%)
  between operations  14.4 us (3%)
  local copies, waits for them, and re-layouts  13.5 us (3%)
    ppermute x8, waiting for transfers between devices, backward_step(): sent = lax.ppermute(grad_in, 'section', backward_route)  172 us
    all_gather x1, waiting for transfers between devices, body(): lax.all_gather(jnp.concatenate([w_query[0], w_keyval[0]], axis=1), 'dp',...  81.2 us
    ppermute x8, starting transfers between devices, forward_step(): sent = lax.ppermute(hidden_new, 'section', forward_route)  77.6 us
    all_gather x1, waiting for transfers between devices, body(): full_out = lax.all_gather(w_out[0], 'dp', axis=1, tiled=True)  31.7 us
    all_to_all x1, waiting for transfers between devices, body(): lax.all_to_all(packed, 'dp', split_axis=0, concat_axis=0, tiled=True)  26.8 us
    ppermute x5, waiting for transfers between devices, butterfly_sum(): values = values + lax.ppermute(values, axis, route)  18.1 us
    select_n x8, other arithmetic, forward_step(): produced = jnp.where(active, hidden_new, produced)  16.3 us
    mul x16, other arithmetic, rope_tables(): angles = positions.astype(jnp.float32)[..., None] * inverse  12.1 us
  transfers between devices with their start and end apart: 24, of which 17 were waited for; matrix products, arithmetic and copies ran while one was open for 8% of the time, Pallas kernels for 0%

profile of v5, /device:TPU:32, one launch (start us, length us, event | category | flops | bytes accessed | tf_op | source)
XLA Modules:
  0.0 537.3 jit_solution(15578795356155467267)
XLA Ops:
  8.0 1.6 pad_maximum_fusion.5
  10.9 2.9 convert_reduce_fusion.4
  19.2 2.4 pad_maximum_fusion.3
  21.6 11.4 %all-to-all-start = ((bf16[32,4,2,2048]{3,2,1,0:T(2,128)(2,1)}), bf16[32,4,2,2048]{3,2,1,0:T(2,128)(2,1)S(1)}, u32[]{:S(2)}, u32[]{:S(2)}) async-start(bf16[32,4,2,2048]{3,2,1,0:T(2,128)(2,1)} %pad_maximum_fusion.3), calls=%async_computation | async-start | bytes 2097152 | tf_op jit(solution)/shard_map/all_to_all | solution.py:145
  37.8 26.8 %all-to-all-done = bf16[32,4,2,2048]{3,2,1,0:T(2,128)(2,1)S(1)} async-done(((bf16[32,4,2,2048]{3,2,1,0:T(2,128)(2,1)}), bf16[32,4,2,2048]{3,2,1,0:T(2,128)(2,1)S(1)}, u32[]{:S(2)}, u32[]{:S(2)}) %all-to-all-start) | async-done | bytes 1048608 | tf_op jit(solution)/shard_map/all_to_all | solution.py:145
  66.9 31.7 %all-gather.6.cloned.1.call-done = bf16[1,1024,2048]{1,2,0:T(8,128)(2,1)} async-done(((bf16[1,1024,64]{1,2,0:T(8,128)(2,1)}), bf16[1,1024,2048]{1,2,0:T(8,128)(2,1)}) %all-gather.6.cloned.1.call-update) | async-done | bytes 4194320 | tf_op jit(solution)/shard_map/all_gather | solution.py:129
  98.6 6.5 %copy.70 = bf16[1024,2048]{1,0:T(8,128)(2,1)} copy(bf16[1024,2048]{0,1:T(8,128)(2,1)} %bitcast.207) | data formatting | bytes 8388608
  105.1 81.2 %all-gather.4.cloned.1.call-done = bf16[2048,1536]{1,0:T(8,128)(2,1)} async-done(((bf16[64,1536]{1,0:T(8,128)(2,1)}), bf16[2048,1536]{1,0:T(8,128)(2,1)}) %all-gather.4.cloned.1.call-update) | async-done | bytes 6291472 | tf_op jit(solution)/shard_map/all_gather | solution.py:126
  186.3 112.3 %while.40 = (s32[]{:T(128)}, bf16[128,2048]{1,0:T(8,128)(2,1)S(1)}, bf16[128,2048]{1,0:T(8,128)(2,1)S(1)}, bf16[128,2048]{1,0:T(8,128)(2,1)}, s32[]{:T(128)}, /*...) while((s32[]{:T(128)}, bf16[128,2048]{1,0:T(8,128)(2,1)S(1)}, ...), condition=%wide.region_14.15_spmd.clone.clone.clone, body=%wide.region_8.14_spmd.clone.clone.clone.sunk | while | flops 1451809152 | bytes 27447244 | solution.py:180
  187.2 10.6 %conditional.10 = (bf16[128,2048]{1,0:T(8,128)(2,1)S(1)}) conditional(s32[]{:T(128)} %convert_element_type.310, () %tuple.155, (bf16[128,2048]{1,0:T(8,128)(2,1)S(1)}, f32[1,2048]{1,0:T(1,128)S(1)}, f32[1,2048]{1,0:T(1,128)S(1)}, bf16[2048,1536]{1,0:T(8,128)(2,1)}, s32[128]{0:T(128)}, /*index=5*/f32[128,1,32]{0,2,1:T(8,128)S(1)}, ...), branch_computations={%region_9.9_spmd, %region_10.13_spmd} | conditional | flops 1450756480 | bytes 21007396 | solution.py:175
  187.4 3.8 fusion.18
  194.8 2.9 fusion.13
  197.8 1.3 collective-permute-start
  201.5 12.8 %collective-permute-start = (bf16[128,2048]{1,0:T(8,128)(2,1)S(1)}, bf16[128,2048]{1,0:T(8,128)(2,1)S(1)}, u32[]{:S(2)}, u32[]{:S(2)}) collective-permute-start(bf16[128,2048]{1,0:T(8,128)(2,1)S(1)} %get-tuple-element.1224), channel_id=1, source_target_pairs={{0,32},{32,64},{64,96},{96,128},{128,160},{160,192},{192,224},{1,3... | collective-permute-start | bytes 1572872 | tf_op jit(solution)/shard_map/while/body/eval_jaxpr/ppermute | solution.py:177
  214.4 2.2 select_select_fusion.3
  217.5 5.8 %collective-permute-start = (bf16[128,2048]{1,0:T(8,128)(2,1)S(1)}, bf16[128,2048]{1,0:T(8,128)(2,1)S(1)}, u32[]{:S(2)}, u32[]{:S(2)}) collective-permute-start(bf16[128,2048]{1,0:T(8,128)(2,1)S(1)} %get-tuple-element.1224), channel_id=1, source_target_pairs={{0,32},{32,64},{64,96},{96,128},{128,160},{160,192},{192,224},{1,3... | collective-permute-start | bytes 1572872 | tf_op jit(solution)/shard_map/while/body/eval_jaxpr/ppermute | solution.py:177
  223.3 2.2 select_select_fusion.3
  226.4 18.8 %collective-permute-start = (bf16[128,2048]{1,0:T(8,128)(2,1)S(1)}, bf16[128,2048]{1,0:T(8,128)(2,1)S(1)}, u32[]{:S(2)}, u32[]{:S(2)}) collective-permute-start(bf16[128,2048]{1,0:T(8,128)(2,1)S(1)} %get-tuple-element.1224), channel_id=1, source_target_pairs={{0,32},{32,64},{64,96},{96,128},{128,160},{160,192},{192,224},{1,3... | collective-permute-start | bytes 1572872 | tf_op jit(solution)/shard_map/while/body/eval_jaxpr/ppermute | solution.py:177
  245.3 2.2 select_select_fusion.3
  248.4 8.3 %collective-permute-start = (bf16[128,2048]{1,0:T(8,128)(2,1)S(1)}, bf16[128,2048]{1,0:T(8,128)(2,1)S(1)}, u32[]{:S(2)}, u32[]{:S(2)}) collective-permute-start(bf16[128,2048]{1,0:T(8,128)(2,1)S(1)} %get-tuple-element.1224), channel_id=1, source_target_pairs={{0,32},{32,64},{64,96},{96,128},{128,160},{160,192},{192,224},{1,3... | collective-permute-start | bytes 1572872 | tf_op jit(solution)/shard_map/while/body/eval_jaxpr/ppermute | solution.py:177
  256.7 2.2 select_select_fusion.3
  259.8 8.3 %collective-permute-start = (bf16[128,2048]{1,0:T(8,128)(2,1)S(1)}, bf16[128,2048]{1,0:T(8,128)(2,1)S(1)}, u32[]{:S(2)}, u32[]{:S(2)}) collective-permute-start(bf16[128,2048]{1,0:T(8,128)(2,1)S(1)} %get-tuple-element.1224), channel_id=1, source_target_pairs={{0,32},{32,64},{64,96},{96,128},{128,160},{160,192},{192,224},{1,3... | collective-permute-start | bytes 1572872 | tf_op jit(solution)/shard_map/while/body/eval_jaxpr/ppermute | solution.py:177
  268.1 2.2 select_select_fusion.3
  271.2 8.3 %collective-permute-start = (bf16[128,2048]{1,0:T(8,128)(2,1)S(1)}, bf16[128,2048]{1,0:T(8,128)(2,1)S(1)}, u32[]{:S(2)}, u32[]{:S(2)}) collective-permute-start(bf16[128,2048]{1,0:T(8,128)(2,1)S(1)} %get-tuple-element.1224), channel_id=1, source_target_pairs={{0,32},{32,64},{64,96},{96,128},{128,160},{160,192},{192,224},{1,3... | collective-permute-start | bytes 1572872 | tf_op jit(solution)/shard_map/while/body/eval_jaxpr/ppermute | solution.py:177
  279.5 2.2 select_select_fusion.3
  282.6 13.8 %collective-permute-start = (bf16[128,2048]{1,0:T(8,128)(2,1)S(1)}, bf16[128,2048]{1,0:T(8,128)(2,1)S(1)}, u32[]{:S(2)}, u32[]{:S(2)}) collective-permute-start(bf16[128,2048]{1,0:T(8,128)(2,1)S(1)} %get-tuple-element.1224), channel_id=1, source_target_pairs={{0,32},{32,64},{64,96},{96,128},{128,160},{160,192},{192,224},{1,3... | collective-permute-start | bytes 1572872 | tf_op jit(solution)/shard_map/while/body/eval_jaxpr/ppermute | solution.py:177
  296.4 2.2 select_select_fusion.3
  298.7 205.7 %while.41 = (s32[]{:T(128)}, bf16[128,2048]{1,0:T(8,128)(2,1)S(1)}, f32[2048]{0:T(1024)}, s32[]{:T(128)}, bf16[1024,2048]{1,0:T(8,128)(2,1)}, /*index=5*/bf16[12...) while((s32[]{:T(128)}, bf16[128,2048]{1,0:T(8,128)(2,1)S(1)}, ...), condition=%wide.region_26.27_spmd.clone.clone.clone, body=%wide.region_15.26_spmd.clone.clone.clone.sunk | while | flops 2335709952 | bytes 65174600 | solution.py:198
  301.1 8.3 %collective-permute-done.1 = bf16[128,2048]{1,0:T(8,128)(2,1)S(1)} collective-permute-done((bf16[128,2048]{1,0:T(8,128)(2,1)S(1)}, bf16[128,2048]{1,0:T(8,128)(2,1)S(1)}, u32[]{:S(2)}, u32[]{:S(2)}) %collective-permute-start.1) | collective-permute-done | bytes 524320 | tf_op jit(solution)/shard_map/while/body/eval_jaxpr/ppermute | solution.py:195
  311.7 9.9 %collective-permute-done.1 = bf16[128,2048]{1,0:T(8,128)(2,1)S(1)} collective-permute-done((bf16[128,2048]{1,0:T(8,128)(2,1)S(1)}, bf16[128,2048]{1,0:T(8,128)(2,1)S(1)}, u32[]{:S(2)}, u32[]{:S(2)}) %collective-permute-start.1) | collective-permute-done | bytes 524320 | tf_op jit(solution)/shard_map/while/body/eval_jaxpr/ppermute | solution.py:195
  323.8 9.2 %collective-permute-done.1 = bf16[128,2048]{1,0:T(8,128)(2,1)S(1)} collective-permute-done((bf16[128,2048]{1,0:T(8,128)(2,1)S(1)}, bf16[128,2048]{1,0:T(8,128)(2,1)S(1)}, u32[]{:S(2)}, u32[]{:S(2)}) %collective-permute-start.1) | collective-permute-done | bytes 524320 | tf_op jit(solution)/shard_map/while/body/eval_jaxpr/ppermute | solution.py:195
  335.2 14.6 %collective-permute-done.1 = bf16[128,2048]{1,0:T(8,128)(2,1)S(1)} collective-permute-done((bf16[128,2048]{1,0:T(8,128)(2,1)S(1)}, bf16[128,2048]{1,0:T(8,128)(2,1)S(1)}, u32[]{:S(2)}, u32[]{:S(2)}) %collective-permute-start.1) | collective-permute-done | bytes 524320 | tf_op jit(solution)/shard_map/while/body/eval_jaxpr/ppermute | solution.py:195
  352.1 9.2 %collective-permute-done.1 = bf16[128,2048]{1,0:T(8,128)(2,1)S(1)} collective-permute-done((bf16[128,2048]{1,0:T(8,128)(2,1)S(1)}, bf16[128,2048]{1,0:T(8,128)(2,1)S(1)}, u32[]{:S(2)}, u32[]{:S(2)}) %collective-permute-start.1) | collective-permute-done | bytes 524320 | tf_op jit(solution)/shard_map/while/body/eval_jaxpr/ppermute | solution.py:195
  363.4 9.2 %collective-permute-done.1 = bf16[128,2048]{1,0:T(8,128)(2,1)S(1)} collective-permute-done((bf16[128,2048]{1,0:T(8,128)(2,1)S(1)}, bf16[128,2048]{1,0:T(8,128)(2,1)S(1)}, u32[]{:S(2)}, u32[]{:S(2)}) %collective-permute-start.1) | collective-permute-done | bytes 524320 | tf_op jit(solution)/shard_map/while/body/eval_jaxpr/ppermute | solution.py:195
  374.8 109.1 %collective-permute-done.1 = bf16[128,2048]{1,0:T(8,128)(2,1)S(1)} collective-permute-done((bf16[128,2048]{1,0:T(8,128)(2,1)S(1)}, bf16[128,2048]{1,0:T(8,128)(2,1)S(1)}, u32[]{:S(2)}, u32[]{:S(2)}) %collective-permute-start.1) | collective-permute-done | bytes 524320 | tf_op jit(solution)/shard_map/while/body/eval_jaxpr/ppermute | solution.py:195
  484.7 15.9 %conditional.11 = (bf16[128,2048]{1,0:T(8,128)(2,1)S(1)}, f32[2048]{0:T(1024)S(1)}) conditional(s32[]{:T(128)} %convert_element_type.311, () %tuple.158, (bf16[128,2048]{1,0:T(8,128)(2,1)S(1)}, bf16[1024,2048]{1,0:T(8,128)(2,1)}, s32[128]{0:T(128)}, bf16[128,2048]{1,0:T(8,128)(2,1)S(1)}, f32[1,2048]{1,0:T(1,128)S(1)}, ...), branch_computations={%region_16.16_spmd, %region_17.25_spmd} | conditional | flops 2335701760 | bytes 62838848 | solution.py:192
  484.7 3.7 convolution_convert_fusion.4
  489.8 3.8 fusion.55
  497.9 2.3 multiply_reduce_fusion.1
  501.9 2.5 collective-permute-done.1
  504.9 3.3 collective-permute-done.2
  509.0 1.8 collective-permute-start.3
  510.7 2.8 collective-permute-done.3
  513.5 2.7 collective-permute-start.4
  516.2 4.9 collective-permute-done.4
  521.3 3.4 collective-permute-done.5
  524.7 1.5 collective-permute-start.6
  526.2 3.7 collective-permute-done.6
  (269 shorter events, 52.3 us)
Async XLA Ops:
  7.2 25.8 %copy-start.6 = (s32[4,32]{1,0:T(4,128)S(1)}, s32[4,32]{1,0:T(4,128)}, u32[]{:S(2)}) copy-start(s32[4,32]{1,0:T(4,128)} %param.19) | copy-start | bytes 1540
  7.2 91.4 %all-gather.6.cloned.1.call-start = ((), (), s32[]{:S(2)}) async-start(), calls=%async_computation.2 | async-start | bytes 4325376 | tf_op jit(solution)/shard_map/all_gather | solution.py:129
  7.9 178.4 %all-gather.4.cloned.1.call-start = ((), (), s32[]{:S(2)}) async-start(), calls=%async_computation.1 | async-start | bytes 6488064 | tf_op jit(solution)/shard_map/all_gather | solution.py:126
  21.6 43.0 %all-to-all-start = ((bf16[32,4,2,2048]{3,2,1,0:T(2,128)(2,1)}), bf16[32,4,2,2048]{3,2,1,0:T(2,128)(2,1)S(1)}, u32[]{:S(2)}, u32[]{:S(2)}) async-start(bf16[32,4,2,2048]{3,2,1,0:T(2,128)(2,1)} %pad_maximum_fusion.3), calls=%async_computation | async-start | bytes 2097152 | tf_op jit(solution)/shard_map/all_to_all | solution.py:145
  65.5 120.8 %copy-start.1 = (f32[1,2048]{1,0:T(1,128)S(1)}, f32[1,2048]{1,0:T(1,128)}, u32[]{:S(2)}) copy-start(f32[1,2048]{1,0:T(1,128)} %param.22) | copy-start | bytes 24580
  65.5 120.8 %copy-start.2 = (f32[1,2048]{1,0:T(1,128)S(1)}, f32[1,2048]{1,0:T(1,128)}, u32[]{:S(2)}) copy-start(f32[1,2048]{1,0:T(1,128)} %param.21) | copy-start | bytes 24580
  186.3 112.3 %copy-start = (bf16[4,32,2048]{2,1,0:T(8,128)(2,1)S(1)}, bf16[4,32,2048]{2,1,0:T(8,128)(2,1)}, u32[]{:S(2)}) copy-start(bf16[4,32,2048]{2,1,0:T(8,128)(2,1)} %param.20) | copy-start | bytes 1572868
  192.1 0.7 copy-start.3
  197.8 2.8 collective-permute-start
  201.5 15.0 %collective-permute-start = (bf16[128,2048]{1,0:T(8,128)(2,1)S(1)}, bf16[128,2048]{1,0:T(8,128)(2,1)S(1)}, u32[]{:S(2)}, u32[]{:S(2)}) collective-permute-start(bf16[128,2048]{1,0:T(8,128)(2,1)S(1)} %get-tuple-element.1224), channel_id=1, source_target_pairs={{0,32},{32,64},{64,96},{96,128},{128,160},{160,192},{192,224},{1,3... | collective-permute-start | bytes 1572872 | tf_op jit(solution)/shard_map/while/body/eval_jaxpr/ppermute | solution.py:177
  217.5 8.0 %collective-permute-start = (bf16[128,2048]{1,0:T(8,128)(2,1)S(1)}, bf16[128,2048]{1,0:T(8,128)(2,1)S(1)}, u32[]{:S(2)}, u32[]{:S(2)}) collective-permute-start(bf16[128,2048]{1,0:T(8,128)(2,1)S(1)} %get-tuple-element.1224), channel_id=1, source_target_pairs={{0,32},{32,64},{64,96},{96,128},{128,160},{160,192},{192,224},{1,3... | collective-permute-start | bytes 1572872 | tf_op jit(solution)/shard_map/while/body/eval_jaxpr/ppermute | solution.py:177
  226.4 21.0 %collective-permute-start = (bf16[128,2048]{1,0:T(8,128)(2,1)S(1)}, bf16[128,2048]{1,0:T(8,128)(2,1)S(1)}, u32[]{:S(2)}, u32[]{:S(2)}) collective-permute-start(bf16[128,2048]{1,0:T(8,128)(2,1)S(1)} %get-tuple-element.1224), channel_id=1, source_target_pairs={{0,32},{32,64},{64,96},{96,128},{128,160},{160,192},{192,224},{1,3... | collective-permute-start | bytes 1572872 | tf_op jit(solution)/shard_map/while/body/eval_jaxpr/ppermute | solution.py:177
  248.4 10.5 %collective-permute-start = (bf16[128,2048]{1,0:T(8,128)(2,1)S(1)}, bf16[128,2048]{1,0:T(8,128)(2,1)S(1)}, u32[]{:S(2)}, u32[]{:S(2)}) collective-permute-start(bf16[128,2048]{1,0:T(8,128)(2,1)S(1)} %get-tuple-element.1224), channel_id=1, source_target_pairs={{0,32},{32,64},{64,96},{96,128},{128,160},{160,192},{192,224},{1,3... | collective-permute-start | bytes 1572872 | tf_op jit(solution)/shard_map/while/body/eval_jaxpr/ppermute | solution.py:177
  259.8 10.5 %collective-permute-start = (bf16[128,2048]{1,0:T(8,128)(2,1)S(1)}, bf16[128,2048]{1,0:T(8,128)(2,1)S(1)}, u32[]{:S(2)}, u32[]{:S(2)}) collective-permute-start(bf16[128,2048]{1,0:T(8,128)(2,1)S(1)} %get-tuple-element.1224), channel_id=1, source_target_pairs={{0,32},{32,64},{64,96},{96,128},{128,160},{160,192},{192,224},{1,3... | collective-permute-start | bytes 1572872 | tf_op jit(solution)/shard_map/while/body/eval_jaxpr/ppermute | solution.py:177
  271.2 10.5 %collective-permute-start = (bf16[128,2048]{1,0:T(8,128)(2,1)S(1)}, bf16[128,2048]{1,0:T(8,128)(2,1)S(1)}, u32[]{:S(2)}, u32[]{:S(2)}) collective-permute-start(bf16[128,2048]{1,0:T(8,128)(2,1)S(1)} %get-tuple-element.1224), channel_id=1, source_target_pairs={{0,32},{32,64},{64,96},{96,128},{128,160},{160,192},{192,224},{1,3... | collective-permute-start | bytes 1572872 | tf_op jit(solution)/shard_map/while/body/eval_jaxpr/ppermute | solution.py:177
  282.6 16.0 %collective-permute-start = (bf16[128,2048]{1,0:T(8,128)(2,1)S(1)}, bf16[128,2048]{1,0:T(8,128)(2,1)S(1)}, u32[]{:S(2)}, u32[]{:S(2)}) collective-permute-start(bf16[128,2048]{1,0:T(8,128)(2,1)S(1)} %get-tuple-element.1224), channel_id=1, source_target_pairs={{0,32},{32,64},{64,96},{96,128},{128,160},{160,192},{192,224},{1,3... | collective-permute-start | bytes 1572872 | tf_op jit(solution)/shard_map/while/body/eval_jaxpr/ppermute | solution.py:177
  299.7 1.4 copy-start.4
  299.8 9.7 %collective-permute-start.1 = (bf16[128,2048]{1,0:T(8,128)(2,1)S(1)}, bf16[128,2048]{1,0:T(8,128)(2,1)S(1)}, u32[]{:S(2)}, u32[]{:S(2)}) collective-permute-start(bf16[128,2048]{1,0:T(8,128)(2,1)S(1)} %get-tuple-element.1128), channel_id=1, source_target_pairs={{32,0},{64,32},{96,64},{128,96},{160,128},{192,160},{224,192},{33,... | collective-permute-start | bytes 1572872 | tf_op jit(solution)/shard_map/while/body/eval_jaxpr/ppermute | solution.py:195
  301.1 8.4 %copy-start.5 = (f32[2048]{0:T(1024)}, f32[2048]{0:T(1024)S(1)}, u32[]{:S(2)}) copy-start(f32[2048]{0:T(1024)S(1)} %select_add_fusion.2) | copy-start | bytes 24580 | tf_op jit(solution)/shard_map/while
  310.3 1.4 copy-start.4
  310.4 11.2 %collective-permute-start.1 = (bf16[128,2048]{1,0:T(8,128)(2,1)S(1)}, bf16[128,2048]{1,0:T(8,128)(2,1)S(1)}, u32[]{:S(2)}, u32[]{:S(2)}) collective-permute-start(bf16[128,2048]{1,0:T(8,128)(2,1)S(1)} %get-tuple-element.1128), channel_id=1, source_target_pairs={{32,0},{64,32},{96,64},{128,96},{160,128},{192,160},{224,192},{33,... | collective-permute-start | bytes 1572872 | tf_op jit(solution)/shard_map/while/body/eval_jaxpr/ppermute | solution.py:195
  311.7 9.9 %copy-start.5 = (f32[2048]{0:T(1024)}, f32[2048]{0:T(1024)S(1)}, u32[]{:S(2)}) copy-start(f32[2048]{0:T(1024)S(1)} %select_add_fusion.2) | copy-start | bytes 24580 | tf_op jit(solution)/shard_map/while
  322.4 1.4 copy-start.4
  322.5 10.5 %collective-permute-start.1 = (bf16[128,2048]{1,0:T(8,128)(2,1)S(1)}, bf16[128,2048]{1,0:T(8,128)(2,1)S(1)}, u32[]{:S(2)}, u32[]{:S(2)}) collective-permute-start(bf16[128,2048]{1,0:T(8,128)(2,1)S(1)} %get-tuple-element.1128), channel_id=1, source_target_pairs={{32,0},{64,32},{96,64},{128,96},{160,128},{192,160},{224,192},{33,... | collective-permute-start | bytes 1572872 | tf_op jit(solution)/shard_map/while/body/eval_jaxpr/ppermute | solution.py:195
  323.8 9.2 %copy-start.5 = (f32[2048]{0:T(1024)}, f32[2048]{0:T(1024)S(1)}, u32[]{:S(2)}) copy-start(f32[2048]{0:T(1024)S(1)} %select_add_fusion.2) | copy-start | bytes 24580 | tf_op jit(solution)/shard_map/while
  333.8 1.4 copy-start.4
  333.9 15.9 %collective-permute-start.1 = (bf16[128,2048]{1,0:T(8,128)(2,1)S(1)}, bf16[128,2048]{1,0:T(8,128)(2,1)S(1)}, u32[]{:S(2)}, u32[]{:S(2)}) collective-permute-start(bf16[128,2048]{1,0:T(8,128)(2,1)S(1)} %get-tuple-element.1128), channel_id=1, source_target_pairs={{32,0},{64,32},{96,64},{128,96},{160,128},{192,160},{224,192},{33,... | collective-permute-start | bytes 1572872 | tf_op jit(solution)/shard_map/while/body/eval_jaxpr/ppermute | solution.py:195
  335.2 14.6 %copy-start.5 = (f32[2048]{0:T(1024)}, f32[2048]{0:T(1024)S(1)}, u32[]{:S(2)}) copy-start(f32[2048]{0:T(1024)S(1)} %select_add_fusion.2) | copy-start | bytes 24580 | tf_op jit(solution)/shard_map/while
  350.6 1.4 copy-start.4
  350.7 10.5 %collective-permute-start.1 = (bf16[128,2048]{1,0:T(8,128)(2,1)S(1)}, bf16[128,2048]{1,0:T(8,128)(2,1)S(1)}, u32[]{:S(2)}, u32[]{:S(2)}) collective-permute-start(bf16[128,2048]{1,0:T(8,128)(2,1)S(1)} %get-tuple-element.1128), channel_id=1, source_target_pairs={{32,0},{64,32},{96,64},{128,96},{160,128},{192,160},{224,192},{33,... | collective-permute-start | bytes 1572872 | tf_op jit(solution)/shard_map/while/body/eval_jaxpr/ppermute | solution.py:195
  352.0 9.2 %copy-start.5 = (f32[2048]{0:T(1024)}, f32[2048]{0:T(1024)S(1)}, u32[]{:S(2)}) copy-start(f32[2048]{0:T(1024)S(1)} %select_add_fusion.2) | copy-start | bytes 24580 | tf_op jit(solution)/shard_map/while
  362.0 1.4 copy-start.4
  362.1 10.5 %collective-permute-start.1 = (bf16[128,2048]{1,0:T(8,128)(2,1)S(1)}, bf16[128,2048]{1,0:T(8,128)(2,1)S(1)}, u32[]{:S(2)}, u32[]{:S(2)}) collective-permute-start(bf16[128,2048]{1,0:T(8,128)(2,1)S(1)} %get-tuple-element.1128), channel_id=1, source_target_pairs={{32,0},{64,32},{96,64},{128,96},{160,128},{192,160},{224,192},{33,... | collective-permute-start | bytes 1572872 | tf_op jit(solution)/shard_map/while/body/eval_jaxpr/ppermute | solution.py:195
  363.4 9.2 %copy-start.5 = (f32[2048]{0:T(1024)}, f32[2048]{0:T(1024)S(1)}, u32[]{:S(2)}) copy-start(f32[2048]{0:T(1024)S(1)} %select_add_fusion.2) | copy-start | bytes 24580 | tf_op jit(solution)/shard_map/while
  373.4 1.4 copy-start.4
  373.5 110.4 %collective-permute-start.1 = (bf16[128,2048]{1,0:T(8,128)(2,1)S(1)}, bf16[128,2048]{1,0:T(8,128)(2,1)S(1)}, u32[]{:S(2)}, u32[]{:S(2)}) collective-permute-start(bf16[128,2048]{1,0:T(8,128)(2,1)S(1)} %get-tuple-element.1128), channel_id=1, source_target_pairs={{32,0},{64,32},{96,64},{128,96},{160,128},{192,160},{224,192},{33,... | collective-permute-start | bytes 1572872 | tf_op jit(solution)/shard_map/while/body/eval_jaxpr/ppermute | solution.py:195
  374.8 109.1 %copy-start.5 = (f32[2048]{0:T(1024)}, f32[2048]{0:T(1024)S(1)}, u32[]{:S(2)}) copy-start(f32[2048]{0:T(1024)S(1)} %select_add_fusion.2) | copy-start | bytes 24580 | tf_op jit(solution)/shard_map/while
  484.7 17.2 %copy-start.4 = (f32[2048]{0:T(1024)S(1)}, f32[2048]{0:T(1024)}, u32[]{:S(2)}) copy-start(f32[2048]{0:T(1024)} %get-tuple-element.1194) | copy-start | bytes 24580 | tf_op jit(solution)/shard_map/while
  494.8 2.7 slice-start
  495.7 2.2 slice-start.1
  500.6 3.8 collective-permute-start.1
  501.9 2.5 copy-start.5
  504.4 3.9 collective-permute-start.2
  509.0 4.5 collective-permute-start.3
  513.5 7.6 %collective-permute-start.4 = (f32[2048]{0:T(1024)S(1)}, f32[2048]{0:T(1024)S(1)}, u32[]{:S(2)}, u32[]{:S(2)}) collective-permute-start(f32[2048]{0:T(1024)S(1)} %add.336), channel_id=1, source_target_pairs={{0,4},{1,5},{2,6},{3,7},{4,0},{5,1},{6,2},{7,3},{8,12},{9,13},{10,... | collective-permute-start | bytes 24584 | tf_op jit(solution)/shard_map/ppermute | solution.py:83
  521.1 3.7 collective-permute-start.5
  524.7 5.2 collective-permute-start.6
Sparse Core Ops, SparseCore 0:
  10.6 87.9 all-gather.5
  101.1 85.1 all-gather.3

commit v6 on v5

--- a/solution.py
+++ b/solution.py
@@ -30,20 +30,22 @@
     )
 
 
-def layer(hidden_in, steering, gain_row, w_qkv, w_out, tables, allowed):
-    row_count, width = hidden_in.shape
-    head_size = HD
-    query_heads = w_out.shape[0] // head_size
-    kv_heads = (w_qkv.shape[1] - query_heads * head_size) // (2 * head_size)
-    group_size = query_heads // kv_heads
+def normalize(hidden_in, steering, gain_row):
     residual = hidden_in.astype(jnp.float32) + steering
     normed = (
         residual
         * lax.rsqrt(jnp.mean(residual * residual, axis=-1, keepdims=True) + EPSILON)
         * gain_row
     ).astype(jnp.bfloat16)
-    projected_in = jnp.dot(normed, w_qkv, preferred_element_type=jnp.float32)
+    return (residual, normed)
+
+
+def attend(projected_in, tables, allowed, query_heads):
+    row_count = projected_in.shape[0]
+    head_size = HD
     query_cols = query_heads * head_size
+    kv_heads = (projected_in.shape[1] - query_cols) // (2 * head_size)
+    group_size = query_heads // kv_heads
     queries = projected_in[:, :query_cols].reshape(row_count, query_heads, head_size)
     keyval = projected_in[:, query_cols:]
     key_rows = rotate(
@@ -69,10 +71,44 @@
     mixed_heads = jnp.einsum(
         "kgrs,skd->rkgd", weights, values, preferred_element_type=jnp.float32
     ).astype(jnp.bfloat16)
-    mixed_heads = mixed_heads.reshape(row_count, query_heads * head_size)
+    return mixed_heads.reshape(row_count, query_heads * head_size)
+
+
+def project_in(normed, w_qkv):
+    return jnp.dot(normed, w_qkv, preferred_element_type=jnp.float32)
+
+
+def project_out(residual, mixed_heads, w_out):
     return (residual + jnp.dot(mixed_heads, w_out, preferred_element_type=jnp.float32)).astype(
         jnp.bfloat16
     )
+
+
+def layer_forward(hidden_in, steering, gain_row, w_qkv, w_out, tables, allowed):
+    residual, normed = normalize(hidden_in, steering, gain_row)
+    projected_in = project_in(normed, w_qkv)
+    mixed_heads = attend(projected_in, tables, allowed, w_out.shape[0] // HD)
+    return (project_out(residual, mixed_heads, w_out), projected_in)
+
+
+def layer_backward(
+    hidden_in, steering, projected_in, upstream, gain_row, w_qkv, w_out, tables, allowed
+):
+    query_heads = w_out.shape[0] // HD
+    (residual, normed), normalize_pull = jax.vjp(
+        lambda h, s: normalize(h, s, gain_row), hidden_in, steering
+    )
+    mixed_heads, attend_pull = jax.vjp(
+        lambda p: attend(p, tables, allowed, query_heads), projected_in
+    )
+    unused_out, out_pull = jax.vjp(
+        lambda r, m: project_out(r, m, w_out), residual, mixed_heads
+    )
+    grad_residual, grad_mixed = out_pull(upstream)
+    (grad_projected,) = attend_pull(grad_mixed)
+    unused_proj, in_pull = jax.vjp(lambda n: project_in(n, w_qkv), normed)
+    (grad_normed,) = in_pull(grad_projected)
+    return normalize_pull((grad_residual, grad_normed))
 
 
 def butterfly_sum(values, axis):
@@ -162,23 +198,30 @@
     cotangent = cotangent.reshape(flat_count, width)
 
     def run_layer(hidden_in, steer_vec):
-        return layer(hidden_in, steer_vec, gain_row, full_qkv, full_out, tables, allowed)
+        return layer_forward(hidden_in, steer_vec, gain_row, full_qkv, full_out, tables, allowed)
 
     zero_block = jnp.zeros((flat_count, width), jnp.bfloat16)
+    zero_proj = jnp.zeros((flat_count, full_qkv.shape[1]), jnp.float32)
     forward_route = [(i, i + 1) for i in range(section_count - 1)]
     backward_route = [(i + 1, i) for i in range(section_count - 1)]
 
     def forward_step(carry, unused):
-        hidden_in, kept, produced, step = carry
+        hidden_in, kept, produced, saved, step = carry
         active = section_idx == step
         kept = jnp.where(active, hidden_in, kept)
-        hidden_new = lax.cond(active, lambda: run_layer(hidden_in, steering), lambda: zero_block)
+        hidden_new, projected = lax.cond(
+            active, lambda: run_layer(hidden_in, steering), lambda: (zero_block, zero_proj)
+        )
         produced = jnp.where(active, hidden_new, produced)
+        saved = jnp.where(active, projected, saved)
         sent = lax.ppermute(hidden_new, "section", forward_route)
-        return ((sent, kept, produced, step + 1), None)
-
-    (unused_in, kept, produced, unused_step), unused_ys = lax.scan(
-        forward_step, (grouped, zero_block, zero_block, jnp.int32(0)), None, length=section_count
+        return ((sent, kept, produced, saved, step + 1), None)
+
+    (unused_in, kept, produced, saved, unused_step), unused_ys = lax.scan(
+        forward_step,
+        (grouped, zero_block, zero_block, zero_proj, jnp.int32(0)),
+        None,
+        length=section_count,
     )
 
     def backward_step(carry, unused):
@@ -186,8 +229,9 @@
         active = section_idx == step
 
         def differentiate():
-            unused_out, pullback = jax.vjp(run_layer, kept, steering)
-            return pullback(upstream)
+            return layer_backward(
+                kept, steering, saved, upstream, gain_row, full_qkv, full_out, tables, allowed
+            )
 
         grad_in, steer_part = lax.cond(
             active, differentiate, lambda: (zero_block, jnp.zeros_like(steering))

time: 539 us -> 556 us (1.032)
  waiting for transfers between devices: 331 us -> 296 us
  other arithmetic: 45.2 us -> 72.9 us
  local copies, waits for them, and re-layouts: 13.5 us -> 37.2 us
    ppermute x8, waiting for transfers between devices: 172 us -> 135 us  [backward_step(): sent = lax.ppermute(grad_in, 'section', backward_route)]
    select_n x0 -> x8, other arithmetic: none -> 15.7 us  [forward_step(): saved = jnp.where(active, projected, saved)]
    broadcast_in_dim x14, local copies, waits for them, and re-layouts: 0.64 us -> 12.1 us  [body(): zero_block = jnp.zeros((flat_count, width), jnp.bfloat16)]
    ge x32, local copies, waits for them, and re-layouts: 0.24 us -> 10.1 us  [body(): flat_index[:, None] >= flat_index[None, :]]
    add x8, other arithmetic: 0.05 us -> 9.76 us  [backward_step(): return ((sent, grad_sum + steer_part, step - 1), None)]
    dot_general x12 -> x11, matrix products: 19.7 us -> 16.3 us  [the longest x2 6.79 us: project_in(): return jnp.dot(normed, w_qkv, preferred_element_type=jnp.float32)]
  transfers between devices with their start and end apart: 24 -> 24, of which waited for: 17 -> 16; matrix products, arithmetic and copies ran while one was open for 8% -> 12% of each run, Pallas kernels for 0% -> 0%
where the time goes in v6:
time: 556 us; the launch traced here: 551 us
  waiting for transfers between devices  296 us (53%)
  starting transfers between devices  108 us (19%)
  other arithmetic  72.9 us (13%)
  local copies, waits for them, and re-layouts  37.2 us (7%)
  matrix products  21.2 us (4%)
  between operations  14.4 us (3%)
    ppermute x8, waiting for transfers between devices, backward_step(): sent = lax.ppermute(grad_in, 'section', backward_route)  135 us
    all_gather x1, waiting for transfers between devices, body(): lax.all_gather(jnp.concatenate([w_query[0], w_keyval[0]], axis=1), 'dp',...  81.3 us
    ppermute x8, starting transfers between devices, forward_step(): sent = lax.ppermute(hidden_new, 'section', forward_route)  80.1 us
    all_gather x1, waiting for transfers between devices, body(): full_out = lax.all_gather(w_out[0], 'dp', axis=1, tiled=True)  34.3 us
    all_to_all x1, waiting for transfers between devices, body(): lax.all_to_all(packed, 'dp', split_axis=0, concat_axis=0, tiled=True)  26.4 us
    ppermute x5, waiting for transfers between devices, butterfly_sum(): values = values + lax.ppermute(values, axis, route)  18.2 us
    select_n x8, other arithmetic, forward_step(): produced = jnp.where(active, hidden_new, produced)  17.4 us
    select_n x8, other arithmetic, forward_step(): saved = jnp.where(active, projected, saved)  15.7 us
  transfers between devices with their start and end apart: 24, of which 16 were waited for; matrix products, arithmetic and copies ran while one was open for 12% of the time, Pallas kernels for 0%

profile of v6, /device:TPU:32, one launch (start us, length us, event | category | flops | bytes accessed | tf_op | source)
XLA Modules:
  0.0 551.5 jit_solution(7337382310976432749)
XLA Ops:
  10.9 2.9 convert_reduce_fusion.4
  17.4 2.4 pad_maximum_fusion.3
  19.8 11.4 %all-to-all-start = ((bf16[32,4,2,2048]{3,2,1,0:T(2,128)(2,1)}), bf16[32,4,2,2048]{3,2,1,0:T(2,128)(2,1)S(1)}, u32[]{:S(2)}, u32[]{:S(2)}) async-start(bf16[32,4,2,2048]{3,2,1,0:T(2,128)(2,1)} %pad_maximum_fusion.3), calls=%async_computation | async-start | bytes 2097152 | tf_op jit(solution)/shard_map/all_to_all | solution.py:181
  35.9 26.4 %all-to-all-done = bf16[32,4,2,2048]{3,2,1,0:T(2,128)(2,1)S(1)} async-done(((bf16[32,4,2,2048]{3,2,1,0:T(2,128)(2,1)}), bf16[32,4,2,2048]{3,2,1,0:T(2,128)(2,1)S(1)}, u32[]{:S(2)}, u32[]{:S(2)}) %all-to-all-start) | async-done | bytes 1048608 | tf_op jit(solution)/shard_map/all_to_all | solution.py:181
  64.6 34.3 %all-gather.6.cloned.1.call-done = bf16[1,1024,2048]{1,2,0:T(8,128)(2,1)} async-done(((bf16[1,1024,64]{1,2,0:T(8,128)(2,1)}), bf16[1,1024,2048]{1,2,0:T(8,128)(2,1)}) %all-gather.6.cloned.1.call-update) | async-done | bytes 4194320 | tf_op jit(solution)/shard_map/all_gather | solution.py:165
  98.9 6.6 %copy.54 = bf16[1024,2048]{1,0:T(8,128)(2,1)} copy(bf16[1024,2048]{0,1:T(8,128)(2,1)} %bitcast.204) | data formatting | bytes 8388608
  105.4 81.3 %all-gather.4.cloned.1.call-done = bf16[2048,1536]{1,0:T(8,128)(2,1)} async-done(((bf16[64,1536]{1,0:T(8,128)(2,1)}), bf16[2048,1536]{1,0:T(8,128)(2,1)}) %all-gather.4.cloned.1.call-update) | async-done | bytes 6291472 | tf_op jit(solution)/shard_map/all_gather | solution.py:162
  186.7 151.1 %while.42 = (s32[]{:T(128)}, bf16[128,2048]{1,0:T(8,128)(2,1)S(1)}, bf16[128,2048]{1,0:T(8,128)(2,1)S(1)}, bf16[128,2048]{1,0:T(8,128)(2,1)}, f32[128,1536]{1,0:...) while((s32[]{:T(128)}, bf16[128,2048]{1,0:T(8,128)(2,1)S(1)}, ...), condition=%wide.region_14.15_spmd.clone.clone.clone, body=%wide.region_8.14_spmd.clone.clone.clone.sunk | while | flops 1452202368 | bytes 36360256 | solution.py:220
  188.8 14.8 %conditional.10 = (bf16[128,2048]{1,0:T(8,128)(2,1)}, f32[128,1536]{1,0:T(8,128)S(1)}) conditional(s32[]{:T(128)} %convert_element_type.302, () %tuple.161, (bf16[128,2048]{1,0:T(8,128)(2,1)S(1)}, f32[1,2048]{1,0:T(1,128)S(1)}, f32[1,2048]{1,0:T(1,128)}, bf16[2048,1536]{1,0:T(8,128)(2,1)}, s32[128]{0:T(128)}, ...), branch_computations={%region_9.9_spmd, %region_10.13_spmd} | conditional | flops 1450756480 | bytes 27561116 | solution.py:212
  189.0 3.8 fusion.18
  199.7 3.9 fusion.13
  204.9 2.2 select_select_fusion.5
  211.0 14.7 %collective-permute-start = (bf16[128,2048]{1,0:T(8,128)(2,1)}, bf16[128,2048]{1,0:T(8,128)(2,1)S(1)}, u32[]{:S(2)}, u32[]{:S(2)}) collective-permute-start(bf16[128,2048]{1,0:T(8,128)(2,1)} %get-tuple-element.1221), channel_id=1, source_target_pairs={{0,32},{32,64},{64,96},{96,128},{128,160},{160,192},{192,224},{1,3... | collective-permute-start | bytes 1572872 | tf_op jit(solution)/shard_map/while/body/eval_jaxpr/ppermute | solution.py:217
  225.7 2.2 select_select_fusion.5
  227.9 2.1 select_select_fusion.6
  233.0 4.0 collective-permute-start
  237.1 2.2 select_select_fusion.5
  239.2 2.1 select_select_fusion.6
  244.3 20.3 %collective-permute-start = (bf16[128,2048]{1,0:T(8,128)(2,1)}, bf16[128,2048]{1,0:T(8,128)(2,1)S(1)}, u32[]{:S(2)}, u32[]{:S(2)}) collective-permute-start(bf16[128,2048]{1,0:T(8,128)(2,1)} %get-tuple-element.1221), channel_id=1, source_target_pairs={{0,32},{32,64},{64,96},{96,128},{128,160},{160,192},{192,224},{1,3... | collective-permute-start | bytes 1572872 | tf_op jit(solution)/shard_map/while/body/eval_jaxpr/ppermute | solution.py:217
  264.6 2.2 select_select_fusion.5
  266.8 2.1 select_select_fusion.6
  271.9 6.4 %collective-permute-start = (bf16[128,2048]{1,0:T(8,128)(2,1)}, bf16[128,2048]{1,0:T(8,128)(2,1)S(1)}, u32[]{:S(2)}, u32[]{:S(2)}) collective-permute-start(bf16[128,2048]{1,0:T(8,128)(2,1)} %get-tuple-element.1221), channel_id=1, source_target_pairs={{0,32},{32,64},{64,96},{96,128},{128,160},{160,192},{192,224},{1,3... | collective-permute-start | bytes 1572872 | tf_op jit(solution)/shard_map/while/body/eval_jaxpr/ppermute | solution.py:217
  278.3 2.2 select_select_fusion.5
  280.5 2.1 select_select_fusion.6
  285.6 9.1 %collective-permute-start = (bf16[128,2048]{1,0:T(8,128)(2,1)}, bf16[128,2048]{1,0:T(8,128)(2,1)S(1)}, u32[]{:S(2)}, u32[]{:S(2)}) collective-permute-start(bf16[128,2048]{1,0:T(8,128)(2,1)} %get-tuple-element.1221), channel_id=1, source_target_pairs={{0,32},{32,64},{64,96},{96,128},{128,160},{160,192},{192,224},{1,3... | collective-permute-start | bytes 1572872 | tf_op jit(solution)/shard_map/while/body/eval_jaxpr/ppermute | solution.py:217
  294.7 2.2 select_select_fusion.5
  296.8 2.1 select_select_fusion.6
  301.9 6.4 %collective-permute-start = (bf16[128,2048]{1,0:T(8,128)(2,1)}, bf16[128,2048]{1,0:T(8,128)(2,1)S(1)}, u32[]{:S(2)}, u32[]{:S(2)}) collective-permute-start(bf16[128,2048]{1,0:T(8,128)(2,1)} %get-tuple-element.1221), channel_id=1, source_target_pairs={{0,32},{32,64},{64,96},{96,128},{128,160},{160,192},{192,224},{1,3... | collective-permute-start | bytes 1572872 | tf_op jit(solution)/shard_map/while/body/eval_jaxpr/ppermute | solution.py:217
  308.3 2.2 select_select_fusion.5
  315.6 17.9 %collective-permute-start = (bf16[128,2048]{1,0:T(8,128)(2,1)}, bf16[128,2048]{1,0:T(8,128)(2,1)S(1)}, u32[]{:S(2)}, u32[]{:S(2)}) collective-permute-start(bf16[128,2048]{1,0:T(8,128)(2,1)} %get-tuple-element.1221), channel_id=1, source_target_pairs={{0,32},{32,64},{64,96},{96,128},{128,160},{160,192},{192,224},{1,3... | collective-permute-start | bytes 1572872 | tf_op jit(solution)/shard_map/while/body/eval_jaxpr/ppermute | solution.py:217
  333.5 2.2 select_select_fusion.5
  335.7 2.1 select_select_fusion.6
  339.3 179.2 %while.43 = (s32[]{:T(128)}, bf16[128,2048]{1,0:T(8,128)(2,1)S(1)}, f32[2048]{0:T(1024)}, s32[]{:T(128)}, bf16[1024,2048]{1,0:T(8,128)(2,1)}, /*index=5*/f32[128...) while((s32[]{:T(128)}, bf16[128,2048]{1,0:T(8,128)(2,1)S(1)}, ...), condition=%wide.region_26.27_spmd.clone.clone.clone, body=%wide.region_15.26_spmd.clone.clone.clone.sunk | while | flops 1528568320 | bytes 74914072 | solution.py:242
  343.1 6.1 %collective-permute-done.1 = bf16[128,2048]{1,0:T(8,128)(2,1)S(1)} collective-permute-done((bf16[128,2048]{1,0:T(8,128)(2,1)}, bf16[128,2048]{1,0:T(8,128)(2,1)S(1)}, u32[]{:S(2)}, u32[]{:S(2)}) %collective-permute-start.1) | collective-permute-done | bytes 524320 | tf_op jit(solution)/shard_map/while/body/eval_jaxpr/ppermute | solution.py:239
  353.4 11.4 %collective-permute-done.1 = bf16[128,2048]{1,0:T(8,128)(2,1)S(1)} collective-permute-done((bf16[128,2048]{1,0:T(8,128)(2,1)}, bf16[128,2048]{1,0:T(8,128)(2,1)S(1)}, u32[]{:S(2)}, u32[]{:S(2)}) %collective-permute-start.1) | collective-permute-done | bytes 524320 | tf_op jit(solution)/shard_map/while/body/eval_jaxpr/ppermute | solution.py:239
  369.1 8.1 %collective-permute-done.1 = bf16[128,2048]{1,0:T(8,128)(2,1)S(1)} collective-permute-done((bf16[128,2048]{1,0:T(8,128)(2,1)}, bf16[128,2048]{1,0:T(8,128)(2,1)S(1)}, u32[]{:S(2)}, u32[]{:S(2)}) %collective-permute-start.1) | collective-permute-done | bytes 524320 | tf_op jit(solution)/shard_map/while/body/eval_jaxpr/ppermute | solution.py:239
  381.4 17.6 %collective-permute-done.1 = bf16[128,2048]{1,0:T(8,128)(2,1)S(1)} collective-permute-done((bf16[128,2048]{1,0:T(8,128)(2,1)}, bf16[128,2048]{1,0:T(8,128)(2,1)S(1)}, u32[]{:S(2)}, u32[]{:S(2)}) %collective-permute-start.1) | collective-permute-done | bytes 524320 | tf_op jit(solution)/shard_map/while/body/eval_jaxpr/ppermute | solution.py:239
  403.2 8.1 %collective-permute-done.1 = bf16[128,2048]{1,0:T(8,128)(2,1)S(1)} collective-permute-done((bf16[128,2048]{1,0:T(8,128)(2,1)}, bf16[128,2048]{1,0:T(8,128)(2,1)S(1)}, u32[]{:S(2)}, u32[]{:S(2)}) %collective-permute-start.1) | collective-permute-done | bytes 524320 | tf_op jit(solution)/shard_map/while/body/eval_jaxpr/ppermute | solution.py:239
  415.6 8.7 %collective-permute-done.1 = bf16[128,2048]{1,0:T(8,128)(2,1)S(1)} collective-permute-done((bf16[128,2048]{1,0:T(8,128)(2,1)}, bf16[128,2048]{1,0:T(8,128)(2,1)S(1)}, u32[]{:S(2)}, u32[]{:S(2)}) %collective-permute-start.1) | collective-permute-done | bytes 524320 | tf_op jit(solution)/shard_map/while/body/eval_jaxpr/ppermute | solution.py:239
  428.6 73.7 %collective-permute-done.1 = bf16[128,2048]{1,0:T(8,128)(2,1)S(1)} collective-permute-done((bf16[128,2048]{1,0:T(8,128)(2,1)}, bf16[128,2048]{1,0:T(8,128)(2,1)S(1)}, u32[]{:S(2)}, u32[]{:S(2)}) %collective-permute-start.1) | collective-permute-done | bytes 524320 | tf_op jit(solution)/shard_map/while/body/eval_jaxpr/ppermute | solution.py:239
  503.0 11.5 %conditional.11 = (bf16[128,2048]{1,0:T(8,128)(2,1)}, f32[2048]{0:T(1024)S(1)}) conditional(s32[]{:T(128)} %convert_element_type.303, () %tuple.164, (bf16[128,2048]{1,0:T(8,128)(2,1)S(1)}, bf16[1024,2048]{1,0:T(8,128)(2,1)}, s32[128]{0:T(128)}, f32[128,1536]{0,1:T(8,128)S(1)}, f32[128,1,32]{0,2,1:T(8,128)S(1)}, ...), branch_computations={%region_16.16_spmd, %region_17.25_spmd} | conditional | flops 1528560128 | bytes 72643904 | solution.py:236
  510.3 3.0 multiply_reduce_fusion.2
  519.0 3.3 collective-permute-done.2
  524.8 2.8 collective-permute-done.3
  527.6 2.7 collective-permute-start.4
  530.3 4.9 collective-permute-done.4
  535.4 3.4 collective-permute-done.5
  540.3 3.7 collective-permute-done.6
  (274 shorter events, 109.2 us)
Async XLA Ops:
  7.2 9.4 %copy-start.16 = (bf16[4,32,2048]{2,1,0:T(8,128)(2,1)S(1)}, bf16[4,32,2048]{2,1,0:T(8,128)(2,1)}, u32[]{:S(2)}) copy-start(bf16[4,32,2048]{2,1,0:T(8,128)(2,1)} %param.17) | copy-start | bytes 1572868
  7.2 91.7 %all-gather.6.cloned.1.call-start = ((), (), s32[]{:S(2)}) async-start(), calls=%async_computation.2 | async-start | bytes 4325376 | tf_op jit(solution)/shard_map/all_gather | solution.py:165
  7.9 178.8 %all-gather.4.cloned.1.call-start = ((), (), s32[]{:S(2)}) async-start(), calls=%async_computation.1 | async-start | bytes 6488064 | tf_op jit(solution)/shard_map/all_gather | solution.py:162
  9.6 21.5 %copy-start.17 = (s32[4,32]{1,0:T(4,128)S(1)}, s32[4,32]{1,0:T(4,128)}, u32[]{:S(2)}) copy-start(s32[4,32]{1,0:T(4,128)} %param.19) | copy-start | bytes 1540
  19.8 42.6 %all-to-all-start = ((bf16[32,4,2,2048]{3,2,1,0:T(2,128)(2,1)}), bf16[32,4,2,2048]{3,2,1,0:T(2,128)(2,1)S(1)}, u32[]{:S(2)}, u32[]{:S(2)}) async-start(bf16[32,4,2,2048]{3,2,1,0:T(2,128)(2,1)} %pad_maximum_fusion.3), calls=%async_computation | async-start | bytes 2097152 | tf_op jit(solution)/shard_map/all_to_all | solution.py:181
  98.9 87.9 %copy-start.4 = (f32[1,2048]{1,0:T(1,128)S(1)}, f32[1,2048]{1,0:T(1,128)}, u32[]{:S(2)}) copy-start(f32[1,2048]{1,0:T(1,128)} %param.22) | copy-start | bytes 24580
  186.7 152.5 %copy-start.3 = (bf16[4,32,2048]{2,1,0:T(8,128)(2,1)S(1)}, bf16[4,32,2048]{2,1,0:T(8,128)(2,1)}, u32[]{:S(2)}) copy-start(bf16[4,32,2048]{2,1,0:T(8,128)(2,1)} %param.20) | copy-start | bytes 1572868
  192.9 6.8 %copy-start.1 = (f32[128,1536]{1,0:T(8,128)}, f32[128,1536]{1,0:T(8,128)S(1)}, u32[]{:S(2)}) copy-start(f32[128,1536]{1,0:T(8,128)S(1)} %fusion.18) | copy-start | bytes 2359300 | tf_op jit(solution)/shard_map/while/body/eval_jaxpr/cond
  194.1 1.0 copy-start.13
  194.1 1.0 copy-start.14
  195.1 0.6 copy-start.15
  199.7 3.9 copy-start.2
  203.6 4.5 collective-permute-start
  211.0 19.0 %collective-permute-start = (bf16[128,2048]{1,0:T(8,128)(2,1)}, bf16[128,2048]{1,0:T(8,128)(2,1)S(1)}, u32[]{:S(2)}, u32[]{:S(2)}) collective-permute-start(bf16[128,2048]{1,0:T(8,128)(2,1)} %get-tuple-element.1221), channel_id=1, source_target_pairs={{0,32},{32,64},{64,96},{96,128},{128,160},{160,192},{192,224},{1,3... | collective-permute-start | bytes 1572872 | tf_op jit(solution)/shard_map/while/body/eval_jaxpr/ppermute | solution.py:217
  233.0 8.3 %collective-permute-start = (bf16[128,2048]{1,0:T(8,128)(2,1)}, bf16[128,2048]{1,0:T(8,128)(2,1)S(1)}, u32[]{:S(2)}, u32[]{:S(2)}) collective-permute-start(bf16[128,2048]{1,0:T(8,128)(2,1)} %get-tuple-element.1221), channel_id=1, source_target_pairs={{0,32},{32,64},{64,96},{96,128},{128,160},{160,192},{192,224},{1,3... | collective-permute-start | bytes 1572872 | tf_op jit(solution)/shard_map/while/body/eval_jaxpr/ppermute | solution.py:217
  244.3 24.6 %collective-permute-start = (bf16[128,2048]{1,0:T(8,128)(2,1)}, bf16[128,2048]{1,0:T(8,128)(2,1)S(1)}, u32[]{:S(2)}, u32[]{:S(2)}) collective-permute-start(bf16[128,2048]{1,0:T(8,128)(2,1)} %get-tuple-element.1221), channel_id=1, source_target_pairs={{0,32},{32,64},{64,96},{96,128},{128,160},{160,192},{192,224},{1,3... | collective-permute-start | bytes 1572872 | tf_op jit(solution)/shard_map/while/body/eval_jaxpr/ppermute | solution.py:217
  271.9 10.7 %collective-permute-start = (bf16[128,2048]{1,0:T(8,128)(2,1)}, bf16[128,2048]{1,0:T(8,128)(2,1)S(1)}, u32[]{:S(2)}, u32[]{:S(2)}) collective-permute-start(bf16[128,2048]{1,0:T(8,128)(2,1)} %get-tuple-element.1221), channel_id=1, source_target_pairs={{0,32},{32,64},{64,96},{96,128},{128,160},{160,192},{192,224},{1,3... | collective-permute-start | bytes 1572872 | tf_op jit(solution)/shard_map/while/body/eval_jaxpr/ppermute | solution.py:217
  285.6 13.4 %collective-permute-start = (bf16[128,2048]{1,0:T(8,128)(2,1)}, bf16[128,2048]{1,0:T(8,128)(2,1)S(1)}, u32[]{:S(2)}, u32[]{:S(2)}) collective-permute-start(bf16[128,2048]{1,0:T(8,128)(2,1)} %get-tuple-element.1221), channel_id=1, source_target_pairs={{0,32},{32,64},{64,96},{96,128},{128,160},{160,192},{192,224},{1,3... | collective-permute-start | bytes 1572872 | tf_op jit(solution)/shard_map/while/body/eval_jaxpr/ppermute | solution.py:217
  301.9 10.7 %collective-permute-start = (bf16[128,2048]{1,0:T(8,128)(2,1)}, bf16[128,2048]{1,0:T(8,128)(2,1)S(1)}, u32[]{:S(2)}, u32[]{:S(2)}) collective-permute-start(bf16[128,2048]{1,0:T(8,128)(2,1)} %get-tuple-element.1221), channel_id=1, source_target_pairs={{0,32},{32,64},{64,96},{96,128},{128,160},{160,192},{192,224},{1,3... | collective-permute-start | bytes 1572872 | tf_op jit(solution)/shard_map/while/body/eval_jaxpr/ppermute | solution.py:217
  315.6 22.2 %collective-permute-start = (bf16[128,2048]{1,0:T(8,128)(2,1)}, bf16[128,2048]{1,0:T(8,128)(2,1)S(1)}, u32[]{:S(2)}, u32[]{:S(2)}) collective-permute-start(bf16[128,2048]{1,0:T(8,128)(2,1)} %get-tuple-element.1221), channel_id=1, source_target_pairs={{0,32},{32,64},{64,96},{96,128},{128,160},{160,192},{192,224},{1,3... | collective-permute-start | bytes 1572872 | tf_op jit(solution)/shard_map/while/body/eval_jaxpr/ppermute | solution.py:217
  341.2 8.0 %collective-permute-start.1 = (bf16[128,2048]{1,0:T(8,128)(2,1)}, bf16[128,2048]{1,0:T(8,128)(2,1)S(1)}, u32[]{:S(2)}, u32[]{:S(2)}) collective-permute-start(bf16[128,2048]{1,0:T(8,128)(2,1)} %get-tuple-element.1238), channel_id=1, source_target_pairs={{32,0},{64,32},{96,64},{128,96},{160,128},{192,160},{224,192},{33,... | collective-permute-start | bytes 1572872 | tf_op jit(solution)/shard_map/while/body/eval_jaxpr/ppermute | solution.py:239
  350.8 14.0 %collective-permute-start.1 = (bf16[128,2048]{1,0:T(8,128)(2,1)}, bf16[128,2048]{1,0:T(8,128)(2,1)S(1)}, u32[]{:S(2)}, u32[]{:S(2)}) collective-permute-start(bf16[128,2048]{1,0:T(8,128)(2,1)} %get-tuple-element.1238), channel_id=1, source_target_pairs={{32,0},{64,32},{96,64},{128,96},{160,128},{192,160},{224,192},{33,... | collective-permute-start | bytes 1572872 | tf_op jit(solution)/shard_map/while/body/eval_jaxpr/ppermute | solution.py:239
  366.5 10.7 %collective-permute-start.1 = (bf16[128,2048]{1,0:T(8,128)(2,1)}, bf16[128,2048]{1,0:T(8,128)(2,1)S(1)}, u32[]{:S(2)}, u32[]{:S(2)}) collective-permute-start(bf16[128,2048]{1,0:T(8,128)(2,1)} %get-tuple-element.1238), channel_id=1, source_target_pairs={{32,0},{64,32},{96,64},{128,96},{160,128},{192,160},{224,192},{33,... | collective-permute-start | bytes 1572872 | tf_op jit(solution)/shard_map/while/body/eval_jaxpr/ppermute | solution.py:239
  378.8 20.2 %collective-permute-start.1 = (bf16[128,2048]{1,0:T(8,128)(2,1)}, bf16[128,2048]{1,0:T(8,128)(2,1)S(1)}, u32[]{:S(2)}, u32[]{:S(2)}) collective-permute-start(bf16[128,2048]{1,0:T(8,128)(2,1)} %get-tuple-element.1238), channel_id=1, source_target_pairs={{32,0},{64,32},{96,64},{128,96},{160,128},{192,160},{224,192},{33,... | collective-permute-start | bytes 1572872 | tf_op jit(solution)/shard_map/while/body/eval_jaxpr/ppermute | solution.py:239
  400.6 10.7 %collective-permute-start.1 = (bf16[128,2048]{1,0:T(8,128)(2,1)}, bf16[128,2048]{1,0:T(8,128)(2,1)S(1)}, u32[]{:S(2)}, u32[]{:S(2)}) collective-permute-start(bf16[128,2048]{1,0:T(8,128)(2,1)} %get-tuple-element.1238), channel_id=1, source_target_pairs={{32,0},{64,32},{96,64},{128,96},{160,128},{192,160},{224,192},{33,... | collective-permute-start | bytes 1572872 | tf_op jit(solution)/shard_map/while/body/eval_jaxpr/ppermute | solution.py:239
  413.0 11.3 %collective-permute-start.1 = (bf16[128,2048]{1,0:T(8,128)(2,1)}, bf16[128,2048]{1,0:T(8,128)(2,1)S(1)}, u32[]{:S(2)}, u32[]{:S(2)}) collective-permute-start(bf16[128,2048]{1,0:T(8,128)(2,1)} %get-tuple-element.1238), channel_id=1, source_target_pairs={{32,0},{64,32},{96,64},{128,96},{160,128},{192,160},{224,192},{33,... | collective-permute-start | bytes 1572872 | tf_op jit(solution)/shard_map/while/body/eval_jaxpr/ppermute | solution.py:239
  426.0 76.3 %collective-permute-start.1 = (bf16[128,2048]{1,0:T(8,128)(2,1)}, bf16[128,2048]{1,0:T(8,128)(2,1)S(1)}, u32[]{:S(2)}, u32[]{:S(2)}) collective-permute-start(bf16[128,2048]{1,0:T(8,128)(2,1)} %get-tuple-element.1238), channel_id=1, source_target_pairs={{32,0},{64,32},{96,64},{128,96},{160,128},{192,160},{224,192},{33,... | collective-permute-start | bytes 1572872 | tf_op jit(solution)/shard_map/while/body/eval_jaxpr/ppermute | solution.py:239
  503.1 2.3 copy-start
  503.3 1.7 copy-start.7
  503.3 1.7 copy-start.5
  503.4 1.6 copy-start.9
  503.4 1.6 copy-start.11
  507.1 2.8 slice-start
  507.5 1.6 copy-start.6
  507.5 1.7 copy-start.8
  507.5 2.0 copy-start.10
  507.5 2.0 copy-start.12
  508.0 2.3 slice-start.1
  514.5 4.0 collective-permute-start.1
  518.5 3.9 collective-permute-start.2
  523.1 4.5 collective-permute-start.3
  527.6 7.6 %collective-permute-start.4 = (f32[2048]{0:T(1024)S(1)}, f32[2048]{0:T(1024)S(1)}, u32[]{:S(2)}, u32[]{:S(2)}) collective-permute-start(f32[2048]{0:T(1024)S(1)} %add.336), channel_id=1, source_target_pairs={{0,4},{1,5},{2,6},{3,7},{4,0},{5,1},{6,2},{7,3},{8,12},{9,13},{10,... | collective-permute-start | bytes 24584 | tf_op jit(solution)/shard_map/ppermute | solution.py:119
  535.2 3.7 collective-permute-start.5
  538.9 5.2 collective-permute-start.6
Sparse Core Ops, SparseCore 0:
  10.6 88.2 all-gather.5
  101.4 85.2 all-gather.3

commit v7 on v6

--- a/solution.py
+++ b/solution.py
@@ -40,7 +40,7 @@
     return (residual, normed)
 
 
-def attend(projected_in, tables, allowed, query_heads):
+def rope_stage(projected_in, tables, query_heads):
     row_count = projected_in.shape[0]
     head_size = HD
     query_cols = query_heads * head_size
@@ -61,6 +61,11 @@
         .astype(jnp.bfloat16)
         .reshape(row_count, kv_heads, group_size, head_size)
     )
+    return (queries, key_rows, values)
+
+
+def attend(queries, key_rows, values, allowed):
+    row_count, kv_heads, group_size, head_size = queries.shape
     scores = jnp.einsum(
         "rkgd,skd->kgrs", queries, key_rows, preferred_element_type=jnp.float32
     ) * head_size ** (-0.5)
@@ -71,7 +76,7 @@
     mixed_heads = jnp.einsum(
         "kgrs,skd->rkgd", weights, values, preferred_element_type=jnp.float32
     ).astype(jnp.bfloat16)
-    return mixed_heads.reshape(row_count, query_heads * head_size)
+    return mixed_heads.reshape(row_count, kv_heads * group_size * head_size)
 
 
 def project_in(normed, w_qkv):
@@ -87,25 +92,27 @@
 def layer_forward(hidden_in, steering, gain_row, w_qkv, w_out, tables, allowed):
     residual, normed = normalize(hidden_in, steering, gain_row)
     projected_in = project_in(normed, w_qkv)
-    mixed_heads = attend(projected_in, tables, allowed, w_out.shape[0] // HD)
-    return (project_out(residual, mixed_heads, w_out), projected_in)
-
-
-def layer_backward(
-    hidden_in, steering, projected_in, upstream, gain_row, w_qkv, w_out, tables, allowed
-):
+    rotated = rope_stage(projected_in, tables, w_out.shape[0] // HD)
+    mixed_heads = attend(*rotated, allowed)
+    return (project_out(residual, mixed_heads, w_out), rotated)
+
+
+def layer_backward(hidden_in, steering, rotated, upstream, gain_row, w_qkv, w_out, tables, allowed):
     query_heads = w_out.shape[0] // HD
     (residual, normed), normalize_pull = jax.vjp(
         lambda h, s: normalize(h, s, gain_row), hidden_in, steering
     )
-    mixed_heads, attend_pull = jax.vjp(
-        lambda p: attend(p, tables, allowed, query_heads), projected_in
-    )
+    mixed_heads, attend_pull = jax.vjp(lambda q, k, v: attend(q, k, v, allowed), *rotated)
     unused_out, out_pull = jax.vjp(
         lambda r, m: project_out(r, m, w_out), residual, mixed_heads
     )
     grad_residual, grad_mixed = out_pull(upstream)
-    (grad_projected,) = attend_pull(grad_mixed)
+    grad_rotated = attend_pull(grad_mixed)
+    linear_point = jnp.zeros((hidden_in.shape[0], w_qkv.shape[1]), jnp.float32)
+    unused_rot, rope_pull = jax.vjp(
+        lambda p: rope_stage(p, tables, query_heads), linear_point
+    )
+    (grad_projected,) = rope_pull(grad_rotated)
     unused_proj, in_pull = jax.vjp(lambda n: project_in(n, w_qkv), normed)
     (grad_normed,) = in_pull(grad_projected)
     return normalize_pull((grad_residual, grad_normed))
@@ -201,7 +208,10 @@
         return layer_forward(hidden_in, steer_vec, gain_row, full_qkv, full_out, tables, allowed)
 
     zero_block = jnp.zeros((flat_count, width), jnp.bfloat16)
-    zero_proj = jnp.zeros((flat_count, full_qkv.shape[1]), jnp.float32)
+    zero_proj = jax.tree_util.tree_map(
+        lambda leaf: jnp.zeros(leaf.shape, leaf.dtype),
+        jax.eval_shape(lambda: run_layer(zero_block, steering)[1]),
+    )
     forward_route = [(i, i + 1) for i in range(section_count - 1)]
     backward_route = [(i + 1, i) for i in range(section_count - 1)]
 
@@ -213,7 +223,9 @@
             active, lambda: run_layer(hidden_in, steering), lambda: (zero_block, zero_proj)
         )
         produced = jnp.where(active, hidden_new, produced)
-        saved = jnp.where(active, projected, saved)
+        saved = jax.tree_util.tree_map(
+            lambda new, old: jnp.where(active, new, old), projected, saved
+        )
         sent = lax.ppermute(hidden_new, "section", forward_route)
         return ((sent, kept, produced, saved, step + 1), None)
 

time: 556 us -> 585 us (1.052)
  waiting for transfers between devices: 296 us -> 321 us
  starting transfers between devices: 108 us -> 120 us
    ppermute x8, waiting for transfers between devices: 135 us -> 160 us  [backward_step(): sent = lax.ppermute(grad_in, 'section', backward_route)]
    broadcast_in_dim x14, local copies, waits for them, and re-layouts: 12.1 us -> 0.64 us  [body(): zero_block = jnp.zeros((flat_count, width), jnp.bfloat16)]
    ppermute x8, starting transfers between devices: 80.1 us -> 91.3 us  [forward_step(): sent = lax.ppermute(hidden_new, 'section', forward_route)]
    ge x32, local copies, waits for them, and re-layouts: 10.1 us -> 0.24 us  [body(): flat_index[:, None] >= flat_index[None, :]]
    another operation x7 -> x21, local copies, waits for them, and re-layouts: 0.01 us -> 8.75 us
    while x8, local copies, waits for them, and re-layouts: 0.33 us -> 8.34 us
    select_n x8 -> x16, other arithmetic: 15.7 us -> 12.3 us  [forward_step(): jnp.where(active, new, old)]
  transfers between devices with their start and end apart: 24 -> 24, of which waited for: 16 -> 16; matrix products, arithmetic and copies ran while one was open for 12% -> 11% of each run, Pallas kernels for 0% -> 0%
where the time goes in v7:
time: 585 us; the launch traced here: 582 us
  waiting for transfers between devices  321 us (55%)
  starting transfers between devices  120 us (21%)
  other arithmetic  67.1 us (11%)
  local copies, waits for them, and re-layouts  33.5 us (6%)
  matrix products  25 us (4%)
  between operations  14.3 us (2%)
    ppermute x8, waiting for transfers between devices, backward_step(): sent = lax.ppermute(grad_in, 'section', backward_route)  160 us
    ppermute x8, starting transfers between devices, forward_step(): sent = lax.ppermute(hidden_new, 'section', forward_route)  91.3 us
    all_gather x1, waiting for transfers between devices, body(): lax.all_gather(jnp.concatenate([w_query[0], w_keyval[0]], axis=1), 'dp',...  81.3 us
    all_gather x1, waiting for transfers between devices, body(): full_out = lax.all_gather(w_out[0], 'dp', axis=1, tiled=True)  34.3 us
    all_to_all x1, waiting for transfers between devices, body(): lax.all_to_all(packed, 'dp', split_axis=0, concat_axis=0, tiled=True)  26.4 us
    ppermute x5, waiting for transfers between devices, butterfly_sum(): values = values + lax.ppermute(values, axis, route)  18.2 us
    select_n x8, other arithmetic, forward_step(): produced = jnp.where(active, hidden_new, produced)  16.2 us
    select_n x16, other arithmetic, forward_step(): jnp.where(active, new, old)  12.3 us
  transfers between devices with their start and end apart: 24, of which 16 were waited for; matrix products, arithmetic and copies ran while one was open for 11% of the time, Pallas kernels for 0%

profile of v7, /device:TPU:32, one launch (start us, length us, event | category | flops | bytes accessed | tf_op | source)
XLA Modules:
  0.0 582.0 jit_solution(16458348993164564343)
XLA Ops:
  8.0 1.6 pad_maximum_fusion.4
  10.9 2.9 convert_reduce_fusion.4
  17.4 2.4 pad_maximum_fusion.2
  19.8 11.4 %all-to-all-start = ((bf16[32,4,2,2048]{3,2,1,0:T(2,128)(2,1)}), bf16[32,4,2,2048]{3,2,1,0:T(2,128)(2,1)S(1)}, u32[]{:S(2)}, u32[]{:S(2)}) async-start(bf16[32,4,2,2048]{3,2,1,0:T(2,128)(2,1)} %pad_maximum_fusion.2), calls=%async_computation | async-start | bytes 2097152 | tf_op jit(solution)/shard_map/all_to_all | solution.py:188
  35.9 26.4 %all-to-all-done = bf16[32,4,2,2048]{3,2,1,0:T(2,128)(2,1)S(1)} async-done(((bf16[32,4,2,2048]{3,2,1,0:T(2,128)(2,1)}), bf16[32,4,2,2048]{3,2,1,0:T(2,128)(2,1)S(1)}, u32[]{:S(2)}, u32[]{:S(2)}) %all-to-all-start) | async-done | bytes 1048608 | tf_op jit(solution)/shard_map/all_to_all | solution.py:188
  64.6 34.3 %all-gather.6.cloned.1.call-done = bf16[1,1024,2048]{1,2,0:T(8,128)(2,1)} async-done(((bf16[1,1024,64]{1,2,0:T(8,128)(2,1)}), bf16[1,1024,2048]{1,2,0:T(8,128)(2,1)}) %all-gather.6.cloned.1.call-update) | async-done | bytes 4194320 | tf_op jit(solution)/shard_map/all_gather | solution.py:172
  98.8 6.6 %copy.55 = bf16[1024,2048]{1,0:T(8,128)(2,1)} copy(bf16[1024,2048]{0,1:T(8,128)(2,1)} %bitcast.203) | data formatting | bytes 8388608
  105.4 81.3 %all-gather.4.cloned.1.call-done = bf16[2048,1536]{1,0:T(8,128)(2,1)} async-done(((bf16[64,1536]{1,0:T(8,128)(2,1)}), bf16[2048,1536]{1,0:T(8,128)(2,1)}) %all-gather.4.cloned.1.call-update) | async-done | bytes 6291472 | tf_op jit(solution)/shard_map/all_gather | solution.py:169
  186.7 161.3 %while.46 = (s32[]{:T(128)}, bf16[128,2048]{1,0:T(8,128)(2,1)S(1)}, bf16[128,2048]{1,0:T(8,128)(2,1)S(1)}, bf16[128,2048]{1,0:T(8,128)(2,1)}, bf16[128,4,4,64]{0...) while((s32[]{:T(128)}, bf16[128,2048]{1,0:T(8,128)(2,1)S(1)}, ...), condition=%wide.region_14.15_spmd.clone.clone.clone, body=%wide.region_8.14_spmd.clone.clone.clone.sunk | while | flops 1451547008 | bytes 31313940 | solution.py:232
  187.5 17.2 %conditional.10 = (bf16[128,2048]{1,0:T(8,128)(2,1)S(1)}, bf16[128,4,4,64]{0,3,2,1:T(8,128)(2,1)S(1)}, bf16[128,4,64]{0,2,1:T(8,128)(2,1)}, bf16[128,4,64]{0,2,1:T(8,128)(2,1)}) conditional(s32[]{:T(128)} %convert_element_type.295, () %tuple.162, (bf16[128,2048]{1,0:T(8,128)(2,1)S(1)}, f32[1,2048]{1,0:T(1,128)S(1)}, f32[1,2048]{1,0:T(1,128)}, ...), branch_computations={%region_9.9_spmd, %region_10.13_spmd} | conditional | flops 1450101120 | bytes 23694424 | solution.py:222
  187.8 3.8 fusion.18
  195.5 2.2 fusion.17
  199.8 2.0 convolution_convert_fusion
  201.8 3.0 fusion.13
  204.8 2.1 collective-permute-start
  206.9 1.5 select_select_fusion.10
  212.8 17.1 %collective-permute-start = (bf16[128,2048]{1,0:T(8,128)(2,1)S(1)}, bf16[128,2048]{1,0:T(8,128)(2,1)}, u32[]{:S(2)}, u32[]{:S(2)}) collective-permute-start(bf16[128,2048]{1,0:T(8,128)(2,1)S(1)} %get-tuple-element.1374), channel_id=1, source_target_pairs={{0,32},{32,64},{64,96},{96,128},{128,160},{160,192},{192,224},{1,3... | collective-permute-start | bytes 1572872 | tf_op jit(solution)/shard_map/while/body/eval_jaxpr/ppermute | solution.py:229
  231.4 2.2 select_select_fusion.8
  236.7 4.3 collective-permute-start
  242.6 2.2 select_select_fusion.8
  247.9 22.7 %collective-permute-start = (bf16[128,2048]{1,0:T(8,128)(2,1)S(1)}, bf16[128,2048]{1,0:T(8,128)(2,1)}, u32[]{:S(2)}, u32[]{:S(2)}) collective-permute-start(bf16[128,2048]{1,0:T(8,128)(2,1)S(1)} %get-tuple-element.1374), channel_id=1, source_target_pairs={{0,32},{32,64},{64,96},{96,128},{128,160},{160,192},{192,224},{1,3... | collective-permute-start | bytes 1572872 | tf_op jit(solution)/shard_map/while/body/eval_jaxpr/ppermute | solution.py:229
  272.2 2.2 select_select_fusion.8
  277.5 6.9 %collective-permute-start = (bf16[128,2048]{1,0:T(8,128)(2,1)S(1)}, bf16[128,2048]{1,0:T(8,128)(2,1)}, u32[]{:S(2)}, u32[]{:S(2)}) collective-permute-start(bf16[128,2048]{1,0:T(8,128)(2,1)S(1)} %get-tuple-element.1374), channel_id=1, source_target_pairs={{0,32},{32,64},{64,96},{96,128},{128,160},{160,192},{192,224},{1,3... | collective-permute-start | bytes 1572872 | tf_op jit(solution)/shard_map/while/body/eval_jaxpr/ppermute | solution.py:229
  286.0 2.2 select_select_fusion.8
  291.3 11.1 %collective-permute-start = (bf16[128,2048]{1,0:T(8,128)(2,1)S(1)}, bf16[128,2048]{1,0:T(8,128)(2,1)}, u32[]{:S(2)}, u32[]{:S(2)}) collective-permute-start(bf16[128,2048]{1,0:T(8,128)(2,1)S(1)} %get-tuple-element.1374), channel_id=1, source_target_pairs={{0,32},{32,64},{64,96},{96,128},{128,160},{160,192},{192,224},{1,3... | collective-permute-start | bytes 1572872 | tf_op jit(solution)/shard_map/while/body/eval_jaxpr/ppermute | solution.py:229
  304.0 2.2 select_select_fusion.8
  309.3 6.9 %collective-permute-start = (bf16[128,2048]{1,0:T(8,128)(2,1)S(1)}, bf16[128,2048]{1,0:T(8,128)(2,1)}, u32[]{:S(2)}, u32[]{:S(2)}) collective-permute-start(bf16[128,2048]{1,0:T(8,128)(2,1)S(1)} %get-tuple-element.1374), channel_id=1, source_target_pairs={{0,32},{32,64},{64,96},{96,128},{128,160},{160,192},{192,224},{1,3... | collective-permute-start | bytes 1572872 | tf_op jit(solution)/shard_map/while/body/eval_jaxpr/ppermute | solution.py:229
  317.8 2.2 select_select_fusion.8
  323.1 20.2 %collective-permute-start = (bf16[128,2048]{1,0:T(8,128)(2,1)S(1)}, bf16[128,2048]{1,0:T(8,128)(2,1)}, u32[]{:S(2)}, u32[]{:S(2)}) collective-permute-start(bf16[128,2048]{1,0:T(8,128)(2,1)S(1)} %get-tuple-element.1374), channel_id=1, source_target_pairs={{0,32},{32,64},{64,96},{96,128},{128,160},{160,192},{192,224},{1,3... | collective-permute-start | bytes 1572872 | tf_op jit(solution)/shard_map/while/body/eval_jaxpr/ppermute | solution.py:229
  344.8 2.2 select_select_fusion.8
  348.0 201.0 %while.47 = (s32[]{:T(128)}, bf16[128,2048]{1,0:T(8,128)(2,1)S(1)}, f32[2048]{0:T(1024)}, s32[]{:T(128)}, bf16[1024,2048]{1,0:T(8,128)(2,1)}, /*index=5*/bf16[12...) while((s32[]{:T(128)}, bf16[128,2048]{1,0:T(8,128)(2,1)S(1)}, ...), condition=%wide.region_26.27_spmd.clone.clone.clone, body=%wide.region_15.26_spmd.clone.clone.clone.sunk | while | flops 1526602240 | bytes 53024824 | solution.py:254
  350.8 5.6 collective-permute-done.1
  359.8 12.9 %collective-permute-done.1 = bf16[128,2048]{1,0:T(8,128)(2,1)S(1)} collective-permute-done((bf16[128,2048]{1,0:T(8,128)(2,1)S(1)}, bf16[128,2048]{1,0:T(8,128)(2,1)S(1)}, u32[]{:S(2)}, u32[]{:S(2)}) %collective-permute-start.1) | collective-permute-done | bytes 524320 | tf_op jit(solution)/shard_map/while/body/eval_jaxpr/ppermute | solution.py:251
  376.2 7.9 %collective-permute-done.1 = bf16[128,2048]{1,0:T(8,128)(2,1)S(1)} collective-permute-done((bf16[128,2048]{1,0:T(8,128)(2,1)S(1)}, bf16[128,2048]{1,0:T(8,128)(2,1)S(1)}, u32[]{:S(2)}, u32[]{:S(2)}) %collective-permute-start.1) | collective-permute-done | bytes 524320 | tf_op jit(solution)/shard_map/while/body/eval_jaxpr/ppermute | solution.py:251
  387.6 19.8 %collective-permute-done.1 = bf16[128,2048]{1,0:T(8,128)(2,1)S(1)} collective-permute-done((bf16[128,2048]{1,0:T(8,128)(2,1)S(1)}, bf16[128,2048]{1,0:T(8,128)(2,1)S(1)}, u32[]{:S(2)}, u32[]{:S(2)}) %collective-permute-start.1) | collective-permute-done | bytes 524320 | tf_op jit(solution)/shard_map/while/body/eval_jaxpr/ppermute | solution.py:251
  410.8 7.9 %collective-permute-done.1 = bf16[128,2048]{1,0:T(8,128)(2,1)S(1)} collective-permute-done((bf16[128,2048]{1,0:T(8,128)(2,1)S(1)}, bf16[128,2048]{1,0:T(8,128)(2,1)S(1)}, u32[]{:S(2)}, u32[]{:S(2)}) %collective-permute-start.1) | collective-permute-done | bytes 524320 | tf_op jit(solution)/shard_map/while/body/eval_jaxpr/ppermute | solution.py:251
  422.2 10.7 %collective-permute-done.1 = bf16[128,2048]{1,0:T(8,128)(2,1)S(1)} collective-permute-done((bf16[128,2048]{1,0:T(8,128)(2,1)S(1)}, bf16[128,2048]{1,0:T(8,128)(2,1)S(1)}, u32[]{:S(2)}, u32[]{:S(2)}) %collective-permute-start.1) | collective-permute-done | bytes 524320 | tf_op jit(solution)/shard_map/while/body/eval_jaxpr/ppermute | solution.py:251
  436.4 94.4 %collective-permute-done.1 = bf16[128,2048]{1,0:T(8,128)(2,1)S(1)} collective-permute-done((bf16[128,2048]{1,0:T(8,128)(2,1)S(1)}, bf16[128,2048]{1,0:T(8,128)(2,1)S(1)}, u32[]{:S(2)}, u32[]{:S(2)}) %collective-permute-start.1) | collective-permute-done | bytes 524320 | tf_op jit(solution)/shard_map/while/body/eval_jaxpr/ppermute | solution.py:251
  531.6 13.6 %conditional.11 = (bf16[128,2048]{1,0:T(8,128)(2,1)S(1)}, f32[2048]{0:T(1024)S(1)}) conditional(s32[]{:T(128)} %convert_element_type.296, () %tuple.165, (bf16[128,2048]{1,0:T(8,128)(2,1)S(1)}, bf16[1024,2048]{1,0:T(8,128)(2,1)}, s32[128]{0:T(128)}, bf16[128,4,64]{0,2,1:T(8,128)(2,1)S(1)}, bf16[128,4,4,64]{0,3,2,1:T(8,128)(2,1)S(1)}, ...), branch_computations={%region_16.16_spmd, %region_17.25_spmd} | conditional | flops 1526594048 | bytes 50754624 | solution.py:248
  533.0 3.7 convolution_convert_fusion.4
  541.8 3.0 multiply_reduce_fusion.2
  549.6 3.3 collective-permute-done.2
  553.6 1.7 collective-permute-start.3
  555.3 2.8 collective-permute-done.3
  558.1 2.7 collective-permute-start.4
  560.8 4.9 collective-permute-done.4
  565.9 3.5 collective-permute-done.5
  570.8 3.7 collective-permute-done.6
  (270 shorter events, 102.5 us)
Async XLA Ops:
  7.2 9.4 %copy-start.4 = (bf16[4,32,2048]{2,1,0:T(8,128)(2,1)S(1)}, bf16[4,32,2048]{2,1,0:T(8,128)(2,1)}, u32[]{:S(2)}) copy-start(bf16[4,32,2048]{2,1,0:T(8,128)(2,1)} %param.17) | copy-start | bytes 1572868
  7.2 91.7 %all-gather.6.cloned.1.call-start = ((), (), s32[]{:S(2)}) async-start(), calls=%async_computation.2 | async-start | bytes 4325376 | tf_op jit(solution)/shard_map/all_gather | solution.py:172
  7.9 178.8 %all-gather.4.cloned.1.call-start = ((), (), s32[]{:S(2)}) async-start(), calls=%async_computation.1 | async-start | bytes 6488064 | tf_op jit(solution)/shard_map/all_gather | solution.py:169
  9.6 21.5 %copy-start.5 = (s32[4,32]{1,0:T(4,128)S(1)}, s32[4,32]{1,0:T(4,128)}, u32[]{:S(2)}) copy-start(s32[4,32]{1,0:T(4,128)} %param.19) | copy-start | bytes 1540
  19.8 42.5 %all-to-all-start = ((bf16[32,4,2,2048]{3,2,1,0:T(2,128)(2,1)}), bf16[32,4,2,2048]{3,2,1,0:T(2,128)(2,1)S(1)}, u32[]{:S(2)}, u32[]{:S(2)}) async-start(bf16[32,4,2,2048]{3,2,1,0:T(2,128)(2,1)} %pad_maximum_fusion.2), calls=%async_computation | async-start | bytes 2097152 | tf_op jit(solution)/shard_map/all_to_all | solution.py:188
  98.8 87.9 %copy-start.3 = (f32[1,2048]{1,0:T(1,128)S(1)}, f32[1,2048]{1,0:T(1,128)}, u32[]{:S(2)}) copy-start(f32[1,2048]{1,0:T(1,128)} %param.22) | copy-start | bytes 24580
  186.7 161.3 %copy-start = (bf16[4,32,2048]{2,1,0:T(8,128)(2,1)S(1)}, bf16[4,32,2048]{2,1,0:T(8,128)(2,1)}, u32[]{:S(2)}) copy-start(bf16[4,32,2048]{2,1,0:T(8,128)(2,1)} %param.20) | copy-start | bytes 1572868
  194.0 7.8 %copy-start.1 = (bf16[128,4,4,64]{0,3,2,1:T(8,128)(2,1)}, bf16[128,4,4,64]{0,3,2,1:T(8,128)(2,1)S(1)}, u32[]{:S(2)}) copy-start(bf16[128,4,4,64]{0,3,2,1:T(8,128)(2,1)S(1)} %pad_maximum_fusion) | copy-start | bytes 786436 | tf_op jit(solution)/shard_map/while/body/eval_jaxpr/cond
  201.7 3.0 copy-start.2
  204.8 4.8 collective-permute-start
  212.8 20.8 %collective-permute-start = (bf16[128,2048]{1,0:T(8,128)(2,1)S(1)}, bf16[128,2048]{1,0:T(8,128)(2,1)}, u32[]{:S(2)}, u32[]{:S(2)}) collective-permute-start(bf16[128,2048]{1,0:T(8,128)(2,1)S(1)} %get-tuple-element.1374), channel_id=1, source_target_pairs={{0,32},{32,64},{64,96},{96,128},{128,160},{160,192},{192,224},{1,3... | collective-permute-start | bytes 1572872 | tf_op jit(solution)/shard_map/while/body/eval_jaxpr/ppermute | solution.py:229
  236.7 8.0 %collective-permute-start = (bf16[128,2048]{1,0:T(8,128)(2,1)S(1)}, bf16[128,2048]{1,0:T(8,128)(2,1)}, u32[]{:S(2)}, u32[]{:S(2)}) collective-permute-start(bf16[128,2048]{1,0:T(8,128)(2,1)S(1)} %get-tuple-element.1374), channel_id=1, source_target_pairs={{0,32},{32,64},{64,96},{96,128},{128,160},{160,192},{192,224},{1,3... | collective-permute-start | bytes 1572872 | tf_op jit(solution)/shard_map/while/body/eval_jaxpr/ppermute | solution.py:229
  247.9 26.4 %collective-permute-start = (bf16[128,2048]{1,0:T(8,128)(2,1)S(1)}, bf16[128,2048]{1,0:T(8,128)(2,1)}, u32[]{:S(2)}, u32[]{:S(2)}) collective-permute-start(bf16[128,2048]{1,0:T(8,128)(2,1)S(1)} %get-tuple-element.1374), channel_id=1, source_target_pairs={{0,32},{32,64},{64,96},{96,128},{128,160},{160,192},{192,224},{1,3... | collective-permute-start | bytes 1572872 | tf_op jit(solution)/shard_map/while/body/eval_jaxpr/ppermute | solution.py:229
  277.5 10.6 %collective-permute-start = (bf16[128,2048]{1,0:T(8,128)(2,1)S(1)}, bf16[128,2048]{1,0:T(8,128)(2,1)}, u32[]{:S(2)}, u32[]{:S(2)}) collective-permute-start(bf16[128,2048]{1,0:T(8,128)(2,1)S(1)} %get-tuple-element.1374), channel_id=1, source_target_pairs={{0,32},{32,64},{64,96},{96,128},{128,160},{160,192},{192,224},{1,3... | collective-permute-start | bytes 1572872 | tf_op jit(solution)/shard_map/while/body/eval_jaxpr/ppermute | solution.py:229
  291.3 14.8 %collective-permute-start = (bf16[128,2048]{1,0:T(8,128)(2,1)S(1)}, bf16[128,2048]{1,0:T(8,128)(2,1)}, u32[]{:S(2)}, u32[]{:S(2)}) collective-permute-start(bf16[128,2048]{1,0:T(8,128)(2,1)S(1)} %get-tuple-element.1374), channel_id=1, source_target_pairs={{0,32},{32,64},{64,96},{96,128},{128,160},{160,192},{192,224},{1,3... | collective-permute-start | bytes 1572872 | tf_op jit(solution)/shard_map/while/body/eval_jaxpr/ppermute | solution.py:229
  309.3 10.6 %collective-permute-start = (bf16[128,2048]{1,0:T(8,128)(2,1)S(1)}, bf16[128,2048]{1,0:T(8,128)(2,1)}, u32[]{:S(2)}, u32[]{:S(2)}) collective-permute-start(bf16[128,2048]{1,0:T(8,128)(2,1)S(1)} %get-tuple-element.1374), channel_id=1, source_target_pairs={{0,32},{32,64},{64,96},{96,128},{128,160},{160,192},{192,224},{1,3... | collective-permute-start | bytes 1572872 | tf_op jit(solution)/shard_map/while/body/eval_jaxpr/ppermute | solution.py:229
  323.1 23.9 %collective-permute-start = (bf16[128,2048]{1,0:T(8,128)(2,1)S(1)}, bf16[128,2048]{1,0:T(8,128)(2,1)}, u32[]{:S(2)}, u32[]{:S(2)}) collective-permute-start(bf16[128,2048]{1,0:T(8,128)(2,1)S(1)} %get-tuple-element.1374), channel_id=1, source_target_pairs={{0,32},{32,64},{64,96},{96,128},{128,160},{160,192},{192,224},{1,3... | collective-permute-start | bytes 1572872 | tf_op jit(solution)/shard_map/while/body/eval_jaxpr/ppermute | solution.py:229
  348.9 7.5 %collective-permute-start.1 = (bf16[128,2048]{1,0:T(8,128)(2,1)S(1)}, bf16[128,2048]{1,0:T(8,128)(2,1)S(1)}, u32[]{:S(2)}, u32[]{:S(2)}) collective-permute-start(bf16[128,2048]{1,0:T(8,128)(2,1)S(1)} %get-tuple-element.1397), channel_id=1, source_target_pairs={{32,0},{64,32},{96,64},{128,96},{160,128},{192,160},{224,192},{33,... | collective-permute-start | bytes 1572872 | tf_op jit(solution)/shard_map/while/body/eval_jaxpr/ppermute | solution.py:251
  357.2 15.6 %collective-permute-start.1 = (bf16[128,2048]{1,0:T(8,128)(2,1)S(1)}, bf16[128,2048]{1,0:T(8,128)(2,1)S(1)}, u32[]{:S(2)}, u32[]{:S(2)}) collective-permute-start(bf16[128,2048]{1,0:T(8,128)(2,1)S(1)} %get-tuple-element.1397), channel_id=1, source_target_pairs={{32,0},{64,32},{96,64},{128,96},{160,128},{192,160},{224,192},{33,... | collective-permute-start | bytes 1572872 | tf_op jit(solution)/shard_map/while/body/eval_jaxpr/ppermute | solution.py:251
  373.6 10.5 %collective-permute-start.1 = (bf16[128,2048]{1,0:T(8,128)(2,1)S(1)}, bf16[128,2048]{1,0:T(8,128)(2,1)S(1)}, u32[]{:S(2)}, u32[]{:S(2)}) collective-permute-start(bf16[128,2048]{1,0:T(8,128)(2,1)S(1)} %get-tuple-element.1397), channel_id=1, source_target_pairs={{32,0},{64,32},{96,64},{128,96},{160,128},{192,160},{224,192},{33,... | collective-permute-start | bytes 1572872 | tf_op jit(solution)/shard_map/while/body/eval_jaxpr/ppermute | solution.py:251
  385.0 22.4 %collective-permute-start.1 = (bf16[128,2048]{1,0:T(8,128)(2,1)S(1)}, bf16[128,2048]{1,0:T(8,128)(2,1)S(1)}, u32[]{:S(2)}, u32[]{:S(2)}) collective-permute-start(bf16[128,2048]{1,0:T(8,128)(2,1)S(1)} %get-tuple-element.1397), channel_id=1, source_target_pairs={{32,0},{64,32},{96,64},{128,96},{160,128},{192,160},{224,192},{33,... | collective-permute-start | bytes 1572872 | tf_op jit(solution)/shard_map/while/body/eval_jaxpr/ppermute | solution.py:251
  408.2 10.5 %collective-permute-start.1 = (bf16[128,2048]{1,0:T(8,128)(2,1)S(1)}, bf16[128,2048]{1,0:T(8,128)(2,1)S(1)}, u32[]{:S(2)}, u32[]{:S(2)}) collective-permute-start(bf16[128,2048]{1,0:T(8,128)(2,1)S(1)} %get-tuple-element.1397), channel_id=1, source_target_pairs={{32,0},{64,32},{96,64},{128,96},{160,128},{192,160},{224,192},{33,... | collective-permute-start | bytes 1572872 | tf_op jit(solution)/shard_map/while/body/eval_jaxpr/ppermute | solution.py:251
  419.6 13.3 %collective-permute-start.1 = (bf16[128,2048]{1,0:T(8,128)(2,1)S(1)}, bf16[128,2048]{1,0:T(8,128)(2,1)S(1)}, u32[]{:S(2)}, u32[]{:S(2)}) collective-permute-start(bf16[128,2048]{1,0:T(8,128)(2,1)S(1)} %get-tuple-element.1397), channel_id=1, source_target_pairs={{32,0},{64,32},{96,64},{128,96},{160,128},{192,160},{224,192},{33,... | collective-permute-start | bytes 1572872 | tf_op jit(solution)/shard_map/while/body/eval_jaxpr/ppermute | solution.py:251
  433.8 97.0 %collective-permute-start.1 = (bf16[128,2048]{1,0:T(8,128)(2,1)S(1)}, bf16[128,2048]{1,0:T(8,128)(2,1)S(1)}, u32[]{:S(2)}, u32[]{:S(2)}) collective-permute-start(bf16[128,2048]{1,0:T(8,128)(2,1)S(1)} %get-tuple-element.1397), channel_id=1, source_target_pairs={{32,0},{64,32},{96,64},{128,96},{160,128},{192,160},{224,192},{33,... | collective-permute-start | bytes 1572872 | tf_op jit(solution)/shard_map/while/body/eval_jaxpr/ppermute | solution.py:251
  538.7 2.2 slice-start
  539.7 2.1 slice-start.1
  545.2 3.8 collective-permute-start.1
  549.0 3.9 collective-permute-start.2
  553.6 4.5 collective-permute-start.3
  558.1 7.6 %collective-permute-start.4 = (f32[2048]{0:T(1024)S(1)}, f32[2048]{0:T(1024)S(1)}, u32[]{:S(2)}, u32[]{:S(2)}) collective-permute-start(f32[2048]{0:T(1024)S(1)} %add.330), channel_id=1, source_target_pairs={{0,4},{1,5},{2,6},{3,7},{4,0},{5,1},{6,2},{7,3},{8,12},{9,13},{10,... | collective-permute-start | bytes 24584 | tf_op jit(solution)/shard_map/ppermute | solution.py:126
  565.7 3.7 collective-permute-start.5
  569.4 5.2 collective-permute-start.6
Sparse Core Ops, SparseCore 0:
  10.6 88.2 all-gather.5
  101.4 85.2 all-gather.3

commit v8 on v6

--- a/solution.py
+++ b/solution.py
@@ -202,30 +202,30 @@
 
     zero_block = jnp.zeros((flat_count, width), jnp.bfloat16)
     zero_proj = jnp.zeros((flat_count, full_qkv.shape[1]), jnp.float32)
+
+    def precompute(hidden_in):
+        return project_in(normalize(hidden_in, steering, gain_row)[1], full_qkv)
     forward_route = [(i, i + 1) for i in range(section_count - 1)]
     backward_route = [(i + 1, i) for i in range(section_count - 1)]
 
     def forward_step(carry, unused):
-        hidden_in, kept, produced, saved, step = carry
+        hidden_in, kept, produced, step = carry
         active = section_idx == step
         kept = jnp.where(active, hidden_in, kept)
-        hidden_new, projected = lax.cond(
-            active, lambda: run_layer(hidden_in, steering), lambda: (zero_block, zero_proj)
-        )
+        hidden_new = lax.cond(active, lambda: run_layer(hidden_in, steering)[0], lambda: zero_block)
         produced = jnp.where(active, hidden_new, produced)
-        saved = jnp.where(active, projected, saved)
         sent = lax.ppermute(hidden_new, "section", forward_route)
-        return ((sent, kept, produced, saved, step + 1), None)
-
-    (unused_in, kept, produced, saved, unused_step), unused_ys = lax.scan(
-        forward_step,
-        (grouped, zero_block, zero_block, zero_proj, jnp.int32(0)),
-        None,
-        length=section_count,
+        return ((sent, kept, produced, step + 1), None)
+
+    (unused_in, kept, produced, unused_step), unused_ys = lax.scan(
+        forward_step, (grouped, zero_block, zero_block, jnp.int32(0)), None, length=section_count
+    )
+    first_saved = lax.cond(
+        section_idx == section_count - 1, lambda: precompute(kept), lambda: zero_proj
     )
 
     def backward_step(carry, unused):
-        upstream, grad_sum, step = carry
+        upstream, grad_sum, step, saved = carry
         active = section_idx == step
 
         def differentiate():
@@ -237,11 +237,14 @@
             active, differentiate, lambda: (zero_block, jnp.zeros_like(steering))
         )
         sent = lax.ppermute(grad_in, "section", backward_route)
-        return ((sent, grad_sum + steer_part, step - 1), None)
-
-    (unused_grad, grad_sum, unused_step), unused_zs = lax.scan(
+        next_saved = lax.cond(
+            section_idx == step - 1, lambda: precompute(kept), lambda: zero_proj
+        )
+        return ((sent, grad_sum + steer_part, step - 1, next_saved), None)
+
+    (unused_grad, grad_sum, unused_step, unused_saved), unused_zs = lax.scan(
         backward_step,
-        (cotangent, jnp.zeros_like(steering), jnp.int32(section_count - 1)),
+        (cotangent, jnp.zeros_like(steering), jnp.int32(section_count - 1), first_saved),
         None,
         length=section_count,
     )

time: 556 us -> 512 us (0.921)
  other arithmetic: 72.9 us -> 30.9 us
  local copies, waits for them, and re-layouts: 37.2 us -> 22.5 us
  waiting for transfers between devices: 296 us -> 309 us
    select_n x8 -> x0, other arithmetic: 15.7 us -> none  [forward_step(): saved = jnp.where(active, projected, saved)]
    select_n x8, other arithmetic: 17.4 us -> 2.87 us  [forward_step(): produced = jnp.where(active, hidden_new, produced)]
    broadcast_in_dim x14, local copies, waits for them, and re-layouts: 12.1 us -> 0.64 us  [body(): zero_block = jnp.zeros((flat_count, width), jnp.bfloat16)]
    ge x32, local copies, waits for them, and re-layouts: 10.1 us -> 0.24 us  [body(): flat_index[:, None] >= flat_index[None, :]]
    add x8, other arithmetic: 9.76 us -> 0.04 us  [backward_step(): return ((sent, grad_sum + steer_part, step - 1, next_saved), None)]
    ppermute x8, waiting for transfers between devices: 0.02 us -> 8.92 us  [forward_step(): sent = lax.ppermute(hidden_new, 'section', forward_route)]
    broadcast_in_dim x7 -> x8, local copies, waits for them, and re-layouts: 0.47 us -> 7.73 us  [body(): zero_proj = jnp.zeros((flat_count, full_qkv.shape[1]), jnp.float32)]
    ppermute x8, waiting for transfers between devices: 135 us -> 141 us  [backward_step(): sent = lax.ppermute(grad_in, 'section', backward_route)]
  transfers between devices with their start and end apart: 24 -> 24, of which waited for: 16 -> 24; matrix products, arithmetic and copies ran while one was open for 12% -> 8% of each run, Pallas kernels for 0% -> 0%
where the time goes in v8:
time: 512 us; the launch traced here: 510 us
  waiting for transfers between devices  309 us (60%)
  starting transfers between devices  106 us (21%)
  other arithmetic  30.9 us (6%)
  matrix products  25.8 us (5%)
  local copies, waits for them, and re-layouts  22.5 us (4%)
  between operations  14.4 us (3%)
    ppermute x8, waiting for transfers between devices, backward_step(): sent = lax.ppermute(grad_in, 'section', backward_route)  141 us
    all_gather x1, waiting for transfers between devices, body(): lax.all_gather(jnp.concatenate([w_query[0], w_keyval[0]], axis=1), 'dp',...  81.9 us
    ppermute x8, starting transfers between devices, forward_step(): sent = lax.ppermute(hidden_new, 'section', forward_route)  77.9 us
    all_gather x1, waiting for transfers between devices, body(): full_out = lax.all_gather(w_out[0], 'dp', axis=1, tiled=True)  31.5 us
    all_to_all x1, waiting for transfers between devices, body(): lax.all_to_all(packed, 'dp', split_axis=0, concat_axis=0, tiled=True)  26.9 us
    ppermute x5, waiting for transfers between devices, butterfly_sum(): values = values + lax.ppermute(values, axis, route)  17.9 us
    mul x16, other arithmetic, rope_tables(): angles = positions.astype(jnp.float32)[..., None] * inverse  12.1 us
    all_to_all x1, starting transfers between devices, body(): lax.all_to_all(packed, 'dp', split_axis=0, concat_axis=0, tiled=True)  11.4 us
  transfers between devices with their start and end apart: 24, of which 24 were waited for; matrix products, arithmetic and copies ran while one was open for 8% of the time, Pallas kernels for 0%

profile of v8, /device:TPU:32, one launch (start us, length us, event | category | flops | bytes accessed | tf_op | source)
XLA Modules:
  0.0 510.5 jit_solution(10807979238344157801)
XLA Ops:
  8.0 1.6 pad_maximum_fusion.5
  10.9 2.9 convert_reduce_fusion.4
  19.2 2.4 pad_maximum_fusion.3
  21.6 11.4 %all-to-all-start = ((bf16[32,4,2,2048]{3,2,1,0:T(2,128)(2,1)}), bf16[32,4,2,2048]{3,2,1,0:T(2,128)(2,1)S(1)}, u32[]{:S(2)}, u32[]{:S(2)}) async-start(bf16[32,4,2,2048]{3,2,1,0:T(2,128)(2,1)} %pad_maximum_fusion.3), calls=%async_computation | async-start | bytes 2097152 | tf_op jit(solution)/shard_map/all_to_all | solution.py:181
  37.7 26.9 %all-to-all-done = bf16[32,4,2,2048]{3,2,1,0:T(2,128)(2,1)S(1)} async-done(((bf16[32,4,2,2048]{3,2,1,0:T(2,128)(2,1)}), bf16[32,4,2,2048]{3,2,1,0:T(2,128)(2,1)S(1)}, u32[]{:S(2)}, u32[]{:S(2)}) %all-to-all-start) | async-done | bytes 1048608 | tf_op jit(solution)/shard_map/all_to_all | solution.py:181
  66.9 31.5 %all-gather.6.cloned.1.call-done = bf16[1,1024,2048]{1,2,0:T(8,128)(2,1)} async-done(((bf16[1,1024,64]{1,2,0:T(8,128)(2,1)}), bf16[1,1024,2048]{1,2,0:T(8,128)(2,1)}) %all-gather.6.cloned.1.call-update) | async-done | bytes 4194320 | tf_op jit(solution)/shard_map/all_gather | solution.py:165
  98.4 6.5 %copy.55 = bf16[1024,2048]{1,0:T(8,128)(2,1)} copy(bf16[1024,2048]{0,1:T(8,128)(2,1)} %bitcast.214) | data formatting | bytes 8388608
  104.9 81.9 %all-gather.4.cloned.1.call-done = bf16[2048,1536]{1,0:T(8,128)(2,1)} async-done(((bf16[64,1536]{1,0:T(8,128)(2,1)}), bf16[2048,1536]{1,0:T(8,128)(2,1)}) %all-gather.4.cloned.1.call-update) | async-done | bytes 6291472 | tf_op jit(solution)/shard_map/all_gather | solution.py:162
  186.8 107.0 %while.42 = (s32[]{:T(128)}, bf16[128,2048]{1,0:T(8,128)(2,1)S(1)}, bf16[128,2048]{1,0:T(8,128)(2,1)S(1)}, bf16[128,2048]{1,0:T(8,128)(2,1)S(1)}, s32[]{:T(128)}...) while((s32[]{:T(128)}, bf16[128,2048]{1,0:T(8,128)(2,1)S(1)}, ...), condition=%wide.region_14.15_spmd.clone.clone.clone, body=%wide.region_8.14_spmd.clone.clone.clone.sunk | while | flops 1451809152 | bytes 27381680 | solution.py:220
  187.6 9.8 %conditional.17 = (bf16[128,2048]{1,0:T(8,128)(2,1)S(1)}) conditional(s32[]{:T(128)} %convert_element_type.348, () %tuple.183, (bf16[128,2048]{1,0:T(8,128)(2,1)S(1)}, f32[1,2048]{1,0:T(1,128)S(1)}, f32[1,2048]{1,0:T(1,128)S(1)}, bf16[2048,1536]{1,0:T(8,128)(2,1)}, s32[128]{0:T(128)}, /*index=5*/f32[128,1,32]{0,2,1:T(8,128)S(1)}, ...), branch_computations={%region_9.9_spmd, %region_10.13_spmd} | conditional | flops 1450756480 | bytes 20941832 | solution.py:215
  187.9 3.8 fusion.18
  194.5 2.9 fusion.13
  197.4 1.3 collective-permute-start
  201.2 12.0 %collective-permute-start = (bf16[128,2048]{1,0:T(8,128)(2,1)S(1)}, bf16[128,2048]{1,0:T(8,128)(2,1)S(1)}, u32[]{:S(2)}, u32[]{:S(2)}) collective-permute-start(bf16[128,2048]{1,0:T(8,128)(2,1)S(1)} %get-tuple-element.1353), channel_id=1, source_target_pairs={{0,32},{32,64},{64,96},{96,128},{128,160},{160,192},{192,224},{1,3... | collective-permute-start | bytes 1572872 | tf_op jit(solution)/shard_map/while/body/eval_jaxpr/ppermute | solution.py:217
  215.6 6.5 %collective-permute-start = (bf16[128,2048]{1,0:T(8,128)(2,1)S(1)}, bf16[128,2048]{1,0:T(8,128)(2,1)S(1)}, u32[]{:S(2)}, u32[]{:S(2)}) collective-permute-start(bf16[128,2048]{1,0:T(8,128)(2,1)S(1)} %get-tuple-element.1353), channel_id=1, source_target_pairs={{0,32},{32,64},{64,96},{96,128},{128,160},{160,192},{192,224},{1,3... | collective-permute-start | bytes 1572872 | tf_op jit(solution)/shard_map/while/body/eval_jaxpr/ppermute | solution.py:217
  224.6 18.7 %collective-permute-start = (bf16[128,2048]{1,0:T(8,128)(2,1)S(1)}, bf16[128,2048]{1,0:T(8,128)(2,1)S(1)}, u32[]{:S(2)}, u32[]{:S(2)}) collective-permute-start(bf16[128,2048]{1,0:T(8,128)(2,1)S(1)} %get-tuple-element.1353), channel_id=1, source_target_pairs={{0,32},{32,64},{64,96},{96,128},{128,160},{160,192},{192,224},{1,3... | collective-permute-start | bytes 1572872 | tf_op jit(solution)/shard_map/while/body/eval_jaxpr/ppermute | solution.py:217
  245.8 9.0 %collective-permute-start = (bf16[128,2048]{1,0:T(8,128)(2,1)S(1)}, bf16[128,2048]{1,0:T(8,128)(2,1)S(1)}, u32[]{:S(2)}, u32[]{:S(2)}) collective-permute-start(bf16[128,2048]{1,0:T(8,128)(2,1)S(1)} %get-tuple-element.1353), channel_id=1, source_target_pairs={{0,32},{32,64},{64,96},{96,128},{128,160},{160,192},{192,224},{1,3... | collective-permute-start | bytes 1572872 | tf_op jit(solution)/shard_map/while/body/eval_jaxpr/ppermute | solution.py:217
  257.2 9.0 %collective-permute-start = (bf16[128,2048]{1,0:T(8,128)(2,1)S(1)}, bf16[128,2048]{1,0:T(8,128)(2,1)S(1)}, u32[]{:S(2)}, u32[]{:S(2)}) collective-permute-start(bf16[128,2048]{1,0:T(8,128)(2,1)S(1)} %get-tuple-element.1353), channel_id=1, source_target_pairs={{0,32},{32,64},{64,96},{96,128},{128,160},{160,192},{192,224},{1,3... | collective-permute-start | bytes 1572872 | tf_op jit(solution)/shard_map/while/body/eval_jaxpr/ppermute | solution.py:217
  268.6 9.0 %collective-permute-start = (bf16[128,2048]{1,0:T(8,128)(2,1)S(1)}, bf16[128,2048]{1,0:T(8,128)(2,1)S(1)}, u32[]{:S(2)}, u32[]{:S(2)}) collective-permute-start(bf16[128,2048]{1,0:T(8,128)(2,1)S(1)} %get-tuple-element.1353), channel_id=1, source_target_pairs={{0,32},{32,64},{64,96},{96,128},{128,160},{160,192},{192,224},{1,3... | collective-permute-start | bytes 1572872 | tf_op jit(solution)/shard_map/while/body/eval_jaxpr/ppermute | solution.py:217
  280.1 12.2 %collective-permute-start = (bf16[128,2048]{1,0:T(8,128)(2,1)S(1)}, bf16[128,2048]{1,0:T(8,128)(2,1)S(1)}, u32[]{:S(2)}, u32[]{:S(2)}) collective-permute-start(bf16[128,2048]{1,0:T(8,128)(2,1)S(1)} %get-tuple-element.1353), channel_id=1, source_target_pairs={{0,32},{32,64},{64,96},{96,128},{128,160},{160,192},{192,224},{1,3... | collective-permute-start | bytes 1572872 | tf_op jit(solution)/shard_map/while/body/eval_jaxpr/ppermute | solution.py:217
  295.3 183.1 %while.43 = (s32[]{:T(128)}, bf16[128,2048]{1,0:T(8,128)(2,1)S(1)}, f32[2048]{0:T(1024)S(1)}, f32[128,1536]{1,0:T(8,128)}, s32[]{:T(128)}, /*index=5*/bf16[1024,...) while((s32[]{:T(128)}, bf16[128,2048]{1,0:T(8,128)(2,1)S(1)}, ...), condition=%wide.region_32.33_spmd.clone.clone.clone, body=%wide.region_18.32_spmd.clone.clone.clone.sunk | while | flops 2336233984 | bytes 65241192 | solution.py:245
  296.2 1.3 collective-permute-start.1
  298.5 8.1 %collective-permute-done.1 = bf16[128,2048]{1,0:T(8,128)(2,1)S(1)} collective-permute-done((bf16[128,2048]{1,0:T(8,128)(2,1)S(1)}, bf16[128,2048]{1,0:T(8,128)(2,1)S(1)}, u32[]{:S(2)}, u32[]{:S(2)}) %collective-permute-start.1) | collective-permute-done | bytes 524320 | tf_op jit(solution)/shard_map/while/body/eval_jaxpr/ppermute | solution.py:239
  307.4 1.3 collective-permute-start.1
  309.7 9.0 %collective-permute-done.1 = bf16[128,2048]{1,0:T(8,128)(2,1)S(1)} collective-permute-done((bf16[128,2048]{1,0:T(8,128)(2,1)S(1)}, bf16[128,2048]{1,0:T(8,128)(2,1)S(1)}, u32[]{:S(2)}, u32[]{:S(2)}) %collective-permute-start.1) | collective-permute-done | bytes 524320 | tf_op jit(solution)/shard_map/while/body/eval_jaxpr/ppermute | solution.py:239
  319.5 1.3 collective-permute-start.1
  321.8 8.2 %collective-permute-done.1 = bf16[128,2048]{1,0:T(8,128)(2,1)S(1)} collective-permute-done((bf16[128,2048]{1,0:T(8,128)(2,1)S(1)}, bf16[128,2048]{1,0:T(8,128)(2,1)S(1)}, u32[]{:S(2)}, u32[]{:S(2)}) %collective-permute-start.1) | collective-permute-done | bytes 524320 | tf_op jit(solution)/shard_map/while/body/eval_jaxpr/ppermute | solution.py:239
  333.2 12.1 %collective-permute-done.1 = bf16[128,2048]{1,0:T(8,128)(2,1)S(1)} collective-permute-done((bf16[128,2048]{1,0:T(8,128)(2,1)S(1)}, bf16[128,2048]{1,0:T(8,128)(2,1)S(1)}, u32[]{:S(2)}, u32[]{:S(2)}) %collective-permute-start.1) | collective-permute-done | bytes 524320 | tf_op jit(solution)/shard_map/while/body/eval_jaxpr/ppermute | solution.py:239
  346.1 1.3 collective-permute-start.1
  348.4 8.2 %collective-permute-done.1 = bf16[128,2048]{1,0:T(8,128)(2,1)S(1)} collective-permute-done((bf16[128,2048]{1,0:T(8,128)(2,1)S(1)}, bf16[128,2048]{1,0:T(8,128)(2,1)S(1)}, u32[]{:S(2)}, u32[]{:S(2)}) %collective-permute-start.1) | collective-permute-done | bytes 524320 | tf_op jit(solution)/shard_map/while/body/eval_jaxpr/ppermute | solution.py:239
  359.8 8.8 %collective-permute-done.1 = bf16[128,2048]{1,0:T(8,128)(2,1)S(1)} collective-permute-done((bf16[128,2048]{1,0:T(8,128)(2,1)S(1)}, bf16[128,2048]{1,0:T(8,128)(2,1)S(1)}, u32[]{:S(2)}, u32[]{:S(2)}) %collective-permute-start.1) | collective-permute-done | bytes 524320 | tf_op jit(solution)/shard_map/while/body/eval_jaxpr/ppermute | solution.py:239
  369.5 1.3 collective-permute-start.1
  370.8 5.0 conditional.19
  371.1 4.7 fusion.69
  375.8 85.3 %collective-permute-done.1 = bf16[128,2048]{1,0:T(8,128)(2,1)S(1)} collective-permute-done((bf16[128,2048]{1,0:T(8,128)(2,1)S(1)}, bf16[128,2048]{1,0:T(8,128)(2,1)S(1)}, u32[]{:S(2)}, u32[]{:S(2)}) %collective-permute-start.1) | collective-permute-done | bytes 524320 | tf_op jit(solution)/shard_map/while/body/eval_jaxpr/ppermute | solution.py:239
  461.8 12.8 %conditional.18 = (bf16[128,2048]{1,0:T(8,128)(2,1)S(1)}, f32[2048]{0:T(1024)S(1)}) conditional(s32[]{:T(128)} %convert_element_type.349, () %tuple.186, (bf16[128,2048]{1,0:T(8,128)(2,1)S(1)}, bf16[1024,2048]{1,0:T(8,128)(2,1)}, s32[128]{0:T(128)}, f32[128,1536]{1,0:T(8,128)}, f32[128,1,32]{0,2,1:T(8,128)S(1)}, ...), branch_computations={%region_19.19_spmd, %region_20.28_spmd} | conditional | flops 1528560128 | bytes 54817856 | solution.py:236
  462.8 3.7 convolution_convert_fusion.4
  466.7 1.4 copy.50
  471.9 2.3 multiply_reduce_fusion.3
  476.9 1.5 collective-permute-done.1
  479.0 3.1 collective-permute-done.2
  482.1 1.8 collective-permute-start.3
  483.8 2.8 collective-permute-done.3
  486.6 2.7 collective-permute-start.4
  489.3 4.9 collective-permute-done.4
  494.4 3.4 collective-permute-done.5
  497.9 1.5 collective-permute-start.6
  499.3 3.7 collective-permute-done.6
  (254 shorter events, 70.0 us)
Async XLA Ops:
  7.2 25.8 %copy-start.5 = (s32[4,32]{1,0:T(4,128)S(1)}, s32[4,32]{1,0:T(4,128)}, u32[]{:S(2)}) copy-start(s32[4,32]{1,0:T(4,128)} %param.23) | copy-start | bytes 1540
  7.2 91.2 %all-gather.6.cloned.1.call-start = ((), (), s32[]{:S(2)}) async-start(), calls=%async_computation.2 | async-start | bytes 4325376 | tf_op jit(solution)/shard_map/all_gather | solution.py:165
  7.9 178.9 %all-gather.4.cloned.1.call-start = ((), (), s32[]{:S(2)}) async-start(), calls=%async_computation.1 | async-start | bytes 6488064 | tf_op jit(solution)/shard_map/all_gather | solution.py:162
  21.6 43.0 %all-to-all-start = ((bf16[32,4,2,2048]{3,2,1,0:T(2,128)(2,1)}), bf16[32,4,2,2048]{3,2,1,0:T(2,128)(2,1)S(1)}, u32[]{:S(2)}, u32[]{:S(2)}) async-start(bf16[32,4,2,2048]{3,2,1,0:T(2,128)(2,1)} %pad_maximum_fusion.3), calls=%async_computation | async-start | bytes 2097152 | tf_op jit(solution)/shard_map/all_to_all | solution.py:181
  65.5 121.3 %copy-start.2 = (f32[1,2048]{1,0:T(1,128)S(1)}, f32[1,2048]{1,0:T(1,128)}, u32[]{:S(2)}) copy-start(f32[1,2048]{1,0:T(1,128)} %param.26) | copy-start | bytes 24580
  65.5 121.3 %copy-start.3 = (f32[1,2048]{1,0:T(1,128)S(1)}, f32[1,2048]{1,0:T(1,128)}, u32[]{:S(2)}) copy-start(f32[1,2048]{1,0:T(1,128)} %param.25) | copy-start | bytes 24580
  197.4 2.8 collective-permute-start
  201.2 13.5 %collective-permute-start = (bf16[128,2048]{1,0:T(8,128)(2,1)S(1)}, bf16[128,2048]{1,0:T(8,128)(2,1)S(1)}, u32[]{:S(2)}, u32[]{:S(2)}) collective-permute-start(bf16[128,2048]{1,0:T(8,128)(2,1)S(1)} %get-tuple-element.1353), channel_id=1, source_target_pairs={{0,32},{32,64},{64,96},{96,128},{128,160},{160,192},{192,224},{1,3... | collective-permute-start | bytes 1572872 | tf_op jit(solution)/shard_map/while/body/eval_jaxpr/ppermute | solution.py:217
  215.6 8.0 %collective-permute-start = (bf16[128,2048]{1,0:T(8,128)(2,1)S(1)}, bf16[128,2048]{1,0:T(8,128)(2,1)S(1)}, u32[]{:S(2)}, u32[]{:S(2)}) collective-permute-start(bf16[128,2048]{1,0:T(8,128)(2,1)S(1)} %get-tuple-element.1353), channel_id=1, source_target_pairs={{0,32},{32,64},{64,96},{96,128},{128,160},{160,192},{192,224},{1,3... | collective-permute-start | bytes 1572872 | tf_op jit(solution)/shard_map/while/body/eval_jaxpr/ppermute | solution.py:217
  224.6 20.2 %collective-permute-start = (bf16[128,2048]{1,0:T(8,128)(2,1)S(1)}, bf16[128,2048]{1,0:T(8,128)(2,1)S(1)}, u32[]{:S(2)}, u32[]{:S(2)}) collective-permute-start(bf16[128,2048]{1,0:T(8,128)(2,1)S(1)} %get-tuple-element.1353), channel_id=1, source_target_pairs={{0,32},{32,64},{64,96},{96,128},{128,160},{160,192},{192,224},{1,3... | collective-permute-start | bytes 1572872 | tf_op jit(solution)/shard_map/while/body/eval_jaxpr/ppermute | solution.py:217
  245.8 10.5 %collective-permute-start = (bf16[128,2048]{1,0:T(8,128)(2,1)S(1)}, bf16[128,2048]{1,0:T(8,128)(2,1)S(1)}, u32[]{:S(2)}, u32[]{:S(2)}) collective-permute-start(bf16[128,2048]{1,0:T(8,128)(2,1)S(1)} %get-tuple-element.1353), channel_id=1, source_target_pairs={{0,32},{32,64},{64,96},{96,128},{128,160},{160,192},{192,224},{1,3... | collective-permute-start | bytes 1572872 | tf_op jit(solution)/shard_map/while/body/eval_jaxpr/ppermute | solution.py:217
  257.2 10.5 %collective-permute-start = (bf16[128,2048]{1,0:T(8,128)(2,1)S(1)}, bf16[128,2048]{1,0:T(8,128)(2,1)S(1)}, u32[]{:S(2)}, u32[]{:S(2)}) collective-permute-start(bf16[128,2048]{1,0:T(8,128)(2,1)S(1)} %get-tuple-element.1353), channel_id=1, source_target_pairs={{0,32},{32,64},{64,96},{96,128},{128,160},{160,192},{192,224},{1,3... | collective-permute-start | bytes 1572872 | tf_op jit(solution)/shard_map/while/body/eval_jaxpr/ppermute | solution.py:217
  268.6 10.5 %collective-permute-start = (bf16[128,2048]{1,0:T(8,128)(2,1)S(1)}, bf16[128,2048]{1,0:T(8,128)(2,1)S(1)}, u32[]{:S(2)}, u32[]{:S(2)}) collective-permute-start(bf16[128,2048]{1,0:T(8,128)(2,1)S(1)} %get-tuple-element.1353), channel_id=1, source_target_pairs={{0,32},{32,64},{64,96},{96,128},{128,160},{160,192},{192,224},{1,3... | collective-permute-start | bytes 1572872 | tf_op jit(solution)/shard_map/while/body/eval_jaxpr/ppermute | solution.py:217
  280.1 13.7 %collective-permute-start = (bf16[128,2048]{1,0:T(8,128)(2,1)S(1)}, bf16[128,2048]{1,0:T(8,128)(2,1)S(1)}, u32[]{:S(2)}, u32[]{:S(2)}) collective-permute-start(bf16[128,2048]{1,0:T(8,128)(2,1)S(1)} %get-tuple-element.1353), channel_id=1, source_target_pairs={{0,32},{32,64},{64,96},{96,128},{128,160},{160,192},{192,224},{1,3... | collective-permute-start | bytes 1572872 | tf_op jit(solution)/shard_map/while/body/eval_jaxpr/ppermute | solution.py:217
  293.9 1.4 copy-start.1
  293.9 1.4 copy-start
  293.9 1.4 copy-start.4
  296.2 10.4 %collective-permute-start.1 = (bf16[128,2048]{1,0:T(8,128)(2,1)S(1)}, bf16[128,2048]{1,0:T(8,128)(2,1)S(1)}, u32[]{:S(2)}, u32[]{:S(2)}) collective-permute-start(bf16[128,2048]{1,0:T(8,128)(2,1)S(1)} %get-tuple-element.1250), channel_id=1, source_target_pairs={{32,0},{64,32},{96,64},{128,96},{160,128},{192,160},{224,192},{33,... | collective-permute-start | bytes 1572872 | tf_op jit(solution)/shard_map/while/body/eval_jaxpr/ppermute | solution.py:239
  307.4 11.2 %collective-permute-start.1 = (bf16[128,2048]{1,0:T(8,128)(2,1)S(1)}, bf16[128,2048]{1,0:T(8,128)(2,1)S(1)}, u32[]{:S(2)}, u32[]{:S(2)}) collective-permute-start(bf16[128,2048]{1,0:T(8,128)(2,1)S(1)} %get-tuple-element.1250), channel_id=1, source_target_pairs={{32,0},{64,32},{96,64},{128,96},{160,128},{192,160},{224,192},{33,... | collective-permute-start | bytes 1572872 | tf_op jit(solution)/shard_map/while/body/eval_jaxpr/ppermute | solution.py:239
  319.5 10.5 %collective-permute-start.1 = (bf16[128,2048]{1,0:T(8,128)(2,1)S(1)}, bf16[128,2048]{1,0:T(8,128)(2,1)S(1)}, u32[]{:S(2)}, u32[]{:S(2)}) collective-permute-start(bf16[128,2048]{1,0:T(8,128)(2,1)S(1)} %get-tuple-element.1250), channel_id=1, source_target_pairs={{32,0},{64,32},{96,64},{128,96},{160,128},{192,160},{224,192},{33,... | collective-permute-start | bytes 1572872 | tf_op jit(solution)/shard_map/while/body/eval_jaxpr/ppermute | solution.py:239
  330.9 14.4 %collective-permute-start.1 = (bf16[128,2048]{1,0:T(8,128)(2,1)S(1)}, bf16[128,2048]{1,0:T(8,128)(2,1)S(1)}, u32[]{:S(2)}, u32[]{:S(2)}) collective-permute-start(bf16[128,2048]{1,0:T(8,128)(2,1)S(1)} %get-tuple-element.1250), channel_id=1, source_target_pairs={{32,0},{64,32},{96,64},{128,96},{160,128},{192,160},{224,192},{33,... | collective-permute-start | bytes 1572872 | tf_op jit(solution)/shard_map/while/body/eval_jaxpr/ppermute | solution.py:239
  346.1 10.5 %collective-permute-start.1 = (bf16[128,2048]{1,0:T(8,128)(2,1)S(1)}, bf16[128,2048]{1,0:T(8,128)(2,1)S(1)}, u32[]{:S(2)}, u32[]{:S(2)}) collective-permute-start(bf16[128,2048]{1,0:T(8,128)(2,1)S(1)} %get-tuple-element.1250), channel_id=1, source_target_pairs={{32,0},{64,32},{96,64},{128,96},{160,128},{192,160},{224,192},{33,... | collective-permute-start | bytes 1572872 | tf_op jit(solution)/shard_map/while/body/eval_jaxpr/ppermute | solution.py:239
  357.5 11.1 %collective-permute-start.1 = (bf16[128,2048]{1,0:T(8,128)(2,1)S(1)}, bf16[128,2048]{1,0:T(8,128)(2,1)S(1)}, u32[]{:S(2)}, u32[]{:S(2)}) collective-permute-start(bf16[128,2048]{1,0:T(8,128)(2,1)S(1)} %get-tuple-element.1250), channel_id=1, source_target_pairs={{32,0},{64,32},{96,64},{128,96},{160,128},{192,160},{224,192},{33,... | collective-permute-start | bytes 1572872 | tf_op jit(solution)/shard_map/while/body/eval_jaxpr/ppermute | solution.py:239
  369.5 91.6 %collective-permute-start.1 = (bf16[128,2048]{1,0:T(8,128)(2,1)S(1)}, bf16[128,2048]{1,0:T(8,128)(2,1)S(1)}, u32[]{:S(2)}, u32[]{:S(2)}) collective-permute-start(bf16[128,2048]{1,0:T(8,128)(2,1)S(1)} %get-tuple-element.1250), channel_id=1, source_target_pairs={{32,0},{64,32},{96,64},{128,96},{160,128},{192,160},{224,192},{33,... | collective-permute-start | bytes 1572872 | tf_op jit(solution)/shard_map/while/body/eval_jaxpr/ppermute | solution.py:239
  468.8 2.7 slice-start
  469.7 2.2 slice-start.1
  474.6 3.8 collective-permute-start.1
  478.4 3.7 collective-permute-start.2
  482.1 4.5 collective-permute-start.3
  486.6 7.6 %collective-permute-start.4 = (f32[2048]{0:T(1024)S(1)}, f32[2048]{0:T(1024)S(1)}, u32[]{:S(2)}, u32[]{:S(2)}) collective-permute-start(f32[2048]{0:T(1024)S(1)} %add.376), channel_id=1, source_target_pairs={{0,4},{1,5},{2,6},{3,7},{4,0},{5,1},{6,2},{7,3},{8,12},{9,13},{10,... | collective-permute-start | bytes 24584 | tf_op jit(solution)/shard_map/ppermute | solution.py:119
  494.2 3.7 collective-permute-start.5
  497.9 5.2 %collective-permute-start.6 = (f32[2048]{0:T(1024)S(1)}, f32[2048]{0:T(1024)S(1)}, u32[]{:S(2)}, u32[]{:S(2)}) collective-permute-start(f32[2048]{0:T(1024)S(1)} %add.378), channel_id=1, source_target_pairs={{0,16},{1,17},{2,18},{3,19},{4,20},{5,21},{6,22},{7,23},{8,24},{9,... | collective-permute-start | bytes 24584 | tf_op jit(solution)/shard_map/ppermute | solution.py:119
Sparse Core Ops, SparseCore 0:
  10.6 87.7 all-gather.5
  101.5 85.2 all-gather.3

commit v9 on v8

--- a/solution.py
+++ b/solution.py
@@ -162,7 +162,12 @@
     full_qkv = lax.all_gather(
         jnp.concatenate([w_query[0], w_keyval[0]], axis=1), "dp", axis=0, tiled=True
     )
-    full_out = lax.all_gather(w_out[0], "dp", axis=1, tiled=True)
+    out_block = w_out[0]
+    spread = jnp.broadcast_to(out_block[None], (dp_count,) + out_block.shape)
+    arrived_out = lax.all_to_all(spread, "dp", split_axis=0, concat_axis=0, tiled=True)
+    full_out = lax.optimization_barrier(
+        arrived_out.transpose(1, 0, 2).reshape(out_block.shape[0], dp_count * out_block.shape[1])
+    )
     gain_row = gain[0]
     steering = steer[0]
     plans = [

time: 512 us -> 554 us (1.082)
  blocking collectives: 0 us -> 44.4 us
  other arithmetic: 30.9 us -> 48.4 us
  starting transfers between devices: 106 us -> 90.2 us
  waiting for transfers between devices: 309 us -> 295 us
  local copies, waits for them, and re-layouts: 22.5 us -> 30.8 us
    all_to_all x1, waiting for transfers between devices: 26.9 us -> 119 us  [body(): lax.all_to_all(spread, 'dp', split_axis=0, concat_axis=0, tiled=True)]
    all_gather x1, waiting for transfers between devices: 81.9 us -> 0.01 us  [body(): lax.all_gather(jnp.concatenate([w_query[0], w_keyval[0]], axis=1), 'dp',...]
    all_to_all x0 -> x1, blocking collectives: none -> 44.4 us  [body(): lax.all_to_all(packed, 'dp', split_axis=0, concat_axis=0, tiled=True)]
    all_gather x1 -> x0, waiting for transfers between devices: 31.5 us -> none  [body(): full_out = lax.all_gather(w_out[0], 'dp', axis=1, tiled=True)]
    select_n x8, other arithmetic: 2.87 us -> 16.3 us  [forward_step(): produced = jnp.where(active, hidden_new, produced)]
    ppermute x8, waiting for transfers between devices: 141 us -> 151 us  [backward_step(): sent = lax.ppermute(grad_in, 'section', backward_route)]
    ppermute x8, waiting for transfers between devices: 8.92 us -> 0.37 us  [forward_step(): sent = lax.ppermute(hidden_new, 'section', forward_route)]
    ppermute x8, starting transfers between devices: 77.9 us -> 71.8 us  [forward_step(): sent = lax.ppermute(hidden_new, 'section', forward_route)]
  transfers between devices with their start and end apart: 24 -> 23, of which waited for: 24 -> 15; matrix products, arithmetic and copies ran while one was open for 8% -> 10% of each run, Pallas kernels for 0% -> 0%
where the time goes in v9:
time: 554 us; the launch traced here: 552 us
  waiting for transfers between devices  295 us (53%)
  starting transfers between devices  90.2 us (16%)
  other arithmetic  48.4 us (9%)
  blocking collectives  44.4 us (8%)
  local copies, waits for them, and re-layouts  30.8 us (6%)
  matrix products  27.8 us (5%)
  between operations  14.4 us (3%)
    ppermute x8, waiting for transfers between devices, backward_step(): sent = lax.ppermute(grad_in, 'section', backward_route)  151 us
    all_to_all x1, waiting for transfers between devices, body(): lax.all_to_all(spread, 'dp', split_axis=0, concat_axis=0, tiled=True)  119 us
    ppermute x8, starting transfers between devices, forward_step(): sent = lax.ppermute(hidden_new, 'section', forward_route)  71.8 us
    all_to_all x1, blocking collectives, body(): lax.all_to_all(packed, 'dp', split_axis=0, concat_axis=0, tiled=True)  44.4 us
    ppermute x5, waiting for transfers between devices, butterfly_sum(): values = values + lax.ppermute(values, axis, route)  23.9 us
    mul x16, other arithmetic, rope_tables(): angles = positions.astype(jnp.float32)[..., None] * inverse  16.8 us
    select_n x8, other arithmetic, forward_step(): produced = jnp.where(active, hidden_new, produced)  16.3 us
    ppermute x8, starting transfers between devices, backward_step(): sent = lax.ppermute(grad_in, 'section', backward_route)  11.3 us
  transfers between devices with their start and end apart: 23, of which 15 were waited for; matrix products, arithmetic and copies ran while one was open for 10% of the time, Pallas kernels for 0%

profile of v9, /device:TPU:32, one launch (start us, length us, event | category | flops | bytes accessed | tf_op | source)
XLA Modules:
  0.0 552.2 jit_solution(663739358381064766)
XLA Ops:
  7.2 1.7 pad_maximum_fusion.5
  10.2 2.9 convert_reduce_fusion.4
  18.5 1.6 pad_maximum_fusion.3
  20.1 44.4 %all_to_all.10 = bf16[32,4,2,2048]{3,2,1,0:T(2,128)(2,1)S(1)} all-to-all(bf16[32,4,2,2048]{3,2,1,0:T(2,128)(2,1)S(1)} %pad_maximum_fusion.3), channel_id=1, replica_groups=mesh['section'=8,'dp'=32] {'dp'}, dimensions={0} | all-to-all | bytes 2097152 | tf_op jit(solution)/shard_map/all_to_all | solution.py:186
  64.4 2.6 broadcast_in_dim.89
  67.0 6.2 %all-to-all-start.1 = ((bf16[32,1024,64]{1,2,0:T(8,128)(2,1)}), bf16[32,1024,64]{1,2,0:T(8,128)(2,1)}, u32[]{:S(2)}, u32[]{:S(2)}) async-start(bf16[32,1024,64]{1,2,0:T(8,128)(2,1)} %broadcast_in_dim.89), calls=%async_computation.1 | async-start | bytes 8388608 | tf_op jit(solution)/shard_map/all_to_all | solution.py:167
  80.3 119.0 %all-to-all-done.1 = bf16[32,1024,64]{1,2,0:T(8,128)(2,1)} async-done(((bf16[32,1024,64]{1,2,0:T(8,128)(2,1)}), bf16[32,1024,64]{1,2,0:T(8,128)(2,1)}, u32[]{:S(2)}, u32[]{:S(2)}) %all-to-all-start.1) | async-done | bytes 4194336 | tf_op jit(solution)/shard_map/all_to_all | solution.py:167
  199.3 6.5 %copy.56 = bf16[1024,2048]{1,0:T(8,128)(2,1)} copy(bf16[1024,2048]{0,1:T(8,128)(2,1)} %bitcast.77) | data formatting | bytes 8388608
  205.8 109.8 %while.42 = (s32[]{:T(128)}, bf16[128,2048]{1,0:T(8,128)(2,1)S(1)}, bf16[128,2048]{1,0:T(8,128)(2,1)S(1)}, bf16[128,2048]{1,0:T(8,128)(2,1)}, s32[]{:T(128)}, /*...) while((s32[]{:T(128)}, bf16[128,2048]{1,0:T(8,128)(2,1)S(1)}, ...), condition=%wide.region_14.15_spmd.clone.clone.clone, body=%wide.region_8.14_spmd.clone.clone.clone.sunk | while | flops 1451809152 | bytes 27449312 | solution.py:225
  207.2 9.1 %conditional.17 = (bf16[128,2048]{1,0:T(8,128)(2,1)S(1)}) conditional(s32[]{:T(128)} %convert_element_type.348, () %tuple.185, (bf16[128,2048]{1,0:T(8,128)(2,1)S(1)}, f32[1,2048]{1,0:T(1,128)S(1)}, f32[1,2048]{1,0:T(1,128)S(1)}, bf16[2048,1536]{1,0:T(8,128)(2,1)}, s32[128]{0:T(128)}, /*index=5*/f32[128,1,32]{0,2,1:T(8,128)}, ...), branch_computations={%region_9.9_spmd, %region_10.13_spmd} | conditional | flops 1450756480 | bytes 21009472 | solution.py:220
  207.5 3.8 fusion.18
  213.5 2.9 fusion.13
  220.7 11.4 %collective-permute-start = (bf16[128,2048]{1,0:T(8,128)(2,1)S(1)}, bf16[128,2048]{1,0:T(8,128)(2,1)S(1)}, u32[]{:S(2)}, u32[]{:S(2)}) collective-permute-start(bf16[128,2048]{1,0:T(8,128)(2,1)S(1)} %get-tuple-element.1378), channel_id=1, source_target_pairs={{0,32},{32,64},{64,96},{96,128},{128,160},{160,192},{192,224},{1,3... | collective-permute-start | bytes 1572872 | tf_op jit(solution)/shard_map/while/body/eval_jaxpr/ppermute | solution.py:222
  232.1 2.2 select_select_fusion.3
  235.8 5.8 %collective-permute-start = (bf16[128,2048]{1,0:T(8,128)(2,1)S(1)}, bf16[128,2048]{1,0:T(8,128)(2,1)S(1)}, u32[]{:S(2)}, u32[]{:S(2)}) collective-permute-start(bf16[128,2048]{1,0:T(8,128)(2,1)S(1)} %get-tuple-element.1378), channel_id=1, source_target_pairs={{0,32},{32,64},{64,96},{96,128},{128,160},{160,192},{192,224},{1,3... | collective-permute-start | bytes 1572872 | tf_op jit(solution)/shard_map/while/body/eval_jaxpr/ppermute | solution.py:222
  241.7 2.2 select_select_fusion.3
  245.4 17.4 %collective-permute-start = (bf16[128,2048]{1,0:T(8,128)(2,1)S(1)}, bf16[128,2048]{1,0:T(8,128)(2,1)S(1)}, u32[]{:S(2)}, u32[]{:S(2)}) collective-permute-start(bf16[128,2048]{1,0:T(8,128)(2,1)S(1)} %get-tuple-element.1378), channel_id=1, source_target_pairs={{0,32},{32,64},{64,96},{96,128},{128,160},{160,192},{192,224},{1,3... | collective-permute-start | bytes 1572872 | tf_op jit(solution)/shard_map/while/body/eval_jaxpr/ppermute | solution.py:222
  262.8 2.2 select_select_fusion.3
  266.4 8.3 %collective-permute-start = (bf16[128,2048]{1,0:T(8,128)(2,1)S(1)}, bf16[128,2048]{1,0:T(8,128)(2,1)S(1)}, u32[]{:S(2)}, u32[]{:S(2)}) collective-permute-start(bf16[128,2048]{1,0:T(8,128)(2,1)S(1)} %get-tuple-element.1378), channel_id=1, source_target_pairs={{0,32},{32,64},{64,96},{96,128},{128,160},{160,192},{192,224},{1,3... | collective-permute-start | bytes 1572872 | tf_op jit(solution)/shard_map/while/body/eval_jaxpr/ppermute | solution.py:222
  274.8 2.2 select_select_fusion.3
  278.5 8.3 %collective-permute-start = (bf16[128,2048]{1,0:T(8,128)(2,1)S(1)}, bf16[128,2048]{1,0:T(8,128)(2,1)S(1)}, u32[]{:S(2)}, u32[]{:S(2)}) collective-permute-start(bf16[128,2048]{1,0:T(8,128)(2,1)S(1)} %get-tuple-element.1378), channel_id=1, source_target_pairs={{0,32},{32,64},{64,96},{96,128},{128,160},{160,192},{192,224},{1,3... | collective-permute-start | bytes 1572872 | tf_op jit(solution)/shard_map/while/body/eval_jaxpr/ppermute | solution.py:222
  286.8 2.2 select_select_fusion.3
  290.5 8.3 %collective-permute-start = (bf16[128,2048]{1,0:T(8,128)(2,1)S(1)}, bf16[128,2048]{1,0:T(8,128)(2,1)S(1)}, u32[]{:S(2)}, u32[]{:S(2)}) collective-permute-start(bf16[128,2048]{1,0:T(8,128)(2,1)S(1)} %get-tuple-element.1378), channel_id=1, source_target_pairs={{0,32},{32,64},{64,96},{96,128},{128,160},{160,192},{192,224},{1,3... | collective-permute-start | bytes 1572872 | tf_op jit(solution)/shard_map/while/body/eval_jaxpr/ppermute | solution.py:222
  298.8 2.2 select_select_fusion.3
  302.5 10.9 %collective-permute-start = (bf16[128,2048]{1,0:T(8,128)(2,1)S(1)}, bf16[128,2048]{1,0:T(8,128)(2,1)S(1)}, u32[]{:S(2)}, u32[]{:S(2)}) collective-permute-start(bf16[128,2048]{1,0:T(8,128)(2,1)S(1)} %get-tuple-element.1378), channel_id=1, source_target_pairs={{0,32},{32,64},{64,96},{96,128},{128,160},{160,192},{192,224},{1,3... | collective-permute-start | bytes 1572872 | tf_op jit(solution)/shard_map/while/body/eval_jaxpr/ppermute | solution.py:222
  313.4 2.2 select_select_fusion.3
  316.7 202.5 %while.43 = (s32[]{:T(128)}, bf16[128,2048]{1,0:T(8,128)(2,1)S(1)}, f32[2048]{0:T(1024)}, f32[128,1536]{1,0:T(8,128)}, s32[]{:T(128)}, /*index=5*/bf16[1024,2048...) while((s32[]{:T(128)}, bf16[128,2048]{1,0:T(8,128)(2,1)S(1)}, ...), condition=%wide.region_32.33_spmd.clone.clone.clone, body=%wide.region_18.32_spmd.clone.clone.clone.sunk | while | flops 2336233984 | bytes 66357492 | solution.py:250
  318.4 1.4 collective-permute-start.1
  320.8 7.6 %collective-permute-done.1 = bf16[128,2048]{1,0:T(8,128)(2,1)S(1)} collective-permute-done((bf16[128,2048]{1,0:T(8,128)(2,1)}, bf16[128,2048]{1,0:T(8,128)(2,1)S(1)}, u32[]{:S(2)}, u32[]{:S(2)}) %collective-permute-start.1) | collective-permute-done | bytes 524320 | tf_op jit(solution)/shard_map/while/body/eval_jaxpr/ppermute | solution.py:244
  330.1 1.4 collective-permute-start.1
  332.5 9.2 %collective-permute-done.1 = bf16[128,2048]{1,0:T(8,128)(2,1)S(1)} collective-permute-done((bf16[128,2048]{1,0:T(8,128)(2,1)}, bf16[128,2048]{1,0:T(8,128)(2,1)S(1)}, u32[]{:S(2)}, u32[]{:S(2)}) %collective-permute-start.1) | collective-permute-done | bytes 524320 | tf_op jit(solution)/shard_map/while/body/eval_jaxpr/ppermute | solution.py:244
  345.7 8.4 %collective-permute-done.1 = bf16[128,2048]{1,0:T(8,128)(2,1)S(1)} collective-permute-done((bf16[128,2048]{1,0:T(8,128)(2,1)}, bf16[128,2048]{1,0:T(8,128)(2,1)S(1)}, u32[]{:S(2)}, u32[]{:S(2)}) %collective-permute-start.1) | collective-permute-done | bytes 524320 | tf_op jit(solution)/shard_map/while/body/eval_jaxpr/ppermute | solution.py:244
  358.2 11.0 %collective-permute-done.1 = bf16[128,2048]{1,0:T(8,128)(2,1)S(1)} collective-permute-done((bf16[128,2048]{1,0:T(8,128)(2,1)}, bf16[128,2048]{1,0:T(8,128)(2,1)S(1)}, u32[]{:S(2)}, u32[]{:S(2)}) %collective-permute-start.1) | collective-permute-done | bytes 524320 | tf_op jit(solution)/shard_map/while/body/eval_jaxpr/ppermute | solution.py:244
  373.3 8.4 %collective-permute-done.1 = bf16[128,2048]{1,0:T(8,128)(2,1)S(1)} collective-permute-done((bf16[128,2048]{1,0:T(8,128)(2,1)}, bf16[128,2048]{1,0:T(8,128)(2,1)S(1)}, u32[]{:S(2)}, u32[]{:S(2)}) %collective-permute-start.1) | collective-permute-done | bytes 524320 | tf_op jit(solution)/shard_map/while/body/eval_jaxpr/ppermute | solution.py:244
  385.7 8.4 %collective-permute-done.1 = bf16[128,2048]{1,0:T(8,128)(2,1)S(1)} collective-permute-done((bf16[128,2048]{1,0:T(8,128)(2,1)}, bf16[128,2048]{1,0:T(8,128)(2,1)S(1)}, u32[]{:S(2)}, u32[]{:S(2)}) %collective-permute-start.1) | collective-permute-done | bytes 524320 | tf_op jit(solution)/shard_map/while/body/eval_jaxpr/ppermute | solution.py:244
  397.2 5.0 conditional.19
  397.5 4.7 fusion.69
  402.2 96.8 %collective-permute-done.1 = bf16[128,2048]{1,0:T(8,128)(2,1)S(1)} collective-permute-done((bf16[128,2048]{1,0:T(8,128)(2,1)}, bf16[128,2048]{1,0:T(8,128)(2,1)S(1)}, u32[]{:S(2)}, u32[]{:S(2)}) %collective-permute-start.1) | collective-permute-done | bytes 524320 | tf_op jit(solution)/shard_map/while/body/eval_jaxpr/ppermute | solution.py:244
  499.8 15.3 %conditional.18 = (bf16[128,2048]{1,0:T(8,128)(2,1)}, f32[2048]{0:T(1024)S(1)}) conditional(s32[]{:T(128)} %convert_element_type.349, () %tuple.188, (bf16[128,2048]{1,0:T(8,128)(2,1)S(1)}, bf16[1024,2048]{1,0:T(8,128)(2,1)}, s32[128]{0:T(128)S(1)}, f32[128,1536]{1,0:T(8,128)}, f32[128,1,32]{0,2,1:T(8,128)S(1)}, ...), branch_computations={%region_19.19_spmd, %region_20.28_spmd} | conditional | flops 1528560128 | bytes 55866488 | solution.py:241
  502.2 3.7 convolution_convert_fusion.4
  506.8 1.5 fusion.43
  511.6 2.3 multiply_reduce_fusion.3
  517.5 1.7 collective-permute-done.1
  519.2 3.9 collective-permute-done.2
  523.8 4.5 collective-permute-done.3
  528.3 7.6 %collective-permute-done.4 = f32[2048]{0:T(1024)S(1)} collective-permute-done((f32[2048]{0:T(1024)S(1)}, f32[2048]{0:T(1024)S(1)}, u32[]{:S(2)}, u32[]{:S(2)}) %collective-permute-start.4) | collective-permute-done | bytes 8224 | tf_op jit(solution)/shard_map/ppermute | solution.py:119
  535.9 3.6 collective-permute-done.5
  540.4 4.3 collective-permute-done.6
  (309 shorter events, 83.1 us)
Async XLA Ops:
  7.2 57.3 %copy-start.11 = (bf16[1,1024,64]{1,2,0:T(8,128)(2,1)S(1)}, bf16[1,1024,64]{1,2,0:T(8,128)(2,1)}, u32[]{:S(2)}) copy-start(bf16[1,1024,64]{1,2,0:T(8,128)(2,1)} %param.29) | copy-start | bytes 393220
  7.2 198.7 %all-gather.2.cloned.1.call-start = ((), (), s32[]{:S(2)}) async-start(), calls=%async_computation.2 | async-start | bytes 6488064 | tf_op jit(solution)/shard_map/all_gather | solution.py:162
  64.4 8.8 %copy-start.12 = (s32[4,32]{1,0:T(4,128)S(1)}, s32[4,32]{1,0:T(4,128)}, u32[]{:S(2)}) copy-start(s32[4,32]{1,0:T(4,128)} %param.23) | copy-start | bytes 1540
  67.0 132.3 %all-to-all-start.1 = ((bf16[32,1024,64]{1,2,0:T(8,128)(2,1)}), bf16[32,1024,64]{1,2,0:T(8,128)(2,1)}, u32[]{:S(2)}, u32[]{:S(2)}) async-start(bf16[32,1024,64]{1,2,0:T(8,128)(2,1)} %broadcast_in_dim.89), calls=%async_computation.1 | async-start | bytes 8388608 | tf_op jit(solution)/shard_map/all_to_all | solution.py:167
  78.9 126.9 %copy-start.1 = (f32[1,2048]{1,0:T(1,128)S(1)}, f32[1,2048]{1,0:T(1,128)}, u32[]{:S(2)}) copy-start(f32[1,2048]{1,0:T(1,128)} %param.26) | copy-start | bytes 24580
  79.0 126.9 %copy-start.5 = (f32[1,2048]{1,0:T(1,128)S(1)}, f32[1,2048]{1,0:T(1,128)}, u32[]{:S(2)}) copy-start(f32[1,2048]{1,0:T(1,128)} %param.25) | copy-start | bytes 24580
  207.3 4.3 copy-start.2
  207.3 4.7 copy-start.8
  216.4 2.8 collective-permute-start
  220.7 13.6 %collective-permute-start = (bf16[128,2048]{1,0:T(8,128)(2,1)S(1)}, bf16[128,2048]{1,0:T(8,128)(2,1)S(1)}, u32[]{:S(2)}, u32[]{:S(2)}) collective-permute-start(bf16[128,2048]{1,0:T(8,128)(2,1)S(1)} %get-tuple-element.1378), channel_id=1, source_target_pairs={{0,32},{32,64},{64,96},{96,128},{128,160},{160,192},{192,224},{1,3... | collective-permute-start | bytes 1572872 | tf_op jit(solution)/shard_map/while/body/eval_jaxpr/ppermute | solution.py:222
  235.8 8.0 %collective-permute-start = (bf16[128,2048]{1,0:T(8,128)(2,1)S(1)}, bf16[128,2048]{1,0:T(8,128)(2,1)S(1)}, u32[]{:S(2)}, u32[]{:S(2)}) collective-permute-start(bf16[128,2048]{1,0:T(8,128)(2,1)S(1)} %get-tuple-element.1378), channel_id=1, source_target_pairs={{0,32},{32,64},{64,96},{96,128},{128,160},{160,192},{192,224},{1,3... | collective-permute-start | bytes 1572872 | tf_op jit(solution)/shard_map/while/body/eval_jaxpr/ppermute | solution.py:222
  245.4 19.6 %collective-permute-start = (bf16[128,2048]{1,0:T(8,128)(2,1)S(1)}, bf16[128,2048]{1,0:T(8,128)(2,1)S(1)}, u32[]{:S(2)}, u32[]{:S(2)}) collective-permute-start(bf16[128,2048]{1,0:T(8,128)(2,1)S(1)} %get-tuple-element.1378), channel_id=1, source_target_pairs={{0,32},{32,64},{64,96},{96,128},{128,160},{160,192},{192,224},{1,3... | collective-permute-start | bytes 1572872 | tf_op jit(solution)/shard_map/while/body/eval_jaxpr/ppermute | solution.py:222
  266.4 10.5 %collective-permute-start = (bf16[128,2048]{1,0:T(8,128)(2,1)S(1)}, bf16[128,2048]{1,0:T(8,128)(2,1)S(1)}, u32[]{:S(2)}, u32[]{:S(2)}) collective-permute-start(bf16[128,2048]{1,0:T(8,128)(2,1)S(1)} %get-tuple-element.1378), channel_id=1, source_target_pairs={{0,32},{32,64},{64,96},{96,128},{128,160},{160,192},{192,224},{1,3... | collective-permute-start | bytes 1572872 | tf_op jit(solution)/shard_map/while/body/eval_jaxpr/ppermute | solution.py:222
  278.5 10.5 %collective-permute-start = (bf16[128,2048]{1,0:T(8,128)(2,1)S(1)}, bf16[128,2048]{1,0:T(8,128)(2,1)S(1)}, u32[]{:S(2)}, u32[]{:S(2)}) collective-permute-start(bf16[128,2048]{1,0:T(8,128)(2,1)S(1)} %get-tuple-element.1378), channel_id=1, source_target_pairs={{0,32},{32,64},{64,96},{96,128},{128,160},{160,192},{192,224},{1,3... | collective-permute-start | bytes 1572872 | tf_op jit(solution)/shard_map/while/body/eval_jaxpr/ppermute | solution.py:222
  290.5 10.5 %collective-permute-start = (bf16[128,2048]{1,0:T(8,128)(2,1)S(1)}, bf16[128,2048]{1,0:T(8,128)(2,1)S(1)}, u32[]{:S(2)}, u32[]{:S(2)}) collective-permute-start(bf16[128,2048]{1,0:T(8,128)(2,1)S(1)} %get-tuple-element.1378), channel_id=1, source_target_pairs={{0,32},{32,64},{64,96},{96,128},{128,160},{160,192},{192,224},{1,3... | collective-permute-start | bytes 1572872 | tf_op jit(solution)/shard_map/while/body/eval_jaxpr/ppermute | solution.py:222
  302.5 13.1 %collective-permute-start = (bf16[128,2048]{1,0:T(8,128)(2,1)S(1)}, bf16[128,2048]{1,0:T(8,128)(2,1)S(1)}, u32[]{:S(2)}, u32[]{:S(2)}) collective-permute-start(bf16[128,2048]{1,0:T(8,128)(2,1)S(1)} %get-tuple-element.1378), channel_id=1, source_target_pairs={{0,32},{32,64},{64,96},{96,128},{128,160},{160,192},{192,224},{1,3... | collective-permute-start | bytes 1572872 | tf_op jit(solution)/shard_map/while/body/eval_jaxpr/ppermute | solution.py:222
  318.4 2.4 copy-start.6
  318.4 10.0 %copy-start.10 = (s32[128]{0:T(128)S(1)}, s32[128]{0:T(128)}, u32[]{:S(2)}) copy-start(s32[128]{0:T(128)} %get-tuple-element.1413) | copy-start | bytes 1540 | tf_op jit(solution)/shard_map/while
  318.4 10.0 %collective-permute-start.1 = (bf16[128,2048]{1,0:T(8,128)(2,1)}, bf16[128,2048]{1,0:T(8,128)(2,1)S(1)}, u32[]{:S(2)}, u32[]{:S(2)}) collective-permute-start(bf16[128,2048]{1,0:T(8,128)(2,1)} %get-tuple-element.1275), channel_id=1, source_target_pairs={{32,0},{64,32},{96,64},{128,96},{160,128},{192,160},{224,192},{33,... | collective-permute-start | bytes 1572872 | tf_op jit(solution)/shard_map/while/body/eval_jaxpr/ppermute | solution.py:244
  320.8 7.6 %copy-start.7 = (f32[2048]{0:T(1024)}, f32[2048]{0:T(1024)S(1)}, u32[]{:S(2)}) copy-start(f32[2048]{0:T(1024)S(1)} %select_add_fusion.2) | copy-start | bytes 24580 | tf_op jit(solution)/shard_map/while
  330.1 11.6 %copy-start.10 = (s32[128]{0:T(128)S(1)}, s32[128]{0:T(128)}, u32[]{:S(2)}) copy-start(s32[128]{0:T(128)} %get-tuple-element.1413) | copy-start | bytes 1540 | tf_op jit(solution)/shard_map/while
  330.1 11.6 %collective-permute-start.1 = (bf16[128,2048]{1,0:T(8,128)(2,1)}, bf16[128,2048]{1,0:T(8,128)(2,1)S(1)}, u32[]{:S(2)}, u32[]{:S(2)}) collective-permute-start(bf16[128,2048]{1,0:T(8,128)(2,1)} %get-tuple-element.1275), channel_id=1, source_target_pairs={{32,0},{64,32},{96,64},{128,96},{160,128},{192,160},{224,192},{33,... | collective-permute-start | bytes 1572872 | tf_op jit(solution)/shard_map/while/body/eval_jaxpr/ppermute | solution.py:244
  332.5 9.2 %copy-start.7 = (f32[2048]{0:T(1024)}, f32[2048]{0:T(1024)S(1)}, u32[]{:S(2)}) copy-start(f32[2048]{0:T(1024)S(1)} %select_add_fusion.2) | copy-start | bytes 24580 | tf_op jit(solution)/shard_map/while
  343.3 10.8 %copy-start.10 = (s32[128]{0:T(128)S(1)}, s32[128]{0:T(128)}, u32[]{:S(2)}) copy-start(s32[128]{0:T(128)} %get-tuple-element.1413) | copy-start | bytes 1540 | tf_op jit(solution)/shard_map/while
  343.3 10.8 %collective-permute-start.1 = (bf16[128,2048]{1,0:T(8,128)(2,1)}, bf16[128,2048]{1,0:T(8,128)(2,1)S(1)}, u32[]{:S(2)}, u32[]{:S(2)}) collective-permute-start(bf16[128,2048]{1,0:T(8,128)(2,1)} %get-tuple-element.1275), channel_id=1, source_target_pairs={{32,0},{64,32},{96,64},{128,96},{160,128},{192,160},{224,192},{33,... | collective-permute-start | bytes 1572872 | tf_op jit(solution)/shard_map/while/body/eval_jaxpr/ppermute | solution.py:244
  345.7 8.4 %copy-start.7 = (f32[2048]{0:T(1024)}, f32[2048]{0:T(1024)S(1)}, u32[]{:S(2)}) copy-start(f32[2048]{0:T(1024)S(1)} %select_add_fusion.2) | copy-start | bytes 24580 | tf_op jit(solution)/shard_map/while
  355.8 13.4 %copy-start.10 = (s32[128]{0:T(128)S(1)}, s32[128]{0:T(128)}, u32[]{:S(2)}) copy-start(s32[128]{0:T(128)} %get-tuple-element.1413) | copy-start | bytes 1540 | tf_op jit(solution)/shard_map/while
  355.8 13.4 %collective-permute-start.1 = (bf16[128,2048]{1,0:T(8,128)(2,1)}, bf16[128,2048]{1,0:T(8,128)(2,1)S(1)}, u32[]{:S(2)}, u32[]{:S(2)}) collective-permute-start(bf16[128,2048]{1,0:T(8,128)(2,1)} %get-tuple-element.1275), channel_id=1, source_target_pairs={{32,0},{64,32},{96,64},{128,96},{160,128},{192,160},{224,192},{33,... | collective-permute-start | bytes 1572872 | tf_op jit(solution)/shard_map/while/body/eval_jaxpr/ppermute | solution.py:244
  358.2 11.0 %copy-start.7 = (f32[2048]{0:T(1024)}, f32[2048]{0:T(1024)S(1)}, u32[]{:S(2)}) copy-start(f32[2048]{0:T(1024)S(1)} %select_add_fusion.2) | copy-start | bytes 24580 | tf_op jit(solution)/shard_map/while
  370.8 10.8 %copy-start.10 = (s32[128]{0:T(128)S(1)}, s32[128]{0:T(128)}, u32[]{:S(2)}) copy-start(s32[128]{0:T(128)} %get-tuple-element.1413) | copy-start | bytes 1540 | tf_op jit(solution)/shard_map/while
  370.8 10.8 %collective-permute-start.1 = (bf16[128,2048]{1,0:T(8,128)(2,1)}, bf16[128,2048]{1,0:T(8,128)(2,1)S(1)}, u32[]{:S(2)}, u32[]{:S(2)}) collective-permute-start(bf16[128,2048]{1,0:T(8,128)(2,1)} %get-tuple-element.1275), channel_id=1, source_target_pairs={{32,0},{64,32},{96,64},{128,96},{160,128},{192,160},{224,192},{33,... | collective-permute-start | bytes 1572872 | tf_op jit(solution)/shard_map/while/body/eval_jaxpr/ppermute | solution.py:244
  373.3 8.4 %copy-start.7 = (f32[2048]{0:T(1024)}, f32[2048]{0:T(1024)S(1)}, u32[]{:S(2)}) copy-start(f32[2048]{0:T(1024)S(1)} %select_add_fusion.2) | copy-start | bytes 24580 | tf_op jit(solution)/shard_map/while
  383.3 10.8 %copy-start.10 = (s32[128]{0:T(128)S(1)}, s32[128]{0:T(128)}, u32[]{:S(2)}) copy-start(s32[128]{0:T(128)} %get-tuple-element.1413) | copy-start | bytes 1540 | tf_op jit(solution)/shard_map/while
  383.3 10.8 %collective-permute-start.1 = (bf16[128,2048]{1,0:T(8,128)(2,1)}, bf16[128,2048]{1,0:T(8,128)(2,1)S(1)}, u32[]{:S(2)}, u32[]{:S(2)}) collective-permute-start(bf16[128,2048]{1,0:T(8,128)(2,1)} %get-tuple-element.1275), channel_id=1, source_target_pairs={{32,0},{64,32},{96,64},{128,96},{160,128},{192,160},{224,192},{33,... | collective-permute-start | bytes 1572872 | tf_op jit(solution)/shard_map/while/body/eval_jaxpr/ppermute | solution.py:244
  385.7 8.4 %copy-start.7 = (f32[2048]{0:T(1024)}, f32[2048]{0:T(1024)S(1)}, u32[]{:S(2)}) copy-start(f32[2048]{0:T(1024)S(1)} %select_add_fusion.2) | copy-start | bytes 24580 | tf_op jit(solution)/shard_map/while
  395.8 6.4 %copy-start.6 = (f32[2048]{0:T(1024)S(1)}, f32[2048]{0:T(1024)}, u32[]{:S(2)}) copy-start(f32[2048]{0:T(1024)} %get-tuple-element.1343) | copy-start | bytes 24580 | tf_op jit(solution)/shard_map/while
  395.8 103.2 %copy-start.10 = (s32[128]{0:T(128)S(1)}, s32[128]{0:T(128)}, u32[]{:S(2)}) copy-start(s32[128]{0:T(128)} %get-tuple-element.1413) | copy-start | bytes 1540 | tf_op jit(solution)/shard_map/while
  395.8 103.2 %collective-permute-start.1 = (bf16[128,2048]{1,0:T(8,128)(2,1)}, bf16[128,2048]{1,0:T(8,128)(2,1)S(1)}, u32[]{:S(2)}, u32[]{:S(2)}) collective-permute-start(bf16[128,2048]{1,0:T(8,128)(2,1)} %get-tuple-element.1275), channel_id=1, source_target_pairs={{32,0},{64,32},{96,64},{128,96},{160,128},{192,160},{224,192},{33,... | collective-permute-start | bytes 1572872 | tf_op jit(solution)/shard_map/while/body/eval_jaxpr/ppermute | solution.py:244
  402.2 96.8 %copy-start.7 = (f32[2048]{0:T(1024)}, f32[2048]{0:T(1024)S(1)}, u32[]{:S(2)}) copy-start(f32[2048]{0:T(1024)S(1)} %select_add_fusion.2) | copy-start | bytes 24580 | tf_op jit(solution)/shard_map/while
  506.0 4.9 copy-start.4
  506.8 4.8 slice-start
  515.1 4.1 copy-start.10
  515.1 4.1 collective-permute-start.1
  519.2 3.9 collective-permute-start.2
  523.8 4.5 collective-permute-start.3
  528.3 7.6 %collective-permute-start.4 = (f32[2048]{0:T(1024)S(1)}, f32[2048]{0:T(1024)S(1)}, u32[]{:S(2)}, u32[]{:S(2)}) collective-permute-start(f32[2048]{0:T(1024)S(1)} %add.376), channel_id=1, source_target_pairs={{0,4},{1,5},{2,6},{3,7},{4,0},{5,1},{6,2},{7,3},{8,12},{9,13},{10,... | collective-permute-start | bytes 24584 | tf_op jit(solution)/shard_map/ppermute | solution.py:119
  535.9 3.7 collective-permute-start.5
  539.6 5.2 collective-permute-start.6
  (11 other events, 21.0 us)
Sparse Core Ops, SparseCore 0:
  10.6 166.2 all-gather.1

commit v10 on v8

--- a/solution.py
+++ b/solution.py
@@ -209,17 +209,17 @@
     backward_route = [(i + 1, i) for i in range(section_count - 1)]
 
     def forward_step(carry, unused):
-        hidden_in, kept, produced, step = carry
+        hidden_in, step = carry
         active = section_idx == step
-        kept = jnp.where(active, hidden_in, kept)
         hidden_new = lax.cond(active, lambda: run_layer(hidden_in, steering)[0], lambda: zero_block)
-        produced = jnp.where(active, hidden_new, produced)
         sent = lax.ppermute(hidden_new, "section", forward_route)
-        return ((sent, kept, produced, step + 1), None)
-
-    (unused_in, kept, produced, unused_step), unused_ys = lax.scan(
-        forward_step, (grouped, zero_block, zero_block, jnp.int32(0)), None, length=section_count
-    )
+        return ((sent, step + 1), (hidden_in, hidden_new))
+
+    unused_carry, (inputs_seen, outputs_made) = lax.scan(
+        forward_step, (grouped, jnp.int32(0)), None, length=section_count
+    )
+    kept = lax.dynamic_index_in_dim(inputs_seen, section_idx, 0, keepdims=False)
+    produced = lax.dynamic_index_in_dim(outputs_made, section_idx, 0, keepdims=False)
     first_saved = lax.cond(
         section_idx == section_count - 1, lambda: precompute(kept), lambda: zero_proj
     )

time: 512 us -> 529 us (1.033)
  local copies, waits for them, and re-layouts: 22.5 us -> 46.9 us
  waiting for transfers between devices: 309 us -> 301 us
    broadcast_in_dim x14, local copies, waits for them, and re-layouts: 0.64 us -> 11.9 us  [body(): zero_block = jnp.zeros((flat_count, width), jnp.bfloat16)]
    dynamic_update_slice x0 -> x8, local copies, waits for them, and re-layouts: none -> 8.52 us  [body(): lax.scan(forward_step, (grouped, jnp.int32(0)), None, length=section_count)]
  transfers between devices with their start and end apart: 24 -> 24, of which waited for: 24 -> 24; matrix products, arithmetic and copies ran while one was open for 8% -> 9% of each run, Pallas kernels for 0% -> 0%
where the time goes in v10:
time: 529 us; the launch traced here: 526 us
  waiting for transfers between devices  301 us (57%)
  starting transfers between devices  110 us (21%)
  local copies, waits for them, and re-layouts  46.9 us (9%)
  other arithmetic  29.4 us (6%)
  matrix products  22.5 us (4%)
  between operations  14.4 us (3%)
    ppermute x8, waiting for transfers between devices, backward_step(): sent = lax.ppermute(grad_in, 'section', backward_route)  137 us
    ppermute x8, starting transfers between devices, forward_step(): sent = lax.ppermute(hidden_new, 'section', forward_route)  82.1 us
    all_gather x1, waiting for transfers between devices, body(): lax.all_gather(jnp.concatenate([w_query[0], w_keyval[0]], axis=1), 'dp',...  81.9 us
    all_gather x1, waiting for transfers between devices, body(): full_out = lax.all_gather(w_out[0], 'dp', axis=1, tiled=True)  34.4 us
    all_to_all x1, waiting for transfers between devices, body(): lax.all_to_all(packed, 'dp', split_axis=0, concat_axis=0, tiled=True)  26.5 us
    ppermute x5, waiting for transfers between devices, butterfly_sum(): values = values + lax.ppermute(values, axis, route)  16.3 us
    broadcast_in_dim x14, local copies, waits for them, and re-layouts, body(): zero_block = jnp.zeros((flat_count, width), jnp.bfloat16)  11.9 us
    mul x16, other arithmetic, rope_tables(): angles = positions.astype(jnp.float32)[..., None] * inverse  11.8 us
  transfers between devices with their start and end apart: 24, of which 24 were waited for; matrix products, arithmetic and copies ran while one was open for 9% of the time, Pallas kernels for 0%

profile of v10, /device:TPU:32, one launch (start us, length us, event | category | flops | bytes accessed | tf_op | source)
XLA Modules:
  0.0 526.5 jit_solution(1744524365210009121)
XLA Ops:
  8.0 1.6 pad_maximum_fusion.5
  10.9 2.9 convert_reduce_fusion.4
  17.4 2.4 pad_maximum_fusion.3
  19.8 11.4 %all-to-all-start = ((bf16[32,4,2,2048]{3,2,1,0:T(2,128)(2,1)}), bf16[32,4,2,2048]{3,2,1,0:T(2,128)(2,1)S(1)}, u32[]{:S(2)}, u32[]{:S(2)}) async-start(bf16[32,4,2,2048]{3,2,1,0:T(2,128)(2,1)} %pad_maximum_fusion.3), calls=%async_computation | async-start | bytes 2097152 | tf_op jit(solution)/shard_map/all_to_all | solution.py:181
  35.9 26.5 %all-to-all-done = bf16[32,4,2,2048]{3,2,1,0:T(2,128)(2,1)S(1)} async-done(((bf16[32,4,2,2048]{3,2,1,0:T(2,128)(2,1)}), bf16[32,4,2,2048]{3,2,1,0:T(2,128)(2,1)S(1)}, u32[]{:S(2)}, u32[]{:S(2)}) %all-to-all-start) | async-done | bytes 1048608 | tf_op jit(solution)/shard_map/all_to_all | solution.py:181
  64.6 34.4 %all-gather.6.cloned.1.call-done = bf16[1,1024,2048]{1,2,0:T(8,128)(2,1)} async-done(((bf16[1,1024,64]{1,2,0:T(8,128)(2,1)}), bf16[1,1024,2048]{1,2,0:T(8,128)(2,1)}) %all-gather.6.cloned.1.call-update) | async-done | bytes 4194320 | tf_op jit(solution)/shard_map/all_gather | solution.py:165
  99.0 6.6 %copy.55 = bf16[1024,2048]{1,0:T(8,128)(2,1)} copy(bf16[1024,2048]{0,1:T(8,128)(2,1)} %bitcast.220) | data formatting | bytes 8388608
  105.6 81.9 %all-gather.4.cloned.1.call-done = bf16[2048,1536]{1,0:T(8,128)(2,1)} async-done(((bf16[64,1536]{1,0:T(8,128)(2,1)}), bf16[2048,1536]{1,0:T(8,128)(2,1)}) %all-gather.4.cloned.1.call-update) | async-done | bytes 6291472 | tf_op jit(solution)/shard_map/all_gather | solution.py:162
  187.4 120.5 %while.41 = (s32[]{:T(128)}, bf16[128,2048]{1,0:T(8,128)(2,1)S(1)}, bf16[8,128,2048]{2,1,0:T(8,128)(2,1)}, bf16[8,128,2048]{2,1,0:T(8,128)(2,1)}, s32[]{:T(128)}...) while((s32[]{:T(128)}, bf16[128,2048]{1,0:T(8,128)(2,1)S(1)}, ...), condition=%wide.region_14.15_spmd.clone.clone, body=%wide.region_8.14_spmd.clone.clone.sunk | while | flops 1450760576 | bytes 27381672 | solution.py:218
  188.2 11.7 %conditional.16 = (bf16[128,2048]{1,0:T(8,128)(2,1)}, bf16[1,128,2048]{2,1,0:T(8,128)(2,1)S(1)}) conditional(s32[]{:T(128)} %convert_element_type.347, () %tuple.181, (bf16[128,2048]{1,0:T(8,128)(2,1)S(1)}, f32[1,2048]{1,0:T(1,128)S(1)}, f32[1,2048]{1,0:T(1,128)S(1)}, bf16[2048,1536]{1,0:T(8,128)(2,1)}, s32[128]{0:T(128)}, ...), branch_computations={%region_9.9_spmd, %region_10.13_spmd} | conditional | flops 1450756480 | bytes 21990416 | solution.py:214
  188.5 3.8 fusion.18
  195.1 3.7 fusion.13
  199.9 1.3 collective-permute-start
  204.6 13.0 %collective-permute-start = (bf16[128,2048]{1,0:T(8,128)(2,1)}, bf16[128,2048]{1,0:T(8,128)(2,1)S(1)}, u32[]{:S(2)}, u32[]{:S(2)}) collective-permute-start(bf16[128,2048]{1,0:T(8,128)(2,1)} %get-tuple-element.1192), channel_id=1, source_target_pairs={{0,32},{32,64},{64,96},{96,128},{128,160},{160,192},{192,224},{1,3... | collective-permute-start | bytes 1572872 | tf_op jit(solution)/shard_map/while/body/eval_jaxpr/ppermute | solution.py:215
  221.1 6.6 %collective-permute-start = (bf16[128,2048]{1,0:T(8,128)(2,1)}, bf16[128,2048]{1,0:T(8,128)(2,1)S(1)}, u32[]{:S(2)}, u32[]{:S(2)}) collective-permute-start(bf16[128,2048]{1,0:T(8,128)(2,1)} %get-tuple-element.1192), channel_id=1, source_target_pairs={{0,32},{32,64},{64,96},{96,128},{128,160},{160,192},{192,224},{1,3... | collective-permute-start | bytes 1572872 | tf_op jit(solution)/shard_map/while/body/eval_jaxpr/ppermute | solution.py:215
  231.2 19.7 %collective-permute-start = (bf16[128,2048]{1,0:T(8,128)(2,1)}, bf16[128,2048]{1,0:T(8,128)(2,1)S(1)}, u32[]{:S(2)}, u32[]{:S(2)}) collective-permute-start(bf16[128,2048]{1,0:T(8,128)(2,1)} %get-tuple-element.1192), channel_id=1, source_target_pairs={{0,32},{32,64},{64,96},{96,128},{128,160},{160,192},{192,224},{1,3... | collective-permute-start | bytes 1572872 | tf_op jit(solution)/shard_map/while/body/eval_jaxpr/ppermute | solution.py:215
  254.4 9.0 %collective-permute-start = (bf16[128,2048]{1,0:T(8,128)(2,1)}, bf16[128,2048]{1,0:T(8,128)(2,1)S(1)}, u32[]{:S(2)}, u32[]{:S(2)}) collective-permute-start(bf16[128,2048]{1,0:T(8,128)(2,1)} %get-tuple-element.1192), channel_id=1, source_target_pairs={{0,32},{32,64},{64,96},{96,128},{128,160},{160,192},{192,224},{1,3... | collective-permute-start | bytes 1572872 | tf_op jit(solution)/shard_map/while/body/eval_jaxpr/ppermute | solution.py:215
  266.9 9.0 %collective-permute-start = (bf16[128,2048]{1,0:T(8,128)(2,1)}, bf16[128,2048]{1,0:T(8,128)(2,1)S(1)}, u32[]{:S(2)}, u32[]{:S(2)}) collective-permute-start(bf16[128,2048]{1,0:T(8,128)(2,1)} %get-tuple-element.1192), channel_id=1, source_target_pairs={{0,32},{32,64},{64,96},{96,128},{128,160},{160,192},{192,224},{1,3... | collective-permute-start | bytes 1572872 | tf_op jit(solution)/shard_map/while/body/eval_jaxpr/ppermute | solution.py:215
  279.4 9.0 %collective-permute-start = (bf16[128,2048]{1,0:T(8,128)(2,1)}, bf16[128,2048]{1,0:T(8,128)(2,1)S(1)}, u32[]{:S(2)}, u32[]{:S(2)}) collective-permute-start(bf16[128,2048]{1,0:T(8,128)(2,1)} %get-tuple-element.1192), channel_id=1, source_target_pairs={{0,32},{32,64},{64,96},{96,128},{128,160},{160,192},{192,224},{1,3... | collective-permute-start | bytes 1572872 | tf_op jit(solution)/shard_map/while/body/eval_jaxpr/ppermute | solution.py:215
  291.8 14.3 %collective-permute-start = (bf16[128,2048]{1,0:T(8,128)(2,1)}, bf16[128,2048]{1,0:T(8,128)(2,1)S(1)}, u32[]{:S(2)}, u32[]{:S(2)}) collective-permute-start(bf16[128,2048]{1,0:T(8,128)(2,1)} %get-tuple-element.1192), channel_id=1, source_target_pairs={{0,32},{32,64},{64,96},{96,128},{128,160},{160,192},{192,224},{1,3... | collective-permute-start | bytes 1572872 | tf_op jit(solution)/shard_map/while/body/eval_jaxpr/ppermute | solution.py:215
  310.1 183.4 %while.42 = (s32[]{:T(128)}, bf16[128,2048]{1,0:T(8,128)(2,1)S(1)}, f32[2048]{0:T(1024)}, f32[128,1536]{1,0:T(8,128)}, s32[]{:T(128)}, /*index=5*/bf16[1024,2048...) while((s32[]{:T(128)}, bf16[128,2048]{1,0:T(8,128)(2,1)S(1)}, ...), condition=%wide.region_32.33_spmd.clone.clone.clone, body=%wide.region_18.32_spmd.clone.clone.clone.sunk | while | flops 2336233984 | bytes 84705680 | solution.py:245
  311.8 1.3 collective-permute-start.1
  314.1 8.3 %collective-permute-done.1 = bf16[128,2048]{1,0:T(8,128)(2,1)S(1)} collective-permute-done((bf16[128,2048]{1,0:T(8,128)(2,1)}, bf16[128,2048]{1,0:T(8,128)(2,1)S(1)}, u32[]{:S(2)}, u32[]{:S(2)}) %collective-permute-start.1) | collective-permute-done | bytes 524320 | tf_op jit(solution)/shard_map/while/body/eval_jaxpr/ppermute | solution.py:239
  324.0 1.3 collective-permute-start.1
  326.3 9.0 %collective-permute-done.1 = bf16[128,2048]{1,0:T(8,128)(2,1)S(1)} collective-permute-done((bf16[128,2048]{1,0:T(8,128)(2,1)}, bf16[128,2048]{1,0:T(8,128)(2,1)S(1)}, u32[]{:S(2)}, u32[]{:S(2)}) %collective-permute-start.1) | collective-permute-done | bytes 524320 | tf_op jit(solution)/shard_map/while/body/eval_jaxpr/ppermute | solution.py:239
  336.9 1.3 collective-permute-start.1
  339.2 8.4 %collective-permute-done.1 = bf16[128,2048]{1,0:T(8,128)(2,1)S(1)} collective-permute-done((bf16[128,2048]{1,0:T(8,128)(2,1)}, bf16[128,2048]{1,0:T(8,128)(2,1)S(1)}, u32[]{:S(2)}, u32[]{:S(2)}) %collective-permute-start.1) | collective-permute-done | bytes 524320 | tf_op jit(solution)/shard_map/while/body/eval_jaxpr/ppermute | solution.py:239
  349.3 1.3 collective-permute-start.1
  351.6 14.2 %collective-permute-done.1 = bf16[128,2048]{1,0:T(8,128)(2,1)S(1)} collective-permute-done((bf16[128,2048]{1,0:T(8,128)(2,1)}, bf16[128,2048]{1,0:T(8,128)(2,1)S(1)}, u32[]{:S(2)}, u32[]{:S(2)}) %collective-permute-start.1) | collective-permute-done | bytes 524320 | tf_op jit(solution)/shard_map/while/body/eval_jaxpr/ppermute | solution.py:239
  369.7 8.4 %collective-permute-done.1 = bf16[128,2048]{1,0:T(8,128)(2,1)S(1)} collective-permute-done((bf16[128,2048]{1,0:T(8,128)(2,1)}, bf16[128,2048]{1,0:T(8,128)(2,1)S(1)}, u32[]{:S(2)}, u32[]{:S(2)}) %collective-permute-start.1) | collective-permute-done | bytes 524320 | tf_op jit(solution)/shard_map/while/body/eval_jaxpr/ppermute | solution.py:239
  382.1 8.9 %collective-permute-done.1 = bf16[128,2048]{1,0:T(8,128)(2,1)S(1)} collective-permute-done((bf16[128,2048]{1,0:T(8,128)(2,1)}, bf16[128,2048]{1,0:T(8,128)(2,1)S(1)}, u32[]{:S(2)}, u32[]{:S(2)}) %collective-permute-start.1) | collective-permute-done | bytes 524320 | tf_op jit(solution)/shard_map/while/body/eval_jaxpr/ppermute | solution.py:239
  393.9 5.0 conditional.18
  394.2 4.7 fusion.69
  398.9 77.6 %collective-permute-done.1 = bf16[128,2048]{1,0:T(8,128)(2,1)S(1)} collective-permute-done((bf16[128,2048]{1,0:T(8,128)(2,1)}, bf16[128,2048]{1,0:T(8,128)(2,1)S(1)}, u32[]{:S(2)}, u32[]{:S(2)}) %collective-permute-start.1) | collective-permute-done | bytes 524320 | tf_op jit(solution)/shard_map/while/body/eval_jaxpr/ppermute | solution.py:239
  477.3 12.3 %conditional.17 = (bf16[128,2048]{1,0:T(8,128)(2,1)}, f32[2048]{0:T(1024)S(1)}) conditional(s32[]{:T(128)} %convert_element_type.348, () %tuple.184, (bf16[128,2048]{1,0:T(8,128)(2,1)S(1)}, bf16[1024,2048]{1,0:T(8,128)(2,1)}, s32[128]{0:T(128)}, f32[128,1536]{1,0:T(8,128)}, f32[128,1,32]{0,2,1:T(8,128)S(1)}, ...), branch_computations={%region_19.19_spmd, %region_20.28_spmd} | conditional | flops 1528560128 | bytes 74216768 | solution.py:236
  477.4 1.4 copy.50
  481.1 1.5 convolution_convert_fusion.4
  486.0 2.3 multiply_reduce_fusion.3
  491.8 1.7 collective-permute-done.1
  494.1 3.3 collective-permute-done.2
  498.1 1.7 collective-permute-start.3
  499.8 2.8 collective-permute-done.3
  502.6 2.7 collective-permute-start.4
  505.3 4.9 collective-permute-done.4
  510.4 3.4 collective-permute-done.5
  513.9 1.4 collective-permute-start.6
  515.3 1.9 constant_dynamic-slice_fusion.4
  517.2 1.8 collective-permute-done.6
  (312 shorter events, 97.9 us)
Async XLA Ops:
  7.2 9.4 %copy-start.12 = (bf16[4,32,2048]{2,1,0:T(8,128)(2,1)S(1)}, bf16[4,32,2048]{2,1,0:T(8,128)(2,1)}, u32[]{:S(2)}) copy-start(bf16[4,32,2048]{2,1,0:T(8,128)(2,1)} %param.21) | copy-start | bytes 1572868
  7.2 91.8 %all-gather.6.cloned.1.call-start = ((), (), s32[]{:S(2)}) async-start(), calls=%async_computation.2 | async-start | bytes 4325376 | tf_op jit(solution)/shard_map/all_gather | solution.py:165
  7.9 179.5 %all-gather.4.cloned.1.call-start = ((), (), s32[]{:S(2)}) async-start(), calls=%async_computation.1 | async-start | bytes 6488064 | tf_op jit(solution)/shard_map/all_gather | solution.py:162
  9.6 21.5 %copy-start.15 = (s32[4,32]{1,0:T(4,128)S(1)}, s32[4,32]{1,0:T(4,128)}, u32[]{:S(2)}) copy-start(s32[4,32]{1,0:T(4,128)} %param.23) | copy-start | bytes 1540
  19.8 42.6 %all-to-all-start = ((bf16[32,4,2,2048]{3,2,1,0:T(2,128)(2,1)}), bf16[32,4,2,2048]{3,2,1,0:T(2,128)(2,1)S(1)}, u32[]{:S(2)}, u32[]{:S(2)}) async-start(bf16[32,4,2,2048]{3,2,1,0:T(2,128)(2,1)} %pad_maximum_fusion.3), calls=%async_computation | async-start | bytes 2097152 | tf_op jit(solution)/shard_map/all_to_all | solution.py:181
  99.0 88.4 %copy-start.2 = (f32[1,2048]{1,0:T(1,128)S(1)}, f32[1,2048]{1,0:T(1,128)}, u32[]{:S(2)}) copy-start(f32[1,2048]{1,0:T(1,128)} %param.26) | copy-start | bytes 24580
  99.0 88.4 %copy-start.11 = (f32[1,2048]{1,0:T(1,128)S(1)}, f32[1,2048]{1,0:T(1,128)}, u32[]{:S(2)}) copy-start(f32[1,2048]{1,0:T(1,128)} %param.25) | copy-start | bytes 24580
  199.9 3.0 collective-permute-start
  204.6 14.7 %collective-permute-start = (bf16[128,2048]{1,0:T(8,128)(2,1)}, bf16[128,2048]{1,0:T(8,128)(2,1)S(1)}, u32[]{:S(2)}, u32[]{:S(2)}) collective-permute-start(bf16[128,2048]{1,0:T(8,128)(2,1)} %get-tuple-element.1192), channel_id=1, source_target_pairs={{0,32},{32,64},{64,96},{96,128},{128,160},{160,192},{192,224},{1,3... | collective-permute-start | bytes 1572872 | tf_op jit(solution)/shard_map/while/body/eval_jaxpr/ppermute | solution.py:215
  221.1 8.3 %collective-permute-start = (bf16[128,2048]{1,0:T(8,128)(2,1)}, bf16[128,2048]{1,0:T(8,128)(2,1)S(1)}, u32[]{:S(2)}, u32[]{:S(2)}) collective-permute-start(bf16[128,2048]{1,0:T(8,128)(2,1)} %get-tuple-element.1192), channel_id=1, source_target_pairs={{0,32},{32,64},{64,96},{96,128},{128,160},{160,192},{192,224},{1,3... | collective-permute-start | bytes 1572872 | tf_op jit(solution)/shard_map/while/body/eval_jaxpr/ppermute | solution.py:215
  231.2 21.4 %collective-permute-start = (bf16[128,2048]{1,0:T(8,128)(2,1)}, bf16[128,2048]{1,0:T(8,128)(2,1)S(1)}, u32[]{:S(2)}, u32[]{:S(2)}) collective-permute-start(bf16[128,2048]{1,0:T(8,128)(2,1)} %get-tuple-element.1192), channel_id=1, source_target_pairs={{0,32},{32,64},{64,96},{96,128},{128,160},{160,192},{192,224},{1,3... | collective-permute-start | bytes 1572872 | tf_op jit(solution)/shard_map/while/body/eval_jaxpr/ppermute | solution.py:215
  254.4 10.7 %collective-permute-start = (bf16[128,2048]{1,0:T(8,128)(2,1)}, bf16[128,2048]{1,0:T(8,128)(2,1)S(1)}, u32[]{:S(2)}, u32[]{:S(2)}) collective-permute-start(bf16[128,2048]{1,0:T(8,128)(2,1)} %get-tuple-element.1192), channel_id=1, source_target_pairs={{0,32},{32,64},{64,96},{96,128},{128,160},{160,192},{192,224},{1,3... | collective-permute-start | bytes 1572872 | tf_op jit(solution)/shard_map/while/body/eval_jaxpr/ppermute | solution.py:215
  266.9 10.7 %collective-permute-start = (bf16[128,2048]{1,0:T(8,128)(2,1)}, bf16[128,2048]{1,0:T(8,128)(2,1)S(1)}, u32[]{:S(2)}, u32[]{:S(2)}) collective-permute-start(bf16[128,2048]{1,0:T(8,128)(2,1)} %get-tuple-element.1192), channel_id=1, source_target_pairs={{0,32},{32,64},{64,96},{96,128},{128,160},{160,192},{192,224},{1,3... | collective-permute-start | bytes 1572872 | tf_op jit(solution)/shard_map/while/body/eval_jaxpr/ppermute | solution.py:215
  279.4 10.7 %collective-permute-start = (bf16[128,2048]{1,0:T(8,128)(2,1)}, bf16[128,2048]{1,0:T(8,128)(2,1)S(1)}, u32[]{:S(2)}, u32[]{:S(2)}) collective-permute-start(bf16[128,2048]{1,0:T(8,128)(2,1)} %get-tuple-element.1192), channel_id=1, source_target_pairs={{0,32},{32,64},{64,96},{96,128},{128,160},{160,192},{192,224},{1,3... | collective-permute-start | bytes 1572872 | tf_op jit(solution)/shard_map/while/body/eval_jaxpr/ppermute | solution.py:215
  291.8 16.0 %collective-permute-start = (bf16[128,2048]{1,0:T(8,128)(2,1)}, bf16[128,2048]{1,0:T(8,128)(2,1)S(1)}, u32[]{:S(2)}, u32[]{:S(2)}) collective-permute-start(bf16[128,2048]{1,0:T(8,128)(2,1)} %get-tuple-element.1192), channel_id=1, source_target_pairs={{0,32},{32,64},{64,96},{96,128},{128,160},{160,192},{192,224},{1,3... | collective-permute-start | bytes 1572872 | tf_op jit(solution)/shard_map/while/body/eval_jaxpr/ppermute | solution.py:215
  311.8 10.6 %collective-permute-start.1 = (bf16[128,2048]{1,0:T(8,128)(2,1)}, bf16[128,2048]{1,0:T(8,128)(2,1)S(1)}, u32[]{:S(2)}, u32[]{:S(2)}) collective-permute-start(bf16[128,2048]{1,0:T(8,128)(2,1)} %get-tuple-element.1209), channel_id=1, source_target_pairs={{32,0},{64,32},{96,64},{128,96},{160,128},{192,160},{224,192},{33,... | collective-permute-start | bytes 1572872 | tf_op jit(solution)/shard_map/while/body/eval_jaxpr/ppermute | solution.py:239
  314.0 8.3 %copy-start.14 = (f32[2048]{0:T(1024)}, f32[2048]{0:T(1024)S(1)}, u32[]{:S(2)}) copy-start(f32[2048]{0:T(1024)S(1)} %select_add_fusion.2) | copy-start | bytes 24580 | tf_op jit(solution)/shard_map/while
  324.0 11.3 %collective-permute-start.1 = (bf16[128,2048]{1,0:T(8,128)(2,1)}, bf16[128,2048]{1,0:T(8,128)(2,1)S(1)}, u32[]{:S(2)}, u32[]{:S(2)}) collective-permute-start(bf16[128,2048]{1,0:T(8,128)(2,1)} %get-tuple-element.1209), channel_id=1, source_target_pairs={{32,0},{64,32},{96,64},{128,96},{160,128},{192,160},{224,192},{33,... | collective-permute-start | bytes 1572872 | tf_op jit(solution)/shard_map/while/body/eval_jaxpr/ppermute | solution.py:239
  326.3 9.0 %copy-start.14 = (f32[2048]{0:T(1024)}, f32[2048]{0:T(1024)S(1)}, u32[]{:S(2)}) copy-start(f32[2048]{0:T(1024)S(1)} %select_add_fusion.2) | copy-start | bytes 24580 | tf_op jit(solution)/shard_map/while
  336.9 10.7 %collective-permute-start.1 = (bf16[128,2048]{1,0:T(8,128)(2,1)}, bf16[128,2048]{1,0:T(8,128)(2,1)S(1)}, u32[]{:S(2)}, u32[]{:S(2)}) collective-permute-start(bf16[128,2048]{1,0:T(8,128)(2,1)} %get-tuple-element.1209), channel_id=1, source_target_pairs={{32,0},{64,32},{96,64},{128,96},{160,128},{192,160},{224,192},{33,... | collective-permute-start | bytes 1572872 | tf_op jit(solution)/shard_map/while/body/eval_jaxpr/ppermute | solution.py:239
  339.2 8.4 %copy-start.14 = (f32[2048]{0:T(1024)}, f32[2048]{0:T(1024)S(1)}, u32[]{:S(2)}) copy-start(f32[2048]{0:T(1024)S(1)} %select_add_fusion.2) | copy-start | bytes 24580 | tf_op jit(solution)/shard_map/while
  349.3 16.5 %collective-permute-start.1 = (bf16[128,2048]{1,0:T(8,128)(2,1)}, bf16[128,2048]{1,0:T(8,128)(2,1)S(1)}, u32[]{:S(2)}, u32[]{:S(2)}) collective-permute-start(bf16[128,2048]{1,0:T(8,128)(2,1)} %get-tuple-element.1209), channel_id=1, source_target_pairs={{32,0},{64,32},{96,64},{128,96},{160,128},{192,160},{224,192},{33,... | collective-permute-start | bytes 1572872 | tf_op jit(solution)/shard_map/while/body/eval_jaxpr/ppermute | solution.py:239
  351.6 14.3 %copy-start.14 = (f32[2048]{0:T(1024)}, f32[2048]{0:T(1024)S(1)}, u32[]{:S(2)}) copy-start(f32[2048]{0:T(1024)S(1)} %select_add_fusion.2) | copy-start | bytes 24580 | tf_op jit(solution)/shard_map/while
  367.4 10.7 %collective-permute-start.1 = (bf16[128,2048]{1,0:T(8,128)(2,1)}, bf16[128,2048]{1,0:T(8,128)(2,1)S(1)}, u32[]{:S(2)}, u32[]{:S(2)}) collective-permute-start(bf16[128,2048]{1,0:T(8,128)(2,1)} %get-tuple-element.1209), channel_id=1, source_target_pairs={{32,0},{64,32},{96,64},{128,96},{160,128},{192,160},{224,192},{33,... | collective-permute-start | bytes 1572872 | tf_op jit(solution)/shard_map/while/body/eval_jaxpr/ppermute | solution.py:239
  369.7 8.4 %copy-start.14 = (f32[2048]{0:T(1024)}, f32[2048]{0:T(1024)S(1)}, u32[]{:S(2)}) copy-start(f32[2048]{0:T(1024)S(1)} %select_add_fusion.2) | copy-start | bytes 24580 | tf_op jit(solution)/shard_map/while
  379.8 11.2 %collective-permute-start.1 = (bf16[128,2048]{1,0:T(8,128)(2,1)}, bf16[128,2048]{1,0:T(8,128)(2,1)S(1)}, u32[]{:S(2)}, u32[]{:S(2)}) collective-permute-start(bf16[128,2048]{1,0:T(8,128)(2,1)} %get-tuple-element.1209), channel_id=1, source_target_pairs={{32,0},{64,32},{96,64},{128,96},{160,128},{192,160},{224,192},{33,... | collective-permute-start | bytes 1572872 | tf_op jit(solution)/shard_map/while/body/eval_jaxpr/ppermute | solution.py:239
  382.1 8.9 %copy-start.14 = (f32[2048]{0:T(1024)}, f32[2048]{0:T(1024)S(1)}, u32[]{:S(2)}) copy-start(f32[2048]{0:T(1024)S(1)} %select_add_fusion.2) | copy-start | bytes 24580 | tf_op jit(solution)/shard_map/while
  392.6 83.9 %collective-permute-start.1 = (bf16[128,2048]{1,0:T(8,128)(2,1)}, bf16[128,2048]{1,0:T(8,128)(2,1)S(1)}, u32[]{:S(2)}, u32[]{:S(2)}) collective-permute-start(bf16[128,2048]{1,0:T(8,128)(2,1)} %get-tuple-element.1209), channel_id=1, source_target_pairs={{32,0},{64,32},{96,64},{128,96},{160,128},{192,160},{224,192},{33,... | collective-permute-start | bytes 1572872 | tf_op jit(solution)/shard_map/while/body/eval_jaxpr/ppermute | solution.py:239
  393.9 5.0 copy-start.13
  398.9 77.6 %copy-start.14 = (f32[2048]{0:T(1024)}, f32[2048]{0:T(1024)S(1)}, u32[]{:S(2)}) copy-start(f32[2048]{0:T(1024)S(1)} %select_add_fusion.2) | copy-start | bytes 24580 | tf_op jit(solution)/shard_map/while
  478.8 2.3 copy-start
  478.9 1.6 copy-start.3
  478.9 1.6 copy-start.5
  479.0 1.6 copy-start.7
  479.0 1.6 copy-start.9
  482.8 2.8 slice-start
  483.2 1.7 copy-start.4
  483.2 1.7 copy-start.6
  483.2 2.0 copy-start.8
  483.2 2.0 copy-start.10
  483.8 2.3 slice-start.1
  489.5 4.0 collective-permute-start.1
  491.8 1.7 copy-start.14
  493.5 3.9 collective-permute-start.2
  498.1 4.5 collective-permute-start.3
  502.6 7.6 %collective-permute-start.4 = (f32[2048]{0:T(1024)S(1)}, f32[2048]{0:T(1024)S(1)}, u32[]{:S(2)}, u32[]{:S(2)}) collective-permute-start(f32[2048]{0:T(1024)S(1)} %add.382), channel_id=1, source_target_pairs={{0,4},{1,5},{2,6},{3,7},{4,0},{5,1},{6,2},{7,3},{8,12},{9,13},{10,... | collective-permute-start | bytes 24584 | tf_op jit(solution)/shard_map/ppermute | solution.py:119
  510.2 3.7 collective-permute-start.5
  513.9 5.2 collective-permute-start.6
  (8 other events, 8.1 us)
Sparse Core Ops, SparseCore 0:
  10.6 88.3 all-gather.5
  102.1 85.2 all-gather.3

commit v11 on v8

--- a/solution.py
+++ b/solution.py
@@ -113,11 +113,25 @@
 
 def butterfly_sum(values, axis):
     count = lax.axis_size(axis)
-    distance = 1
-    while distance < count:
-        route = [(i, i ^ distance) for i in range(count)]
-        values = values + lax.ppermute(values, axis, route)
-        distance *= 2
+    index = lax.axis_index(axis)
+    stride = 1
+    while stride < count:
+        fan = 4 if count % (stride * 4) == 0 else 2
+        local = (index // stride) % fan
+        received = [values]
+        for offset in range(1, fan):
+            route = [
+                (i, (i // (stride * fan)) * stride * fan + ((i // stride) % fan ^ offset) * stride + i % stride)
+                for i in range(count)
+            ]
+            received.append(lax.ppermute(values, axis, route))
+        stacked = jnp.stack(received)
+        ordered = [lax.dynamic_index_in_dim(stacked, local ^ m, 0, keepdims=False) for m in range(fan)]
+        if fan == 4:
+            values = (ordered[0] + ordered[1]) + (ordered[2] + ordered[3])
+        else:
+            values = ordered[0] + ordered[1]
+        stride *= fan
     return values
 
 

time: 512 us -> 511 us (level)
  waiting for transfers between devices: 309 us -> 302 us
  starting transfers between devices: 106 us -> 112 us
    ppermute x5 -> x7, waiting for transfers between devices: 17.9 us -> 11.3 us  [butterfly_sum(): received.append(lax.ppermute(values, axis, route))]
    ppermute x5 -> x7, starting transfers between devices: 6.66 us -> 12.5 us  [butterfly_sum(): received.append(lax.ppermute(values, axis, route))]
  transfers between devices with their start and end apart: 24 -> 26, of which waited for: 24 -> 25; matrix products, arithmetic and copies ran while one was open for 8% -> 8% of each run, Pallas kernels for 0% -> 0%
where the time goes in v11:
time: 511 us; the launch traced here: 510 us
  waiting for transfers between devices  302 us (59%)
  starting transfers between devices  112 us (22%)
  other arithmetic  31.1 us (6%)
  matrix products  25.8 us (5%)
  local copies, waits for them, and re-layouts  22.5 us (4%)
  between operations  14.4 us (3%)
    ppermute x8, waiting for transfers between devices, backward_step(): sent = lax.ppermute(grad_in, 'section', backward_route)  141 us
    all_gather x1, waiting for transfers between devices, body(): lax.all_gather(jnp.concatenate([w_query[0], w_keyval[0]], axis=1), 'dp',...  81.9 us
    ppermute x8, starting transfers between devices, forward_step(): sent = lax.ppermute(hidden_new, 'section', forward_route)  77.9 us
    all_gather x1, waiting for transfers between devices, body(): full_out = lax.all_gather(w_out[0], 'dp', axis=1, tiled=True)  31.5 us
    all_to_all x1, waiting for transfers between devices, body(): lax.all_to_all(packed, 'dp', split_axis=0, concat_axis=0, tiled=True)  26.9 us
    ppermute x7, starting transfers between devices, butterfly_sum(): received.append(lax.ppermute(values, axis, route))  12.5 us
    mul x16, other arithmetic, rope_tables(): angles = positions.astype(jnp.float32)[..., None] * inverse  12.1 us
    all_to_all x1, starting transfers between devices, body(): lax.all_to_all(packed, 'dp', split_axis=0, concat_axis=0, tiled=True)  11.4 us
  transfers between devices with their start and end apart: 26, of which 25 were waited for; matrix products, arithmetic and copies ran while one was open for 8% of the time, Pallas kernels for 0%

profile of v11, /device:TPU:32, one launch (start us, length us, event | category | flops | bytes accessed | tf_op | source)
XLA Modules:
  0.0 509.9 jit_solution(17521883404294243884)
XLA Ops:
  8.0 1.6 pad_maximum_fusion.5
  10.9 2.9 convert_reduce_fusion.4
  19.2 2.4 pad_maximum_fusion.3
  21.6 11.4 %all-to-all-start = ((bf16[32,4,2,2048]{3,2,1,0:T(2,128)(2,1)}), bf16[32,4,2,2048]{3,2,1,0:T(2,128)(2,1)S(1)}, u32[]{:S(2)}, u32[]{:S(2)}) async-start(bf16[32,4,2,2048]{3,2,1,0:T(2,128)(2,1)} %pad_maximum_fusion.3), calls=%async_computation | async-start | bytes 2097152 | tf_op jit(solution)/shard_map/all_to_all | solution.py:195
  37.7 26.9 %all-to-all-done = bf16[32,4,2,2048]{3,2,1,0:T(2,128)(2,1)S(1)} async-done(((bf16[32,4,2,2048]{3,2,1,0:T(2,128)(2,1)}), bf16[32,4,2,2048]{3,2,1,0:T(2,128)(2,1)S(1)}, u32[]{:S(2)}, u32[]{:S(2)}) %all-to-all-start) | async-done | bytes 1048608 | tf_op jit(solution)/shard_map/all_to_all | solution.py:195
  66.9 31.5 %all-gather.6.cloned.1.call-done = bf16[1,1024,2048]{1,2,0:T(8,128)(2,1)} async-done(((bf16[1,1024,64]{1,2,0:T(8,128)(2,1)}), bf16[1,1024,2048]{1,2,0:T(8,128)(2,1)}) %all-gather.6.cloned.1.call-update) | async-done | bytes 4194320 | tf_op jit(solution)/shard_map/all_gather | solution.py:179
  98.4 6.5 %copy.55 = bf16[1024,2048]{1,0:T(8,128)(2,1)} copy(bf16[1024,2048]{0,1:T(8,128)(2,1)} %bitcast.223) | data formatting | bytes 8388608
  104.9 81.9 %all-gather.4.cloned.1.call-done = bf16[2048,1536]{1,0:T(8,128)(2,1)} async-done(((bf16[64,1536]{1,0:T(8,128)(2,1)}), bf16[2048,1536]{1,0:T(8,128)(2,1)}) %all-gather.4.cloned.1.call-update) | async-done | bytes 6291472 | tf_op jit(solution)/shard_map/all_gather | solution.py:176
  186.8 107.0 %while.42 = (s32[]{:T(128)}, bf16[128,2048]{1,0:T(8,128)(2,1)S(1)}, bf16[128,2048]{1,0:T(8,128)(2,1)S(1)}, bf16[128,2048]{1,0:T(8,128)(2,1)S(1)}, s32[]{:T(128)}...) while((s32[]{:T(128)}, bf16[128,2048]{1,0:T(8,128)(2,1)S(1)}, ...), condition=%wide.region_14.15_spmd.clone.clone.clone, body=%wide.region_8.14_spmd.clone.clone.clone.sunk | while | flops 1451809152 | bytes 27381680 | solution.py:234
  187.6 9.8 %conditional.17 = (bf16[128,2048]{1,0:T(8,128)(2,1)S(1)}) conditional(s32[]{:T(128)} %convert_element_type.348, () %tuple.183, (bf16[128,2048]{1,0:T(8,128)(2,1)S(1)}, f32[1,2048]{1,0:T(1,128)S(1)}, f32[1,2048]{1,0:T(1,128)S(1)}, bf16[2048,1536]{1,0:T(8,128)(2,1)}, s32[128]{0:T(128)}, /*index=5*/f32[128,1,32]{0,2,1:T(8,128)S(1)}, ...), branch_computations={%region_9.9_spmd, %region_10.13_spmd} | conditional | flops 1450756480 | bytes 20941832 | solution.py:229
  187.9 3.8 fusion.18
  194.5 2.9 fusion.13
  197.4 1.3 collective-permute-start
  201.2 12.0 %collective-permute-start = (bf16[128,2048]{1,0:T(8,128)(2,1)S(1)}, bf16[128,2048]{1,0:T(8,128)(2,1)S(1)}, u32[]{:S(2)}, u32[]{:S(2)}) collective-permute-start(bf16[128,2048]{1,0:T(8,128)(2,1)S(1)} %get-tuple-element.1353), channel_id=1, source_target_pairs={{0,32},{32,64},{64,96},{96,128},{128,160},{160,192},{192,224},{1,3... | collective-permute-start | bytes 1572872 | tf_op jit(solution)/shard_map/while/body/eval_jaxpr/ppermute | solution.py:231
  215.6 6.5 %collective-permute-start = (bf16[128,2048]{1,0:T(8,128)(2,1)S(1)}, bf16[128,2048]{1,0:T(8,128)(2,1)S(1)}, u32[]{:S(2)}, u32[]{:S(2)}) collective-permute-start(bf16[128,2048]{1,0:T(8,128)(2,1)S(1)} %get-tuple-element.1353), channel_id=1, source_target_pairs={{0,32},{32,64},{64,96},{96,128},{128,160},{160,192},{192,224},{1,3... | collective-permute-start | bytes 1572872 | tf_op jit(solution)/shard_map/while/body/eval_jaxpr/ppermute | solution.py:231
  224.6 18.7 %collective-permute-start = (bf16[128,2048]{1,0:T(8,128)(2,1)S(1)}, bf16[128,2048]{1,0:T(8,128)(2,1)S(1)}, u32[]{:S(2)}, u32[]{:S(2)}) collective-permute-start(bf16[128,2048]{1,0:T(8,128)(2,1)S(1)} %get-tuple-element.1353), channel_id=1, source_target_pairs={{0,32},{32,64},{64,96},{96,128},{128,160},{160,192},{192,224},{1,3... | collective-permute-start | bytes 1572872 | tf_op jit(solution)/shard_map/while/body/eval_jaxpr/ppermute | solution.py:231
  245.8 9.0 %collective-permute-start = (bf16[128,2048]{1,0:T(8,128)(2,1)S(1)}, bf16[128,2048]{1,0:T(8,128)(2,1)S(1)}, u32[]{:S(2)}, u32[]{:S(2)}) collective-permute-start(bf16[128,2048]{1,0:T(8,128)(2,1)S(1)} %get-tuple-element.1353), channel_id=1, source_target_pairs={{0,32},{32,64},{64,96},{96,128},{128,160},{160,192},{192,224},{1,3... | collective-permute-start | bytes 1572872 | tf_op jit(solution)/shard_map/while/body/eval_jaxpr/ppermute | solution.py:231
  257.2 9.0 %collective-permute-start = (bf16[128,2048]{1,0:T(8,128)(2,1)S(1)}, bf16[128,2048]{1,0:T(8,128)(2,1)S(1)}, u32[]{:S(2)}, u32[]{:S(2)}) collective-permute-start(bf16[128,2048]{1,0:T(8,128)(2,1)S(1)} %get-tuple-element.1353), channel_id=1, source_target_pairs={{0,32},{32,64},{64,96},{96,128},{128,160},{160,192},{192,224},{1,3... | collective-permute-start | bytes 1572872 | tf_op jit(solution)/shard_map/while/body/eval_jaxpr/ppermute | solution.py:231
  268.6 9.0 %collective-permute-start = (bf16[128,2048]{1,0:T(8,128)(2,1)S(1)}, bf16[128,2048]{1,0:T(8,128)(2,1)S(1)}, u32[]{:S(2)}, u32[]{:S(2)}) collective-permute-start(bf16[128,2048]{1,0:T(8,128)(2,1)S(1)} %get-tuple-element.1353), channel_id=1, source_target_pairs={{0,32},{32,64},{64,96},{96,128},{128,160},{160,192},{192,224},{1,3... | collective-permute-start | bytes 1572872 | tf_op jit(solution)/shard_map/while/body/eval_jaxpr/ppermute | solution.py:231
  280.1 12.2 %collective-permute-start = (bf16[128,2048]{1,0:T(8,128)(2,1)S(1)}, bf16[128,2048]{1,0:T(8,128)(2,1)S(1)}, u32[]{:S(2)}, u32[]{:S(2)}) collective-permute-start(bf16[128,2048]{1,0:T(8,128)(2,1)S(1)} %get-tuple-element.1353), channel_id=1, source_target_pairs={{0,32},{32,64},{64,96},{96,128},{128,160},{160,192},{192,224},{1,3... | collective-permute-start | bytes 1572872 | tf_op jit(solution)/shard_map/while/body/eval_jaxpr/ppermute | solution.py:231
  295.3 183.1 %while.43 = (s32[]{:T(128)}, bf16[128,2048]{1,0:T(8,128)(2,1)S(1)}, f32[2048]{0:T(1024)S(1)}, f32[128,1536]{1,0:T(8,128)}, s32[]{:T(128)}, /*index=5*/bf16[1024,...) while((s32[]{:T(128)}, bf16[128,2048]{1,0:T(8,128)(2,1)S(1)}, ...), condition=%wide.region_32.33_spmd.clone.clone.clone, body=%wide.region_18.32_spmd.clone.clone.clone.sunk | while | flops 2336233984 | bytes 65241192 | solution.py:259
  296.2 1.3 collective-permute-start.1
  298.5 8.1 %collective-permute-done.1 = bf16[128,2048]{1,0:T(8,128)(2,1)S(1)} collective-permute-done((bf16[128,2048]{1,0:T(8,128)(2,1)S(1)}, bf16[128,2048]{1,0:T(8,128)(2,1)S(1)}, u32[]{:S(2)}, u32[]{:S(2)}) %collective-permute-start.1) | collective-permute-done | bytes 524320 | tf_op jit(solution)/shard_map/while/body/eval_jaxpr/ppermute | solution.py:253
  307.4 1.3 collective-permute-start.1
  309.7 9.0 %collective-permute-done.1 = bf16[128,2048]{1,0:T(8,128)(2,1)S(1)} collective-permute-done((bf16[128,2048]{1,0:T(8,128)(2,1)S(1)}, bf16[128,2048]{1,0:T(8,128)(2,1)S(1)}, u32[]{:S(2)}, u32[]{:S(2)}) %collective-permute-start.1) | collective-permute-done | bytes 524320 | tf_op jit(solution)/shard_map/while/body/eval_jaxpr/ppermute | solution.py:253
  319.5 1.3 collective-permute-start.1
  321.8 8.2 %collective-permute-done.1 = bf16[128,2048]{1,0:T(8,128)(2,1)S(1)} collective-permute-done((bf16[128,2048]{1,0:T(8,128)(2,1)S(1)}, bf16[128,2048]{1,0:T(8,128)(2,1)S(1)}, u32[]{:S(2)}, u32[]{:S(2)}) %collective-permute-start.1) | collective-permute-done | bytes 524320 | tf_op jit(solution)/shard_map/while/body/eval_jaxpr/ppermute | solution.py:253
  330.9 1.3 collective-permute-start.1
  333.2 12.1 %collective-permute-done.1 = bf16[128,2048]{1,0:T(8,128)(2,1)S(1)} collective-permute-done((bf16[128,2048]{1,0:T(8,128)(2,1)S(1)}, bf16[128,2048]{1,0:T(8,128)(2,1)S(1)}, u32[]{:S(2)}, u32[]{:S(2)}) %collective-permute-start.1) | collective-permute-done | bytes 524320 | tf_op jit(solution)/shard_map/while/body/eval_jaxpr/ppermute | solution.py:253
  346.1 1.3 collective-permute-start.1
  348.4 8.2 %collective-permute-done.1 = bf16[128,2048]{1,0:T(8,128)(2,1)S(1)} collective-permute-done((bf16[128,2048]{1,0:T(8,128)(2,1)S(1)}, bf16[128,2048]{1,0:T(8,128)(2,1)S(1)}, u32[]{:S(2)}, u32[]{:S(2)}) %collective-permute-start.1) | collective-permute-done | bytes 524320 | tf_op jit(solution)/shard_map/while/body/eval_jaxpr/ppermute | solution.py:253
  359.8 8.8 %collective-permute-done.1 = bf16[128,2048]{1,0:T(8,128)(2,1)S(1)} collective-permute-done((bf16[128,2048]{1,0:T(8,128)(2,1)S(1)}, bf16[128,2048]{1,0:T(8,128)(2,1)S(1)}, u32[]{:S(2)}, u32[]{:S(2)}) %collective-permute-start.1) | collective-permute-done | bytes 524320 | tf_op jit(solution)/shard_map/while/body/eval_jaxpr/ppermute | solution.py:253
  370.8 5.0 conditional.19
  371.1 4.7 fusion.69
  375.8 85.3 %collective-permute-done.1 = bf16[128,2048]{1,0:T(8,128)(2,1)S(1)} collective-permute-done((bf16[128,2048]{1,0:T(8,128)(2,1)S(1)}, bf16[128,2048]{1,0:T(8,128)(2,1)S(1)}, u32[]{:S(2)}, u32[]{:S(2)}) %collective-permute-start.1) | collective-permute-done | bytes 524320 | tf_op jit(solution)/shard_map/while/body/eval_jaxpr/ppermute | solution.py:253
  461.8 12.8 %conditional.18 = (bf16[128,2048]{1,0:T(8,128)(2,1)S(1)}, f32[2048]{0:T(1024)S(1)}) conditional(s32[]{:T(128)} %convert_element_type.349, () %tuple.186, (bf16[128,2048]{1,0:T(8,128)(2,1)S(1)}, bf16[1024,2048]{1,0:T(8,128)(2,1)}, s32[128]{0:T(128)}, f32[128,1536]{1,0:T(8,128)}, f32[128,1,32]{0,2,1:T(8,128)S(1)}, ...), branch_computations={%region_19.19_spmd, %region_20.28_spmd} | conditional | flops 1528560128 | bytes 54817856 | solution.py:250
  462.8 3.7 convolution_convert_fusion.4
  466.7 1.4 copy.50
  471.9 2.3 multiply_reduce_fusion.3
  476.9 1.5 collective-permute-done.1
  479.4 1.9 collective-permute-start.3
  482.1 1.9 collective-permute-done.3
  485.1 2.6 collective-permute-start.7
  487.7 1.8 collective-permute-start.6
  489.5 3.0 collective-permute-start.5
  493.6 3.5 collective-permute-done.5
  497.2 1.5 collective-permute-start.8
  498.7 3.7 collective-permute-done.8
  (258 shorter events, 73.2 us)
Async XLA Ops:
  7.2 25.8 %copy-start.5 = (s32[4,32]{1,0:T(4,128)S(1)}, s32[4,32]{1,0:T(4,128)}, u32[]{:S(2)}) copy-start(s32[4,32]{1,0:T(4,128)} %param.23) | copy-start | bytes 1540
  7.2 91.2 %all-gather.6.cloned.1.call-start = ((), (), s32[]{:S(2)}) async-start(), calls=%async_computation.2 | async-start | bytes 4325376 | tf_op jit(solution)/shard_map/all_gather | solution.py:179
  7.9 178.9 %all-gather.4.cloned.1.call-start = ((), (), s32[]{:S(2)}) async-start(), calls=%async_computation.1 | async-start | bytes 6488064 | tf_op jit(solution)/shard_map/all_gather | solution.py:176
  21.6 43.0 %all-to-all-start = ((bf16[32,4,2,2048]{3,2,1,0:T(2,128)(2,1)}), bf16[32,4,2,2048]{3,2,1,0:T(2,128)(2,1)S(1)}, u32[]{:S(2)}, u32[]{:S(2)}) async-start(bf16[32,4,2,2048]{3,2,1,0:T(2,128)(2,1)} %pad_maximum_fusion.3), calls=%async_computation | async-start | bytes 2097152 | tf_op jit(solution)/shard_map/all_to_all | solution.py:195
  65.5 121.3 %copy-start.2 = (f32[1,2048]{1,0:T(1,128)S(1)}, f32[1,2048]{1,0:T(1,128)}, u32[]{:S(2)}) copy-start(f32[1,2048]{1,0:T(1,128)} %param.26) | copy-start | bytes 24580
  65.5 121.3 %copy-start.3 = (f32[1,2048]{1,0:T(1,128)S(1)}, f32[1,2048]{1,0:T(1,128)}, u32[]{:S(2)}) copy-start(f32[1,2048]{1,0:T(1,128)} %param.25) | copy-start | bytes 24580
  197.4 2.8 collective-permute-start
  201.2 13.5 %collective-permute-start = (bf16[128,2048]{1,0:T(8,128)(2,1)S(1)}, bf16[128,2048]{1,0:T(8,128)(2,1)S(1)}, u32[]{:S(2)}, u32[]{:S(2)}) collective-permute-start(bf16[128,2048]{1,0:T(8,128)(2,1)S(1)} %get-tuple-element.1353), channel_id=1, source_target_pairs={{0,32},{32,64},{64,96},{96,128},{128,160},{160,192},{192,224},{1,3... | collective-permute-start | bytes 1572872 | tf_op jit(solution)/shard_map/while/body/eval_jaxpr/ppermute | solution.py:231
  215.6 8.0 %collective-permute-start = (bf16[128,2048]{1,0:T(8,128)(2,1)S(1)}, bf16[128,2048]{1,0:T(8,128)(2,1)S(1)}, u32[]{:S(2)}, u32[]{:S(2)}) collective-permute-start(bf16[128,2048]{1,0:T(8,128)(2,1)S(1)} %get-tuple-element.1353), channel_id=1, source_target_pairs={{0,32},{32,64},{64,96},{96,128},{128,160},{160,192},{192,224},{1,3... | collective-permute-start | bytes 1572872 | tf_op jit(solution)/shard_map/while/body/eval_jaxpr/ppermute | solution.py:231
  224.6 20.2 %collective-permute-start = (bf16[128,2048]{1,0:T(8,128)(2,1)S(1)}, bf16[128,2048]{1,0:T(8,128)(2,1)S(1)}, u32[]{:S(2)}, u32[]{:S(2)}) collective-permute-start(bf16[128,2048]{1,0:T(8,128)(2,1)S(1)} %get-tuple-element.1353), channel_id=1, source_target_pairs={{0,32},{32,64},{64,96},{96,128},{128,160},{160,192},{192,224},{1,3... | collective-permute-start | bytes 1572872 | tf_op jit(solution)/shard_map/while/body/eval_jaxpr/ppermute | solution.py:231
  245.8 10.5 %collective-permute-start = (bf16[128,2048]{1,0:T(8,128)(2,1)S(1)}, bf16[128,2048]{1,0:T(8,128)(2,1)S(1)}, u32[]{:S(2)}, u32[]{:S(2)}) collective-permute-start(bf16[128,2048]{1,0:T(8,128)(2,1)S(1)} %get-tuple-element.1353), channel_id=1, source_target_pairs={{0,32},{32,64},{64,96},{96,128},{128,160},{160,192},{192,224},{1,3... | collective-permute-start | bytes 1572872 | tf_op jit(solution)/shard_map/while/body/eval_jaxpr/ppermute | solution.py:231
  257.2 10.5 %collective-permute-start = (bf16[128,2048]{1,0:T(8,128)(2,1)S(1)}, bf16[128,2048]{1,0:T(8,128)(2,1)S(1)}, u32[]{:S(2)}, u32[]{:S(2)}) collective-permute-start(bf16[128,2048]{1,0:T(8,128)(2,1)S(1)} %get-tuple-element.1353), channel_id=1, source_target_pairs={{0,32},{32,64},{64,96},{96,128},{128,160},{160,192},{192,224},{1,3... | collective-permute-start | bytes 1572872 | tf_op jit(solution)/shard_map/while/body/eval_jaxpr/ppermute | solution.py:231
  268.6 10.5 %collective-permute-start = (bf16[128,2048]{1,0:T(8,128)(2,1)S(1)}, bf16[128,2048]{1,0:T(8,128)(2,1)S(1)}, u32[]{:S(2)}, u32[]{:S(2)}) collective-permute-start(bf16[128,2048]{1,0:T(8,128)(2,1)S(1)} %get-tuple-element.1353), channel_id=1, source_target_pairs={{0,32},{32,64},{64,96},{96,128},{128,160},{160,192},{192,224},{1,3... | collective-permute-start | bytes 1572872 | tf_op jit(solution)/shard_map/while/body/eval_jaxpr/ppermute | solution.py:231
  280.1 13.7 %collective-permute-start = (bf16[128,2048]{1,0:T(8,128)(2,1)S(1)}, bf16[128,2048]{1,0:T(8,128)(2,1)S(1)}, u32[]{:S(2)}, u32[]{:S(2)}) collective-permute-start(bf16[128,2048]{1,0:T(8,128)(2,1)S(1)} %get-tuple-element.1353), channel_id=1, source_target_pairs={{0,32},{32,64},{64,96},{96,128},{128,160},{160,192},{192,224},{1,3... | collective-permute-start | bytes 1572872 | tf_op jit(solution)/shard_map/while/body/eval_jaxpr/ppermute | solution.py:231
  293.9 1.4 copy-start.1
  293.9 1.4 copy-start
  293.9 1.4 copy-start.4
  296.2 10.4 %collective-permute-start.1 = (bf16[128,2048]{1,0:T(8,128)(2,1)S(1)}, bf16[128,2048]{1,0:T(8,128)(2,1)S(1)}, u32[]{:S(2)}, u32[]{:S(2)}) collective-permute-start(bf16[128,2048]{1,0:T(8,128)(2,1)S(1)} %get-tuple-element.1250), channel_id=1, source_target_pairs={{32,0},{64,32},{96,64},{128,96},{160,128},{192,160},{224,192},{33,... | collective-permute-start | bytes 1572872 | tf_op jit(solution)/shard_map/while/body/eval_jaxpr/ppermute | solution.py:253
  307.4 11.2 %collective-permute-start.1 = (bf16[128,2048]{1,0:T(8,128)(2,1)S(1)}, bf16[128,2048]{1,0:T(8,128)(2,1)S(1)}, u32[]{:S(2)}, u32[]{:S(2)}) collective-permute-start(bf16[128,2048]{1,0:T(8,128)(2,1)S(1)} %get-tuple-element.1250), channel_id=1, source_target_pairs={{32,0},{64,32},{96,64},{128,96},{160,128},{192,160},{224,192},{33,... | collective-permute-start | bytes 1572872 | tf_op jit(solution)/shard_map/while/body/eval_jaxpr/ppermute | solution.py:253
  319.5 10.5 %collective-permute-start.1 = (bf16[128,2048]{1,0:T(8,128)(2,1)S(1)}, bf16[128,2048]{1,0:T(8,128)(2,1)S(1)}, u32[]{:S(2)}, u32[]{:S(2)}) collective-permute-start(bf16[128,2048]{1,0:T(8,128)(2,1)S(1)} %get-tuple-element.1250), channel_id=1, source_target_pairs={{32,0},{64,32},{96,64},{128,96},{160,128},{192,160},{224,192},{33,... | collective-permute-start | bytes 1572872 | tf_op jit(solution)/shard_map/while/body/eval_jaxpr/ppermute | solution.py:253
  330.9 14.4 %collective-permute-start.1 = (bf16[128,2048]{1,0:T(8,128)(2,1)S(1)}, bf16[128,2048]{1,0:T(8,128)(2,1)S(1)}, u32[]{:S(2)}, u32[]{:S(2)}) collective-permute-start(bf16[128,2048]{1,0:T(8,128)(2,1)S(1)} %get-tuple-element.1250), channel_id=1, source_target_pairs={{32,0},{64,32},{96,64},{128,96},{160,128},{192,160},{224,192},{33,... | collective-permute-start | bytes 1572872 | tf_op jit(solution)/shard_map/while/body/eval_jaxpr/ppermute | solution.py:253
  346.1 10.5 %collective-permute-start.1 = (bf16[128,2048]{1,0:T(8,128)(2,1)S(1)}, bf16[128,2048]{1,0:T(8,128)(2,1)S(1)}, u32[]{:S(2)}, u32[]{:S(2)}) collective-permute-start(bf16[128,2048]{1,0:T(8,128)(2,1)S(1)} %get-tuple-element.1250), channel_id=1, source_target_pairs={{32,0},{64,32},{96,64},{128,96},{160,128},{192,160},{224,192},{33,... | collective-permute-start | bytes 1572872 | tf_op jit(solution)/shard_map/while/body/eval_jaxpr/ppermute | solution.py:253
  357.5 11.1 %collective-permute-start.1 = (bf16[128,2048]{1,0:T(8,128)(2,1)S(1)}, bf16[128,2048]{1,0:T(8,128)(2,1)S(1)}, u32[]{:S(2)}, u32[]{:S(2)}) collective-permute-start(bf16[128,2048]{1,0:T(8,128)(2,1)S(1)} %get-tuple-element.1250), channel_id=1, source_target_pairs={{32,0},{64,32},{96,64},{128,96},{160,128},{192,160},{224,192},{33,... | collective-permute-start | bytes 1572872 | tf_op jit(solution)/shard_map/while/body/eval_jaxpr/ppermute | solution.py:253
  369.5 91.6 %collective-permute-start.1 = (bf16[128,2048]{1,0:T(8,128)(2,1)S(1)}, bf16[128,2048]{1,0:T(8,128)(2,1)S(1)}, u32[]{:S(2)}, u32[]{:S(2)}) collective-permute-start(bf16[128,2048]{1,0:T(8,128)(2,1)S(1)} %get-tuple-element.1250), channel_id=1, source_target_pairs={{32,0},{64,32},{96,64},{128,96},{160,128},{192,160},{224,192},{33,... | collective-permute-start | bytes 1572872 | tf_op jit(solution)/shard_map/while/body/eval_jaxpr/ppermute | solution.py:253
  468.8 2.7 slice-start
  469.7 2.2 slice-start.1
  474.6 3.8 collective-permute-start.1
  478.4 3.7 collective-permute-start.4
  479.4 4.6 collective-permute-start.3
  481.3 3.7 collective-permute-start.2
  485.1 8.5 %collective-permute-start.7 = (f32[2048]{0:T(1024)S(1)}, f32[2048]{0:T(1024)S(1)}, u32[]{:S(2)}, u32[]{:S(2)}) collective-permute-start(f32[2048]{0:T(1024)S(1)} %bitcast.245), channel_id=1, source_target_pairs={{0,12},{1,13},{2,14},{3,15},{4,8},{5,9},{6,10},{7,11},{8,4},{9,5},... | collective-permute-start | bytes 24584 | tf_op jit(solution)/shard_map/ppermute | solution.py:127
  487.7 5.9 %collective-permute-start.6 = (f32[2048]{0:T(1024)S(1)}, f32[2048]{0:T(1024)S(1)}, u32[]{:S(2)}, u32[]{:S(2)}) collective-permute-start(f32[2048]{0:T(1024)S(1)} %bitcast.246), channel_id=1, source_target_pairs={{0,8},{1,9},{2,10},{3,11},{4,12},{5,13},{6,14},{7,15},{8,0},{9,1},... | collective-permute-start | bytes 24584 | tf_op jit(solution)/shard_map/ppermute | solution.py:127
  489.5 7.6 %collective-permute-start.5 = (f32[2048]{0:T(1024)S(1)}, f32[2048]{0:T(1024)S(1)}, u32[]{:S(2)}, u32[]{:S(2)}) collective-permute-start(f32[2048]{0:T(1024)S(1)} %bitcast.247), channel_id=1, source_target_pairs={{0,4},{1,5},{2,6},{3,7},{4,0},{5,1},{6,2},{7,3},{8,12},{9,13},{10,... | collective-permute-start | bytes 24584 | tf_op jit(solution)/shard_map/ppermute | solution.py:127
  497.2 5.2 %collective-permute-start.8 = (f32[2048]{0:T(1024)S(1)}, f32[2048]{0:T(1024)S(1)}, u32[]{:S(2)}, u32[]{:S(2)}) collective-permute-start(f32[2048]{0:T(1024)S(1)} %bitcast.244), channel_id=1, source_target_pairs={{0,16},{1,17},{2,18},{3,19},{4,20},{5,21},{6,22},{7,23},{8,24},{9,... | collective-permute-start | bytes 24584 | tf_op jit(solution)/shard_map/ppermute | solution.py:127
Sparse Core Ops, SparseCore 0:
  10.6 87.7 all-gather.5
  101.5 85.2 all-gather.3

commit v12 on v11

--- a/solution.py
+++ b/solution.py
@@ -231,8 +231,27 @@
         sent = lax.ppermute(hidden_new, "section", forward_route)
         return ((sent, kept, produced, step + 1), None)
 
+    query_heads = full_out.shape[0] // HD
+
+    def first_front():
+        residual, normed = normalize(grouped, steering, gain_row)
+        return (residual, attend(project_in(normed, full_qkv), tables, allowed, query_heads))
+
+    lead = section_idx == 0
+    first_residual, first_mixed = lax.cond(
+        lead,
+        first_front,
+        lambda: (jnp.zeros((flat_count, width), jnp.float32), jnp.zeros((flat_count, full_out.shape[0]), jnp.bfloat16)),
+    )
+    first_out = lax.cond(
+        lead, lambda: project_out(first_residual, first_mixed, full_out), lambda: zero_block
+    )
+    first_sent = lax.ppermute(first_out, "section", forward_route)
     (unused_in, kept, produced, unused_step), unused_ys = lax.scan(
-        forward_step, (grouped, zero_block, zero_block, jnp.int32(0)), None, length=section_count
+        forward_step,
+        (first_sent, grouped, first_out, jnp.int32(1)),
+        None,
+        length=section_count - 1,
     )
     first_saved = lax.cond(
         section_idx == section_count - 1, lambda: precompute(kept), lambda: zero_proj

time: 511 us -> 546 us (1.068)
  other arithmetic: 31.1 us -> 49.6 us
  waiting for transfers between devices: 302 us -> 311 us
  local copies, waits for them, and re-layouts: 22.5 us -> 28.2 us
    all_gather x1, waiting for transfers between devices: 81.9 us -> 39.6 us  [body(): lax.all_gather(jnp.concatenate([w_query[0], w_keyval[0]], axis=1), 'dp',...]
    all_gather x1, waiting for transfers between devices: 31.5 us -> 72.9 us  [body(): full_out = lax.all_gather(w_out[0], 'dp', axis=1, tiled=True)]
    ppermute x8, waiting for transfers between devices: 141 us -> 159 us  [backward_step(): sent = lax.ppermute(grad_in, 'section', backward_route)]
    select_n x8 -> x7, other arithmetic: 2.87 us -> 14.7 us  [forward_step(): produced = jnp.where(active, hidden_new, produced)]
    ppermute x8 -> x7, waiting for transfers between devices: 8.92 us -> 0.02 us  [forward_step(): sent = lax.ppermute(hidden_new, 'section', forward_route)]
    ppermute x8 -> x7, starting transfers between devices: 77.9 us -> 71.7 us  [forward_step(): sent = lax.ppermute(hidden_new, 'section', forward_route)]
    broadcast_in_dim x14, local copies, waits for them, and re-layouts: 0.64 us -> 6.29 us  [body(): zero_block = jnp.zeros((flat_count, width), jnp.bfloat16)]
  transfers between devices with their start and end apart: 26 -> 26, of which waited for: 25 -> 17; matrix products, arithmetic and copies ran while one was open for 8% -> 11% of each run, Pallas kernels for 0% -> 0%
where the time goes in v12:
time: 546 us; the launch traced here: 543 us
  waiting for transfers between devices  311 us (57%)
  starting transfers between devices  108 us (20%)
  other arithmetic  49.6 us (9%)
  matrix products  30 us (5%)
  local copies, waits for them, and re-layouts  28.2 us (5%)
  between operations  14.4 us (3%)
    ppermute x8, waiting for transfers between devices, backward_step(): sent = lax.ppermute(grad_in, 'section', backward_route)  159 us
    all_gather x1, waiting for transfers between devices, body(): full_out = lax.all_gather(w_out[0], 'dp', axis=1, tiled=True)  72.9 us
    ppermute x7, starting transfers between devices, forward_step(): sent = lax.ppermute(hidden_new, 'section', forward_route)  71.7 us
    all_gather x1, waiting for transfers between devices, body(): lax.all_gather(jnp.concatenate([w_query[0], w_keyval[0]], axis=1), 'dp',...  39.6 us
    all_to_all x1, waiting for transfers between devices, body(): lax.all_to_all(packed, 'dp', split_axis=0, concat_axis=0, tiled=True)  27.8 us
    mul x16, other arithmetic, rope_tables(): angles = positions.astype(jnp.float32)[..., None] * inverse  16.3 us
    select_n x7, other arithmetic, forward_step(): produced = jnp.where(active, hidden_new, produced)  14.7 us
    ppermute x7, starting transfers between devices, butterfly_sum(): received.append(lax.ppermute(values, axis, route))  12.6 us
  transfers between devices with their start and end apart: 26, of which 17 were waited for; matrix products, arithmetic and copies ran while one was open for 11% of the time, Pallas kernels for 0%

profile of v12, /device:TPU:32, one launch (start us, length us, event | category | flops | bytes accessed | tf_op | source)
XLA Modules:
  0.0 542.8 jit_solution(621268602056792958)
XLA Ops:
  7.2 1.6 pad_maximum_fusion.5
  10.9 2.9 convert_reduce_fusion.4
  19.2 2.4 pad_maximum_fusion.3
  21.6 11.4 %all-to-all-start = ((bf16[32,4,2,2048]{3,2,1,0:T(2,128)(2,1)}), bf16[32,4,2,2048]{3,2,1,0:T(2,128)(2,1)S(1)}, u32[]{:S(2)}, u32[]{:S(2)}) async-start(bf16[32,4,2,2048]{3,2,1,0:T(2,128)(2,1)} %pad_maximum_fusion.3), calls=%async_computation | async-start | bytes 2097152 | tf_op jit(solution)/shard_map/all_to_all | solution.py:195
  38.5 27.8 %all-to-all-done = bf16[32,4,2,2048]{3,2,1,0:T(2,128)(2,1)S(1)} async-done(((bf16[32,4,2,2048]{3,2,1,0:T(2,128)(2,1)}), bf16[32,4,2,2048]{3,2,1,0:T(2,128)(2,1)S(1)}, u32[]{:S(2)}, u32[]{:S(2)}) %all-to-all-start) | async-done | bytes 1048608 | tf_op jit(solution)/shard_map/all_to_all | solution.py:195
  68.6 39.6 %all-gather.4.cloned.1.call-done = bf16[2048,1536]{1,0:T(8,128)(2,1)} async-done(((bf16[64,1536]{1,0:T(8,128)(2,1)}), bf16[2048,1536]{1,0:T(8,128)(2,1)}) %all-gather.4.cloned.1.call-update) | async-done | bytes 6291472 | tf_op jit(solution)/shard_map/all_gather | solution.py:176
  108.2 8.2 %conditional.6 = (f32[128,2048]{1,0:T(8,128)}, bf16[128,1024]{0,1:T(8,128)(2,1)S(1)}) conditional(s32[]{:T(128)} %convert_element_type.227, () %tuple.87, (bf16[128,2048]{1,0:T(8,128)(2,1)S(1)}, f32[1,2048]{1,0:T(1,128)S(1)}, f32[1,2048]{1,0:T(1,128)S(1)}, bf16[2048,1536]{1,0:T(8,128)(2,1)}, s32[128]{0:T(128)}, ...), branch_computations={%region_8.9_spmd, %region_9.13_spmd} | conditional | flops 912312704 | bytes 16993296 | solution.py:241
  109.4 4.2 fusion.17
  116.4 72.9 %all-gather.6.cloned.1.call-done = bf16[1,1024,2048]{1,2,0:T(8,128)(2,1)} async-done(((bf16[1,1024,64]{1,2,0:T(8,128)(2,1)}), bf16[1,1024,2048]{1,2,0:T(8,128)(2,1)}) %all-gather.6.cloned.1.call-update) | async-done | bytes 4194320 | tf_op jit(solution)/shard_map/all_gather | solution.py:179
  189.3 4.8 conditional.7
  189.3 4.8 fusion.31
  195.4 6.6 %copy.81 = bf16[1024,2048]{1,0:T(8,128)(2,1)} copy(bf16[1024,2048]{0,1:T(8,128)(2,1)} %bitcast.244) | data formatting | bytes 8388608
  201.9 97.1 %while.41 = (s32[]{:T(128)}, bf16[128,2048]{1,0:T(8,128)(2,1)S(1)}, bf16[128,2048]{1,0:T(8,128)(2,1)S(1)}, bf16[128,2048]{1,0:T(8,128)(2,1)}, s32[]{:T(128)}, /*...) while((s32[]{:T(128)}, bf16[128,2048]{1,0:T(8,128)(2,1)S(1)}, ...), condition=%wide.region_21.22_spmd.clone.clone, body=%wide.region_15.21_spmd.clone.clone.sunk | while | flops 1451284864 | bytes 27447216 | solution.py:250
  203.4 10.0 %collective-permute-start = (bf16[128,2048]{1,0:T(8,128)(2,1)S(1)}, bf16[128,2048]{1,0:T(8,128)(2,1)S(1)}, u32[]{:S(2)}, u32[]{:S(2)}) collective-permute-start(bf16[128,2048]{1,0:T(8,128)(2,1)S(1)} %get-tuple-element.1372), channel_id=1, source_target_pairs={{0,32},{32,64},{64,96},{96,128},{128,160},{160,192},{192,224},{1,3... | collective-permute-start | bytes 1572872 | tf_op jit(solution)/shard_map/while/body/eval_jaxpr/ppermute | solution.py:231
  213.4 2.1 broadcast_select_fusion.3
  217.0 5.9 %collective-permute-start = (bf16[128,2048]{1,0:T(8,128)(2,1)S(1)}, bf16[128,2048]{1,0:T(8,128)(2,1)S(1)}, u32[]{:S(2)}, u32[]{:S(2)}) collective-permute-start(bf16[128,2048]{1,0:T(8,128)(2,1)S(1)} %get-tuple-element.1372), channel_id=1, source_target_pairs={{0,32},{32,64},{64,96},{96,128},{128,160},{160,192},{192,224},{1,3... | collective-permute-start | bytes 1572872 | tf_op jit(solution)/shard_map/while/body/eval_jaxpr/ppermute | solution.py:231
  222.9 2.1 broadcast_select_fusion.3
  226.6 18.2 %collective-permute-start = (bf16[128,2048]{1,0:T(8,128)(2,1)S(1)}, bf16[128,2048]{1,0:T(8,128)(2,1)S(1)}, u32[]{:S(2)}, u32[]{:S(2)}) collective-permute-start(bf16[128,2048]{1,0:T(8,128)(2,1)S(1)} %get-tuple-element.1372), channel_id=1, source_target_pairs={{0,32},{32,64},{64,96},{96,128},{128,160},{160,192},{192,224},{1,3... | collective-permute-start | bytes 1572872 | tf_op jit(solution)/shard_map/while/body/eval_jaxpr/ppermute | solution.py:231
  244.8 2.1 broadcast_select_fusion.3
  248.4 8.4 %collective-permute-start = (bf16[128,2048]{1,0:T(8,128)(2,1)S(1)}, bf16[128,2048]{1,0:T(8,128)(2,1)S(1)}, u32[]{:S(2)}, u32[]{:S(2)}) collective-permute-start(bf16[128,2048]{1,0:T(8,128)(2,1)S(1)} %get-tuple-element.1372), channel_id=1, source_target_pairs={{0,32},{32,64},{64,96},{96,128},{128,160},{160,192},{192,224},{1,3... | collective-permute-start | bytes 1572872 | tf_op jit(solution)/shard_map/while/body/eval_jaxpr/ppermute | solution.py:231
  256.8 2.1 broadcast_select_fusion.3
  260.4 8.4 %collective-permute-start = (bf16[128,2048]{1,0:T(8,128)(2,1)S(1)}, bf16[128,2048]{1,0:T(8,128)(2,1)S(1)}, u32[]{:S(2)}, u32[]{:S(2)}) collective-permute-start(bf16[128,2048]{1,0:T(8,128)(2,1)S(1)} %get-tuple-element.1372), channel_id=1, source_target_pairs={{0,32},{32,64},{64,96},{96,128},{128,160},{160,192},{192,224},{1,3... | collective-permute-start | bytes 1572872 | tf_op jit(solution)/shard_map/while/body/eval_jaxpr/ppermute | solution.py:231
  268.8 2.1 broadcast_select_fusion.3
  272.4 8.4 %collective-permute-start = (bf16[128,2048]{1,0:T(8,128)(2,1)S(1)}, bf16[128,2048]{1,0:T(8,128)(2,1)S(1)}, u32[]{:S(2)}, u32[]{:S(2)}) collective-permute-start(bf16[128,2048]{1,0:T(8,128)(2,1)S(1)} %get-tuple-element.1372), channel_id=1, source_target_pairs={{0,32},{32,64},{64,96},{96,128},{128,160},{160,192},{192,224},{1,3... | collective-permute-start | bytes 1572872 | tf_op jit(solution)/shard_map/while/body/eval_jaxpr/ppermute | solution.py:231
  280.8 2.1 broadcast_select_fusion.3
  284.5 12.4 %collective-permute-start = (bf16[128,2048]{1,0:T(8,128)(2,1)S(1)}, bf16[128,2048]{1,0:T(8,128)(2,1)S(1)}, u32[]{:S(2)}, u32[]{:S(2)}) collective-permute-start(bf16[128,2048]{1,0:T(8,128)(2,1)S(1)} %get-tuple-element.1372), channel_id=1, source_target_pairs={{0,32},{32,64},{64,96},{96,128},{128,160},{160,192},{192,224},{1,3... | collective-permute-start | bytes 1572872 | tf_op jit(solution)/shard_map/while/body/eval_jaxpr/ppermute | solution.py:231
  296.9 2.1 broadcast_select_fusion.3
  300.1 210.9 %while.42 = (s32[]{:T(128)}, bf16[128,2048]{1,0:T(8,128)(2,1)S(1)}, f32[2048]{0:T(1024)}, f32[128,1536]{1,0:T(8,128)}, s32[]{:T(128)}, /*index=5*/bf16[1024,2048...) while((s32[]{:T(128)}, bf16[128,2048]{1,0:T(8,128)(2,1)S(1)}, ...), condition=%wide.region_39.40_spmd.clone.clone.clone, body=%wide.region_25.39_spmd.clone.clone.clone.sunk | while | flops 2336233984 | bytes 66355408 | solution.py:278
  304.2 7.7 %collective-permute-done.1 = bf16[128,2048]{1,0:T(8,128)(2,1)S(1)} collective-permute-done((bf16[128,2048]{1,0:T(8,128)(2,1)}, bf16[128,2048]{1,0:T(8,128)(2,1)S(1)}, u32[]{:S(2)}, u32[]{:S(2)}) %collective-permute-start.1) | collective-permute-done | bytes 524320 | tf_op jit(solution)/shard_map/while/body/eval_jaxpr/ppermute | solution.py:272
  316.0 9.2 %collective-permute-done.1 = bf16[128,2048]{1,0:T(8,128)(2,1)S(1)} collective-permute-done((bf16[128,2048]{1,0:T(8,128)(2,1)}, bf16[128,2048]{1,0:T(8,128)(2,1)S(1)}, u32[]{:S(2)}, u32[]{:S(2)}) %collective-permute-start.1) | collective-permute-done | bytes 524320 | tf_op jit(solution)/shard_map/while/body/eval_jaxpr/ppermute | solution.py:272
  329.2 8.4 %collective-permute-done.1 = bf16[128,2048]{1,0:T(8,128)(2,1)S(1)} collective-permute-done((bf16[128,2048]{1,0:T(8,128)(2,1)}, bf16[128,2048]{1,0:T(8,128)(2,1)S(1)}, u32[]{:S(2)}, u32[]{:S(2)}) %collective-permute-start.1) | collective-permute-done | bytes 524320 | tf_op jit(solution)/shard_map/while/body/eval_jaxpr/ppermute | solution.py:272
  341.7 12.4 %collective-permute-done.1 = bf16[128,2048]{1,0:T(8,128)(2,1)S(1)} collective-permute-done((bf16[128,2048]{1,0:T(8,128)(2,1)}, bf16[128,2048]{1,0:T(8,128)(2,1)S(1)}, u32[]{:S(2)}, u32[]{:S(2)}) %collective-permute-start.1) | collective-permute-done | bytes 524320 | tf_op jit(solution)/shard_map/while/body/eval_jaxpr/ppermute | solution.py:272
  358.2 8.4 %collective-permute-done.1 = bf16[128,2048]{1,0:T(8,128)(2,1)S(1)} collective-permute-done((bf16[128,2048]{1,0:T(8,128)(2,1)}, bf16[128,2048]{1,0:T(8,128)(2,1)S(1)}, u32[]{:S(2)}, u32[]{:S(2)}) %collective-permute-start.1) | collective-permute-done | bytes 524320 | tf_op jit(solution)/shard_map/while/body/eval_jaxpr/ppermute | solution.py:272
  370.7 8.4 %collective-permute-done.1 = bf16[128,2048]{1,0:T(8,128)(2,1)S(1)} collective-permute-done((bf16[128,2048]{1,0:T(8,128)(2,1)}, bf16[128,2048]{1,0:T(8,128)(2,1)S(1)}, u32[]{:S(2)}, u32[]{:S(2)}) %collective-permute-start.1) | collective-permute-done | bytes 524320 | tf_op jit(solution)/shard_map/while/body/eval_jaxpr/ppermute | solution.py:272
  382.2 5.0 conditional.22
  382.5 4.7 fusion.89
  387.2 102.9 %collective-permute-done.1 = bf16[128,2048]{1,0:T(8,128)(2,1)S(1)} collective-permute-done((bf16[128,2048]{1,0:T(8,128)(2,1)}, bf16[128,2048]{1,0:T(8,128)(2,1)S(1)}, u32[]{:S(2)}, u32[]{:S(2)}) %collective-permute-start.1) | collective-permute-done | bytes 524320 | tf_op jit(solution)/shard_map/while/body/eval_jaxpr/ppermute | solution.py:272
  490.9 16.0 %conditional.21 = (bf16[128,2048]{1,0:T(8,128)(2,1)}, f32[2048]{0:T(1024)S(1)}) conditional(s32[]{:T(128)} %convert_element_type.386, () %tuple.206, (bf16[128,2048]{1,0:T(8,128)(2,1)S(1)}, bf16[1024,2048]{1,0:T(8,128)(2,1)}, s32[128]{0:T(128)}, f32[128,1536]{1,0:T(8,128)}, f32[128,1,32]{0,2,1:T(8,128)S(1)}, ...), branch_computations={%region_26.26_spmd, %region_27.35_spmd} | conditional | flops 1528560128 | bytes 55866488 | solution.py:269
  494.1 3.7 convolution_convert_fusion.5
  498.6 1.5 fusion.63
  503.4 2.3 multiply_reduce_fusion.4
  509.3 1.7 collective-permute-done.1
  514.9 1.7 collective-permute-done.4
  518.1 4.4 collective-permute-start.8
  522.4 2.8 collective-permute-start.6
  526.5 3.5 collective-permute-done.6
  530.1 1.6 collective-permute-start.9
  531.7 3.6 collective-permute-done.9
  (287 shorter events, 92.2 us)
Async XLA Ops:
  7.2 25.8 %copy-start.8 = (s32[4,32]{1,0:T(4,128)S(1)}, s32[4,32]{1,0:T(4,128)}, u32[]{:S(2)}) copy-start(s32[4,32]{1,0:T(4,128)} %param.27) | copy-start | bytes 1540
  7.2 101.0 %all-gather.4.cloned.1.call-start = ((), (), s32[]{:S(2)}) async-start(), calls=%async_computation.1 | async-start | bytes 6488064 | tf_op jit(solution)/shard_map/all_gather | solution.py:176
  8.9 180.4 %all-gather.6.cloned.1.call-start = ((), (), s32[]{:S(2)}) async-start(), calls=%async_computation.2 | async-start | bytes 4325376 | tf_op jit(solution)/shard_map/all_gather | solution.py:179
  17.8 90.3 %copy-start.1 = (f32[1,2048]{1,0:T(1,128)S(1)}, f32[1,2048]{1,0:T(1,128)}, u32[]{:S(2)}) copy-start(f32[1,2048]{1,0:T(1,128)} %param.30) | copy-start | bytes 24580
  17.9 90.3 %copy-start.5 = (f32[1,2048]{1,0:T(1,128)S(1)}, f32[1,2048]{1,0:T(1,128)}, u32[]{:S(2)}) copy-start(f32[1,2048]{1,0:T(1,128)} %param.29) | copy-start | bytes 24580
  21.6 44.7 %all-to-all-start = ((bf16[32,4,2,2048]{3,2,1,0:T(2,128)(2,1)}), bf16[32,4,2,2048]{3,2,1,0:T(2,128)(2,1)S(1)}, u32[]{:S(2)}, u32[]{:S(2)}) async-start(bf16[32,4,2,2048]{3,2,1,0:T(2,128)(2,1)} %pad_maximum_fusion.3), calls=%async_computation | async-start | bytes 2097152 | tf_op jit(solution)/shard_map/all_to_all | solution.py:195
  194.1 7.9 %collective-permute-start.2 = (bf16[128,2048]{1,0:T(8,128)(2,1)}, bf16[128,2048]{1,0:T(8,128)(2,1)S(1)}, u32[]{:S(2)}, u32[]{:S(2)}) collective-permute-start(bf16[128,2048]{1,0:T(8,128)(2,1)} %get-tuple-element.1370), channel_id=1, source_target_pairs={{0,32},{32,64},{64,96},{96,128},{128,160},{160,192},{192,224},{1,3... | collective-permute-start | bytes 1572872 | tf_op jit(solution)/shard_map/ppermute | solution.py:249
  203.4 12.1 %collective-permute-start = (bf16[128,2048]{1,0:T(8,128)(2,1)S(1)}, bf16[128,2048]{1,0:T(8,128)(2,1)S(1)}, u32[]{:S(2)}, u32[]{:S(2)}) collective-permute-start(bf16[128,2048]{1,0:T(8,128)(2,1)S(1)} %get-tuple-element.1372), channel_id=1, source_target_pairs={{0,32},{32,64},{64,96},{96,128},{128,160},{160,192},{192,224},{1,3... | collective-permute-start | bytes 1572872 | tf_op jit(solution)/shard_map/while/body/eval_jaxpr/ppermute | solution.py:231
  217.0 8.0 %collective-permute-start = (bf16[128,2048]{1,0:T(8,128)(2,1)S(1)}, bf16[128,2048]{1,0:T(8,128)(2,1)S(1)}, u32[]{:S(2)}, u32[]{:S(2)}) collective-permute-start(bf16[128,2048]{1,0:T(8,128)(2,1)S(1)} %get-tuple-element.1372), channel_id=1, source_target_pairs={{0,32},{32,64},{64,96},{96,128},{128,160},{160,192},{192,224},{1,3... | collective-permute-start | bytes 1572872 | tf_op jit(solution)/shard_map/while/body/eval_jaxpr/ppermute | solution.py:231
  226.6 20.3 %collective-permute-start = (bf16[128,2048]{1,0:T(8,128)(2,1)S(1)}, bf16[128,2048]{1,0:T(8,128)(2,1)S(1)}, u32[]{:S(2)}, u32[]{:S(2)}) collective-permute-start(bf16[128,2048]{1,0:T(8,128)(2,1)S(1)} %get-tuple-element.1372), channel_id=1, source_target_pairs={{0,32},{32,64},{64,96},{96,128},{128,160},{160,192},{192,224},{1,3... | collective-permute-start | bytes 1572872 | tf_op jit(solution)/shard_map/while/body/eval_jaxpr/ppermute | solution.py:231
  248.4 10.5 %collective-permute-start = (bf16[128,2048]{1,0:T(8,128)(2,1)S(1)}, bf16[128,2048]{1,0:T(8,128)(2,1)S(1)}, u32[]{:S(2)}, u32[]{:S(2)}) collective-permute-start(bf16[128,2048]{1,0:T(8,128)(2,1)S(1)} %get-tuple-element.1372), channel_id=1, source_target_pairs={{0,32},{32,64},{64,96},{96,128},{128,160},{160,192},{192,224},{1,3... | collective-permute-start | bytes 1572872 | tf_op jit(solution)/shard_map/while/body/eval_jaxpr/ppermute | solution.py:231
  260.4 10.5 %collective-permute-start = (bf16[128,2048]{1,0:T(8,128)(2,1)S(1)}, bf16[128,2048]{1,0:T(8,128)(2,1)S(1)}, u32[]{:S(2)}, u32[]{:S(2)}) collective-permute-start(bf16[128,2048]{1,0:T(8,128)(2,1)S(1)} %get-tuple-element.1372), channel_id=1, source_target_pairs={{0,32},{32,64},{64,96},{96,128},{128,160},{160,192},{192,224},{1,3... | collective-permute-start | bytes 1572872 | tf_op jit(solution)/shard_map/while/body/eval_jaxpr/ppermute | solution.py:231
  272.4 10.5 %collective-permute-start = (bf16[128,2048]{1,0:T(8,128)(2,1)S(1)}, bf16[128,2048]{1,0:T(8,128)(2,1)S(1)}, u32[]{:S(2)}, u32[]{:S(2)}) collective-permute-start(bf16[128,2048]{1,0:T(8,128)(2,1)S(1)} %get-tuple-element.1372), channel_id=1, source_target_pairs={{0,32},{32,64},{64,96},{96,128},{128,160},{160,192},{192,224},{1,3... | collective-permute-start | bytes 1572872 | tf_op jit(solution)/shard_map/while/body/eval_jaxpr/ppermute | solution.py:231
  284.5 14.5 %collective-permute-start = (bf16[128,2048]{1,0:T(8,128)(2,1)S(1)}, bf16[128,2048]{1,0:T(8,128)(2,1)S(1)}, u32[]{:S(2)}, u32[]{:S(2)}) collective-permute-start(bf16[128,2048]{1,0:T(8,128)(2,1)S(1)} %get-tuple-element.1372), channel_id=1, source_target_pairs={{0,32},{32,64},{64,96},{96,128},{128,160},{160,192},{192,224},{1,3... | collective-permute-start | bytes 1572872 | tf_op jit(solution)/shard_map/while/body/eval_jaxpr/ppermute | solution.py:231
  301.8 2.4 copy-start.6
  301.8 10.1 %collective-permute-start.1 = (bf16[128,2048]{1,0:T(8,128)(2,1)}, bf16[128,2048]{1,0:T(8,128)(2,1)S(1)}, u32[]{:S(2)}, u32[]{:S(2)}) collective-permute-start(bf16[128,2048]{1,0:T(8,128)(2,1)} %get-tuple-element.1267), channel_id=1, source_target_pairs={{32,0},{64,32},{96,64},{128,96},{160,128},{192,160},{224,192},{33,... | collective-permute-start | bytes 1572872 | tf_op jit(solution)/shard_map/while/body/eval_jaxpr/ppermute | solution.py:272
  304.2 7.7 %copy-start.7 = (f32[2048]{0:T(1024)}, f32[2048]{0:T(1024)S(1)}, u32[]{:S(2)}) copy-start(f32[2048]{0:T(1024)S(1)} %select_add_fusion.2) | copy-start | bytes 24580 | tf_op jit(solution)/shard_map/while
  313.5 2.4 copy-start.6
  313.5 11.6 %collective-permute-start.1 = (bf16[128,2048]{1,0:T(8,128)(2,1)}, bf16[128,2048]{1,0:T(8,128)(2,1)S(1)}, u32[]{:S(2)}, u32[]{:S(2)}) collective-permute-start(bf16[128,2048]{1,0:T(8,128)(2,1)} %get-tuple-element.1267), channel_id=1, source_target_pairs={{32,0},{64,32},{96,64},{128,96},{160,128},{192,160},{224,192},{33,... | collective-permute-start | bytes 1572872 | tf_op jit(solution)/shard_map/while/body/eval_jaxpr/ppermute | solution.py:272
  316.0 9.2 %copy-start.7 = (f32[2048]{0:T(1024)}, f32[2048]{0:T(1024)S(1)}, u32[]{:S(2)}) copy-start(f32[2048]{0:T(1024)S(1)} %select_add_fusion.2) | copy-start | bytes 24580 | tf_op jit(solution)/shard_map/while
  326.8 2.4 copy-start.6
  326.8 10.8 %collective-permute-start.1 = (bf16[128,2048]{1,0:T(8,128)(2,1)}, bf16[128,2048]{1,0:T(8,128)(2,1)S(1)}, u32[]{:S(2)}, u32[]{:S(2)}) collective-permute-start(bf16[128,2048]{1,0:T(8,128)(2,1)} %get-tuple-element.1267), channel_id=1, source_target_pairs={{32,0},{64,32},{96,64},{128,96},{160,128},{192,160},{224,192},{33,... | collective-permute-start | bytes 1572872 | tf_op jit(solution)/shard_map/while/body/eval_jaxpr/ppermute | solution.py:272
  329.2 8.4 %copy-start.7 = (f32[2048]{0:T(1024)}, f32[2048]{0:T(1024)S(1)}, u32[]{:S(2)}) copy-start(f32[2048]{0:T(1024)S(1)} %select_add_fusion.2) | copy-start | bytes 24580 | tf_op jit(solution)/shard_map/while
  339.3 2.4 copy-start.6
  339.3 14.9 %collective-permute-start.1 = (bf16[128,2048]{1,0:T(8,128)(2,1)}, bf16[128,2048]{1,0:T(8,128)(2,1)S(1)}, u32[]{:S(2)}, u32[]{:S(2)}) collective-permute-start(bf16[128,2048]{1,0:T(8,128)(2,1)} %get-tuple-element.1267), channel_id=1, source_target_pairs={{32,0},{64,32},{96,64},{128,96},{160,128},{192,160},{224,192},{33,... | collective-permute-start | bytes 1572872 | tf_op jit(solution)/shard_map/while/body/eval_jaxpr/ppermute | solution.py:272
  341.7 12.4 %copy-start.7 = (f32[2048]{0:T(1024)}, f32[2048]{0:T(1024)S(1)}, u32[]{:S(2)}) copy-start(f32[2048]{0:T(1024)S(1)} %select_add_fusion.2) | copy-start | bytes 24580 | tf_op jit(solution)/shard_map/while
  355.8 2.4 copy-start.6
  355.8 10.8 %collective-permute-start.1 = (bf16[128,2048]{1,0:T(8,128)(2,1)}, bf16[128,2048]{1,0:T(8,128)(2,1)S(1)}, u32[]{:S(2)}, u32[]{:S(2)}) collective-permute-start(bf16[128,2048]{1,0:T(8,128)(2,1)} %get-tuple-element.1267), channel_id=1, source_target_pairs={{32,0},{64,32},{96,64},{128,96},{160,128},{192,160},{224,192},{33,... | collective-permute-start | bytes 1572872 | tf_op jit(solution)/shard_map/while/body/eval_jaxpr/ppermute | solution.py:272
  358.2 8.4 %copy-start.7 = (f32[2048]{0:T(1024)}, f32[2048]{0:T(1024)S(1)}, u32[]{:S(2)}) copy-start(f32[2048]{0:T(1024)S(1)} %select_add_fusion.2) | copy-start | bytes 24580 | tf_op jit(solution)/shard_map/while
  368.3 2.4 copy-start.6
  368.3 10.9 %collective-permute-start.1 = (bf16[128,2048]{1,0:T(8,128)(2,1)}, bf16[128,2048]{1,0:T(8,128)(2,1)S(1)}, u32[]{:S(2)}, u32[]{:S(2)}) collective-permute-start(bf16[128,2048]{1,0:T(8,128)(2,1)} %get-tuple-element.1267), channel_id=1, source_target_pairs={{32,0},{64,32},{96,64},{128,96},{160,128},{192,160},{224,192},{33,... | collective-permute-start | bytes 1572872 | tf_op jit(solution)/shard_map/while/body/eval_jaxpr/ppermute | solution.py:272
  370.7 8.4 %copy-start.7 = (f32[2048]{0:T(1024)}, f32[2048]{0:T(1024)S(1)}, u32[]{:S(2)}) copy-start(f32[2048]{0:T(1024)S(1)} %select_add_fusion.2) | copy-start | bytes 24580 | tf_op jit(solution)/shard_map/while
  380.8 6.4 %copy-start.6 = (f32[2048]{0:T(1024)S(1)}, f32[2048]{0:T(1024)}, u32[]{:S(2)}) copy-start(f32[2048]{0:T(1024)} %get-tuple-element.1336) | copy-start | bytes 24580 | tf_op jit(solution)/shard_map/while
  380.8 109.3 %collective-permute-start.1 = (bf16[128,2048]{1,0:T(8,128)(2,1)}, bf16[128,2048]{1,0:T(8,128)(2,1)S(1)}, u32[]{:S(2)}, u32[]{:S(2)}) collective-permute-start(bf16[128,2048]{1,0:T(8,128)(2,1)} %get-tuple-element.1267), channel_id=1, source_target_pairs={{32,0},{64,32},{96,64},{128,96},{160,128},{192,160},{224,192},{33,... | collective-permute-start | bytes 1572872 | tf_op jit(solution)/shard_map/while/body/eval_jaxpr/ppermute | solution.py:272
  387.2 102.9 %copy-start.7 = (f32[2048]{0:T(1024)}, f32[2048]{0:T(1024)S(1)}, u32[]{:S(2)}) copy-start(f32[2048]{0:T(1024)S(1)} %select_add_fusion.2) | copy-start | bytes 24580 | tf_op jit(solution)/shard_map/while
  497.8 4.9 copy-start.4
  498.6 4.8 slice-start
  501.6 1.9 slice-start.1
  506.9 2.4 copy-start.6
  506.9 4.1 collective-permute-start.1
  509.3 1.7 copy-start.7
  511.1 3.9 collective-permute-start.3
  511.8 4.8 collective-permute-start.4
  513.1 3.9 collective-permute-start.5
  517.7 7.5 %collective-permute-start.7 = (f32[2048]{0:T(1024)S(1)}, f32[2048]{0:T(1024)S(1)}, u32[]{:S(2)}, u32[]{:S(2)}) collective-permute-start(f32[2048]{0:T(1024)S(1)} %bitcast.296), channel_id=1, source_target_pairs={{0,8},{1,9},{2,10},{3,11},{4,12},{5,13},{6,14},{7,15},{8,0},{9,1},... | collective-permute-start | bytes 24584 | tf_op jit(solution)/shard_map/ppermute | solution.py:127
  518.1 8.5 %collective-permute-start.8 = (f32[2048]{0:T(1024)S(1)}, f32[2048]{0:T(1024)S(1)}, u32[]{:S(2)}, u32[]{:S(2)}) collective-permute-start(f32[2048]{0:T(1024)S(1)} %bitcast.297), channel_id=1, source_target_pairs={{0,12},{1,13},{2,14},{3,15},{4,8},{5,9},{6,10},{7,11},{8,4},{9,5},... | collective-permute-start | bytes 24584 | tf_op jit(solution)/shard_map/ppermute | solution.py:127
  522.4 7.6 %collective-permute-start.6 = (f32[2048]{0:T(1024)S(1)}, f32[2048]{0:T(1024)S(1)}, u32[]{:S(2)}, u32[]{:S(2)}) collective-permute-start(f32[2048]{0:T(1024)S(1)} %bitcast.298), channel_id=1, source_target_pairs={{0,4},{1,5},{2,6},{3,7},{4,0},{5,1},{6,2},{7,3},{8,12},{9,13},{10,... | collective-permute-start | bytes 24584 | tf_op jit(solution)/shard_map/ppermute | solution.py:127
  530.1 5.2 collective-permute-start.9
  (2 other events, 2.6 us)
Sparse Core Ops, SparseCore 0:
  11.1 96.9 all-gather.3
  110.8 78.4 all-gather.5
